TPU v7x, 256 devices: a whole 4x4x8 slice. The times are simulated.
256 devices in a mesh: gx: 8 (over x, core), gy: 4 (over y), gz: 8 (over z).
Axes of the slice: x: 4, y: 4, z: 8, core: 2. Of those that a mesh axis runs over, the one named last changes fastest.
Arguments:
- e_field: float32 [3, 256, 64, 1024], P(None, 'gx', 'gy', 'gz'), may hold values from -6 to 6
- h_field: float32 [3, 256, 64, 1024], P(None, 'gx', 'gy', 'gz'), may hold values from -6 to 6
- inv_permittivity: float32 [256, 64, 1024], P('gx', 'gy', 'gz'), may hold values from 0.0833 to 1
- dft_sums: float32 [32, 256, 64, 128], P('gz', 'gx', 'gy'), may hold values from -6 to 6
- omega: float32 [16], replicated, may hold values from 0.2 to 3
- port_z: int32 [32], P('gz'), may hold values from 0 to 1023, as said below
- mode_profiles: bfloat16 [32, 2, 4, 256, 64], P('gz'), may hold values from -0.0234375 to 0.0234375
Outputs:
- e_out: float32 [3, 256, 64, 1024], P(None, 'gx', 'gy', 'gz')
- h_out: float32 [3, 256, 64, 1024], P(None, 'gx', 'gy', 'gz')
- dft_out: float32 [32, 256, 64, 128], P('gz', 'gx', 'gy')
- intersections: float32 [64, 8, 4], P(('gx', 'gy'), 'gz')
Inputs may be any that keep to these rules, and one draw needn't show every extreme that they name: `port_z`: port k lies in the slab of the third dimension that holds cells k // 4 * 128 to that plus 128 - 1.
All inputs are finite; a program needn't handle non-finite values.
Results may differ from a plain program's by a relative error of at most 0.0003.
Values sent between devices are 32-bit elements; how exact they have to be, the bound alone decides.
No kernel may reach another device: no remote copies, remote signals or barrier semaphores. Data moves between devices by JAX's collectives and lax.ppermute only.
A program may use at most 64 MiB of HBM per device.

v0:
```python
import jax
import jax.numpy as jnp
from jax import lax
from jax.sharding import PartitionSpec as P

STEPS = 2
NF = 16
MODES = 2


def shifted(value, axis, steps):
    count = lax.axis_size(axis)
    first, last = (max(0, -steps), min(count, count - steps))
    return lax.ppermute(value, axis, [(source, source + steps) for source in range(first, last)])


def rim_x(face, offset):
    return shifted(face, "gx", offset)


def rim_y(face, offset):
    return shifted(face, "gy", offset)


def rim_z(face, offset):
    return shifted(face, "gz", offset)


def forward(part, dim, mover):
    first = lax.slice_in_dim(part, 0, 1, axis=dim)
    after = mover(first, -1)
    rest = lax.slice_in_dim(part, 1, part.shape[dim], axis=dim)
    return jnp.concatenate([rest, after], axis=dim) - part


def backward(part, dim, mover):
    count = part.shape[dim]
    last = lax.slice_in_dim(part, count - 1, count, axis=dim)
    before = mover(last, 1)
    rest = lax.slice_in_dim(part, 0, count - 1, axis=dim)
    return part - jnp.concatenate([before, rest], axis=dim)


def curl(field, differ):
    along_x = differ(field[1:3], 1, rim_x)
    along_y = differ(jnp.stack([field[0], field[2]]), 2, rim_y)
    along_z = differ(field[0:2], 3, rim_z)
    return jnp.stack([along_y[1] - along_z[1], along_z[0] - along_x[1], along_x[0] - along_y[0]])


def per_device(e_field, h_field, inv_permittivity, dft_sums, omega, port_z, mode_profiles):
    cells_x = e_field.shape[1]
    cells_y = e_field.shape[2]
    cells_z = e_field.shape[3]
    ports_here = dft_sums.shape[0]
    local_z = port_z - lax.axis_index("gz") * cells_z
    select = (local_z[:, None] == jnp.arange(cells_z)[None, :]).astype(jnp.float32)
    e_now = e_field
    h_now = h_field
    dft = dft_sums
    for step in range(STEPS):
        h_now = h_now - 0.5 * curl(e_now, forward)
        e_now = e_now + 0.5 * inv_permittivity * curl(h_now, backward)
        tangent = jnp.stack([e_now[0], e_now[1], h_now[0], h_now[1]])
        planes = jnp.einsum("cxyz,pz->pxyc", tangent, select, precision=lax.Precision.HIGHEST)
        phase = omega * jnp.float32(step + 1)
        trig = jnp.stack([jnp.cos(phase), jnp.sin(phase)])
        increment = planes[:, :, :, :, None, None] * trig[None, None, None, None, :, :]
        dft = dft + increment.reshape(dft.shape)
    shaped = dft.reshape(ports_here, cells_x, cells_y, 4, 2, NF)
    groups = lax.axis_size(("gx", "gy"))
    owned = ports_here * NF // groups
    start_x = lax.axis_index("gx") * cells_x
    start_y = lax.axis_index("gy") * cells_y
    tile = lax.dynamic_slice(
        mode_profiles, (0, 0, 0, start_x, start_y), (ports_here, MODES, 4, cells_x, cells_y)
    )
    partial_sums = jnp.einsum(
        "pxycqf,pmcxy->pfmq", shaped, tile.astype(jnp.float32), precision=lax.Precision.HIGHEST
    )
    partial_sums = partial_sums.reshape(ports_here * NF, MODES * 2)
    result = lax.psum_scatter(partial_sums, ("gx", "gy"), scatter_dimension=0, tiled=True)
    return (e_now, h_now, dft, result.reshape(owned, 1, MODES * 2))


def solution(mesh):
    return jax.shard_map(
        per_device,
        mesh=mesh,
        in_specs=(
            P(None, "gx", "gy", "gz"),
            P(None, "gx", "gy", "gz"),
            P("gx", "gy", "gz"),
            P("gz", "gx", "gy", None),
            P(),
            P("gz"),
            P("gz", None, None, None, None),
        ),
        out_specs=(
            P(None, "gx", "gy", "gz"),
            P(None, "gx", "gy", "gz"),
            P("gz", "gx", "gy", None),
            P(("gx", "gy"), "gz", None),
        ),
        check_vma=False,
    )
```

profile of v0, /device:TPU:96, one launch (start us, length us, event | category | flops | bytes accessed | tf_op | source)
XLA Modules:
  0.0 171.8 jit_solution(12466478576555549716)
XLA Ops:
  0.7 1.5 copy.61
  2.3 0.6 fusion.28
  2.9 1.3 collective-permute-start
  4.2 0.8 slice.295
  5.0 2.0 %collective-permute-start.1 = (f32[2,32,16,1]{3,1,2,0:T(8,128)}, f32[2,32,16,1]{3,1,2,0:T(8,128)}, u32[]{:S(2)}, u32[]{:S(2)}) collective-permute-start(f32[2,32,16,1]{3,1,2,0:T(8,128)} %slice.295), channel_id=1, source_target_pairs={{1,0},{2,1},{3,2},{4,3},{5,4},{6,5},{7,6},{9,8},{10,9},{11,10},{12... | collective-permute-start | bytes 12296 | tf_op jit(solution)/shard_map/ppermute | solution.py:14
  7.0 0.6 slice.233
  7.6 1.3 collective-permute-start.2
  8.9 0.8 fusion.24
  9.7 0.7 broadcast_multiply_fusion
  10.5 0.5 broadcast_subtract_fusion
  11.2 0.6 pad_maximum_fusion.4
  11.7 1.0 slice.294
  12.7 0.8 slice.299
  13.6 1.0 copy.51
  14.6 0.6 mul.85
  15.2 1.4 mul.86
  16.6 1.3 mul.92
  17.8 1.3 mul.93
  19.1 3.6 %copy.63 = f32[4,32,16,128]{1,3,2,0:T(8,128)} copy(f32[4,32,16,128]{3,2,1,0:T(8,128)} %param.10) | data formatting | bytes 2097152 | tf_op args[3]
  22.7 1.3 dynamic-slice
  24.6 1.7 slice_subtract_fusion.4
  26.3 1.1 fusion.20
  27.6 0.3 fusion.13
  28.2 5.0 %collective-permute-start.4 = (f32[2,32,16,1]{3,1,2,0:T(8,128)S(1)}, f32[2,32,16,1]{3,1,2,0:T(8,128)S(1)}, u32[]{:S(2)}, u32[]{:S(2)}) collective-permute-start(f32[2,32,16,1]{3,1,2,0:T(8,128)S(1)} %slice.312), channel_id=1, source_target_pairs={{0,1},{1,2},{2,3},{3,4},{4,5},{5,6},{6,7},{8,9},{9,10},{10,11},{11... | collective-permute-start | bytes 12296 | tf_op jit(solution)/shard_map/ppermute | solution.py:14
  33.3 2.8 %collective-permute-start.5 = (f32[2,1,16,128]{3,1,2,0:T(1,128)S(1)}, f32[2,1,16,128]{3,1,2,0:T(1,128)S(1)}, u32[]{:S(2)}, u32[]{:S(2)}) collective-permute-start(f32[2,1,16,128]{3,1,2,0:T(1,128)S(1)} %slice.317), channel_id=1, source_target_pairs={{0,32},{32,64},{64,96},{96,128},{128,160},{160,192},{192,224},{1,3... | collective-permute-start | bytes 49160 | tf_op jit(solution)/shard_map/ppermute | solution.py:14
  36.2 4.5 %collective-permute-start.3 = (f32[2,32,1,128]{3,1,2,0:T(8,128)S(1)}, f32[2,32,1,128]{3,1,2,0:T(8,128)S(1)}, u32[]{:S(2)}, u32[]{:S(2)}) collective-permute-start(f32[2,32,1,128]{3,1,2,0:T(8,128)S(1)} %fusion.27), channel_id=1, source_target_pairs={{0,8},{8,16},{16,24},{1,9},{9,17},{17,25},{2,10},{10,18},{18,26},{... | collective-permute-start | bytes 98312 | tf_op jit(solution)/shard_map/ppermute | solution.py:14
  40.7 4.7 %collective-permute-done.4 = f32[2,32,16,1]{3,1,2,0:T(8,128)S(1)} collective-permute-done((f32[2,32,16,1]{3,1,2,0:T(8,128)S(1)}, f32[2,32,16,1]{3,1,2,0:T(8,128)S(1)}, u32[]{:S(2)}, u32[]{:S(2)}) %collective-permute-start.4) | collective-permute-done | bytes 4128 | tf_op jit(solution)/shard_map/ppermute | solution.py:14
  45.9 0.4 fusion.14
  46.4 1.9 %collective-permute-start.7 = (f32[2,32,16,1]{3,1,2,0:T(8,128)S(1)}, f32[2,32,16,1]{3,1,2,0:T(8,128)S(1)}, u32[]{:S(2)}, u32[]{:S(2)}) collective-permute-start(f32[2,32,16,1]{3,1,2,0:T(8,128)S(1)} %slice.330), channel_id=1, source_target_pairs={{1,0},{2,1},{3,2},{4,3},{5,4},{6,5},{7,6},{9,8},{10,9},{11,10},{12... | collective-permute-start | bytes 12296 | tf_op jit(solution)/shard_map/ppermute | solution.py:14
  48.4 1.3 collective-permute-start.8
  50.0 1.3 collective-permute-start.6
  51.3 13.0 %collective-permute-done.7 = f32[2,32,16,1]{3,1,2,0:T(8,128)S(1)} collective-permute-done((f32[2,32,16,1]{3,1,2,0:T(8,128)S(1)}, f32[2,32,16,1]{3,1,2,0:T(8,128)S(1)}, u32[]{:S(2)}, u32[]{:S(2)}) %collective-permute-start.7) | collective-permute-done | bytes 4128 | tf_op jit(solution)/shard_map/ppermute | solution.py:14
  64.2 0.3 fusion.36
  64.5 2.1 %convolution_bitcast_fusion.1 = f32[4,32,16,4]{1,0,2,3:T(4,128)S(1)} fusion(f32[2,32,16,128]{3,1,2,0:T(8,128)S(1)} %get-tuple-element.19, f32[2,32,16,128]{3,1,2,0:T(8,128)S(1)} %get-tuple-element.16, s32[4]{0:T(128)S(1)} %copy-done.5), kind=kOutput, calls=%fused_computation.7 | convolution fusion | flops 12845568 | bytes 1081360 | tf_op jit(solution)/shard_map/cxyz,pz->pxyc/dot_general | solution.py:65
  67.1 0.4 fusion.15
  67.7 3.6 %collective-permute-start.10 = (f32[2,32,16,1]{3,1,2,0:T(8,128)S(1)}, f32[2,32,16,1]{3,1,2,0:T(8,128)S(1)}, u32[]{:S(2)}, u32[]{:S(2)}) collective-permute-start(f32[2,32,16,1]{3,1,2,0:T(8,128)S(1)} %slice.348), channel_id=1, source_target_pairs={{0,1},{1,2},{2,3},{3,4},{4,5},{5,6},{6,7},{8,9},{9,10},{10,11},{11... | collective-permute-start | bytes 12296 | tf_op jit(solution)/shard_map/ppermute | solution.py:14
  71.4 1.3 collective-permute-start.11
  72.8 1.3 copy.70
  74.1 4.7 %collective-permute-start.9 = (f32[2,32,1,128]{3,1,2,0:T(8,128)S(1)}, f32[2,32,1,128]{3,1,2,0:T(8,128)S(1)}, u32[]{:S(2)}, u32[]{:S(2)}) collective-permute-start(f32[2,32,1,128]{3,1,2,0:T(8,128)S(1)} %fusion.25), channel_id=1, source_target_pairs={{0,8},{8,16},{16,24},{1,9},{9,17},{17,25},{2,10},{10,18},{18,26},{... | collective-permute-start | bytes 98312 | tf_op jit(solution)/shard_map/ppermute | solution.py:14
  78.9 4.2 %collective-permute-done.10 = f32[2,32,16,1]{3,1,2,0:T(8,128)S(1)} collective-permute-done((f32[2,32,16,1]{3,1,2,0:T(8,128)S(1)}, f32[2,32,16,1]{3,1,2,0:T(8,128)S(1)}, u32[]{:S(2)}, u32[]{:S(2)}) %collective-permute-start.10) | collective-permute-done | bytes 4128 | tf_op jit(solution)/shard_map/ppermute | solution.py:14
  83.6 0.5 fusion.16
  84.2 1.3 copy.69
  85.5 2.1 %convolution_bitcast_fusion = f32[4,32,16,4]{1,0,2,3:T(4,128)S(1)} fusion(f32[2,32,16,128]{3,1,2,0:T(8,128)S(1)} %get-tuple-element.22, f32[2,32,16,128]{3,1,2,0:T(8,128)S(1)} %slice.358, s32[4]{0:T(128)S(1)} %copy-done.5), kind=kOutput, calls=%fused_computation.6 | convolution fusion | flops 12845568 | bytes 1081360 | tf_op jit(solution)/shard_map/cxyz,pz->pxyc/dot_general | solution.py:65
  87.8 2.9 %fusion = f32[4,32,16,128]{1,3,2,0:T(8,128)} fusion(f32[4,32,16,128]{1,3,2,0:T(8,128)S(1)} %copy-done.1, f32[128]{0:T(128)S(1)} %copy-done.7, f32[4,32,16,4]{1,3,2,0:T(4,128)S(1)} %copy.64, f32[128]{0:T(128)S(1)} %copy-done.6, f32[4,32,16,4]{1,3,2,0:T(4,128)S(1)} %copy.62), kind=kLoop, calls=%fused_computation.1 | loop fusion | flops 1048576 | bytes 2163712 | tf_op jit(solution)/shard_map/add | solution.py:69
  90.7 3.6 %copy.71 = f32[4,32,16,128]{3,2,1,0:T(8,128)} copy(f32[4,32,16,128]{1,3,2,0:T(8,128)} %fusion) | data formatting | bytes 2097152
  94.3 9.6 %fusion.4 = f32[4,16,2,2]{1,2,3,0:T(2,128)S(1)} fusion(f32[4,32,16,4,2,16]{1,5,4,3,2,0:T(8,128)} %bitcast.48, bf16[4,2,4,32,16]{3,4,2,1,0:T(8,128)(2,1)S(1)} %constant_dynamic-slice_fusion), kind=kOutput, calls=%fused_computation.8 | convolution fusion | flops 6291456 | bytes 1082368 | tf_op jit(solution)/shard_map/pxycqf,pmcxy->pfmq/dot_general | solution.py:78
  104.0 67.1 %all-reduce = f32[64,4]{0,1:T(4,128)S(1)} all-reduce(f32[64,4]{0,1:T(4,128)S(1)} %reshape.30), channel_id=2, replica_groups=mesh['gx'=8,'gy'=4,'gz'=8] {'gx','gy'}, use_global_device_ids=true, to_apply=%region_0.0.clone | all-reduce | flops 256 | bytes 2048
  171.1 0.7 copy.72
  (68 shorter events, 3.2 us)
Async XLA Ops:
  0.6 10.4 %copy-start = (bf16[4,2,4,256,64]{3,4,2,1,0:T(8,128)(2,1)S(1)}, bf16[4,2,4,256,64]{3,4,2,1,0:T(8,128)(2,1)}, u32[]{:S(2)}) copy-start(bf16[4,2,4,256,64]{3,4,2,1,0:T(8,128)(2,1)} %param.13) | copy-start | bytes 3145732
  0.6 6.4 %copy-start.2 = (f32[3,32,16,128]{3,2,1,0:T(8,128)S(1)}, f32[3,32,16,128]{3,2,1,0:T(8,128)}, u32[]{:S(2)}) copy-start(f32[3,32,16,128]{3,2,1,0:T(8,128)} %param.7) | copy-start | bytes 2359300
  0.7 9.1 %copy-start.4 = (f32[32,16,128]{2,1,0:T(8,128)S(1)}, f32[32,16,128]{2,1,0:T(8,128)}, u32[]{:S(2)}) copy-start(f32[32,16,128]{2,1,0:T(8,128)} %param.9) | copy-start | bytes 786436
  0.7 9.8 %copy-start.8 = (f32[16]{0:T(128)S(1)}, f32[16]{0:T(128)}, u32[]{:S(2)}) copy-start(f32[16]{0:T(128)} %param.11) | copy-start | bytes 196
  0.7 9.8 %copy-start.9 = (s32[4]{0:T(128)S(1)}, s32[4]{0:T(128)}, u32[]{:S(2)}) copy-start(s32[4]{0:T(128)} %param.12) | copy-start | bytes 52
  2.9 23.5 %collective-permute-start = (f32[2,32,1,128]{3,1,2,0:T(8,128)}, f32[2,32,1,128]{3,1,2,0:T(8,128)}, u32[]{:S(2)}, u32[]{:S(2)}) collective-permute-start(f32[2,32,1,128]{3,1,2,0:T(8,128)} %fusion.28), channel_id=1, source_target_pairs={{8,0},{16,8},{24,16},{9,1},{17,9},{25,17},{10,2},{18,10},{26,18},{... | collective-permute-start | bytes 98312 | tf_op jit(solution)/shard_map/ppermute | solution.py:14
  5.0 19.6 %collective-permute-start.1 = (f32[2,32,16,1]{3,1,2,0:T(8,128)}, f32[2,32,16,1]{3,1,2,0:T(8,128)}, u32[]{:S(2)}, u32[]{:S(2)}) collective-permute-start(f32[2,32,16,1]{3,1,2,0:T(8,128)} %slice.295), channel_id=1, source_target_pairs={{1,0},{2,1},{3,2},{4,3},{5,4},{6,5},{7,6},{9,8},{10,9},{11,10},{12... | collective-permute-start | bytes 12296 | tf_op jit(solution)/shard_map/ppermute | solution.py:14
  7.6 17.0 %collective-permute-start.2 = (f32[2,1,16,128]{3,1,2,0:T(1,128)}, f32[2,1,16,128]{3,1,2,0:T(1,128)S(1)}, u32[]{:S(2)}, u32[]{:S(2)}) collective-permute-start(f32[2,1,16,128]{3,1,2,0:T(1,128)} %bitcast), channel_id=1, source_target_pairs={{32,0},{64,32},{96,64},{128,96},{160,128},{192,160},{224,192},{33,... | collective-permute-start | bytes 49160 | tf_op jit(solution)/shard_map/ppermute | solution.py:14
  24.6 3.1 %copy-start.3 = (f32[3,32,16,128]{3,2,1,0:T(8,128)S(1)}, f32[3,32,16,128]{3,2,1,0:T(8,128)}, u32[]{:S(2)}) copy-start(f32[3,32,16,128]{3,2,1,0:T(8,128)} %param.8) | copy-start | bytes 2359300
  28.2 17.2 %collective-permute-start.4 = (f32[2,32,16,1]{3,1,2,0:T(8,128)S(1)}, f32[2,32,16,1]{3,1,2,0:T(8,128)S(1)}, u32[]{:S(2)}, u32[]{:S(2)}) collective-permute-start(f32[2,32,16,1]{3,1,2,0:T(8,128)S(1)} %slice.312), channel_id=1, source_target_pairs={{0,1},{1,2},{2,3},{3,4},{4,5},{5,6},{6,7},{8,9},{9,10},{10,11},{11... | collective-permute-start | bytes 12296 | tf_op jit(solution)/shard_map/ppermute | solution.py:14
  33.3 12.1 %collective-permute-start.5 = (f32[2,1,16,128]{3,1,2,0:T(1,128)S(1)}, f32[2,1,16,128]{3,1,2,0:T(1,128)S(1)}, u32[]{:S(2)}, u32[]{:S(2)}) collective-permute-start(f32[2,1,16,128]{3,1,2,0:T(1,128)S(1)} %slice.317), channel_id=1, source_target_pairs={{0,32},{32,64},{64,96},{96,128},{128,160},{160,192},{192,224},{1,3... | collective-permute-start | bytes 49160 | tf_op jit(solution)/shard_map/ppermute | solution.py:14
  36.2 9.5 %collective-permute-start.3 = (f32[2,32,1,128]{3,1,2,0:T(8,128)S(1)}, f32[2,32,1,128]{3,1,2,0:T(8,128)S(1)}, u32[]{:S(2)}, u32[]{:S(2)}) collective-permute-start(f32[2,32,1,128]{3,1,2,0:T(8,128)S(1)} %fusion.27), channel_id=1, source_target_pairs={{0,8},{8,16},{16,24},{1,9},{9,17},{17,25},{2,10},{10,18},{18,26},{... | collective-permute-start | bytes 98312 | tf_op jit(solution)/shard_map/ppermute | solution.py:14
  46.4 18.1 %copy-start.5 = (s32[4]{0:T(128)S(1)}, s32[4]{0:T(128)}, u32[]{:S(2)}) copy-start(s32[4]{0:T(128)} %broadcast_subtract_fusion) | copy-start | bytes 52
  46.4 17.8 %collective-permute-start.7 = (f32[2,32,16,1]{3,1,2,0:T(8,128)S(1)}, f32[2,32,16,1]{3,1,2,0:T(8,128)S(1)}, u32[]{:S(2)}, u32[]{:S(2)}) collective-permute-start(f32[2,32,16,1]{3,1,2,0:T(8,128)S(1)} %slice.330), channel_id=1, source_target_pairs={{1,0},{2,1},{3,2},{4,3},{5,4},{6,5},{7,6},{9,8},{10,9},{11,10},{12... | collective-permute-start | bytes 12296 | tf_op jit(solution)/shard_map/ppermute | solution.py:14
  48.4 15.9 %collective-permute-start.8 = (f32[2,1,16,128]{3,1,2,0:T(1,128)S(1)}, f32[2,1,16,128]{3,1,2,0:T(1,128)S(1)}, u32[]{:S(2)}, u32[]{:S(2)}) collective-permute-start(f32[2,1,16,128]{3,1,2,0:T(1,128)S(1)} %slice.335), channel_id=1, source_target_pairs={{32,0},{64,32},{96,64},{128,96},{160,128},{192,160},{224,192},{33,... | collective-permute-start | bytes 49160 | tf_op jit(solution)/shard_map/ppermute | solution.py:14
  50.0 16.8 %collective-permute-start.6 = (f32[2,32,1,128]{3,1,2,0:T(8,128)S(1)}, f32[2,32,1,128]{3,1,2,0:T(8,128)S(1)}, u32[]{:S(2)}, u32[]{:S(2)}) collective-permute-start(f32[2,32,1,128]{3,1,2,0:T(8,128)S(1)} %fusion.26), channel_id=1, source_target_pairs={{8,0},{16,8},{24,16},{9,1},{17,9},{25,17},{10,2},{18,10},{26,18},{... | collective-permute-start | bytes 98312 | tf_op jit(solution)/shard_map/ppermute | solution.py:14
  67.7 15.3 %collective-permute-start.10 = (f32[2,32,16,1]{3,1,2,0:T(8,128)S(1)}, f32[2,32,16,1]{3,1,2,0:T(8,128)S(1)}, u32[]{:S(2)}, u32[]{:S(2)}) collective-permute-start(f32[2,32,16,1]{3,1,2,0:T(8,128)S(1)} %slice.348), channel_id=1, source_target_pairs={{0,1},{1,2},{2,3},{3,4},{4,5},{5,6},{6,7},{8,9},{9,10},{10,11},{11... | collective-permute-start | bytes 12296 | tf_op jit(solution)/shard_map/ppermute | solution.py:14
  71.4 11.7 %collective-permute-start.11 = (f32[2,1,16,128]{3,1,2,0:T(1,128)S(1)}, f32[2,1,16,128]{3,1,2,0:T(1,128)S(1)}, u32[]{:S(2)}, u32[]{:S(2)}) collective-permute-start(f32[2,1,16,128]{3,1,2,0:T(1,128)S(1)} %slice.353), channel_id=1, source_target_pairs={{0,32},{32,64},{64,96},{96,128},{128,160},{160,192},{192,224},{1,3... | collective-permute-start | bytes 49160 | tf_op jit(solution)/shard_map/ppermute | solution.py:14
  74.1 9.2 %collective-permute-start.9 = (f32[2,32,1,128]{3,1,2,0:T(8,128)S(1)}, f32[2,32,1,128]{3,1,2,0:T(8,128)S(1)}, u32[]{:S(2)}, u32[]{:S(2)}) collective-permute-start(f32[2,32,1,128]{3,1,2,0:T(8,128)S(1)} %fusion.25), channel_id=1, source_target_pairs={{0,8},{8,16},{16,24},{1,9},{9,17},{17,25},{2,10},{10,18},{18,26},{... | collective-permute-start | bytes 98312 | tf_op jit(solution)/shard_map/ppermute | solution.py:14
  83.6 4.2 %copy-start.1 = (f32[4,32,16,128]{1,3,2,0:T(8,128)S(1)}, f32[4,32,16,128]{1,3,2,0:T(8,128)}, u32[]{:S(2)}) copy-start(f32[4,32,16,128]{1,3,2,0:T(8,128)} %copy.63) | copy-start | bytes 3145732
  83.6 4.2 %copy-start.6 = (f32[128]{0:T(128)S(1)}, f32[128]{0:T(128)}, u32[]{:S(2)}) copy-start(f32[128]{0:T(128)} %mul.86) | copy-start | bytes 1540
  83.6 4.2 %copy-start.7 = (f32[128]{0:T(128)S(1)}, f32[128]{0:T(128)}, u32[]{:S(2)}) copy-start(f32[128]{0:T(128)} %mul.93) | copy-start | bytes 1540
where the time goes:
time: 172 us
  blocking collectives  67.1 us (39%)
  starting transfers between devices  31.1 us (18%)
  local copies, waits for them, and re-layouts  23.8 us (14%)
  waiting for transfers between devices  21.8 us (13%)
  matrix products  13.9 us (8%)
  other arithmetic  12.4 us (7%)
  between operations  1.8 us (1%)
    unnamed x1, blocking collectives  67.1 us
    ppermute x12, starting transfers between devices, shifted(): lax.ppermute(value, axis, [(source, source + steps) for source in range(f...  31.1 us
    ppermute x12, waiting for transfers between devices, shifted(): lax.ppermute(value, axis, [(source, source + steps) for source in range(f...  21.8 us
    unnamed x27, local copies, waits for them, and re-layouts  13.4 us
    dot_general x1, matrix products, per_device(): jnp.einsum('pxycqf,pmcxy->pfmq', shaped, tile.astype(jnp.float32), precis...  9.57 us
    mul x4, local copies, waits for them, and re-layouts, per_device(): planes[:, :, :, :, None, None] * trig[None, None, None, None, :, :]  4.5 us
    dot_general x2, matrix products, per_device(): jnp.einsum('cxyz,pz->pxyc', tangent, select, precision=lax.Precision.HIGH...  4.29 us
  transfers between devices with their start and end apart: 12, of which 3 were waited for; matrix products, arithmetic and copies ran while one was open for 13% of the time, Pallas kernels for 0%

commit v1 on v0

--- a/solution.py
+++ b/solution.py
@@ -79,7 +79,8 @@
         "pxycqf,pmcxy->pfmq", shaped, tile.astype(jnp.float32), precision=lax.Precision.HIGHEST
     )
     partial_sums = partial_sums.reshape(ports_here * NF, MODES * 2)
-    result = lax.psum_scatter(partial_sums, ("gx", "gy"), scatter_dimension=0, tiled=True)
+    pieces = partial_sums.reshape(groups, owned, MODES * 2)
+    result = jnp.sum(lax.all_to_all(pieces, ("gx", "gy"), 0, 0, tiled=False), axis=0)
     return (e_now, h_now, dft, result.reshape(owned, 1, MODES * 2))
 
 

time: 172 us -> 114 us (0.66)
  blocking collectives: 67.1 us -> 0 us
  starting transfers between devices: 31.1 us -> 39.8 us
  waiting for transfers between devices: 21.8 us -> 24.1 us
  matrix products: 13.9 us -> 11.7 us
    unnamed x1 -> x0, blocking collectives: 67.1 us -> none
    all_to_all x0 -> x1, starting transfers between devices: none -> 8.56 us  [per_device(): lax.all_to_all(pieces, ('gx', 'gy'), 0, 0, tiled=False)]
    dot_general x1, matrix products: 9.57 us -> 7.38 us  [per_device(): jnp.einsum('pxycqf,pmcxy->pfmq', shaped, tile.astype(jnp.float32), precis...]
    add x1, other arithmetic: 2.89 us -> 1.16 us  [per_device(): dft = dft + increment.reshape(dft.shape)]
    unnamed x27 -> x33, local copies, waits for them, and re-layouts: 13.4 us -> 14.2 us
  transfers between devices with their start and end apart: 12 -> 13, of which waited for: 3 -> 4; matrix products, arithmetic and copies ran while one was open for 13% -> 24% of each run, Pallas kernels for 0% -> 0%
where the time goes in v1:
time: 114 us; the launch traced here: 113 us
  starting transfers between devices  39.8 us (35%)
  local copies, waits for them, and re-layouts  25.3 us (22%)
  waiting for transfers between devices  24.1 us (21%)
  matrix products  11.7 us (10%)
  other arithmetic  10.7 us (9%)
  between operations  1.27 us (1%)
    ppermute x12, starting transfers between devices, shifted(): lax.ppermute(value, axis, [(source, source + steps) for source in range(f...  31.2 us
    ppermute x12, waiting for transfers between devices, shifted(): lax.ppermute(value, axis, [(source, source + steps) for source in range(f...  23 us
    unnamed x33, local copies, waits for them, and re-layouts  14.2 us
    all_to_all x1, starting transfers between devices, per_device(): lax.all_to_all(pieces, ('gx', 'gy'), 0, 0, tiled=False)  8.56 us
    dot_general x1, matrix products, per_device(): jnp.einsum('pxycqf,pmcxy->pfmq', shaped, tile.astype(jnp.float32), precis...  7.38 us
    mul x4, local copies, waits for them, and re-layouts, per_device(): planes[:, :, :, :, None, None] * trig[None, None, None, None, :, :]  4.51 us
    dot_general x2, matrix products, per_device(): jnp.einsum('cxyz,pz->pxyc', tangent, select, precision=lax.Precision.HIGH...  4.29 us
    sub x3, other arithmetic, forward(): return jnp.concatenate([rest, after], axis=dim) - part  2.93 us
  transfers between devices with their start and end apart: 13, of which 4 were waited for; matrix products, arithmetic and copies ran while one was open for 24% of the time, Pallas kernels for 0%

profile of v1, /device:TPU:96, one launch (start us, length us, event | category | flops | bytes accessed | tf_op | source)
XLA Modules:
  0.0 112.8 jit_solution(4295984849657920862)
XLA Ops:
  0.7 1.5 %copy.60 = f32[3,32,16,128]{3,1,2,0:T(8,128)S(1)} copy(f32[3,32,16,128]{3,2,1,0:T(8,128)} %param.7) | data formatting | bytes 1572864 | tf_op args[0]
  2.3 0.6 fusion.28
  2.9 1.3 %collective-permute-start = (f32[2,32,1,128]{3,1,2,0:T(8,128)}, f32[2,32,1,128]{3,1,2,0:T(8,128)}, u32[]{:S(2)}, u32[]{:S(2)}) collective-permute-start(f32[2,32,1,128]{3,1,2,0:T(8,128)} %fusion.28), channel_id=1, source_target_pairs={{8,0},{16,8},{24,16},{9,1},{17,9},{25,17},{10,2},{18,10},{26,18},{... | collective-permute-start | bytes 98312 | tf_op jit(solution)/shard_map/ppermute | solution.py:14
  4.2 0.8 slice.295
  5.0 2.0 %collective-permute-start.1 = (f32[2,32,16,1]{3,1,2,0:T(8,128)}, f32[2,32,16,1]{3,1,2,0:T(8,128)}, u32[]{:S(2)}, u32[]{:S(2)}) collective-permute-start(f32[2,32,16,1]{3,1,2,0:T(8,128)} %slice.295), channel_id=1, source_target_pairs={{1,0},{2,1},{3,2},{4,3},{5,4},{6,5},{7,6},{9,8},{10,9},{11,10},{12... | collective-permute-start | bytes 12296 | tf_op jit(solution)/shard_map/ppermute | solution.py:14
  7.0 0.6 slice.233
  7.6 1.3 %collective-permute-start.2 = (f32[2,1,16,128]{3,1,2,0:T(1,128)}, f32[2,1,16,128]{3,1,2,0:T(1,128)S(1)}, u32[]{:S(2)}, u32[]{:S(2)}) collective-permute-start(f32[2,1,16,128]{3,1,2,0:T(1,128)} %bitcast), channel_id=1, source_target_pairs={{32,0},{64,32},{96,64},{128,96},{160,128},{192,160},{224,192},{33,... | collective-permute-start | bytes 49160 | tf_op jit(solution)/shard_map/ppermute | solution.py:14
  8.9 0.8 fusion.24
  9.8 0.7 broadcast_multiply_fusion
  10.5 0.5 broadcast_subtract_fusion
  11.2 0.6 pad_maximum_fusion.4
  11.7 1.0 slice.294
  12.7 0.8 slice.299
  13.6 1.0 copy.50
  14.6 0.6 mul.85
  15.2 1.3 %mul.86 = f32[128]{0:T(128)} reshape(f32[4,2,16]{2,1,0:T(2,128)} %mul.85) | data formatting | bytes 1024 | tf_op jit(solution)/shard_map/mul | solution.py:68
  16.6 1.3 %mul.92 = f32[4,2,16]{2,1,0:T(2,128)} broadcast(f32[2,16]{1,0:T(2,128)} %get-tuple-element.52), dimensions={1,2} | broadcast | bytes 640 | tf_op jit(solution)/shard_map/mul | solution.py:68
  17.9 1.3 %mul.93 = f32[128]{0:T(128)} reshape(f32[4,2,16]{2,1,0:T(2,128)} %mul.92) | data formatting | bytes 1024 | tf_op jit(solution)/shard_map/mul | solution.py:68
  19.1 3.6 %copy.62 = f32[4,32,16,128]{1,3,2,0:T(8,128)} copy(f32[4,32,16,128]{3,2,1,0:T(8,128)} %param.10) | data formatting | bytes 2097152 | tf_op args[3]
  22.8 1.7 %slice_subtract_fusion.4 = (f32[2,32,16,128]{3,1,2,0:T(8,128)S(1)}, f32[2,32,16,128]{3,1,2,0:T(8,128)S(1)}) fusion(f32[3,32,16,128]{3,1,2,0:T(8,128)S(1)} %copy.60, f32[2,32,16,1]{3,1,2,0:T(8,128)} %collective-permute-done.1, f32[2,32,16,127]{3,1,2,0:T(8,128)} %slice.294, f32[2,1,16,128]{3,1,2,0:T(1,128)S(1)} %collective-permute-done.2, ...), kind=kLoop, calls=%fused_computation.51 | loop fusion | flops 524288 | bytes 3145728 | tf_op jit(solution)/shard_map/sub | solution.py:33
  24.5 1.1 %fusion.20 = f32[2,32,16,128]{3,1,2,0:T(8,128)S(1)} fusion(f32[1,32,16,128]{3,1,2,0:T(8,128)S(1)} %get-tuple-element.34, f32[1,32,16,128]{3,1,2,0:T(8,128)S(1)} %get-tuple-element.33, f32[2,32,1,128]{3,1,2,0:T(8,128)} %collective-permute-done, f32[2,32,15,128]{3,1,2,0:T(8,128)} %fusion.24), kind=kLoop, calls=%fused_computation.46 | loop fusion | flops 393216 | bytes 1572864 | tf_op jit(solution)/shard_map/sub | solution.py:33
  26.4 5.0 %collective-permute-start.4 = (f32[2,32,16,1]{3,1,2,0:T(8,128)S(1)}, f32[2,32,16,1]{3,1,2,0:T(8,128)S(1)}, u32[]{:S(2)}, u32[]{:S(2)}) collective-permute-start(f32[2,32,16,1]{3,1,2,0:T(8,128)S(1)} %slice.312), channel_id=1, source_target_pairs={{0,1},{1,2},{2,3},{3,4},{4,5},{5,6},{6,7},{8,9},{9,10},{10,11},{11... | collective-permute-start | bytes 12296 | tf_op jit(solution)/shard_map/ppermute | solution.py:14
  31.4 2.8 %collective-permute-start.5 = (f32[2,1,16,128]{3,1,2,0:T(1,128)S(1)}, f32[2,1,16,128]{3,1,2,0:T(1,128)S(1)}, u32[]{:S(2)}, u32[]{:S(2)}) collective-permute-start(f32[2,1,16,128]{3,1,2,0:T(1,128)S(1)} %slice.317), channel_id=1, source_target_pairs={{0,32},{32,64},{64,96},{96,128},{128,160},{160,192},{192,224},{1,3... | collective-permute-start | bytes 49160 | tf_op jit(solution)/shard_map/ppermute | solution.py:14
  34.3 4.5 %collective-permute-start.3 = (f32[2,32,1,128]{3,1,2,0:T(8,128)S(1)}, f32[2,32,1,128]{3,1,2,0:T(8,128)S(1)}, u32[]{:S(2)}, u32[]{:S(2)}) collective-permute-start(f32[2,32,1,128]{3,1,2,0:T(8,128)S(1)} %fusion.27), channel_id=1, source_target_pairs={{0,8},{8,16},{16,24},{1,9},{9,17},{17,25},{2,10},{10,18},{18,26},{... | collective-permute-start | bytes 98312 | tf_op jit(solution)/shard_map/ppermute | solution.py:14
  38.9 4.7 %collective-permute-done.4 = f32[2,32,16,1]{3,1,2,0:T(8,128)S(1)} collective-permute-done((f32[2,32,16,1]{3,1,2,0:T(8,128)S(1)}, f32[2,32,16,1]{3,1,2,0:T(8,128)S(1)}, u32[]{:S(2)}, u32[]{:S(2)}) %collective-permute-start.4) | collective-permute-done | bytes 4128 | tf_op jit(solution)/shard_map/ppermute | solution.py:14
  44.1 0.4 fusion.14
  44.6 1.9 %collective-permute-start.7 = (f32[2,32,16,1]{3,1,2,0:T(8,128)S(1)}, f32[2,32,16,1]{3,1,2,0:T(8,128)S(1)}, u32[]{:S(2)}, u32[]{:S(2)}) collective-permute-start(f32[2,32,16,1]{3,1,2,0:T(8,128)S(1)} %slice.330), channel_id=1, source_target_pairs={{1,0},{2,1},{3,2},{4,3},{5,4},{6,5},{7,6},{9,8},{10,9},{11,10},{12... | collective-permute-start | bytes 12296 | tf_op jit(solution)/shard_map/ppermute | solution.py:14
  46.5 1.3 %collective-permute-start.8 = (f32[2,1,16,128]{3,1,2,0:T(1,128)S(1)}, f32[2,1,16,128]{3,1,2,0:T(1,128)S(1)}, u32[]{:S(2)}, u32[]{:S(2)}) collective-permute-start(f32[2,1,16,128]{3,1,2,0:T(1,128)S(1)} %slice.335), channel_id=1, source_target_pairs={{32,0},{64,32},{96,64},{128,96},{160,128},{192,160},{224,192},{33,... | collective-permute-start | bytes 49160 | tf_op jit(solution)/shard_map/ppermute | solution.py:14
  48.1 1.3 %collective-permute-start.6 = (f32[2,32,1,128]{3,1,2,0:T(8,128)S(1)}, f32[2,32,1,128]{3,1,2,0:T(8,128)S(1)}, u32[]{:S(2)}, u32[]{:S(2)}) collective-permute-start(f32[2,32,1,128]{3,1,2,0:T(8,128)S(1)} %fusion.26), channel_id=1, source_target_pairs={{8,0},{16,8},{24,16},{9,1},{17,9},{25,17},{10,2},{18,10},{26,18},{... | collective-permute-start | bytes 98312 | tf_op jit(solution)/shard_map/ppermute | solution.py:14
  49.4 13.0 %collective-permute-done.7 = f32[2,32,16,1]{3,1,2,0:T(8,128)S(1)} collective-permute-done((f32[2,32,16,1]{3,1,2,0:T(8,128)S(1)}, f32[2,32,16,1]{3,1,2,0:T(8,128)S(1)}, u32[]{:S(2)}, u32[]{:S(2)}) %collective-permute-start.7) | collective-permute-done | bytes 4128 | tf_op jit(solution)/shard_map/ppermute | solution.py:14
  62.7 2.1 %convolution_bitcast_fusion.1 = f32[4,32,16,4]{1,0,2,3:T(4,128)S(1)} fusion(f32[2,32,16,128]{3,1,2,0:T(8,128)S(1)} %get-tuple-element.19, f32[2,32,16,128]{3,1,2,0:T(8,128)S(1)} %get-tuple-element.16, s32[4]{0:T(128)S(1)} %copy-done.8), kind=kOutput, calls=%fused_computation.7 | convolution fusion | flops 12845568 | bytes 1081360 | tf_op jit(solution)/shard_map/cxyz,pz->pxyc/dot_general | solution.py:65
  65.2 0.4 fusion.15
  65.9 3.6 %collective-permute-start.10 = (f32[2,32,16,1]{3,1,2,0:T(8,128)S(1)}, f32[2,32,16,1]{3,1,2,0:T(8,128)S(1)}, u32[]{:S(2)}, u32[]{:S(2)}) collective-permute-start(f32[2,32,16,1]{3,1,2,0:T(8,128)S(1)} %slice.348), channel_id=1, source_target_pairs={{0,1},{1,2},{2,3},{3,4},{4,5},{5,6},{6,7},{8,9},{9,10},{10,11},{11... | collective-permute-start | bytes 12296 | tf_op jit(solution)/shard_map/ppermute | solution.py:14
  69.5 1.3 %collective-permute-start.11 = (f32[2,1,16,128]{3,1,2,0:T(1,128)S(1)}, f32[2,1,16,128]{3,1,2,0:T(1,128)S(1)}, u32[]{:S(2)}, u32[]{:S(2)}) collective-permute-start(f32[2,1,16,128]{3,1,2,0:T(1,128)S(1)} %slice.353), channel_id=1, source_target_pairs={{0,32},{32,64},{64,96},{96,128},{128,160},{160,192},{192,224},{1,3... | collective-permute-start | bytes 49160 | tf_op jit(solution)/shard_map/ppermute | solution.py:14
  71.0 4.9 %collective-permute-start.9 = (f32[2,32,1,128]{3,1,2,0:T(8,128)S(1)}, f32[2,32,1,128]{3,1,2,0:T(8,128)S(1)}, u32[]{:S(2)}, u32[]{:S(2)}) collective-permute-start(f32[2,32,1,128]{3,1,2,0:T(8,128)S(1)} %fusion.25), channel_id=1, source_target_pairs={{0,8},{8,16},{16,24},{1,9},{9,17},{17,25},{2,10},{10,18},{18,26},{... | collective-permute-start | bytes 98312 | tf_op jit(solution)/shard_map/ppermute | solution.py:14
  75.9 5.4 %collective-permute-done.10 = f32[2,32,16,1]{3,1,2,0:T(8,128)S(1)} collective-permute-done((f32[2,32,16,1]{3,1,2,0:T(8,128)S(1)}, f32[2,32,16,1]{3,1,2,0:T(8,128)S(1)}, u32[]{:S(2)}, u32[]{:S(2)}) %collective-permute-start.10) | collective-permute-done | bytes 4128 | tf_op jit(solution)/shard_map/ppermute | solution.py:14
  81.8 0.5 fusion.16
  82.4 2.1 %convolution_bitcast_fusion = f32[4,32,16,4]{1,0,2,3:T(4,128)S(1)} fusion(f32[2,32,16,128]{3,1,2,0:T(8,128)S(1)} %get-tuple-element.22, f32[2,32,16,128]{3,1,2,0:T(8,128)S(1)} %slice.358, s32[4]{0:T(128)S(1)} %copy-done.8), kind=kOutput, calls=%fused_computation.6 | convolution fusion | flops 12845568 | bytes 1081360 | tf_op jit(solution)/shard_map/cxyz,pz->pxyc/dot_general | solution.py:65
  84.7 1.2 %fusion = f32[4,32,16,128]{1,3,2,0:T(8,128)S(1)} fusion(f32[4,32,16,128]{1,3,2,0:T(8,128)S(1)} %copy-done.2, f32[128]{0:T(128)S(1)} %copy-done.10, f32[4,32,16,4]{1,3,2,0:T(4,128)S(1)} %copy.63, f32[128]{0:T(128)S(1)} %copy-done.9, f32[4,32,16,4]{1,3,2,0:T(4,128)S(1)} %copy.61), kind=kLoop, calls=%fused_computation.1 | loop fusion | flops 1048576 | bytes 2163712 | tf_op jit(solution)/shard_map/add | solution.py:69
  85.9 2.0 %copy-done.1 = f32[4,32,16,128]{1,3,2,0:T(8,128)} copy-done((f32[4,32,16,128]{1,3,2,0:T(8,128)}, f32[4,32,16,128]{1,3,2,0:T(8,128)S(1)}, u32[]{:S(2)}) %copy-start.1) | copy-done | bytes 1048600
  87.8 7.4 %fusion.4 = f32[4,16,2,2]{1,2,3,0:T(2,128)S(1)} fusion(f32[4,32,16,4,2,16]{1,5,4,3,2,0:T(8,128)S(1)} %bitcast.42, bf16[4,2,4,32,16]{3,4,2,1,0:T(8,128)(2,1)S(1)} %constant_dynamic-slice_fusion), kind=kOutput, calls=%fused_computation.8 | convolution fusion | flops 6291456 | bytes 1082368 | tf_op jit(solution)/shard_map/pxycqf,pmcxy->pfmq/dot_general | solution.py:78
  95.3 0.7 reshape.31
  96.1 8.6 %all-to-all-start = ((f32[32,2,4]{2,1,0:T(2,128)}), f32[32,2,4]{2,1,0:T(2,128)S(1)}, u32[]{:S(2)}, u32[]{:S(2)}) async-start(f32[32,2,4]{2,1,0:T(2,128)} %reshape.31), calls=%async_computation | async-start | bytes 65536 | tf_op jit(solution)/shard_map/all_to_all | solution.py:83
  104.7 1.3 %copy.71 = f32[3,32,16,128]{3,2,1,0:T(8,128)} copy(f32[3,32,16,128]{3,1,2,0:T(8,128)S(1)} %fusion.15) | data formatting | bytes 1572864
  106.0 3.6 %copy.72 = f32[4,32,16,128]{3,2,1,0:T(8,128)} copy(f32[4,32,16,128]{1,3,2,0:T(8,128)} %copy-done.1) | data formatting | bytes 2097152
  109.6 1.3 %copy.70 = f32[3,32,16,128]{3,2,1,0:T(8,128)} copy(f32[3,32,16,128]{3,1,2,0:T(8,128)S(1)} %fusion.16) | data formatting | bytes 1572864
  110.9 1.1 all-to-all-done
  112.2 0.7 copy.73
  (75 shorter events, 3.9 us)
Async XLA Ops:
  0.6 10.4 %copy-start = (bf16[4,2,4,256,64]{3,4,2,1,0:T(8,128)(2,1)S(1)}, bf16[4,2,4,256,64]{3,4,2,1,0:T(8,128)(2,1)}, u32[]{:S(2)}) copy-start(bf16[4,2,4,256,64]{3,4,2,1,0:T(8,128)(2,1)} %param.13) | copy-start | bytes 3145732
  0.6 6.4 %copy-start.3 = (f32[3,32,16,128]{3,2,1,0:T(8,128)S(1)}, f32[3,32,16,128]{3,2,1,0:T(8,128)}, u32[]{:S(2)}) copy-start(f32[3,32,16,128]{3,2,1,0:T(8,128)} %param.7) | copy-start | bytes 2359300
  0.7 9.1 %copy-start.7 = (f32[32,16,128]{2,1,0:T(8,128)S(1)}, f32[32,16,128]{2,1,0:T(8,128)}, u32[]{:S(2)}) copy-start(f32[32,16,128]{2,1,0:T(8,128)} %param.9) | copy-start | bytes 786436
  0.7 9.8 %copy-start.11 = (f32[16]{0:T(128)S(1)}, f32[16]{0:T(128)}, u32[]{:S(2)}) copy-start(f32[16]{0:T(128)} %param.11) | copy-start | bytes 196
  0.7 9.9 %copy-start.12 = (s32[4]{0:T(128)S(1)}, s32[4]{0:T(128)}, u32[]{:S(2)}) copy-start(s32[4]{0:T(128)} %param.12) | copy-start | bytes 52
  2.9 21.6 %collective-permute-start = (f32[2,32,1,128]{3,1,2,0:T(8,128)}, f32[2,32,1,128]{3,1,2,0:T(8,128)}, u32[]{:S(2)}, u32[]{:S(2)}) collective-permute-start(f32[2,32,1,128]{3,1,2,0:T(8,128)} %fusion.28), channel_id=1, source_target_pairs={{8,0},{16,8},{24,16},{9,1},{17,9},{25,17},{10,2},{18,10},{26,18},{... | collective-permute-start | bytes 98312 | tf_op jit(solution)/shard_map/ppermute | solution.py:14
  5.0 17.8 %collective-permute-start.1 = (f32[2,32,16,1]{3,1,2,0:T(8,128)}, f32[2,32,16,1]{3,1,2,0:T(8,128)}, u32[]{:S(2)}, u32[]{:S(2)}) collective-permute-start(f32[2,32,16,1]{3,1,2,0:T(8,128)} %slice.295), channel_id=1, source_target_pairs={{1,0},{2,1},{3,2},{4,3},{5,4},{6,5},{7,6},{9,8},{10,9},{11,10},{12... | collective-permute-start | bytes 12296 | tf_op jit(solution)/shard_map/ppermute | solution.py:14
  7.6 15.1 %collective-permute-start.2 = (f32[2,1,16,128]{3,1,2,0:T(1,128)}, f32[2,1,16,128]{3,1,2,0:T(1,128)S(1)}, u32[]{:S(2)}, u32[]{:S(2)}) collective-permute-start(f32[2,1,16,128]{3,1,2,0:T(1,128)} %bitcast), channel_id=1, source_target_pairs={{32,0},{64,32},{96,64},{128,96},{160,128},{192,160},{224,192},{33,... | collective-permute-start | bytes 49160 | tf_op jit(solution)/shard_map/ppermute | solution.py:14
  14.6 29.5 %copy-start.5 = (f32[32,16,128]{2,0,1:T(8,128)}, f32[32,16,128]{2,0,1:T(8,128)S(1)}, u32[]{:S(2)}) copy-start(f32[32,16,128]{2,0,1:T(8,128)S(1)} %copy.50) | copy-start | bytes 786436
  22.8 3.0 %copy-start.4 = (f32[3,32,16,128]{3,2,1,0:T(8,128)S(1)}, f32[3,32,16,128]{3,2,1,0:T(8,128)}, u32[]{:S(2)}) copy-start(f32[3,32,16,128]{3,2,1,0:T(8,128)} %param.8) | copy-start | bytes 2359300
  26.4 17.2 %collective-permute-start.4 = (f32[2,32,16,1]{3,1,2,0:T(8,128)S(1)}, f32[2,32,16,1]{3,1,2,0:T(8,128)S(1)}, u32[]{:S(2)}, u32[]{:S(2)}) collective-permute-start(f32[2,32,16,1]{3,1,2,0:T(8,128)S(1)} %slice.312), channel_id=1, source_target_pairs={{0,1},{1,2},{2,3},{3,4},{4,5},{5,6},{6,7},{8,9},{9,10},{10,11},{11... | collective-permute-start | bytes 12296 | tf_op jit(solution)/shard_map/ppermute | solution.py:14
  31.4 12.1 %collective-permute-start.5 = (f32[2,1,16,128]{3,1,2,0:T(1,128)S(1)}, f32[2,1,16,128]{3,1,2,0:T(1,128)S(1)}, u32[]{:S(2)}, u32[]{:S(2)}) collective-permute-start(f32[2,1,16,128]{3,1,2,0:T(1,128)S(1)} %slice.317), channel_id=1, source_target_pairs={{0,32},{32,64},{64,96},{96,128},{128,160},{160,192},{192,224},{1,3... | collective-permute-start | bytes 49160 | tf_op jit(solution)/shard_map/ppermute | solution.py:14
  34.3 9.5 %collective-permute-start.3 = (f32[2,32,1,128]{3,1,2,0:T(8,128)S(1)}, f32[2,32,1,128]{3,1,2,0:T(8,128)S(1)}, u32[]{:S(2)}, u32[]{:S(2)}) collective-permute-start(f32[2,32,1,128]{3,1,2,0:T(8,128)S(1)} %fusion.27), channel_id=1, source_target_pairs={{0,8},{8,16},{16,24},{1,9},{9,17},{17,25},{2,10},{10,18},{18,26},{... | collective-permute-start | bytes 98312 | tf_op jit(solution)/shard_map/ppermute | solution.py:14
  44.6 18.1 %copy-start.8 = (s32[4]{0:T(128)S(1)}, s32[4]{0:T(128)}, u32[]{:S(2)}) copy-start(s32[4]{0:T(128)} %broadcast_subtract_fusion) | copy-start | bytes 52
  44.6 17.8 %collective-permute-start.7 = (f32[2,32,16,1]{3,1,2,0:T(8,128)S(1)}, f32[2,32,16,1]{3,1,2,0:T(8,128)S(1)}, u32[]{:S(2)}, u32[]{:S(2)}) collective-permute-start(f32[2,32,16,1]{3,1,2,0:T(8,128)S(1)} %slice.330), channel_id=1, source_target_pairs={{1,0},{2,1},{3,2},{4,3},{5,4},{6,5},{7,6},{9,8},{10,9},{11,10},{12... | collective-permute-start | bytes 12296 | tf_op jit(solution)/shard_map/ppermute | solution.py:14
  46.5 15.9 %collective-permute-start.8 = (f32[2,1,16,128]{3,1,2,0:T(1,128)S(1)}, f32[2,1,16,128]{3,1,2,0:T(1,128)S(1)}, u32[]{:S(2)}, u32[]{:S(2)}) collective-permute-start(f32[2,1,16,128]{3,1,2,0:T(1,128)S(1)} %slice.335), channel_id=1, source_target_pairs={{32,0},{64,32},{96,64},{128,96},{160,128},{192,160},{224,192},{33,... | collective-permute-start | bytes 49160 | tf_op jit(solution)/shard_map/ppermute | solution.py:14
  48.1 16.8 %collective-permute-start.6 = (f32[2,32,1,128]{3,1,2,0:T(8,128)S(1)}, f32[2,32,1,128]{3,1,2,0:T(8,128)S(1)}, u32[]{:S(2)}, u32[]{:S(2)}) collective-permute-start(f32[2,32,1,128]{3,1,2,0:T(8,128)S(1)} %fusion.26), channel_id=1, source_target_pairs={{8,0},{16,8},{24,16},{9,1},{17,9},{25,17},{10,2},{18,10},{26,18},{... | collective-permute-start | bytes 98312 | tf_op jit(solution)/shard_map/ppermute | solution.py:14
  65.9 15.3 %collective-permute-start.10 = (f32[2,32,16,1]{3,1,2,0:T(8,128)S(1)}, f32[2,32,16,1]{3,1,2,0:T(8,128)S(1)}, u32[]{:S(2)}, u32[]{:S(2)}) collective-permute-start(f32[2,32,16,1]{3,1,2,0:T(8,128)S(1)} %slice.348), channel_id=1, source_target_pairs={{0,1},{1,2},{2,3},{3,4},{4,5},{5,6},{6,7},{8,9},{9,10},{10,11},{11... | collective-permute-start | bytes 12296 | tf_op jit(solution)/shard_map/ppermute | solution.py:14
  69.5 11.7 %collective-permute-start.11 = (f32[2,1,16,128]{3,1,2,0:T(1,128)S(1)}, f32[2,1,16,128]{3,1,2,0:T(1,128)S(1)}, u32[]{:S(2)}, u32[]{:S(2)}) collective-permute-start(f32[2,1,16,128]{3,1,2,0:T(1,128)S(1)} %slice.353), channel_id=1, source_target_pairs={{0,32},{32,64},{64,96},{96,128},{128,160},{160,192},{192,224},{1,3... | collective-permute-start | bytes 49160 | tf_op jit(solution)/shard_map/ppermute | solution.py:14
  71.0 10.8 %copy-start.6 = (f32[32,16,128]{2,0,1:T(8,128)S(1)}, f32[32,16,128]{2,0,1:T(8,128)}, u32[]{:S(2)}) copy-start(f32[32,16,128]{2,0,1:T(8,128)} %copy-done.5) | copy-start | bytes 786436
  71.0 10.5 %collective-permute-start.9 = (f32[2,32,1,128]{3,1,2,0:T(8,128)S(1)}, f32[2,32,1,128]{3,1,2,0:T(8,128)S(1)}, u32[]{:S(2)}, u32[]{:S(2)}) collective-permute-start(f32[2,32,1,128]{3,1,2,0:T(8,128)S(1)} %fusion.25), channel_id=1, source_target_pairs={{0,8},{8,16},{16,24},{1,9},{9,17},{17,25},{2,10},{10,18},{18,26},{... | collective-permute-start | bytes 98312 | tf_op jit(solution)/shard_map/ppermute | solution.py:14
  81.6 3.0 %copy-start.2 = (f32[4,32,16,128]{1,3,2,0:T(8,128)S(1)}, f32[4,32,16,128]{1,3,2,0:T(8,128)}, u32[]{:S(2)}) copy-start(f32[4,32,16,128]{1,3,2,0:T(8,128)} %copy.62) | copy-start | bytes 3145732
  81.6 3.0 %copy-start.9 = (f32[128]{0:T(128)S(1)}, f32[128]{0:T(128)}, u32[]{:S(2)}) copy-start(f32[128]{0:T(128)} %mul.86) | copy-start | bytes 1540
  81.6 3.0 %copy-start.10 = (f32[128]{0:T(128)S(1)}, f32[128]{0:T(128)}, u32[]{:S(2)}) copy-start(f32[128]{0:T(128)} %mul.93) | copy-start | bytes 1540
  85.8 2.0 %copy-start.1 = (f32[4,32,16,128]{1,3,2,0:T(8,128)}, f32[4,32,16,128]{1,3,2,0:T(8,128)S(1)}, u32[]{:S(2)}) copy-start(f32[4,32,16,128]{1,3,2,0:T(8,128)S(1)} %fusion) | copy-start | bytes 3145732
  96.1 15.9 %all-to-all-start = ((f32[32,2,4]{2,1,0:T(2,128)}), f32[32,2,4]{2,1,0:T(2,128)S(1)}, u32[]{:S(2)}, u32[]{:S(2)}) async-start(f32[32,2,4]{2,1,0:T(2,128)} %reshape.31), calls=%async_computation | async-start | bytes 65536 | tf_op jit(solution)/shard_map/all_to_all | solution.py:83

commit v2 on v1

v2 whole, which is shorter than its diff:
```python
import jax
import jax.numpy as jnp
from jax import lax
from jax.sharding import PartitionSpec as P

STEPS = 2
NF = 16
MODES = 2
HALO = 2
AXES = ("gx", "gy", "gz")


def shifted(value, axis, steps):
    count = lax.axis_size(axis)
    first, last = (max(0, -steps), min(count, count - steps))
    return lax.ppermute(value, axis, [(source, source + steps) for source in range(first, last)])


def widen(stack, dim, axis):
    count = stack.shape[dim]
    low = lax.slice_in_dim(stack, 0, HALO, axis=dim)
    high = lax.slice_in_dim(stack, count - HALO, count, axis=dim)
    from_below = shifted(high, axis, 1)
    from_above = shifted(low, axis, -1)
    return jnp.concatenate([from_below, stack, from_above], axis=dim)


def box(value, start, size):
    lead = value.ndim - 3
    return lax.slice(
        value,
        (0,) * lead + tuple(start),
        value.shape[:lead] + tuple(s + n for s, n in zip(start, size)),
    )


def moved(start, dim, step):
    return tuple(s + step if d == dim else s for d, s in enumerate(start))


def differ(value, start, size, dim, step):
    if step > 0:
        return box(value, moved(start, dim, 1), size) - box(value, start, size)
    return box(value, start, size) - box(value, moved(start, dim, -1), size)


def curl(field, start, size, step):
    vx, vy, vz = field[0], field[1], field[2]
    d = lambda v, dim: differ(v, start, size, dim, step)
    return jnp.stack([d(vz, 1) - d(vy, 2), d(vx, 2) - d(vz, 0), d(vy, 0) - d(vx, 1)])


def inside(origin, size, cells):
    masks = []
    for dim, axis in enumerate(AXES):
        count = lax.axis_size(axis)
        first = lax.axis_index(axis) * cells[dim] + origin
        where = first + jnp.arange(size[dim])
        masks.append((where >= 0) & (where < count * cells[dim]))
    return (
        masks[0][:, None, None] & masks[1][None, :, None] & masks[2][None, None, :]
    ).astype(jnp.float32)


def per_device(e_field, h_field, inv_permittivity, dft_sums, omega, port_z, mode_profiles):
    cells = e_field.shape[1:]
    cells_x, cells_y, cells_z = cells
    ports_here = dft_sums.shape[0]
    stack = jnp.concatenate([e_field, h_field, inv_permittivity[None]], axis=0)
    for dim, axis in enumerate(AXES):
        stack = widen(stack, dim + 1, axis)
    e0, h0, inv = stack[0:3], stack[3:6], stack[6]
    n = lambda k: tuple(c + k for c in cells)
    h1 = box(h0, (0, 0, 0), n(3)) - 0.5 * curl(e0, (0, 0, 0), n(3), 1)
    h1 = h1 * inside(-2, n(3), cells)
    e1 = box(e0, (1, 1, 1), n(2)) + 0.5 * box(inv, (1, 1, 1), n(2)) * curl(h1, (1, 1, 1), n(2), -1)
    h2 = box(h1, (1, 1, 1), n(1)) - 0.5 * curl(e1, (0, 0, 0), n(1), 1)
    h2 = h2 * inside(-1, n(1), cells)
    e2 = box(e1, (1, 1, 1), n(0)) + 0.5 * box(inv, (2, 2, 2), n(0)) * curl(h2, (1, 1, 1), n(0), -1)
    e1_here = box(e1, (1, 1, 1), n(0))
    h1_here = box(h1, (2, 2, 2), n(0))
    h2_here = box(h2, (1, 1, 1), n(0))
    local_z = port_z - lax.axis_index("gz") * cells_z
    select = (local_z[:, None] == jnp.arange(cells_z)[None, :]).astype(jnp.float32)
    dft = dft_sums
    for step, (e_now, h_now) in enumerate(((e1_here, h1_here), (e2, h2_here))):
        tangent = jnp.stack([e_now[0], e_now[1], h_now[0], h_now[1]])
        planes = jnp.einsum("cxyz,pz->pxyc", tangent, select, precision=lax.Precision.HIGHEST)
        phase = omega * jnp.float32(step + 1)
        trig = jnp.stack([jnp.cos(phase), jnp.sin(phase)])
        increment = planes[:, :, :, :, None, None] * trig[None, None, None, None, :, :]
        dft = dft + increment.reshape(dft.shape)
    shaped = dft.reshape(ports_here, cells_x, cells_y, 4, 2, NF)
    groups = lax.axis_size(("gx", "gy"))
    owned = ports_here * NF // groups
    start_x = lax.axis_index("gx") * cells_x
    start_y = lax.axis_index("gy") * cells_y
    tile = lax.dynamic_slice(
        mode_profiles, (0, 0, 0, start_x, start_y), (ports_here, MODES, 4, cells_x, cells_y)
    )
    partial_sums = jnp.einsum(
        "pxycqf,pmcxy->pfmq", shaped, tile.astype(jnp.float32), precision=lax.Precision.HIGHEST
    )
    partial_sums = partial_sums.reshape(ports_here * NF, MODES * 2)
    pieces = partial_sums.reshape(groups, owned, MODES * 2)
    result = jnp.sum(lax.all_to_all(pieces, ("gx", "gy"), 0, 0, tiled=False), axis=0)
    return (e2, h2_here, dft, result.reshape(owned, 1, MODES * 2))


def solution(mesh):
    return jax.shard_map(
        per_device,
        mesh=mesh,
        in_specs=(
            P(None, "gx", "gy", "gz"),
            P(None, "gx", "gy", "gz"),
            P("gx", "gy", "gz"),
            P("gz", "gx", "gy", None),
            P(),
            P("gz"),
            P("gz", None, None, None, None),
        ),
        out_specs=(
            P(None, "gx", "gy", "gz"),
            P(None, "gx", "gy", "gz"),
            P("gz", "gx", "gy", None),
            P(("gx", "gy"), "gz", None),
        ),
        check_vma=False,
    )
```

time: 114 us -> 103 us (0.904)
  starting transfers between devices: 39.8 us -> 25.1 us
  waiting for transfers between devices: 24.1 us -> 9.64 us
  local copies, waits for them, and re-layouts: 25.3 us -> 34.6 us
  other arithmetic: 10.7 us -> 19.7 us
    ppermute x12 -> x6, starting transfers between devices: 31.2 us -> 14.8 us  [shifted(): lax.ppermute(value, axis, [(source, source + steps) for source in range(f...]
    ppermute x12 -> x6, waiting for transfers between devices: 23 us -> 9.64 us  [shifted(): lax.ppermute(value, axis, [(source, source + steps) for source in range(f...]
    concatenate x0 -> x2, other arithmetic: none -> 10.4 us  [widen(): return jnp.concatenate([from_below, stack, from_above], axis=dim)]
    ppermute x0 -> x2, local copies, waits for them, and re-layouts: none -> 4.74 us  [shifted(): lax.ppermute(value, axis, [(source, source + steps) for source in range(f...]
    slice x20 -> x4, local copies, waits for them, and re-layouts: 4.3 us -> 8.78 us  [the longest x2 5.93 us: widen(): high = lax.slice_in_dim(stack, count - HALO, count, axis=dim)]
    sub x11 -> x0, other arithmetic: 4.34 us -> none  [the longest x3 2.93 us: forward(): return jnp.concatenate([rest, after], axis=dim) - part]
    mul x4, local copies, waits for them, and re-layouts: 4.51 us -> 0.18 us  [per_device(): planes[:, :, :, :, None, None] * trig[None, None, None, None, :, :]]
    unnamed x33 -> x29, local copies, waits for them, and re-layouts: 14.2 us -> 18.1 us
  transfers between devices with their start and end apart: 13 -> 7, of which waited for: 4 -> 4; matrix products, arithmetic and copies ran while one was open for 24% -> 19% of each run, Pallas kernels for 0% -> 0%
where the time goes in v2:
time: 103 us; the launch traced here: 102 us
  local copies, waits for them, and re-layouts  34.6 us (34%)
  starting transfers between devices  25.1 us (24%)
  other arithmetic  19.7 us (19%)
  matrix products  11.9 us (12%)
  waiting for transfers between devices  9.64 us (9%)
  between operations  1.09 us (1%)
    unnamed x29, local copies, waits for them, and re-layouts  18.1 us
    ppermute x6, starting transfers between devices, shifted(): lax.ppermute(value, axis, [(source, source + steps) for source in range(f...  14.8 us
    concatenate x2, other arithmetic, widen(): return jnp.concatenate([from_below, stack, from_above], axis=dim)  10.4 us
    all_to_all x1, starting transfers between devices, per_device(): lax.all_to_all(pieces, ('gx', 'gy'), 0, 0, tiled=False)  10.4 us
    ppermute x6, waiting for transfers between devices, shifted(): lax.ppermute(value, axis, [(source, source + steps) for source in range(f...  9.64 us
    dot_general x1, matrix products, per_device(): jnp.einsum('pxycqf,pmcxy->pfmq', shaped, tile.astype(jnp.float32), precis...  7.57 us
    slice x2, local copies, waits for them, and re-layouts, widen(): high = lax.slice_in_dim(stack, count - HALO, count, axis=dim)  5.93 us
    ppermute x2, local copies, waits for them, and re-layouts, shifted(): lax.ppermute(value, axis, [(source, source + steps) for source in range(f...  4.74 us
  transfers between devices with their start and end apart: 7, of which 4 were waited for; matrix products, arithmetic and copies ran while one was open for 19% of the time, Pallas kernels for 0%

profile of v2, /device:TPU:96, one launch (start us, length us, event | category | flops | bytes accessed | tf_op | source)
XLA Modules:
  0.0 102.0 jit_solution(17336790478406592763)
XLA Ops:
  0.7 1.5 %copy.35 = f32[3,32,16,128]{3,1,2,0:T(8,128)S(1)} copy(f32[3,32,16,128]{3,2,1,0:T(8,128)} %param.7) | data formatting | bytes 1572864 | tf_op args[0]
  2.2 1.4 %copy.36 = f32[3,32,16,128]{3,1,2,0:T(8,128)S(1)} copy(f32[3,32,16,128]{3,2,1,0:T(8,128)} %param.8) | data formatting | bytes 1572864 | tf_op args[1]
  3.8 1.7 %collective-permute-start = (f32[7,2,16,128]{3,1,2,0:T(2,128)S(1)}, f32[7,2,16,128]{3,1,2,0:T(2,128)S(1)}, u32[]{:S(2)}, u32[]{:S(2)}) collective-permute-start(f32[7,2,16,128]{3,1,2,0:T(2,128)S(1)} %get-tuple-element.33), channel_id=1, source_target_pairs={{0,32},{32,64},{64,96},{96,128},{128,160},{160,192},{192,224},{1,3... | collective-permute-start | bytes 344072 | tf_op jit(solution)/shard_map/ppermute | solution.py:16
  5.5 1.3 %collective-permute-start.1 = (f32[7,2,16,128]{3,1,2,0:T(2,128)S(1)}, f32[7,2,16,128]{3,1,2,0:T(2,128)S(1)}, u32[]{:S(2)}, u32[]{:S(2)}) collective-permute-start(f32[7,2,16,128]{3,1,2,0:T(2,128)S(1)} %get-tuple-element.34), channel_id=1, source_target_pairs={{32,0},{64,32},{96,64},{128,96},{160,128},{192,160},{224,192},{33,... | collective-permute-start | bytes 344072 | tf_op jit(solution)/shard_map/ppermute | solution.py:16
  7.1 1.0 and_convert_fusion.1
  8.3 1.7 %collective-permute-done.1 = f32[7,2,16,128]{3,1,2,0:T(2,128)S(1)} collective-permute-done((f32[7,2,16,128]{3,1,2,0:T(2,128)S(1)}, f32[7,2,16,128]{3,1,2,0:T(2,128)S(1)}, u32[]{:S(2)}, u32[]{:S(2)}) %collective-permute-start.1) | collective-permute-done | bytes 114720 | tf_op jit(solution)/shard_map/ppermute | solution.py:16
  10.1 3.5 %collective-permute-start.2 = (f32[7,36,2,128]{3,1,2,0:T(8,128)S(1)}, f32[7,36,2,128]{3,1,2,0:T(8,128)S(1)}, u32[]{:S(2)}, u32[]{:S(2)}) collective-permute-start(f32[7,36,2,128]{3,1,2,0:T(8,128)S(1)} %get-tuple-element.31), channel_id=1, source_target_pairs={{0,8},{8,16},{16,24},{1,9},{9,17},{17,25},{2,10},{10,18},{18,26},{... | collective-permute-start | bytes 774152 | tf_op jit(solution)/shard_map/ppermute | solution.py:16
  13.6 1.3 %collective-permute-start.3 = (f32[7,36,2,128]{3,1,2,0:T(8,128)S(1)}, f32[7,36,2,128]{3,1,2,0:T(8,128)S(1)}, u32[]{:S(2)}, u32[]{:S(2)}) collective-permute-start(f32[7,36,2,128]{3,1,2,0:T(8,128)S(1)} %get-tuple-element.32), channel_id=1, source_target_pairs={{8,0},{16,8},{24,16},{9,1},{17,9},{25,17},{10,2},{18,10},{26,18},{... | collective-permute-start | bytes 774152 | tf_op jit(solution)/shard_map/ppermute | solution.py:16
  14.9 1.0 %and_convert_fusion = f32[35,19,131]{2,0,1:T(8,128)} fusion(pred[131]{0:T(512)(128)(4,1)S(1)} %compare_and_fusion.3, pred[35,19]{0,1:T(8,128)(4,1)S(1)} %broadcast_and_fusion.1), kind=kLoop, calls=%fused_computation.46 | loop fusion | flops 174230 | bytes 349256 | tf_op jit(solution)/shard_map/convert_element_type | solution.py:62
  16.0 2.3 %collective-permute-done.2 = f32[7,36,2,128]{3,1,2,0:T(8,128)S(1)} collective-permute-done((f32[7,36,2,128]{3,1,2,0:T(8,128)S(1)}, f32[7,36,2,128]{3,1,2,0:T(8,128)S(1)}, u32[]{:S(2)}, u32[]{:S(2)}) %collective-permute-start.2) | collective-permute-done | bytes 258080 | tf_op jit(solution)/shard_map/ppermute | solution.py:16
  18.3 4.7 %collective-permute-done.3 = f32[7,36,2,128]{3,1,2,0:T(8,128)S(1)} collective-permute-done((f32[7,36,2,128]{3,1,2,0:T(8,128)S(1)}, f32[7,36,2,128]{3,1,2,0:T(8,128)S(1)}, u32[]{:S(2)}, u32[]{:S(2)}) %collective-permute-start.3) | collective-permute-done | bytes 258080 | tf_op jit(solution)/shard_map/ppermute | solution.py:16
  23.0 0.4 pad_maximum_fusion.1
  23.4 3.4 %fusion.46 = (f32[7,36,20,2]{3,1,2,0:T(8,128)}, f32[7,36,20,2]{3,1,2,0:T(8,128)}) fusion(f32[7,36,20,128]{3,1,2,0:T(8,128)S(1)} %pad_maximum_fusion.1), kind=kLoop, calls=%fused_computation.124 | loop fusion | bytes 161280 | tf_op jit(solution)/shard_map/slice | solution.py:22
  26.8 2.5 %copy.37 = f32[7,36,20,2]{1,3,2,0:T(2,128)S(1)} copy(f32[7,36,20,2]{3,1,2,0:T(8,128)} %get-tuple-element.20) | data formatting | bytes 80640 | tf_op jit(solution)/shard_map/slice | solution.py:22
  29.3 5.0 %collective-permute-start.4 = (f32[7,36,20,2]{1,3,2,0:T(2,128)S(1)}, f32[7,36,20,2]{1,3,2,0:T(2,128)S(1)}, u32[]{:S(2)}, u32[]{:S(2)}) collective-permute-start(f32[7,36,20,2]{1,3,2,0:T(2,128)S(1)} %copy.37), channel_id=1, source_target_pairs={{0,1},{1,2},{2,3},{3,4},{4,5},{5,6},{6,7},{8,9},{9,10},{10,11},{11... | collective-permute-start | bytes 120968 | tf_op jit(solution)/shard_map/ppermute | solution.py:16
  34.4 2.5 %copy.38 = f32[7,36,20,2]{1,3,2,0:T(2,128)S(1)} copy(f32[7,36,20,2]{3,1,2,0:T(8,128)} %get-tuple-element.21) | data formatting | bytes 80640 | tf_op jit(solution)/shard_map/slice | solution.py:21
  36.9 1.9 %collective-permute-start.5 = (f32[7,36,20,2]{1,3,2,0:T(2,128)S(1)}, f32[7,36,20,2]{1,3,2,0:T(2,128)S(1)}, u32[]{:S(2)}, u32[]{:S(2)}) collective-permute-start(f32[7,36,20,2]{1,3,2,0:T(2,128)S(1)} %copy.38), channel_id=1, source_target_pairs={{1,0},{2,1},{3,2},{4,3},{5,4},{6,5},{7,6},{9,8},{10,9},{11,10},{12... | collective-permute-start | bytes 120968 | tf_op jit(solution)/shard_map/ppermute | solution.py:16
  39.0 3.6 %copy.42 = f32[4,32,16,128]{1,3,2,0:T(8,128)} copy(f32[4,32,16,128]{3,2,1,0:T(8,128)} %param.10) | data formatting | bytes 2097152 | tf_op args[3]
  42.7 2.4 %copy.39 = f32[7,36,20,2]{3,1,2,0:T(8,128)} copy(f32[7,36,20,2]{1,3,2,0:T(2,128)S(1)} %collective-permute-done.4) | data formatting | bytes 80640 | tf_op jit(solution)/shard_map/ppermute | solution.py:16
  45.0 0.9 collective-permute-done.5
  45.9 2.4 %copy.40 = f32[7,36,20,2]{3,1,2,0:T(8,128)} copy(f32[7,36,20,2]{1,3,2,0:T(2,128)S(1)} %collective-permute-done.5) | data formatting | bytes 80640 | tf_op jit(solution)/shard_map/ppermute | solution.py:16
  48.3 10.0 %pad_maximum_fusion = f32[7,36,20,132]{3,1,2,0:T(8,128)S(1)} fusion(f32[7,36,20,2]{3,1,2,0:T(8,128)} %copy.40, f32[7,36,2,128]{3,1,2,0:T(8,128)S(1)} %collective-permute-done.3, f32[7,2,16,128]{3,1,2,0:T(2,128)S(1)} %collective-permute-done.1, f32[1,32,16,128]{3,1,2,0:T(8,128)S(1)} %bitcast.98, f32[3,32,16,128]{3,1,2,0:T(8,128)S(1)} %copy.36, ...), kind=kLoop, calls=%fused_computation | loop fusion | flops 5322240 | bytes 5322240 | tf_op jit(solution)/shard_map/concatenate | solution.py:25
  58.3 0.3 slice_bitcast_fusion.3
  58.6 0.5 fusion.20
  59.1 0.6 copy-done.5
  59.7 0.4 fusion.4
  60.1 0.2 slice_bitcast_fusion.6
  60.6 0.3 slice_multiply_fusion
  60.9 1.5 %fusion.26 = (f32[1,34,18,130]{3,1,2,0:T(8,128)S(1)}, f32[1,34,18,130]{3,1,2,0:T(8,128)S(1)}, f32[1,34,18,130]{3,1,2,0:T(8,128)S(1)}) fusion(f32[35,19,131]{2,0,1:T(8,128)S(1)} %get-tuple-element.24, f32[35,19,131]{2,0,1:T(8,128)S(1)} %get-tuple-element.22, f32[35,19,131]{2,0,1:T(8,128)S(1)} %get-tuple-element.23), kind=kLoop, calls=%fused_computation.60 | loop fusion | flops 716040 | bytes 3818880 | tf_op jit(solution)/shard_map/stack | solution.py:50
  62.4 0.8 slice_add_fusion
  63.1 0.2 slice.357
  63.7 0.4 fusion.32
  64.2 0.6 copy-done.6
  64.8 0.7 fusion.5
  65.9 2.1 %convolution_bitcast_fusion.1 = f32[4,32,16,4]{1,0,2,3:T(4,128)S(1)} fusion(f32[2,32,16,128]{3,1,2,0:T(8,128)S(1)} %slice.358, f32[2,32,16,128]{3,1,2,0:T(8,128)S(1)} %slice.357, s32[4]{0:T(128)S(1)} %broadcast_subtract_fusion), kind=kOutput, calls=%fused_computation.17 | convolution fusion | flops 12845568 | bytes 1081360 | tf_op jit(solution)/shard_map/cxyz,pz->pxyc/dot_general | solution.py:88
  68.2 0.6 fusion.38
  68.8 0.3 slice_add_fusion.1
  69.2 2.1 %convolution_bitcast_fusion = f32[4,32,16,4]{1,0,2,3:T(4,128)S(1)} fusion(f32[2,32,16,128]{3,1,2,0:T(8,128)S(1)} %slice.360, f32[2,32,16,128]{3,1,2,0:T(8,128)S(1)} %slice.359, s32[4]{0:T(128)S(1)} %broadcast_subtract_fusion), kind=kOutput, calls=%fused_computation.16 | convolution fusion | flops 12845568 | bytes 1081360 | tf_op jit(solution)/shard_map/cxyz,pz->pxyc/dot_general | solution.py:88
  71.4 1.2 %fusion = f32[4,32,16,128]{1,3,2,0:T(8,128)S(1)} fusion(f32[4,32,16,128]{1,3,2,0:T(8,128)S(1)} %copy-done.3, f32[128]{0:T(128)S(1)} %mul.143, f32[4,32,16,4]{1,3,2,0:T(4,128)S(1)} %copy.43, f32[128]{0:T(128)S(1)} %mul.136, f32[4,32,16,4]{1,3,2,0:T(4,128)S(1)} %copy.41), kind=kLoop, calls=%fused_computation.2 | loop fusion | flops 1048576 | bytes 2163712 | tf_op jit(solution)/shard_map/add | solution.py:92
  72.6 1.9 %copy-done.2 = f32[4,32,16,128]{1,3,2,0:T(8,128)} copy-done((f32[4,32,16,128]{1,3,2,0:T(8,128)}, f32[4,32,16,128]{1,3,2,0:T(8,128)S(1)}, u32[]{:S(2)}) %copy-start.2) | copy-done | bytes 1048600
  74.6 7.6 %fusion.6 = f32[4,16,2,2]{1,2,3,0:T(2,128)S(1)} fusion(f32[4,32,16,4,2,16]{1,5,4,3,2,0:T(8,128)S(1)} %bitcast.94, bf16[4,2,4,32,16]{3,4,2,1,0:T(8,128)(2,1)S(1)} %constant_dynamic-slice_fusion), kind=kOutput, calls=%fused_computation.18 | convolution fusion | flops 6291456 | bytes 1082368 | tf_op jit(solution)/shard_map/pxycqf,pmcxy->pfmq/dot_general | solution.py:101
  82.3 0.7 reshape.142
  83.0 10.4 %all-to-all-start = ((f32[32,2,4]{2,1,0:T(2,128)}), f32[32,2,4]{2,1,0:T(2,128)S(1)}, u32[]{:S(2)}, u32[]{:S(2)}) async-start(f32[32,2,4]{2,1,0:T(2,128)} %reshape.142), calls=%async_computation | async-start | bytes 65536 | tf_op jit(solution)/shard_map/all_to_all | solution.py:106
  93.4 3.7 %copy.52 = f32[4,32,16,128]{3,2,1,0:T(8,128)} copy(f32[4,32,16,128]{1,3,2,0:T(8,128)} %copy-done.2) | data formatting | bytes 2097152
  97.1 2.5 %copy.50 = f32[3,32,16,128]{3,2,1,0:T(8,128)} copy(f32[3,32,16,128]{3,1,2,0:T(8,128)} %copy-done.4) | data formatting | bytes 1572864
  99.6 0.3 slice.356
  99.9 1.3 %copy.51 = f32[3,32,16,128]{3,2,1,0:T(8,128)} copy(f32[3,32,16,128]{3,1,2,0:T(8,128)S(1)} %slice.356) | data formatting | bytes 1572864
  101.4 0.7 copy.53
  (50 shorter events, 2.4 us)
Async XLA Ops:
  0.6 7.5 %copy-start = (bf16[4,2,4,256,64]{3,4,2,1,0:T(8,128)(2,1)S(1)}, bf16[4,2,4,256,64]{3,4,2,1,0:T(8,128)(2,1)}, u32[]{:S(2)}) copy-start(bf16[4,2,4,256,64]{3,4,2,1,0:T(8,128)(2,1)} %param.13) | copy-start | bytes 3145732
  0.6 2.9 %copy-start.7 = (f32[32,16,128]{2,1,0:T(8,128)S(1)}, f32[32,16,128]{2,1,0:T(8,128)}, u32[]{:S(2)}) copy-start(f32[32,16,128]{2,1,0:T(8,128)} %param.9) | copy-start | bytes 786436
  0.7 6.2 %copy-start.9 = (s32[4]{0:T(128)S(1)}, s32[4]{0:T(128)}, u32[]{:S(2)}) copy-start(s32[4]{0:T(128)} %param.12) | copy-start | bytes 52
  0.7 6.3 %copy-start.8 = (f32[16]{0:T(128)S(1)}, f32[16]{0:T(128)}, u32[]{:S(2)}) copy-start(f32[16]{0:T(128)} %param.11) | copy-start | bytes 196
  3.8 4.5 %collective-permute-start = (f32[7,2,16,128]{3,1,2,0:T(2,128)S(1)}, f32[7,2,16,128]{3,1,2,0:T(2,128)S(1)}, u32[]{:S(2)}, u32[]{:S(2)}) collective-permute-start(f32[7,2,16,128]{3,1,2,0:T(2,128)S(1)} %get-tuple-element.33), channel_id=1, source_target_pairs={{0,32},{32,64},{64,96},{96,128},{128,160},{160,192},{192,224},{1,3... | collective-permute-start | bytes 344072 | tf_op jit(solution)/shard_map/ppermute | solution.py:16
  5.5 4.5 %collective-permute-start.1 = (f32[7,2,16,128]{3,1,2,0:T(2,128)S(1)}, f32[7,2,16,128]{3,1,2,0:T(2,128)S(1)}, u32[]{:S(2)}, u32[]{:S(2)}) collective-permute-start(f32[7,2,16,128]{3,1,2,0:T(2,128)S(1)} %get-tuple-element.34), channel_id=1, source_target_pairs={{32,0},{64,32},{96,64},{128,96},{160,128},{192,160},{224,192},{33,... | collective-permute-start | bytes 344072 | tf_op jit(solution)/shard_map/ppermute | solution.py:16
  10.1 8.2 %collective-permute-start.2 = (f32[7,36,2,128]{3,1,2,0:T(8,128)S(1)}, f32[7,36,2,128]{3,1,2,0:T(8,128)S(1)}, u32[]{:S(2)}, u32[]{:S(2)}) collective-permute-start(f32[7,36,2,128]{3,1,2,0:T(8,128)S(1)} %get-tuple-element.31), channel_id=1, source_target_pairs={{0,8},{8,16},{16,24},{1,9},{9,17},{17,25},{2,10},{10,18},{18,26},{... | collective-permute-start | bytes 774152 | tf_op jit(solution)/shard_map/ppermute | solution.py:16
  13.6 9.4 %collective-permute-start.3 = (f32[7,36,2,128]{3,1,2,0:T(8,128)S(1)}, f32[7,36,2,128]{3,1,2,0:T(8,128)S(1)}, u32[]{:S(2)}, u32[]{:S(2)}) collective-permute-start(f32[7,36,2,128]{3,1,2,0:T(8,128)S(1)} %get-tuple-element.32), channel_id=1, source_target_pairs={{8,0},{16,8},{24,16},{9,1},{17,9},{25,17},{10,2},{18,10},{26,18},{... | collective-permute-start | bytes 774152 | tf_op jit(solution)/shard_map/ppermute | solution.py:16
  29.3 13.3 %collective-permute-start.4 = (f32[7,36,20,2]{1,3,2,0:T(2,128)S(1)}, f32[7,36,20,2]{1,3,2,0:T(2,128)S(1)}, u32[]{:S(2)}, u32[]{:S(2)}) collective-permute-start(f32[7,36,20,2]{1,3,2,0:T(2,128)S(1)} %copy.37), channel_id=1, source_target_pairs={{0,1},{1,2},{2,3},{3,4},{4,5},{5,6},{6,7},{8,9},{9,10},{10,11},{11... | collective-permute-start | bytes 120968 | tf_op jit(solution)/shard_map/ppermute | solution.py:16
  36.9 9.0 %collective-permute-start.5 = (f32[7,36,20,2]{1,3,2,0:T(2,128)S(1)}, f32[7,36,20,2]{1,3,2,0:T(2,128)S(1)}, u32[]{:S(2)}, u32[]{:S(2)}) collective-permute-start(f32[7,36,20,2]{1,3,2,0:T(2,128)S(1)} %copy.38), channel_id=1, source_target_pairs={{1,0},{2,1},{3,2},{4,3},{5,4},{6,5},{7,6},{9,8},{10,9},{11,10},{12... | collective-permute-start | bytes 120968 | tf_op jit(solution)/shard_map/ppermute | solution.py:16
  58.6 1.1 %copy-start.5 = (f32[35,19,131]{2,0,1:T(8,128)S(1)}, f32[35,19,131]{2,0,1:T(8,128)}, u32[]{:S(2)}) copy-start(f32[35,19,131]{2,0,1:T(8,128)} %and_convert_fusion) | copy-start | bytes 1045384
  63.7 1.1 %copy-start.6 = (f32[33,17,129]{2,0,1:T(8,128)S(1)}, f32[33,17,129]{2,0,1:T(8,128)}, u32[]{:S(2)}) copy-start(f32[33,17,129]{2,0,1:T(8,128)} %and_convert_fusion.1) | copy-start | bytes 868432
  68.8 2.7 %copy-start.3 = (f32[4,32,16,128]{1,3,2,0:T(8,128)S(1)}, f32[4,32,16,128]{1,3,2,0:T(8,128)}, u32[]{:S(2)}) copy-start(f32[4,32,16,128]{1,3,2,0:T(8,128)} %copy.42) | copy-start | bytes 3145732
  69.1 3.5 %copy-start.4 = (f32[3,32,16,128]{3,1,2,0:T(8,128)}, f32[3,32,16,128]{3,1,2,0:T(8,128)S(1)}, u32[]{:S(2)}) copy-start(f32[3,32,16,128]{3,1,2,0:T(8,128)S(1)} %slice_add_fusion.1) | copy-start | bytes 2359300
  72.6 1.9 %copy-start.2 = (f32[4,32,16,128]{1,3,2,0:T(8,128)}, f32[4,32,16,128]{1,3,2,0:T(8,128)S(1)}, u32[]{:S(2)}) copy-start(f32[4,32,16,128]{1,3,2,0:T(8,128)S(1)} %fusion) | copy-start | bytes 3145732
  83.0 18.2 %all-to-all-start = ((f32[32,2,4]{2,1,0:T(2,128)}), f32[32,2,4]{2,1,0:T(2,128)S(1)}, u32[]{:S(2)}, u32[]{:S(2)}) async-start(f32[32,2,4]{2,1,0:T(2,128)} %reshape.142), calls=%async_computation | async-start | bytes 65536 | tf_op jit(solution)/shard_map/all_to_all | solution.py:106
  93.4 8.6 %copy-start.1 = (bf16[4,2,4,256,64]{3,4,2,1,0:T(8,128)(2,1)S(1)}, bf16[4,2,4,256,64]{3,4,2,1,0:T(8,128)(2,1)}, u32[]{:S(2)}) copy-start(bf16[4,2,4,256,64]{3,4,2,1,0:T(8,128)(2,1)} %param.13) | copy-start | bytes 3145732

commit v3 on v2

--- a/solution.py
+++ b/solution.py
@@ -81,16 +81,19 @@
     h1_here = box(h1, (2, 2, 2), n(0))
     h2_here = box(h2, (1, 1, 1), n(0))
     local_z = port_z - lax.axis_index("gz") * cells_z
-    select = (local_z[:, None] == jnp.arange(cells_z)[None, :]).astype(jnp.float32)
+    onehot = (local_z[:, None] == jnp.arange(cells_z)[None, :]).astype(jnp.float32)
+    lanes = dft_sums.shape[-1]
+    lane_part = jnp.arange(lanes) // (lanes // 4)
+    spread_of = (lane_part[None, :] == jnp.arange(4)[:, None]).astype(jnp.float32)
     dft = dft_sums
     for step, (e_now, h_now) in enumerate(((e1_here, h1_here), (e2, h2_here))):
         tangent = jnp.stack([e_now[0], e_now[1], h_now[0], h_now[1]])
-        planes = jnp.einsum("cxyz,pz->pxyc", tangent, select, precision=lax.Precision.HIGHEST)
+        planes = jnp.sum(tangent[None] * onehot[:, None, None, None, :], axis=-1)
         phase = omega * jnp.float32(step + 1)
         trig = jnp.stack([jnp.cos(phase), jnp.sin(phase)])
-        increment = planes[:, :, :, :, None, None] * trig[None, None, None, None, :, :]
-        dft = dft + increment.reshape(dft.shape)
-    shaped = dft.reshape(ports_here, cells_x, cells_y, 4, 2, NF)
+        coef = jnp.tile(trig.reshape(-1), 4)
+        spread = jnp.sum(planes[..., None] * spread_of[None, :, None, None, :], axis=1)
+        dft = dft + spread * coef
     groups = lax.axis_size(("gx", "gy"))
     owned = ports_here * NF // groups
     start_x = lax.axis_index("gx") * cells_x
@@ -98,10 +101,11 @@
     tile = lax.dynamic_slice(
         mode_profiles, (0, 0, 0, start_x, start_y), (ports_here, MODES, 4, cells_x, cells_y)
     )
-    partial_sums = jnp.einsum(
-        "pxycqf,pmcxy->pfmq", shaped, tile.astype(jnp.float32), precision=lax.Precision.HIGHEST
-    )
-    partial_sums = partial_sums.reshape(ports_here * NF, MODES * 2)
+    weights = tile.reshape(ports_here, MODES * 4, cells_x, cells_y).astype(jnp.float32)
+    crossed = jnp.einsum("pxyl,pnxy->pnl", dft, weights, precision=lax.Precision.HIGHEST)
+    crossed = crossed.reshape(ports_here, MODES, 4, 4, 2, NF)
+    diagonal = sum(crossed[:, :, c, c] for c in range(4))
+    partial_sums = jnp.transpose(diagonal, (0, 3, 1, 2)).reshape(ports_here * NF, MODES * 2)
     pieces = partial_sums.reshape(groups, owned, MODES * 2)
     result = jnp.sum(lax.all_to_all(pieces, ("gx", "gy"), 0, 0, tiled=False), axis=0)
     return (e2, h2_here, dft, result.reshape(owned, 1, MODES * 2))

time: 103 us -> 119 us (1.16)
  other arithmetic: 19.7 us -> 36.4 us
  local copies, waits for them, and re-layouts: 34.6 us -> 46.9 us
  matrix products: 11.9 us -> 0.98 us
  waiting for transfers between devices: 9.64 us -> 6.74 us
    slice x4 -> x8, local copies, waits for them, and re-layouts: 0.7 us -> 18.2 us  [per_device(): tangent = jnp.stack([e_now[0], e_now[1], h_now[0], h_now[1]])]
    dot_general x3 -> x1, matrix products: 11.9 us -> 0.98 us  [per_device(): jnp.einsum('pxyl,pnxy->pnl', dft, weights, precision=lax.Precision.HIGHEST)]
    another operation x4, other arithmetic: 3.05 us -> 9.67 us  [curl(): jnp.stack([d(vz, 1) - d(vy, 2), d(vx, 2) - d(vz, 0), d(vy, 0) - d(vx, 1)])]
    unnamed x29 -> x52, local copies, waits for them, and re-layouts: 18.1 us -> 11.8 us
    slice x2 -> x1, local copies, waits for them, and re-layouts: 5.93 us -> 0.18 us  [widen(): high = lax.slice_in_dim(stack, count - HALO, count, axis=dim)]
    concatenate x0 -> x1, local copies, waits for them, and re-layouts: none -> 4.66 us  [widen(): return jnp.concatenate([from_below, stack, from_above], axis=dim)]
    slice x1, local copies, waits for them, and re-layouts: 0.31 us -> 4.6 us  [box(): lax.slice(value, (0,) * lead + tuple(start), value.shape[:lead] + tuple((...]
    squeeze x0 -> x2, other arithmetic: none -> 3.32 us  [the longest x1 2.42 us: per_device(): e0, h0, inv = (stack[0:3], stack[3:6], stack[6])]
  transfers between devices with their start and end apart: 7 -> 7, of which waited for: 4 -> 3; matrix products, arithmetic and copies ran while one was open for 19% -> 18% of each run, Pallas kernels for 0% -> 0%
where the time goes in v3:
time: 119 us; the launch traced here: 118 us
  local copies, waits for them, and re-layouts  46.9 us (39%)
  other arithmetic  36.4 us (31%)
  starting transfers between devices  26 us (22%)
  waiting for transfers between devices  6.74 us (6%)
    slice x8, local copies, waits for them, and re-layouts, per_device(): tangent = jnp.stack([e_now[0], e_now[1], h_now[0], h_now[1]])  18.2 us
    ppermute x6, starting transfers between devices, shifted(): lax.ppermute(value, axis, [(source, source + steps) for source in range(f...  15.5 us
    unnamed x52, local copies, waits for them, and re-layouts  11.8 us
    all_to_all x1, starting transfers between devices, per_device(): lax.all_to_all(pieces, ('gx', 'gy'), 0, 0, tiled=False)  10.5 us
    another operation x4, other arithmetic, curl(): jnp.stack([d(vz, 1) - d(vy, 2), d(vx, 2) - d(vz, 0), d(vy, 0) - d(vx, 1)])  9.67 us
    concatenate x2, other arithmetic, widen(): return jnp.concatenate([from_below, stack, from_above], axis=dim)  7.96 us
    ppermute x6, waiting for transfers between devices, shifted(): lax.ppermute(value, axis, [(source, source + steps) for source in range(f...  6.74 us
    concatenate x1, local copies, waits for them, and re-layouts, widen(): return jnp.concatenate([from_below, stack, from_above], axis=dim)  4.66 us
  transfers between devices with their start and end apart: 7, of which 3 were waited for; matrix products, arithmetic and copies ran while one was open for 18% of the time, Pallas kernels for 0%

profile of v3, /device:TPU:96, one launch (start us, length us, event | category | flops | bytes accessed | tf_op | source)
XLA Modules:
  0.0 118.1 jit_solution(4375166370955091277)
XLA Ops:
  0.7 1.0 pad_maximum_fusion.9
  1.7 1.7 %collective-permute-start = (f32[7,2,16,128]{3,2,1,0:T(8,128)S(1)}, f32[7,2,16,128]{3,2,1,0:T(8,128)S(1)}, u32[]{:S(2)}, u32[]{:S(2)}) collective-permute-start(f32[7,2,16,128]{3,2,1,0:T(8,128)S(1)} %get-tuple-element.42), channel_id=1, source_target_pairs={{0,32},{32,64},{64,96},{96,128},{128,160},{160,192},{192,224},{1,3... | collective-permute-start | bytes 344072 | tf_op jit(solution)/shard_map/ppermute | solution.py:16
  3.5 1.3 %collective-permute-start.1 = (f32[7,2,16,128]{3,2,1,0:T(8,128)S(1)}, f32[7,2,16,128]{3,2,1,0:T(8,128)}, u32[]{:S(2)}, u32[]{:S(2)}) collective-permute-start(f32[7,2,16,128]{3,2,1,0:T(8,128)S(1)} %get-tuple-element.43), channel_id=1, source_target_pairs={{32,0},{64,32},{96,64},{128,96},{160,128},{192,160},{224,192},{33,... | collective-permute-start | bytes 344072 | tf_op jit(solution)/shard_map/ppermute | solution.py:16
  5.1 1.2 %and_convert_fusion.1 = f32[33,17,129]{0,2,1:T(8,128)} fusion(pred[33,17]{0,1:T(8,128)(4,1)S(1)} %broadcast_and_fusion, pred[129]{0:T(512)(128)(4,1)S(1)} %compare_and_fusion), kind=kLoop, calls=%fused_computation.75 | loop fusion | flops 144738 | bytes 290166 | tf_op jit(solution)/shard_map/convert_element_type | solution.py:62
  6.4 0.8 constant_dynamic-slice_fusion
  7.1 0.9 collective-permute-done.1
  8.1 1.6 %pad_maximum_fusion.1 = f32[7,36,16,128]{3,2,1,0:T(8,128)S(1)} fusion(f32[7,2,16,128]{3,2,1,0:T(8,128)} %collective-permute-done.1, f32[1,32,16,128]{3,2,1,0:T(8,128)S(1)} %bitcast.74, f32[3,32,16,128]{3,2,1,0:T(8,128)} %param.8, f32[3,32,16,128]{3,2,1,0:T(8,128)} %param.7, f32[7,2,16,128]{3,2,1,0:T(8,128)S(1)} %collective-permute-done), kind=kLoop, calls=%fused_computation.23 | loop fusion | flops 2064384 | bytes 4128768 | tf_op jit(solution)/shard_map/concatenate | solution.py:25
  9.9 4.2 %collective-permute-start.2 = (f32[7,36,2,128]{3,2,1,0:T(2,128)S(1)}, f32[7,36,2,128]{3,2,1,0:T(2,128)}, u32[]{:S(2)}, u32[]{:S(2)}) collective-permute-start(f32[7,36,2,128]{3,2,1,0:T(2,128)S(1)} %get-tuple-element.40), channel_id=1, source_target_pairs={{0,8},{8,16},{16,24},{1,9},{9,17},{17,25},{2,10},{10,18},{18,26},{... | collective-permute-start | bytes 774152 | tf_op jit(solution)/shard_map/ppermute | solution.py:16
  14.1 1.3 %collective-permute-start.3 = (f32[7,36,2,128]{3,2,1,0:T(2,128)S(1)}, f32[7,36,2,128]{3,2,1,0:T(2,128)}, u32[]{:S(2)}, u32[]{:S(2)}) collective-permute-start(f32[7,36,2,128]{3,2,1,0:T(2,128)S(1)} %get-tuple-element.41), channel_id=1, source_target_pairs={{8,0},{16,8},{24,16},{9,1},{17,9},{25,17},{10,2},{18,10},{26,18},{... | collective-permute-start | bytes 774152 | tf_op jit(solution)/shard_map/ppermute | solution.py:16
  15.4 1.2 %and_convert_fusion = f32[35,19,131]{0,2,1:T(8,128)} fusion(pred[35,19]{0,1:T(8,128)(4,1)S(1)} %broadcast_and_fusion.1, pred[131]{0:T(512)(128)(4,1)S(1)} %compare_and_fusion.3), kind=kLoop, calls=%fused_computation.43 | loop fusion | flops 174230 | bytes 349256 | tf_op jit(solution)/shard_map/convert_element_type | solution.py:62
  16.6 4.7 %copy.66 = f32[7,36,16,128]{1,3,2,0:T(8,128)} copy(f32[7,36,16,128]{3,2,1,0:T(8,128)S(1)} %pad_maximum_fusion.1) | data formatting | bytes 4128768 | tf_op jit(solution)/shard_map/concatenate | solution.py:25
  21.3 1.3 %copy.65 = f32[7,36,2,128]{1,3,2,0:T(8,128)S(1)} copy(f32[7,36,2,128]{3,2,1,0:T(2,128)} %collective-permute-done.2) | data formatting | bytes 516096 | tf_op jit(solution)/shard_map/ppermute | solution.py:16
  23.0 1.3 %copy.67 = f32[7,36,2,128]{1,3,2,0:T(8,128)S(1)} copy(f32[7,36,2,128]{3,2,1,0:T(2,128)} %collective-permute-done.3) | data formatting | bytes 516096 | tf_op jit(solution)/shard_map/ppermute | solution.py:16
  24.2 1.3 %pad_maximum_fusion.6 = (f32[7,36,20,2]{1,3,2,0:T(2,128)S(1)}, f32[7,36,20,2]{1,3,2,0:T(2,128)S(1)}) fusion(f32[7,36,2,128]{1,3,2,0:T(8,128)S(1)} %copy.67, f32[7,36,16,128]{1,3,2,0:T(8,128)} %copy.66, f32[7,36,2,128]{1,3,2,0:T(8,128)S(1)} %copy.65), kind=kLoop, calls=%fused_computation.96 | loop fusion | flops 40320 | bytes 2661120 | tf_op jit(solution)/shard_map/slice | solution.py:22
  25.6 5.0 %collective-permute-start.4 = (f32[7,36,20,2]{1,3,2,0:T(2,128)S(1)}, f32[7,36,20,2]{1,3,2,0:T(2,128)S(1)}, u32[]{:S(2)}, u32[]{:S(2)}) collective-permute-start(f32[7,36,20,2]{1,3,2,0:T(2,128)S(1)} %get-tuple-element.29), channel_id=1, source_target_pairs={{0,1},{1,2},{2,3},{3,4},{4,5},{5,6},{6,7},{8,9},{9,10},{10,11},{11... | collective-permute-start | bytes 120968 | tf_op jit(solution)/shard_map/ppermute | solution.py:16
  30.6 1.9 %collective-permute-start.5 = (f32[7,36,20,2]{1,3,2,0:T(2,128)S(1)}, f32[7,36,20,2]{1,3,2,0:T(2,128)}, u32[]{:S(2)}, u32[]{:S(2)}) collective-permute-start(f32[7,36,20,2]{1,3,2,0:T(2,128)S(1)} %get-tuple-element.30), channel_id=1, source_target_pairs={{1,0},{2,1},{3,2},{4,3},{5,4},{6,5},{7,6},{9,8},{10,9},{11,10},{12... | collective-permute-start | bytes 120968 | tf_op jit(solution)/shard_map/ppermute | solution.py:16
  33.6 5.4 %collective-permute-done.5 = f32[7,36,20,2]{1,3,2,0:T(2,128)} collective-permute-done((f32[7,36,20,2]{1,3,2,0:T(2,128)S(1)}, f32[7,36,20,2]{1,3,2,0:T(2,128)}, u32[]{:S(2)}, u32[]{:S(2)}) %collective-permute-start.5) | collective-permute-done | bytes 40352 | tf_op jit(solution)/shard_map/ppermute | solution.py:16
  39.0 2.4 %maximum_bitcast_fusion.3 = (f32[36,20,132]{0,2,1:T(8,128)S(1)}, f32[36,20,132]{0,2,1:T(8,128)S(1)}, f32[36,20,132]{0,2,1:T(8,128)S(1)}) fusion(f32[7,36,20,2]{1,3,2,0:T(2,128)} %collective-permute-done.5, f32[7,36,20,2]{1,3,2,0:T(2,128)S(1)} %collective-permute-done.4, f32[7,36,2,128]{1,3,2,0:T(8,128)S(1)} %copy.67, f32[7,36,16,128]{1,3,2,0:T(8,128)} %copy.66, ...), kind=kLoop, calls=%fused_computation.27 | loop fusion | flops 1140480 | bytes 3801600 | tf_op jit(solution)/shard_map/squeeze | solution.py:72
  41.5 0.9 maximum_bitcast_fusion.2
  42.4 2.5 %fusion.15 = (f32[1,35,19,131]{1,3,2,0:T(8,128)S(1)}, f32[1,35,19,131]{1,3,2,0:T(8,128)}, f32[1,35,19,131]{1,3,2,0:T(8,128)}) fusion(f32[36,20,132]{0,2,1:T(8,128)S(1)} %get-tuple-element.28, f32[36,20,132]{0,2,1:T(8,128)S(1)} %maximum_bitcast_fusion.2, f32[36,20,132]{0,2,1:T(8,128)S(1)} %get-tuple-element.27), kind=kLoop, calls=%fused_computation.41 | loop fusion | flops 784035 | bytes 4181520 | tf_op jit(solution)/shard_map/stack | solution.py:50
  44.8 6.4 %pad_maximum_fusion = f32[7,36,20,132]{1,3,2,0:T(8,128)S(1)} fusion(f32[7,36,20,2]{1,3,2,0:T(2,128)} %collective-permute-done.5, f32[7,36,2,128]{1,3,2,0:T(8,128)S(1)} %copy.67, f32[7,36,16,128]{1,3,2,0:T(8,128)S(1)} %bitcast.72, f32[7,36,2,128]{1,3,2,0:T(8,128)S(1)} %copy.65, f32[7,36,20,2]{1,3,2,0:T(2,128)S(1)} %collective-permute-done.4), kind=kLoop, calls=%fused_computation.2 | loop fusion | flops 2661120 | bytes 5322240 | tf_op jit(solution)/shard_map/concatenate | solution.py:25
  51.2 1.9 %fusion.4 = f32[3,35,19,131]{1,3,2,0:T(8,128)S(1)} fusion(f32[7,36,20,132]{1,3,2,0:T(8,128)S(1)} %pad_maximum_fusion, f32[1,35,19,131]{1,3,2,0:T(8,128)S(1)} %copy-done.8, f32[1,35,19,131]{1,3,2,0:T(8,128)S(1)} %copy-done.7, f32[1,35,19,131]{1,3,2,0:T(8,128)S(1)} %get-tuple-element.44, f32[35,19,131]{0,2,1:T(8,128)} %and_convert_fusion), kind=kLoop, calls=%fused_computation.10 | loop fusion | flops 1306725 | bytes 3484600 | tf_op jit(solution)/shard_map/mul | solution.py:75
  53.4 1.9 %slice.370 = f32[2,32,16,128]{1,3,2,0:T(8,128)} slice(f32[3,35,19,131]{1,3,2,0:T(8,128)S(1)} %fusion.4), slice={[0:2], [2:34], [2:18], [2:130]} | slice | bytes 1048576 | tf_op jit(solution)/shard_map/slice | solution.py:90
  55.7 2.4 %fusion.21 = (f32[1,34,18,130]{1,3,2,0:T(8,128)S(1)}, f32[1,34,18,130]{1,3,2,0:T(8,128)S(1)}, f32[1,34,18,130]{1,3,2,0:T(8,128)S(1)}) fusion(f32[35,19,131]{0,2,1:T(8,128)S(1)} %get-tuple-element.33, f32[35,19,131]{0,2,1:T(8,128)S(1)} %get-tuple-element.31, f32[35,19,131]{0,2,1:T(8,128)S(1)} %get-tuple-element.32), kind=kLoop, calls=%fused_computation.57 | loop fusion | flops 716040 | bytes 3818880 | tf_op jit(solution)/shard_map/stack | solution.py:50
  58.0 1.2 %slice_add_fusion = f32[3,34,18,130]{1,3,2,0:T(8,128)S(1)} fusion(f32[7,36,20,132]{1,3,2,0:T(8,128)S(1)} %pad_maximum_fusion, f32[1,34,18,130]{1,3,2,0:T(8,128)S(1)} %get-tuple-element.49, f32[1,34,18,130]{1,3,2,0:T(8,128)S(1)} %get-tuple-element.48, f32[1,34,18,130]{1,3,2,0:T(8,128)S(1)} %get-tuple-element.47, f32[34,18,130]{0,2,1:T(8,128)S(1)} %slice_multiply_fusion), kind=kLoop, calls=%fused_computation.12 | loop fusion | flops 954720 | bytes 3182400 | tf_op jit(solution)/shard_map/add | solution.py:76
  59.2 2.3 %slice.369 = f32[2,32,16,128]{1,3,2,0:T(8,128)} slice(f32[3,34,18,130]{1,3,2,0:T(8,128)S(1)} %slice_add_fusion), slice={[0:2], [1:33], [1:17], [1:129]} | slice | bytes 1048576 | tf_op jit(solution)/shard_map/slice | solution.py:90
  62.0 1.3 %slice_multiply_fusion.1 = f32[32,16,128]{0,2,1:T(8,128)} fusion(f32[36,20,132]{0,2,1:T(8,128)S(1)} %get-tuple-element.26), kind=kLoop, calls=%fused_computation.89 | loop fusion | flops 65536 | bytes 524288 | tf_op jit(solution)/shard_map/mul | solution.py:79
  63.3 0.8 fusion.27
  64.6 1.1 fusion.5
  65.7 1.5 %slice_bitcast_fusion.8 = (f32[33,17,129]{0,2,1:T(8,128)S(1)}, f32[33,17,129]{0,2,1:T(8,128)S(1)}, f32[33,17,129]{0,2,1:T(8,128)}) fusion(f32[3,33,17,129]{1,3,2,0:T(8,128)S(1)} %fusion.5), kind=kLoop, calls=%fused_computation.62 | loop fusion | bytes 1736856 | tf_op jit(solution)/shard_map/squeeze | solution.py:48
  67.9 2.0 %slice.372 = f32[2,32,16,128]{1,3,2,0:T(8,128)} slice(f32[3,33,17,129]{1,3,2,0:T(8,128)S(1)} %fusion.5), slice={[0:2], [1:33], [1:17], [1:129]} | slice | bytes 1048576 | tf_op jit(solution)/shard_map/slice | solution.py:90
  69.8 3.0 %copy.68 = f32[2,32,16,128]{3,2,1,0:T(8,128)} copy(f32[2,32,16,128]{1,3,2,0:T(8,128)} %slice.369) | data formatting | bytes 1048576 | tf_op jit(solution)/shard_map/slice | solution.py:90
  72.8 3.0 %copy.69 = f32[2,32,16,128]{3,2,1,0:T(8,128)} copy(f32[2,32,16,128]{1,3,2,0:T(8,128)} %slice.370) | data formatting | bytes 1048576 | tf_op jit(solution)/shard_map/slice | solution.py:90
  75.8 4.1 %fusion.33 = (f32[1,32,16,128]{1,3,2,0:T(8,128)S(1)}, f32[1,32,16,128]{1,3,2,0:T(8,128)S(1)}, f32[1,32,16,128]{1,3,2,0:T(8,128)S(1)}) fusion(f32[33,17,129]{0,2,1:T(8,128)} %get-tuple-element.39, f32[33,17,129]{0,2,1:T(8,128)S(1)} %get-tuple-element.37, f32[33,17,129]{0,2,1:T(8,128)S(1)} %get-tuple-element.38), kind=kLoop, calls=%fused_computation.87 | loop fusion | flops 589824 | bytes 3145728 | tf_op jit(solution)/shard_map/stack | solution.py:50
  79.9 1.3 %slice_add_fusion.1 = f32[3,32,16,128]{1,3,2,0:T(8,128)S(1)} fusion(f32[3,34,18,130]{1,3,2,0:T(8,128)S(1)} %copy-done.3, f32[1,32,16,128]{1,3,2,0:T(8,128)S(1)} %get-tuple-element.55, f32[1,32,16,128]{1,3,2,0:T(8,128)S(1)} %get-tuple-element.54, f32[1,32,16,128]{1,3,2,0:T(8,128)S(1)} %get-tuple-element.53, f32[32,16,128]{0,2,1:T(8,128)S(1)} %copy-done.11), kind=kLoop, calls=%fused_computation.17 | loop fusion | flops 786432 | bytes 2621440 | tf_op jit(solution)/shard_map/add | solution.py:79
  81.2 1.7 %copy-done.5 = f32[3,32,16,128]{1,3,2,0:T(8,128)} copy-done((f32[3,32,16,128]{1,3,2,0:T(8,128)}, f32[3,32,16,128]{1,3,2,0:T(8,128)S(1)}, u32[]{:S(2)}) %copy-start.5) | copy-done | bytes 786456
  82.9 1.5 %slice.371 = f32[2,32,16,128]{1,3,2,0:T(8,128)} slice(f32[3,32,16,128]{1,3,2,0:T(8,128)S(1)} %slice_add_fusion.1), slice={[0:2], [0:32], [0:16], [0:128]} | slice | bytes 1048576 | tf_op jit(solution)/shard_map/slice | solution.py:90
  84.4 3.1 %copy.70 = f32[2,32,16,128]{3,2,1,0:T(8,128)} copy(f32[2,32,16,128]{1,3,2,0:T(8,128)} %slice.371) | data formatting | bytes 1048576 | tf_op jit(solution)/shard_map/slice | solution.py:90
  87.5 1.4 %copy.71 = f32[2,32,16,128]{3,2,1,0:T(8,128)} copy(f32[2,32,16,128]{1,3,2,0:T(8,128)S(1)} %copy-done.6) | data formatting | bytes 1048576 | tf_op jit(solution)/shard_map/slice | solution.py:90
  89.0 1.0 copy-done.14
  90.2 1.2 fusion
  91.3 1.5 %multiply_reduce_fusion.2 = (f32[4,32,16,128]{3,2,1,0:T(8,128)S(1)}, f32[4,32,16,128]{3,2,1,0:T(8,128)S(1)}) fusion(f32[4,128]{1,0:T(4,128)S(1)} %get-tuple-element.65, f32[4,4,32,16,128]{4,3,2,1,0:T(8,128)S(1)} %fusion, f32[4,128]{1,0:T(4,128)S(1)} %get-tuple-element.64, f32[4,32,16,128]{3,2,1,0:T(8,128)S(1)} %pad_maximum_fusion.2), kind=kOutput, calls=%fused_computation.6 | output fusion | flops 4726911 | bytes 7344128 | tf_op jit(solution)/shard_map/mul | solution.py:95
  93.8 1.0 convolution_bitcast_fusion
  95.1 0.9 copy.78
  96.0 10.5 %all-to-all-start = ((f32[32,2,4]{2,1,0:T(2,128)}), f32[32,2,4]{2,1,0:T(2,128)S(1)}, u32[]{:S(2)}, u32[]{:S(2)}) async-start(f32[32,2,4]{2,1,0:T(2,128)} %copy.78), calls=%async_computation | async-start | bytes 65536 | tf_op jit(solution)/shard_map/all_to_all | solution.py:110
  106.5 3.1 %copy.81 = f32[3,32,16,128]{3,2,1,0:T(8,128)} copy(f32[3,32,16,128]{1,3,2,0:T(8,128)} %copy-done.5) | data formatting | bytes 1572864
  109.6 4.6 %slice.368 = f32[3,32,16,128]{1,3,2,0:T(8,128)} slice(f32[3,33,17,129]{1,3,2,0:T(8,128)} %copy-done.4), slice={[0:3], [1:33], [1:17], [1:129]} | slice | bytes 1572864 | tf_op jit(solution)/shard_map/slice | solution.py:30
  114.2 3.1 %copy.82 = f32[3,32,16,128]{3,2,1,0:T(8,128)} copy(f32[3,32,16,128]{1,3,2,0:T(8,128)} %slice.368) | data formatting | bytes 1572864
  (86 shorter events, 6.6 us)
Async XLA Ops:
  0.6 5.7 %copy-start = (bf16[4,2,4,256,64]{3,4,2,1,0:T(8,128)(2,1)S(1)}, bf16[4,2,4,256,64]{3,4,2,1,0:T(8,128)(2,1)}, u32[]{:S(2)}) copy-start(bf16[4,2,4,256,64]{3,4,2,1,0:T(8,128)(2,1)} %param.13) | copy-start | bytes 3145732
  0.6 4.2 %copy-start.21 = (s32[4]{0:T(128)S(1)}, s32[4]{0:T(128)}, u32[]{:S(2)}) copy-start(s32[4]{0:T(128)} %param.12) | copy-start | bytes 52
  0.7 4.2 %copy-start.20 = (f32[16]{0:T(128)S(1)}, f32[16]{0:T(128)}, u32[]{:S(2)}) copy-start(f32[16]{0:T(128)} %param.11) | copy-start | bytes 196
  0.7 7.4 %copy-start.17 = (f32[32,16,128]{2,1,0:T(8,128)S(1)}, f32[32,16,128]{2,1,0:T(8,128)}, u32[]{:S(2)}) copy-start(f32[32,16,128]{2,1,0:T(8,128)} %param.9) | copy-start | bytes 786436
  1.7 5.4 %collective-permute-start = (f32[7,2,16,128]{3,2,1,0:T(8,128)S(1)}, f32[7,2,16,128]{3,2,1,0:T(8,128)S(1)}, u32[]{:S(2)}, u32[]{:S(2)}) collective-permute-start(f32[7,2,16,128]{3,2,1,0:T(8,128)S(1)} %get-tuple-element.42), channel_id=1, source_target_pairs={{0,32},{32,64},{64,96},{96,128},{128,160},{160,192},{192,224},{1,3... | collective-permute-start | bytes 344072 | tf_op jit(solution)/shard_map/ppermute | solution.py:16
  3.5 4.6 %collective-permute-start.1 = (f32[7,2,16,128]{3,2,1,0:T(8,128)S(1)}, f32[7,2,16,128]{3,2,1,0:T(8,128)}, u32[]{:S(2)}, u32[]{:S(2)}) collective-permute-start(f32[7,2,16,128]{3,2,1,0:T(8,128)S(1)} %get-tuple-element.43), channel_id=1, source_target_pairs={{32,0},{64,32},{96,64},{128,96},{160,128},{192,160},{224,192},{33,... | collective-permute-start | bytes 344072 | tf_op jit(solution)/shard_map/ppermute | solution.py:16
  9.9 11.4 %collective-permute-start.2 = (f32[7,36,2,128]{3,2,1,0:T(2,128)S(1)}, f32[7,36,2,128]{3,2,1,0:T(2,128)}, u32[]{:S(2)}, u32[]{:S(2)}) collective-permute-start(f32[7,36,2,128]{3,2,1,0:T(2,128)S(1)} %get-tuple-element.40), channel_id=1, source_target_pairs={{0,8},{8,16},{16,24},{1,9},{9,17},{17,25},{2,10},{10,18},{18,26},{... | collective-permute-start | bytes 774152 | tf_op jit(solution)/shard_map/ppermute | solution.py:16
  14.1 8.9 %collective-permute-start.3 = (f32[7,36,2,128]{3,2,1,0:T(2,128)S(1)}, f32[7,36,2,128]{3,2,1,0:T(2,128)}, u32[]{:S(2)}, u32[]{:S(2)}) collective-permute-start(f32[7,36,2,128]{3,2,1,0:T(2,128)S(1)} %get-tuple-element.41), channel_id=1, source_target_pairs={{8,0},{16,8},{24,16},{9,1},{17,9},{25,17},{10,2},{18,10},{26,18},{... | collective-permute-start | bytes 774152 | tf_op jit(solution)/shard_map/ppermute | solution.py:16
  24.2 8.7 %copy-start.19 = (bf16[4,2,4,32,16]{3,4,2,1,0:T(8,128)(2,1)S(1)}, bf16[4,2,4,32,16]{3,4,2,1,0:T(8,128)(2,1)}, u32[]{:S(2)}) copy-start(bf16[4,2,4,32,16]{3,4,2,1,0:T(8,128)(2,1)} %constant_dynamic-slice_fusion) | copy-start | bytes 98308
  25.6 8.0 %collective-permute-start.4 = (f32[7,36,20,2]{1,3,2,0:T(2,128)S(1)}, f32[7,36,20,2]{1,3,2,0:T(2,128)S(1)}, u32[]{:S(2)}, u32[]{:S(2)}) collective-permute-start(f32[7,36,20,2]{1,3,2,0:T(2,128)S(1)} %get-tuple-element.29), channel_id=1, source_target_pairs={{0,1},{1,2},{2,3},{3,4},{4,5},{5,6},{6,7},{8,9},{9,10},{10,11},{11... | collective-permute-start | bytes 120968 | tf_op jit(solution)/shard_map/ppermute | solution.py:16
  30.6 8.4 %collective-permute-start.5 = (f32[7,36,20,2]{1,3,2,0:T(2,128)S(1)}, f32[7,36,20,2]{1,3,2,0:T(2,128)}, u32[]{:S(2)}, u32[]{:S(2)}) collective-permute-start(f32[7,36,20,2]{1,3,2,0:T(2,128)S(1)} %get-tuple-element.30), channel_id=1, source_target_pairs={{1,0},{2,1},{3,2},{4,3},{5,4},{6,5},{7,6},{9,8},{10,9},{11,10},{12... | collective-permute-start | bytes 120968 | tf_op jit(solution)/shard_map/ppermute | solution.py:16
  32.9 8.5 %slice-start = ((s8[7340032]{0:T(1024)(128)(4,1)}), s8[4194304]{0:T(1024)(128)(4,1)S(1)}, s32[]{:S(2)}) async-start(s8[7340032]{0:T(1024)(128)(4,1)} %bitcast.71), calls=%async_computation.1 | async-start | bytes 8388608
  33.6 7.8 %slice-start.1 = ((s8[7340032]{0:T(1024)(128)(4,1)}), s8[3145728]{0:T(1024)(128)(4,1)S(1)}, s32[]{:S(2)}) async-start(s8[7340032]{0:T(1024)(128)(4,1)} %bitcast.71), calls=%async_computation.2 | async-start | bytes 6291456
  44.8 6.4 %copy-start.7 = (f32[1,35,19,131]{1,3,2,0:T(8,128)S(1)}, f32[1,35,19,131]{1,3,2,0:T(8,128)}, u32[]{:S(2)}) copy-start(f32[1,35,19,131]{1,3,2,0:T(8,128)} %get-tuple-element.45) | copy-start | bytes 1045384
  44.8 6.4 %copy-start.8 = (f32[1,35,19,131]{1,3,2,0:T(8,128)S(1)}, f32[1,35,19,131]{1,3,2,0:T(8,128)}, u32[]{:S(2)}) copy-start(f32[1,35,19,131]{1,3,2,0:T(8,128)} %get-tuple-element.46) | copy-start | bytes 1045384
  59.2 2.5 %copy-start.2 = (f32[3,34,18,130]{1,3,2,0:T(8,128)}, f32[3,34,18,130]{1,3,2,0:T(8,128)S(1)}, u32[]{:S(2)}) copy-start(f32[3,34,18,130]{1,3,2,0:T(8,128)S(1)} %slice_add_fusion) | copy-start | bytes 2864164
  63.3 1.3 %copy-start.9 = (f32[33,17,129]{0,2,1:T(8,128)S(1)}, f32[33,17,129]{0,2,1:T(8,128)}, u32[]{:S(2)}) copy-start(f32[33,17,129]{0,2,1:T(8,128)} %and_convert_fusion.1) | copy-start | bytes 868432
  65.7 2.1 %copy-start.4 = (f32[3,33,17,129]{1,3,2,0:T(8,128)}, f32[3,33,17,129]{1,3,2,0:T(8,128)S(1)}, u32[]{:S(2)}) copy-start(f32[3,33,17,129]{1,3,2,0:T(8,128)S(1)} %fusion.5) | copy-start | bytes 2605288
  75.8 4.1 %copy-start.3 = (f32[3,34,18,130]{1,3,2,0:T(8,128)S(1)}, f32[3,34,18,130]{1,3,2,0:T(8,128)}, u32[]{:S(2)}) copy-start(f32[3,34,18,130]{1,3,2,0:T(8,128)} %copy-done.2) | copy-start | bytes 2864164
  75.8 4.1 %copy-start.11 = (f32[32,16,128]{0,2,1:T(8,128)S(1)}, f32[32,16,128]{0,2,1:T(8,128)}, u32[]{:S(2)}) copy-start(f32[32,16,128]{0,2,1:T(8,128)} %slice_multiply_fusion.1) | copy-start | bytes 786436
  81.2 1.7 %copy-start.5 = (f32[3,32,16,128]{1,3,2,0:T(8,128)}, f32[3,32,16,128]{1,3,2,0:T(8,128)S(1)}, u32[]{:S(2)}) copy-start(f32[3,32,16,128]{1,3,2,0:T(8,128)S(1)} %slice_add_fusion.1) | copy-start | bytes 2359300
  84.4 3.1 %copy-start.6 = (f32[2,32,16,128]{1,3,2,0:T(8,128)S(1)}, f32[2,32,16,128]{1,3,2,0:T(8,128)}, u32[]{:S(2)}) copy-start(f32[2,32,16,128]{1,3,2,0:T(8,128)} %slice.372) | copy-start | bytes 1572868
  87.5 1.4 %copy-start.12 = (f32[2,32,16,128]{3,2,1,0:T(8,128)S(1)}, f32[2,32,16,128]{3,2,1,0:T(8,128)}, u32[]{:S(2)}) copy-start(f32[2,32,16,128]{3,2,1,0:T(8,128)} %copy.68) | copy-start | bytes 1572868
  87.5 1.4 %copy-start.13 = (f32[2,32,16,128]{3,2,1,0:T(8,128)S(1)}, f32[2,32,16,128]{3,2,1,0:T(8,128)}, u32[]{:S(2)}) copy-start(f32[2,32,16,128]{3,2,1,0:T(8,128)} %copy.69) | copy-start | bytes 1572868
  88.9 1.0 copy-start.14
  88.9 1.2 %copy-start.15 = (f32[2,32,16,128]{3,2,1,0:T(8,128)S(1)}, f32[2,32,16,128]{3,2,1,0:T(8,128)}, u32[]{:S(2)}) copy-start(f32[2,32,16,128]{3,2,1,0:T(8,128)} %copy.71) | copy-start | bytes 1572868
  91.3 1.5 %copy-start.16 = (f32[4,32,16,128]{3,2,1,0:T(8,128)S(1)}, f32[4,32,16,128]{3,2,1,0:T(8,128)}, u32[]{:S(2)}) copy-start(f32[4,32,16,128]{3,2,1,0:T(8,128)} %param.10) | copy-start | bytes 3145732
  92.9 0.9 copy-start.18
  93.1 16.5 %copy-start.10 = (f32[4,32,16,128]{3,2,1,0:T(8,128)}, f32[4,32,16,128]{3,2,1,0:T(8,128)S(1)}, u32[]{:S(2)}) copy-start(f32[4,32,16,128]{3,2,1,0:T(8,128)S(1)} %multiply_add_fusion) | copy-start | bytes 3145732
  96.0 21.3 %all-to-all-start = ((f32[32,2,4]{2,1,0:T(2,128)}), f32[32,2,4]{2,1,0:T(2,128)S(1)}, u32[]{:S(2)}, u32[]{:S(2)}) async-start(f32[32,2,4]{2,1,0:T(2,128)} %copy.78), calls=%async_computation | async-start | bytes 65536 | tf_op jit(solution)/shard_map/all_to_all | solution.py:110
  109.6 8.5 %copy-start.1 = (bf16[4,2,4,256,64]{3,4,2,1,0:T(8,128)(2,1)S(1)}, bf16[4,2,4,256,64]{3,4,2,1,0:T(8,128)(2,1)}, u32[]{:S(2)}) copy-start(bf16[4,2,4,256,64]{3,4,2,1,0:T(8,128)(2,1)} %param.13) | copy-start | bytes 3145732

commit v4 on v3

--- a/solution.py
+++ b/solution.py
@@ -2,12 +2,17 @@
 import jax.numpy as jnp
 from jax import lax
 from jax.sharding import PartitionSpec as P
+from jax.experimental.layout import Layout, with_layout_constraint
 
 STEPS = 2
 NF = 16
 MODES = 2
 HALO = 2
 AXES = ("gx", "gy", "gz")
+
+
+def pin(value):
+    return with_layout_constraint(value, Layout(tuple(range(value.ndim))))
 
 
 def shifted(value, axis, steps):
@@ -68,15 +73,15 @@
     ports_here = dft_sums.shape[0]
     stack = jnp.concatenate([e_field, h_field, inv_permittivity[None]], axis=0)
     for dim, axis in enumerate(AXES):
-        stack = widen(stack, dim + 1, axis)
+        stack = pin(widen(stack, dim + 1, axis))
     e0, h0, inv = stack[0:3], stack[3:6], stack[6]
     n = lambda k: tuple(c + k for c in cells)
     h1 = box(h0, (0, 0, 0), n(3)) - 0.5 * curl(e0, (0, 0, 0), n(3), 1)
-    h1 = h1 * inside(-2, n(3), cells)
-    e1 = box(e0, (1, 1, 1), n(2)) + 0.5 * box(inv, (1, 1, 1), n(2)) * curl(h1, (1, 1, 1), n(2), -1)
+    h1 = pin(h1 * inside(-2, n(3), cells))
+    e1 = pin(box(e0, (1, 1, 1), n(2)) + 0.5 * box(inv, (1, 1, 1), n(2)) * curl(h1, (1, 1, 1), n(2), -1))
     h2 = box(h1, (1, 1, 1), n(1)) - 0.5 * curl(e1, (0, 0, 0), n(1), 1)
-    h2 = h2 * inside(-1, n(1), cells)
-    e2 = box(e1, (1, 1, 1), n(0)) + 0.5 * box(inv, (2, 2, 2), n(0)) * curl(h2, (1, 1, 1), n(0), -1)
+    h2 = pin(h2 * inside(-1, n(1), cells))
+    e2 = pin(box(e1, (1, 1, 1), n(0)) + 0.5 * box(inv, (2, 2, 2), n(0)) * curl(h2, (1, 1, 1), n(0), -1))
     e1_here = box(e1, (1, 1, 1), n(0))
     h1_here = box(h1, (2, 2, 2), n(0))
     h2_here = box(h2, (1, 1, 1), n(0))
@@ -87,13 +92,13 @@
     spread_of = (lane_part[None, :] == jnp.arange(4)[:, None]).astype(jnp.float32)
     dft = dft_sums
     for step, (e_now, h_now) in enumerate(((e1_here, h1_here), (e2, h2_here))):
-        tangent = jnp.stack([e_now[0], e_now[1], h_now[0], h_now[1]])
+        tangent = pin(jnp.stack([e_now[0], e_now[1], h_now[0], h_now[1]]))
         planes = jnp.sum(tangent[None] * onehot[:, None, None, None, :], axis=-1)
         phase = omega * jnp.float32(step + 1)
         trig = jnp.stack([jnp.cos(phase), jnp.sin(phase)])
         coef = jnp.tile(trig.reshape(-1), 4)
         spread = jnp.sum(planes[..., None] * spread_of[None, :, None, None, :], axis=1)
-        dft = dft + spread * coef
+        dft = pin(dft + spread * coef)
     groups = lax.axis_size(("gx", "gy"))
     owned = ports_here * NF // groups
     start_x = lax.axis_index("gx") * cells_x

time: 119 us -> 94.6 us (0.79)
  local copies, waits for them, and re-layouts: 46.9 us -> 26.3 us
  other arithmetic: 36.4 us -> 24.7 us
  waiting for transfers between devices: 6.74 us -> 15.7 us
    slice x8 -> x5, local copies, waits for them, and re-layouts: 18.2 us -> 3.89 us  [the longest x1 3.24 us: widen(): low = lax.slice_in_dim(stack, 0, HALO, axis=dim)]
    unnamed x52 -> x24, local copies, waits for them, and re-layouts: 11.8 us -> 3.6 us
    slice x1 -> x2, local copies, waits for them, and re-layouts: 0.18 us -> 6.82 us  [widen(): high = lax.slice_in_dim(stack, count - HALO, count, axis=dim)]
    all_to_all x1, waiting for transfers between devices: 0.01 us -> 6.23 us  [per_device(): lax.all_to_all(pieces, ('gx', 'gy'), 0, 0, tiled=False)]
    another operation x4, other arithmetic: 9.67 us -> 3.57 us  [curl(): jnp.stack([d(vz, 1) - d(vy, 2), d(vx, 2) - d(vz, 0), d(vy, 0) - d(vx, 1)])]
    concatenate x1 -> x0, local copies, waits for them, and re-layouts: 4.66 us -> none  [widen(): return jnp.concatenate([from_below, stack, from_above], axis=dim)]
    ppermute x2, local copies, waits for them, and re-layouts: 2.53 us -> 6.25 us  [shifted(): lax.ppermute(value, axis, [(source, source + steps) for source in range(f...]
    slice x1, local copies, waits for them, and re-layouts: 4.6 us -> 1.15 us  [box(): lax.slice(value, (0,) * lead + tuple(start), value.shape[:lead] + tuple((...]
  transfers between devices with their start and end apart: 7 -> 7, of which waited for: 3 -> 5; matrix products, arithmetic and copies ran while one was open for 18% -> 13% of each run, Pallas kernels for 0% -> 0%
where the time goes in v4:
time: 94.6 us; the launch traced here: 93.8 us
  local copies, waits for them, and re-layouts  26.3 us (28%)
  starting transfers between devices  25.1 us (27%)
  other arithmetic  24.7 us (26%)
  waiting for transfers between devices  15.7 us (17%)
  between operations  1.05 us (1%)
  matrix products  0.97 us (1%)
    ppermute x6, starting transfers between devices, shifted(): lax.ppermute(value, axis, [(source, source + steps) for source in range(f...  14.8 us
    all_to_all x1, starting transfers between devices, per_device(): lax.all_to_all(pieces, ('gx', 'gy'), 0, 0, tiled=False)  10.3 us
    concatenate x2, other arithmetic, widen(): return jnp.concatenate([from_below, stack, from_above], axis=dim)  10.1 us
    ppermute x6, waiting for transfers between devices, shifted(): lax.ppermute(value, axis, [(source, source + steps) for source in range(f...  9.49 us
    slice x2, local copies, waits for them, and re-layouts, widen(): high = lax.slice_in_dim(stack, count - HALO, count, axis=dim)  6.82 us
    ppermute x2, local copies, waits for them, and re-layouts, shifted(): lax.ppermute(value, axis, [(source, source + steps) for source in range(f...  6.25 us
    all_to_all x1, waiting for transfers between devices, per_device(): lax.all_to_all(pieces, ('gx', 'gy'), 0, 0, tiled=False)  6.23 us
    unnamed x24, local copies, waits for them, and re-layouts  3.6 us
  transfers between devices with their start and end apart: 7, of which 5 were waited for; matrix products, arithmetic and copies ran while one was open for 13% of the time, Pallas kernels for 0%

profile of v4, /device:TPU:96, one launch (start us, length us, event | category | flops | bytes accessed | tf_op | source)
XLA Modules:
  0.0 93.8 jit_solution(7197069286252594153)
XLA Ops:
  0.7 1.1 %pad_maximum_fusion.11 = (f32[7,2,16,128]{3,2,1,0:T(8,128)S(1)}, f32[7,2,16,128]{3,2,1,0:T(8,128)S(1)}) fusion(f32[1,32,16,128]{3,2,1,0:T(8,128)} %bitcast.71, f32[3,32,16,128]{3,2,1,0:T(8,128)} %param.8, f32[3,32,16,128]{3,2,1,0:T(8,128)} %param.7), kind=kLoop, calls=%fused_computation.101 | loop fusion | flops 114688 | bytes 2064384 | tf_op jit(solution)/shard_map/slice | solution.py:27
  1.8 1.7 %collective-permute-start = (f32[7,2,16,128]{3,2,1,0:T(8,128)S(1)}, f32[7,2,16,128]{3,2,1,0:T(8,128)S(1)}, u32[]{:S(2)}, u32[]{:S(2)}) collective-permute-start(f32[7,2,16,128]{3,2,1,0:T(8,128)S(1)} %get-tuple-element.39), channel_id=1, source_target_pairs={{0,32},{32,64},{64,96},{96,128},{128,160},{160,192},{192,224},{1,3... | collective-permute-start | bytes 344072 | tf_op jit(solution)/shard_map/ppermute | solution.py:21
  3.5 1.3 %collective-permute-start.1 = (f32[7,2,16,128]{3,2,1,0:T(8,128)S(1)}, f32[7,2,16,128]{3,2,1,0:T(8,128)S(1)}, u32[]{:S(2)}, u32[]{:S(2)}) collective-permute-start(f32[7,2,16,128]{3,2,1,0:T(8,128)S(1)} %get-tuple-element.40), channel_id=1, source_target_pairs={{32,0},{64,32},{96,64},{128,96},{160,128},{192,160},{224,192},{33,... | collective-permute-start | bytes 344072 | tf_op jit(solution)/shard_map/ppermute | solution.py:21
  4.9 0.7 broadcast_subtract_fusion
  5.6 0.7 cosine_bitcast_fusion.1
  6.4 1.1 %and_convert_fusion.1 = f32[33,17,129]{2,1,0:T(8,128)} fusion(pred[129]{0:T(512)(128)(4,1)S(1)} %compare_and_fusion, pred[33,17]{1,0:T(8,128)(4,1)S(1)} %broadcast_and_fusion), kind=kLoop, calls=%fused_computation.78 | loop fusion | flops 144738 | bytes 290166 | tf_op jit(solution)/shard_map/convert_element_type | solution.py:67
  7.7 0.3 collective-permute-done.1
  8.2 3.5 %collective-permute-start.2 = (f32[7,36,2,128]{3,2,1,0:T(2,128)S(1)}, f32[7,36,2,128]{3,2,1,0:T(2,128)S(1)}, u32[]{:S(2)}, u32[]{:S(2)}) collective-permute-start(f32[7,36,2,128]{3,2,1,0:T(2,128)S(1)} %get-tuple-element.37), channel_id=1, source_target_pairs={{0,8},{8,16},{16,24},{1,9},{9,17},{17,25},{2,10},{10,18},{18,26},{... | collective-permute-start | bytes 774152 | tf_op jit(solution)/shard_map/ppermute | solution.py:21
  11.7 1.3 %collective-permute-start.3 = (f32[7,36,2,128]{3,2,1,0:T(2,128)S(1)}, f32[7,36,2,128]{3,2,1,0:T(2,128)S(1)}, u32[]{:S(2)}, u32[]{:S(2)}) collective-permute-start(f32[7,36,2,128]{3,2,1,0:T(2,128)S(1)} %get-tuple-element.38), channel_id=1, source_target_pairs={{8,0},{16,8},{24,16},{9,1},{17,9},{25,17},{10,2},{18,10},{26,18},{... | collective-permute-start | bytes 774152 | tf_op jit(solution)/shard_map/ppermute | solution.py:21
  13.0 1.1 %and_convert_fusion = f32[35,19,131]{2,1,0:T(8,128)} fusion(pred[131]{0:T(512)(128)(4,1)S(1)} %compare_and_fusion.3, pred[35,19]{1,0:T(8,128)(4,1)S(1)} %broadcast_and_fusion.1), kind=kLoop, calls=%fused_computation.46 | loop fusion | flops 174230 | bytes 349256 | tf_op jit(solution)/shard_map/convert_element_type | solution.py:67
  14.1 1.7 %collective-permute-done.2 = f32[7,36,2,128]{3,2,1,0:T(2,128)S(1)} collective-permute-done((f32[7,36,2,128]{3,2,1,0:T(2,128)S(1)}, f32[7,36,2,128]{3,2,1,0:T(2,128)S(1)}, u32[]{:S(2)}, u32[]{:S(2)}) %collective-permute-start.2) | collective-permute-done | bytes 258080 | tf_op jit(solution)/shard_map/ppermute | solution.py:21
  15.8 4.7 %collective-permute-done.3 = f32[7,36,2,128]{3,2,1,0:T(2,128)S(1)} collective-permute-done((f32[7,36,2,128]{3,2,1,0:T(2,128)S(1)}, f32[7,36,2,128]{3,2,1,0:T(2,128)S(1)}, u32[]{:S(2)}, u32[]{:S(2)}) %collective-permute-start.3) | collective-permute-done | bytes 258080 | tf_op jit(solution)/shard_map/ppermute | solution.py:21
  20.5 0.5 pad_maximum_fusion.1
  21.0 3.6 %fusion.38 = (f32[7,36,20,2]{3,2,1,0:T(8,128)}, f32[7,36,20,2]{3,2,1,0:T(8,128)}) fusion(f32[7,36,20,128]{3,2,1,0:T(8,128)S(1)} %pad_maximum_fusion.1), kind=kLoop, calls=%fused_computation.130 | loop fusion | bytes 161280 | tf_op jit(solution)/shard_map/slice | solution.py:27
  24.6 3.2 %copy.35 = f32[7,36,20,2]{1,3,2,0:T(2,128)S(1)} copy(f32[7,36,20,2]{3,2,1,0:T(8,128)} %get-tuple-element.26) | data formatting | bytes 80640 | tf_op jit(solution)/shard_map/slice | solution.py:27
  27.8 5.0 %collective-permute-start.4 = (f32[7,36,20,2]{1,3,2,0:T(2,128)S(1)}, f32[7,36,20,2]{1,3,2,0:T(2,128)S(1)}, u32[]{:S(2)}, u32[]{:S(2)}) collective-permute-start(f32[7,36,20,2]{1,3,2,0:T(2,128)S(1)} %copy.35), channel_id=1, source_target_pairs={{0,1},{1,2},{2,3},{3,4},{4,5},{5,6},{6,7},{8,9},{9,10},{10,11},{11... | collective-permute-start | bytes 120968 | tf_op jit(solution)/shard_map/ppermute | solution.py:21
  32.8 3.2 %copy.36 = f32[7,36,20,2]{1,3,2,0:T(2,128)S(1)} copy(f32[7,36,20,2]{3,2,1,0:T(8,128)} %get-tuple-element.27) | data formatting | bytes 80640 | tf_op jit(solution)/shard_map/slice | solution.py:26
  36.1 1.9 %collective-permute-start.5 = (f32[7,36,20,2]{1,3,2,0:T(2,128)S(1)}, f32[7,36,20,2]{1,3,2,0:T(2,128)S(1)}, u32[]{:S(2)}, u32[]{:S(2)}) collective-permute-start(f32[7,36,20,2]{1,3,2,0:T(2,128)S(1)} %copy.36), channel_id=1, source_target_pairs={{1,0},{2,1},{3,2},{4,3},{5,4},{6,5},{7,6},{9,8},{10,9},{11,10},{12... | collective-permute-start | bytes 120968 | tf_op jit(solution)/shard_map/ppermute | solution.py:21
  38.4 0.7 copy.39
  39.1 3.1 %copy.37 = f32[7,36,20,2]{3,2,1,0:T(8,128)} copy(f32[7,36,20,2]{1,3,2,0:T(2,128)S(1)} %collective-permute-done.4) | data formatting | bytes 80640 | tf_op jit(solution)/shard_map/ppermute | solution.py:21
  42.2 2.8 %collective-permute-done.5 = f32[7,36,20,2]{1,3,2,0:T(2,128)S(1)} collective-permute-done((f32[7,36,20,2]{1,3,2,0:T(2,128)S(1)}, f32[7,36,20,2]{1,3,2,0:T(2,128)S(1)}, u32[]{:S(2)}, u32[]{:S(2)}) %collective-permute-start.5) | collective-permute-done | bytes 40352 | tf_op jit(solution)/shard_map/ppermute | solution.py:21
  45.1 3.1 %copy.38 = f32[7,36,20,2]{3,2,1,0:T(8,128)} copy(f32[7,36,20,2]{1,3,2,0:T(2,128)S(1)} %collective-permute-done.5) | data formatting | bytes 80640 | tf_op jit(solution)/shard_map/ppermute | solution.py:21
  48.2 9.6 %pad_maximum_fusion = f32[7,36,20,132]{3,2,1,0:T(8,128)S(1)} fusion(f32[7,36,20,2]{3,2,1,0:T(8,128)} %copy.38, f32[7,36,2,128]{3,2,1,0:T(2,128)S(1)} %collective-permute-done.3, f32[7,2,16,128]{3,2,1,0:T(8,128)S(1)} %collective-permute-done.1, f32[1,32,16,128]{3,2,1,0:T(8,128)S(1)} %bitcast.74, f32[3,32,16,128]{3,2,1,0:T(8,128)S(1)} %copy-done.2, ...), kind=kLoop, calls=%fused_computation.2 | loop fusion | flops 5322240 | bytes 5322240 | tf_op jit(solution)/shard_map/concatenate | solution.py:30
  57.8 0.3 slice_bitcast_fusion.3
  58.1 0.7 fusion.16
  58.8 0.4 copy-done.6
  59.3 0.4 fusion.4
  60.1 0.3 slice_multiply_fusion
  60.4 1.7 %fusion.22 = (f32[1,34,18,130]{3,2,1,0:T(8,128)S(1)}, f32[1,34,18,130]{3,2,1,0:T(8,128)S(1)}, f32[1,34,18,130]{3,2,1,0:T(8,128)S(1)}) fusion(f32[35,19,131]{2,1,0:T(8,128)S(1)} %get-tuple-element.30, f32[35,19,131]{2,1,0:T(8,128)S(1)} %get-tuple-element.28, f32[35,19,131]{2,1,0:T(8,128)S(1)} %get-tuple-element.29), kind=kLoop, calls=%fused_computation.60 | loop fusion | flops 716040 | bytes 3818880 | tf_op jit(solution)/shard_map/stack | solution.py:55
  62.1 0.9 slice_add_fusion
  63.5 0.6 fusion.28
  64.1 0.5 copy-done.7
  64.6 0.8 fusion.5
  65.8 0.6 fusion.34
  66.4 0.3 slice_add_fusion.1
  66.7 0.9 copy-done.8
  67.8 1.2 %fusion = f32[4,4,32,16,128]{4,3,2,1,0:T(8,128)S(1)} fusion(f32[4,32,16,128]{3,2,1,0:T(8,128)S(1)} %pad_maximum_fusion.3, f32[4,128]{1,0:T(4,128)S(1)} %get-tuple-element.61), kind=kOutput, calls=%fused_computation | output fusion | flops 1056895 | bytes 5244928 | tf_op jit(solution)/shard_map/mul | solution.py:100
  68.9 1.5 %multiply_reduce_fusion.2 = (f32[4,32,16,128]{3,2,1,0:T(8,128)S(1)}, f32[4,32,16,128]{3,2,1,0:T(8,128)S(1)}) fusion(f32[4,128]{1,0:T(4,128)S(1)} %get-tuple-element.62, f32[4,4,32,16,128]{4,3,2,1,0:T(8,128)S(1)} %fusion, f32[4,128]{1,0:T(4,128)S(1)} %get-tuple-element.61, f32[4,32,16,128]{3,2,1,0:T(8,128)S(1)} %pad_maximum_fusion.2), kind=kOutput, calls=%fused_computation.6 | output fusion | flops 4726911 | bytes 7344128 | tf_op jit(solution)/shard_map/mul | solution.py:100
  70.5 0.2 multiply_add_fusion
  70.7 1.0 %copy-done.5 = f32[4,32,16,128]{3,2,1,0:T(8,128)} copy-done((f32[4,32,16,128]{3,2,1,0:T(8,128)}, f32[4,32,16,128]{3,2,1,0:T(8,128)S(1)}, u32[]{:S(2)}) %copy-start.5) | copy-done | bytes 1048600
  71.7 1.0 %convolution_bitcast_fusion = f32[4,8,128]{2,1,0:T(8,128)S(1)} fusion(bf16[4,8,32,16]{2,1,3,0:T(8,128)(2,1)S(1)} %bitcast.75, f32[4,32,16,128]{3,2,1,0:T(8,128)S(1)} %multiply_add_fusion), kind=kOutput, calls=%fused_computation.22 | convolution fusion | flops 25165824 | bytes 1097728 | tf_op jit(solution)/shard_map/pxyl,pnxy->pnl/dot_general | solution.py:110
  72.6 0.9 reshape.193
  73.5 0.7 fusion.39
  74.4 0.9 copy.45
  75.3 10.3 %all-to-all-start = ((f32[32,2,4]{2,1,0:T(2,128)}), f32[32,2,4]{2,1,0:T(2,128)S(1)}, u32[]{:S(2)}, u32[]{:S(2)}) async-start(f32[32,2,4]{2,1,0:T(2,128)} %copy.45), calls=%async_computation | async-start | bytes 65536 | tf_op jit(solution)/shard_map/all_to_all | solution.py:115
  85.6 1.2 %slice.372 = f32[3,32,16,128]{3,2,1,0:T(8,128)} slice(f32[3,33,17,129]{3,2,1,0:T(8,128)S(1)} %fusion.5), slice={[0:3], [1:33], [1:17], [1:129]} | slice | bytes 1572864 | tf_op jit(solution)/shard_map/slice | solution.py:35
  86.8 6.2 %all-to-all-done = f32[32,2,4]{2,1,0:T(2,128)S(1)} async-done(((f32[32,2,4]{2,1,0:T(2,128)}), f32[32,2,4]{2,1,0:T(2,128)S(1)}, u32[]{:S(2)}, u32[]{:S(2)}) %all-to-all-start) | async-done | bytes 1056 | tf_op jit(solution)/shard_map/all_to_all | solution.py:115
  93.1 0.7 copy.48
  (53 shorter events, 2.7 us)
Async XLA Ops:
  0.6 7.0 %copy-start = (bf16[4,2,4,256,64]{3,4,2,1,0:T(8,128)(2,1)S(1)}, bf16[4,2,4,256,64]{3,4,2,1,0:T(8,128)(2,1)}, u32[]{:S(2)}) copy-start(bf16[4,2,4,256,64]{3,4,2,1,0:T(8,128)(2,1)} %param.13) | copy-start | bytes 3145732
  0.6 7.4 %copy-start.4 = (f32[32,16,128]{2,1,0:T(8,128)S(1)}, f32[32,16,128]{2,1,0:T(8,128)}, u32[]{:S(2)}) copy-start(f32[32,16,128]{2,1,0:T(8,128)} %param.9) | copy-start | bytes 786436
  0.7 7.3 %copy-start.3 = (f32[3,32,16,128]{3,2,1,0:T(8,128)S(1)}, f32[3,32,16,128]{3,2,1,0:T(8,128)}, u32[]{:S(2)}) copy-start(f32[3,32,16,128]{3,2,1,0:T(8,128)} %param.7) | copy-start | bytes 2359300
  0.7 7.3 %copy-start.2 = (f32[3,32,16,128]{3,2,1,0:T(8,128)S(1)}, f32[3,32,16,128]{3,2,1,0:T(8,128)}, u32[]{:S(2)}) copy-start(f32[3,32,16,128]{3,2,1,0:T(8,128)} %param.8) | copy-start | bytes 2359300
  1.8 6.0 %collective-permute-start = (f32[7,2,16,128]{3,2,1,0:T(8,128)S(1)}, f32[7,2,16,128]{3,2,1,0:T(8,128)S(1)}, u32[]{:S(2)}, u32[]{:S(2)}) collective-permute-start(f32[7,2,16,128]{3,2,1,0:T(8,128)S(1)} %get-tuple-element.39), channel_id=1, source_target_pairs={{0,32},{32,64},{64,96},{96,128},{128,160},{160,192},{192,224},{1,3... | collective-permute-start | bytes 344072 | tf_op jit(solution)/shard_map/ppermute | solution.py:21
  3.5 4.5 %collective-permute-start.1 = (f32[7,2,16,128]{3,2,1,0:T(8,128)S(1)}, f32[7,2,16,128]{3,2,1,0:T(8,128)S(1)}, u32[]{:S(2)}, u32[]{:S(2)}) collective-permute-start(f32[7,2,16,128]{3,2,1,0:T(8,128)S(1)} %get-tuple-element.40), channel_id=1, source_target_pairs={{32,0},{64,32},{96,64},{128,96},{160,128},{192,160},{224,192},{33,... | collective-permute-start | bytes 344072 | tf_op jit(solution)/shard_map/ppermute | solution.py:21
  8.2 7.6 %collective-permute-start.2 = (f32[7,36,2,128]{3,2,1,0:T(2,128)S(1)}, f32[7,36,2,128]{3,2,1,0:T(2,128)S(1)}, u32[]{:S(2)}, u32[]{:S(2)}) collective-permute-start(f32[7,36,2,128]{3,2,1,0:T(2,128)S(1)} %get-tuple-element.37), channel_id=1, source_target_pairs={{0,8},{8,16},{16,24},{1,9},{9,17},{17,25},{2,10},{10,18},{18,26},{... | collective-permute-start | bytes 774152 | tf_op jit(solution)/shard_map/ppermute | solution.py:21
  11.7 8.8 %collective-permute-start.3 = (f32[7,36,2,128]{3,2,1,0:T(2,128)S(1)}, f32[7,36,2,128]{3,2,1,0:T(2,128)S(1)}, u32[]{:S(2)}, u32[]{:S(2)}) collective-permute-start(f32[7,36,2,128]{3,2,1,0:T(2,128)S(1)} %get-tuple-element.38), channel_id=1, source_target_pairs={{8,0},{16,8},{24,16},{9,1},{17,9},{25,17},{10,2},{18,10},{26,18},{... | collective-permute-start | bytes 774152 | tf_op jit(solution)/shard_map/ppermute | solution.py:21
  27.8 11.3 %collective-permute-start.4 = (f32[7,36,20,2]{1,3,2,0:T(2,128)S(1)}, f32[7,36,20,2]{1,3,2,0:T(2,128)S(1)}, u32[]{:S(2)}, u32[]{:S(2)}) collective-permute-start(f32[7,36,20,2]{1,3,2,0:T(2,128)S(1)} %copy.35), channel_id=1, source_target_pairs={{0,1},{1,2},{2,3},{3,4},{4,5},{5,6},{6,7},{8,9},{9,10},{10,11},{11... | collective-permute-start | bytes 120968 | tf_op jit(solution)/shard_map/ppermute | solution.py:21
  36.1 9.0 %collective-permute-start.5 = (f32[7,36,20,2]{1,3,2,0:T(2,128)S(1)}, f32[7,36,20,2]{1,3,2,0:T(2,128)S(1)}, u32[]{:S(2)}, u32[]{:S(2)}) collective-permute-start(f32[7,36,20,2]{1,3,2,0:T(2,128)S(1)} %copy.36), channel_id=1, source_target_pairs={{1,0},{2,1},{3,2},{4,3},{5,4},{6,5},{7,6},{9,8},{10,9},{11,10},{12... | collective-permute-start | bytes 120968 | tf_op jit(solution)/shard_map/ppermute | solution.py:21
  58.1 1.2 %copy-start.6 = (f32[35,19,131]{2,1,0:T(8,128)S(1)}, f32[35,19,131]{2,1,0:T(8,128)}, u32[]{:S(2)}) copy-start(f32[35,19,131]{2,1,0:T(8,128)} %and_convert_fusion) | copy-start | bytes 1045384
  63.5 1.1 %copy-start.7 = (f32[33,17,129]{2,1,0:T(8,128)S(1)}, f32[33,17,129]{2,1,0:T(8,128)}, u32[]{:S(2)}) copy-start(f32[33,17,129]{2,1,0:T(8,128)} %and_convert_fusion.1) | copy-start | bytes 868432
  66.7 0.9 copy-start.8
  68.9 1.6 %copy-start.9 = (f32[4,32,16,128]{3,2,1,0:T(8,128)S(1)}, f32[4,32,16,128]{3,2,1,0:T(8,128)}, u32[]{:S(2)}) copy-start(f32[4,32,16,128]{3,2,1,0:T(8,128)} %param.10) | copy-start | bytes 3145732
  70.4 1.2 %copy-start.10 = (bf16[4,2,4,32,16]{3,2,1,4,0:T(4,128)(2,1)S(1)}, bf16[4,2,4,32,16]{3,2,1,4,0:T(4,128)(2,1)}, u32[]{:S(2)}) copy-start(bf16[4,2,4,32,16]{3,2,1,4,0:T(4,128)(2,1)} %copy.39) | copy-start | bytes 98308
  70.5 23.3 %copy-start.1 = (bf16[4,2,4,256,64]{3,4,2,1,0:T(8,128)(2,1)S(1)}, bf16[4,2,4,256,64]{3,4,2,1,0:T(8,128)(2,1)}, u32[]{:S(2)}) copy-start(bf16[4,2,4,256,64]{3,4,2,1,0:T(8,128)(2,1)} %param.13) | copy-start | bytes 3145732
  70.7 1.0 %copy-start.5 = (f32[4,32,16,128]{3,2,1,0:T(8,128)}, f32[4,32,16,128]{3,2,1,0:T(8,128)S(1)}, u32[]{:S(2)}) copy-start(f32[4,32,16,128]{3,2,1,0:T(8,128)S(1)} %multiply_add_fusion) | copy-start | bytes 3145732
  75.3 17.7 %all-to-all-start = ((f32[32,2,4]{2,1,0:T(2,128)}), f32[32,2,4]{2,1,0:T(2,128)S(1)}, u32[]{:S(2)}, u32[]{:S(2)}) async-start(f32[32,2,4]{2,1,0:T(2,128)} %copy.45), calls=%async_computation | async-start | bytes 65536 | tf_op jit(solution)/shard_map/all_to_all | solution.py:115

commit v5 on v4

--- a/solution.py
+++ b/solution.py
@@ -21,32 +21,27 @@
     return lax.ppermute(value, axis, [(source, source + steps) for source in range(first, last)])
 
 
-def widen(stack, dim, axis):
+def widen(stack, dim, axis, cyclic):
     count = stack.shape[dim]
     low = lax.slice_in_dim(stack, 0, HALO, axis=dim)
     high = lax.slice_in_dim(stack, count - HALO, count, axis=dim)
     from_below = shifted(high, axis, 1)
     from_above = shifted(low, axis, -1)
+    if cyclic:
+        return jnp.concatenate([stack, from_above, from_below], axis=dim)
     return jnp.concatenate([from_below, stack, from_above], axis=dim)
 
 
-def box(value, start, size):
-    lead = value.ndim - 3
-    return lax.slice(
-        value,
-        (0,) * lead + tuple(start),
-        value.shape[:lead] + tuple(s + n for s, n in zip(start, size)),
-    )
-
-
-def moved(start, dim, step):
-    return tuple(s + step if d == dim else s for d, s in enumerate(start))
+def rows(value, start, size):
+    return lax.slice_in_dim(value, start, start + size, axis=value.ndim - 3)
 
 
 def differ(value, start, size, dim, step):
-    if step > 0:
-        return box(value, moved(start, dim, 1), size) - box(value, start, size)
-    return box(value, start, size) - box(value, moved(start, dim, -1), size)
+    here = rows(value, start, size)
+    if dim == 0:
+        return rows(value, start + step, size) - here if step > 0 else here - rows(value, start - 1, size)
+    axis = value.ndim - 3 + dim
+    return jnp.roll(here, -1, axis=axis) - here if step > 0 else here - jnp.roll(here, 1, axis=axis)
 
 
 def curl(field, start, size, step):
@@ -55,13 +50,16 @@
     return jnp.stack([d(vz, 1) - d(vy, 2), d(vx, 2) - d(vz, 0), d(vy, 0) - d(vx, 1)])
 
 
+def cyclic_cells(count):
+    return jnp.concatenate([jnp.arange(count + HALO), jnp.arange(-HALO, 0)])
+
+
 def inside(origin, size, cells):
+    where = [origin + jnp.arange(size), cyclic_cells(cells[1]), cyclic_cells(cells[2])]
     masks = []
     for dim, axis in enumerate(AXES):
-        count = lax.axis_size(axis)
-        first = lax.axis_index(axis) * cells[dim] + origin
-        where = first + jnp.arange(size[dim])
-        masks.append((where >= 0) & (where < count * cells[dim]))
+        first = lax.axis_index(axis) * cells[dim] + where[dim]
+        masks.append((first >= 0) & (first < lax.axis_size(axis) * cells[dim]))
     return (
         masks[0][:, None, None] & masks[1][None, :, None] & masks[2][None, None, :]
     ).astype(jnp.float32)
@@ -72,19 +70,20 @@
     cells_x, cells_y, cells_z = cells
     ports_here = dft_sums.shape[0]
     stack = jnp.concatenate([e_field, h_field, inv_permittivity[None]], axis=0)
-    for dim, axis in enumerate(AXES):
-        stack = pin(widen(stack, dim + 1, axis))
+    for dim in (2, 1, 0):
+        stack = pin(widen(stack, dim + 1, AXES[dim], dim > 0))
     e0, h0, inv = stack[0:3], stack[3:6], stack[6]
-    n = lambda k: tuple(c + k for c in cells)
-    h1 = box(h0, (0, 0, 0), n(3)) - 0.5 * curl(e0, (0, 0, 0), n(3), 1)
-    h1 = pin(h1 * inside(-2, n(3), cells))
-    e1 = pin(box(e0, (1, 1, 1), n(2)) + 0.5 * box(inv, (1, 1, 1), n(2)) * curl(h1, (1, 1, 1), n(2), -1))
-    h2 = box(h1, (1, 1, 1), n(1)) - 0.5 * curl(e1, (0, 0, 0), n(1), 1)
-    h2 = pin(h2 * inside(-1, n(1), cells))
-    e2 = pin(box(e1, (1, 1, 1), n(0)) + 0.5 * box(inv, (2, 2, 2), n(0)) * curl(h2, (1, 1, 1), n(0), -1))
-    e1_here = box(e1, (1, 1, 1), n(0))
-    h1_here = box(h1, (2, 2, 2), n(0))
-    h2_here = box(h2, (1, 1, 1), n(0))
+    h1 = rows(h0, 0, cells_x + 3) - 0.5 * curl(e0, 0, cells_x + 3, 1)
+    h1 = pin(h1 * inside(-2, cells_x + 3, cells))
+    e1 = pin(rows(e0, 1, cells_x + 2) + 0.5 * rows(inv, 1, cells_x + 2) * curl(h1, 1, cells_x + 2, -1))
+    h2 = rows(h1, 1, cells_x + 1) - 0.5 * curl(e1, 0, cells_x + 1, 1)
+    h2 = pin(h2 * inside(-1, cells_x + 1, cells))
+    e2 = pin(rows(e1, 1, cells_x) + 0.5 * rows(inv, 2, cells_x) * curl(h2, 1, cells_x, -1))
+    block = lambda v: v[..., :cells_y, :cells_z]
+    e1_here = block(rows(e1, 1, cells_x))
+    h1_here = block(rows(h1, 2, cells_x))
+    e2 = block(e2)
+    h2_here = block(rows(h2, 1, cells_x))
     local_z = port_z - lax.axis_index("gz") * cells_z
     onehot = (local_z[:, None] == jnp.arange(cells_z)[None, :]).astype(jnp.float32)
     lanes = dft_sums.shape[-1]

time: 94.6 us -> 144 us (1.52)
  local copies, waits for them, and re-layouts: 26.3 us -> 56.4 us
  other arithmetic: 24.7 us -> 41.1 us
  starting transfers between devices: 25.1 us -> 28.5 us
  waiting for transfers between devices: 15.7 us -> 14.1 us
    slice x1 -> x23, local copies, waits for them, and re-layouts: 1.15 us -> 18.1 us  [the longest x8 8.52 us: differ(): jnp.roll(here, 1, axis=axis)]
    concatenate x0 -> x30, local copies, waits for them, and re-layouts: none -> 16.8 us  [the longest x13 9.03 us: differ(): jnp.roll(here, 1, axis=axis)]
    sub x0 -> x5, other arithmetic: none -> 16.5 us  [the longest x4 13.5 us: curl(): d(vz, 1) - d(vy, 2)]
    concatenate x2 -> x1, other arithmetic: 10.1 us -> 3.79 us  [widen(): return jnp.concatenate([from_below, stack, from_above], axis=dim)]
    slice x2 -> x1, local copies, waits for them, and re-layouts: 6.82 us -> 2.31 us  [widen(): high = lax.slice_in_dim(stack, count - HALO, count, axis=dim)]
    mul x4, other arithmetic: 1.66 us -> 6.08 us  [the longest x1 2.31 us: per_device(): h1 = pin(h1 * inside(-2, cells_x + 3, cells))]
    another operation x4 -> x0, other arithmetic: 3.57 us -> none  [curl(): jnp.stack([d(vz, 1) - d(vy, 2), d(vx, 2) - d(vz, 0), d(vy, 0) - d(vx, 1)])]
    all_to_all x1, waiting for transfers between devices: 6.23 us -> 3.2 us  [per_device(): lax.all_to_all(pieces, ('gx', 'gy'), 0, 0, tiled=False)]
  transfers between devices with their start and end apart: 7 -> 7, of which waited for: 5 -> 4; matrix products, arithmetic and copies ran while one was open for 13% -> 11% of each run, Pallas kernels for 0% -> 0%
where the time goes in v5:
time: 144 us; the launch traced here: 142 us
  local copies, waits for them, and re-layouts  56.4 us (39%)
  other arithmetic  41.1 us (29%)
  starting transfers between devices  28.5 us (20%)
  waiting for transfers between devices  14.1 us (10%)
    ppermute x6, starting transfers between devices, shifted(): lax.ppermute(value, axis, [(source, source + steps) for source in range(f...  16.2 us
    sub x4, other arithmetic, curl(): d(vz, 1) - d(vy, 2)  13.5 us
    all_to_all x1, starting transfers between devices, per_device(): lax.all_to_all(pieces, ('gx', 'gy'), 0, 0, tiled=False)  12.3 us
    ppermute x6, waiting for transfers between devices, shifted(): lax.ppermute(value, axis, [(source, source + steps) for source in range(f...  10.9 us
    concatenate x13, local copies, waits for them, and re-layouts, differ(): jnp.roll(here, 1, axis=axis)  9.03 us
    slice x8, local copies, waits for them, and re-layouts, differ(): jnp.roll(here, 1, axis=axis)  8.52 us
    concatenate x17, local copies, waits for them, and re-layouts, differ(): jnp.roll(here, -1, axis=axis) - here  7.76 us
    unnamed x70, local copies, waits for them, and re-layouts  5.97 us
  transfers between devices with their start and end apart: 7, of which 4 were waited for; matrix products, arithmetic and copies ran while one was open for 11% of the time, Pallas kernels for 0%

profile of v5, /device:TPU:96, one launch (start us, length us, event | category | flops | bytes accessed | tf_op | source)
XLA Modules:
  0.0 142.4 jit_solution(11321256129803369643)
XLA Ops:
  0.6 1.7 %pad_maximum_fusion.1 = f32[7,32,16,128]{3,2,1,0:T(8,128)S(1)} fusion(f32[1,32,16,128]{3,2,1,0:T(8,128)} %bitcast.113, f32[3,32,16,128]{3,2,1,0:T(8,128)} %param.8, f32[3,32,16,128]{3,2,1,0:T(8,128)} %param.7), kind=kLoop, calls=%fused_computation.23 | loop fusion | flops 917504 | bytes 3670016 | tf_op jit(solution)/shard_map/concatenate | solution.py:72
  2.3 1.9 %fusion.29 = (f32[7,32,16,2]{3,2,1,0:T(8,128)S(1)}, f32[7,32,16,2]{3,2,1,0:T(8,128)}) fusion(f32[7,32,16,128]{3,2,1,0:T(8,128)S(1)} %pad_maximum_fusion.1), kind=kLoop, calls=%fused_computation.151 | loop fusion | bytes 114688 | tf_op jit(solution)/shard_map/slice | solution.py:26
  4.2 2.3 %copy.88 = f32[7,32,16,2]{1,2,3,0:T(8,128)S(1)} copy(f32[7,32,16,2]{3,2,1,0:T(8,128)} %get-tuple-element.52) | data formatting | bytes 57344 | tf_op jit(solution)/shard_map/slice | solution.py:27
  6.5 5.0 %collective-permute-start.1 = (f32[7,32,16,2]{1,2,3,0:T(8,128)S(1)}, f32[7,32,16,2]{1,2,3,0:T(8,128)S(1)}, u32[]{:S(2)}, u32[]{:S(2)}) collective-permute-start(f32[7,32,16,2]{1,2,3,0:T(8,128)S(1)} %copy.88), channel_id=1, source_target_pairs={{0,1},{1,2},{2,3},{3,4},{4,5},{5,6},{6,7},{8,9},{9,10},{10,11},{11... | collective-permute-start | bytes 86024 | tf_op jit(solution)/shard_map/ppermute | solution.py:21
  11.5 1.5 %copy.87 = f32[7,32,16,2]{1,2,3,0:T(8,128)} copy(f32[7,32,16,2]{3,2,1,0:T(8,128)S(1)} %get-tuple-element.51) | data formatting | bytes 57344 | tf_op jit(solution)/shard_map/slice | solution.py:26
  13.0 1.9 %collective-permute-start = (f32[7,32,16,2]{1,2,3,0:T(8,128)}, f32[7,32,16,2]{1,2,3,0:T(8,128)}, u32[]{:S(2)}, u32[]{:S(2)}) collective-permute-start(f32[7,32,16,2]{1,2,3,0:T(8,128)} %copy.87), channel_id=1, source_target_pairs={{1,0},{2,1},{3,2},{4,3},{5,4},{6,5},{7,6},{9,8},{10,9},{11,10},{12... | collective-permute-start | bytes 86024 | tf_op jit(solution)/shard_map/ppermute | solution.py:21
  16.1 1.1 and_convert_fusion
  17.3 3.9 %collective-permute-done = f32[7,32,16,2]{1,2,3,0:T(8,128)} collective-permute-done((f32[7,32,16,2]{1,2,3,0:T(8,128)}, f32[7,32,16,2]{1,2,3,0:T(8,128)}, u32[]{:S(2)}, u32[]{:S(2)}) %collective-permute-start) | collective-permute-done | bytes 28704 | tf_op jit(solution)/shard_map/ppermute | solution.py:21
  21.2 1.7 %copy.89 = f32[7,32,16,2]{3,2,1,0:T(8,128)S(1)} copy(f32[7,32,16,2]{1,2,3,0:T(8,128)} %collective-permute-done) | data formatting | bytes 57344 | tf_op jit(solution)/shard_map/ppermute | solution.py:21
  23.0 2.0 %copy.90 = f32[7,32,16,2]{3,2,1,0:T(8,128)} copy(f32[7,32,16,2]{1,2,3,0:T(8,128)S(1)} %collective-permute-done.1) | data formatting | bytes 57344 | tf_op jit(solution)/shard_map/ppermute | solution.py:21
  25.0 2.7 %pad_maximum_fusion.14 = (f32[7,32,2,132]{3,2,1,0:T(2,128)S(1)}, f32[7,32,2,132]{3,2,1,0:T(2,128)S(1)}) fusion(f32[7,32,16,2]{3,2,1,0:T(8,128)} %copy.90, f32[7,32,16,2]{3,2,1,0:T(8,128)S(1)} %copy.89, f32[1,32,16,128]{3,2,1,0:T(8,128)S(1)} %bitcast.114, f32[3,32,16,128]{3,2,1,0:T(8,128)} %param.8, f32[3,32,16,128]{3,2,1,0:T(8,128)} %param.7), kind=kLoop, calls=%fused_computation.109 | loop fusion | flops 473088 | bytes 2365440 | tf_op jit(solution)/shard_map/slice | solution.py:26
  27.7 1.3 collective-permute-start.2
  29.0 4.6 %collective-permute-start.3 = (f32[7,32,2,132]{3,2,1,0:T(2,128)S(1)}, f32[7,32,2,132]{3,2,1,0:T(2,128)S(1)}, u32[]{:S(2)}, u32[]{:S(2)}) collective-permute-start(f32[7,32,2,132]{3,2,1,0:T(2,128)S(1)} %get-tuple-element.32), channel_id=1, source_target_pairs={{0,8},{8,16},{16,24},{1,9},{9,17},{17,25},{2,10},{10,18},{18,26},{... | collective-permute-start | bytes 709640 | tf_op jit(solution)/shard_map/ppermute | solution.py:21
  33.6 1.1 and_convert_fusion.1
  34.7 5.7 %collective-permute-done.2 = f32[7,32,2,132]{3,2,1,0:T(2,128)S(1)} collective-permute-done((f32[7,32,2,132]{3,2,1,0:T(2,128)S(1)}, f32[7,32,2,132]{3,2,1,0:T(2,128)S(1)}, u32[]{:S(2)}, u32[]{:S(2)}) %collective-permute-start.2) | collective-permute-done | bytes 236576 | tf_op jit(solution)/shard_map/ppermute | solution.py:21
  40.5 1.2 collective-permute-done.3
  41.6 1.0 pad_maximum_fusion.16
  42.7 2.1 %collective-permute-start.4 = (f32[7,2,20,132]{3,2,1,0:T(8,128)}, f32[7,2,20,132]{3,2,1,0:T(8,128)}, u32[]{:S(2)}, u32[]{:S(2)}) collective-permute-start(f32[7,2,20,132]{3,2,1,0:T(8,128)} %get-tuple-element.22), channel_id=1, source_target_pairs={{0,32},{32,64},{64,96},{96,128},{128,160},{160,192},{192,224},{1,3... | collective-permute-start | bytes 443528 | tf_op jit(solution)/shard_map/ppermute | solution.py:21
  44.8 1.3 collective-permute-start.5
  48.2 2.2 %fusion.24 = f32[32,20,132]{2,1,0:T(8,128)} fusion(f32[7,32,2,132]{3,2,1,0:T(2,128)} %copy-done.16, f32[7,32,2,132]{3,2,1,0:T(2,128)} %copy-done.14, f32[7,32,16,2]{3,2,1,0:T(8,128)} %copy.90, f32[7,32,16,2]{3,2,1,0:T(8,128)S(1)} %copy.89, f32[1,32,16,128]{3,2,1,0:T(8,128)S(1)} %bitcast.116, f32[3,32,16,128]{3,2,1,0:T(8,128)S(1)} %copy-done.8, ...), kind=kLoop, calls=%fused_computation.83 | loop fusion | flops 591360 | bytes 2703360 | tf_op jit(solution)/shard_map/mul | solution.py:81
  50.5 3.8 %pad_maximum_fusion = f32[7,36,20,132]{3,2,1,0:T(8,128)S(1)} fusion(f32[7,2,20,132]{3,2,1,0:T(8,128)} %collective-permute-done.5, f32[7,32,2,132]{3,2,1,0:T(2,128)S(1)} %copy-done.17, f32[7,32,2,132]{3,2,1,0:T(2,128)S(1)} %copy-done.15, f32[7,32,16,2]{3,2,1,0:T(8,128)S(1)} %copy-done.6, f32[7,32,16,2]{3,2,1,0:T(8,128)S(1)} %copy.89, ...), kind=kLoop, calls=%fused_computation.2 | loop fusion | flops 5322240 | bytes 5322240 | tf_op jit(solution)/shard_map/concatenate | solution.py:32
  54.3 1.0 fusion.16
  55.3 1.8 %copy-done.2 = f32[7,36,20,132]{3,2,1,0:T(8,128)} copy-done((f32[7,36,20,132]{3,2,1,0:T(8,128)}, f32[7,36,20,132]{3,2,1,0:T(8,128)S(1)}, u32[]{:S(2)}) %copy-start.2) | copy-done | bytes 2661144
  58.2 3.1 %fusion.13 = (f32[1,35,20,132]{3,2,1,0:T(8,128)}, f32[35,20,132]{2,1,0:T(8,128)S(1)}, f32[1,35,20,132]{3,2,1,0:T(8,128)S(1)}) fusion(f32[1,35,1,132]{3,2,1,0:T(1,128)S(1)} %slice_bitcast_fusion.27, f32[1,35,19,132]{3,2,1,0:T(8,128)S(1)} %slice_bitcast_fusion.3, f32[1,35,20,1]{3,2,1,0:T(8,128)S(1)} %copy.92, f32[1,35,20,131]{3,2,1,0:T(8,128)S(1)} %slice_bitcast_fusion.2, ...), kind=kLoop, calls=%fused_computation.38 | loop fusion | flops 462000 | bytes 2956800 | tf_op jit(solution)/shard_map/sub | solution.py:50
  62.4 2.9 %fusion.12 = (f32[1,35,20,132]{3,2,1,0:T(8,128)S(1)}, f32[1,35,20,132]{3,2,1,0:T(8,128)S(1)}) fusion(f32[7,36,20,132]{3,2,1,0:T(8,128)} %copy-done.2, f32[1,35,20,1]{3,2,1,0:T(8,128)S(1)} %copy.95, f32[1,35,20,131]{3,2,1,0:T(8,128)S(1)} %slice_bitcast_fusion.1, f32[1,35,1,132]{3,2,1,0:T(1,128)S(1)} %reshape_bitcast_fusion, ...), kind=kLoop, calls=%fused_computation.33 | loop fusion | flops 739200 | bytes 3326400 | tf_op jit(solution)/shard_map/sub | solution.py:50
  65.4 2.3 %fusion.4 = f32[3,35,20,132]{3,2,1,0:T(8,128)S(1)} fusion(f32[7,36,20,132]{3,2,1,0:T(8,128)} %copy-done.2, f32[1,35,20,132]{3,2,1,0:T(8,128)S(1)} %get-tuple-element.30, f32[1,35,20,132]{3,2,1,0:T(8,128)S(1)} %get-tuple-element.29, f32[1,35,20,132]{3,2,1,0:T(8,128)S(1)} %copy-done.19, f32[35,20,132]{2,1,0:T(8,128)S(1)} %copy-done.18), kind=kLoop, calls=%fused_computation.10 | loop fusion | flops 1386000 | bytes 3696000 | tf_op jit(solution)/shard_map/mul | solution.py:77
  72.5 1.2 copy.98
  73.7 1.0 copy.99
  74.7 1.2 copy.100
  76.0 1.0 copy.101
  77.0 3.5 %fusion.17 = (f32[1,34,20,132]{3,2,1,0:T(8,128)S(1)}, f32[1,34,20,132]{3,2,1,0:T(8,128)S(1)}, f32[1,34,20,132]{3,2,1,0:T(8,128)S(1)}) fusion(f32[1,34,19,132]{3,2,1,0:T(8,128)} %get-tuple-element.62, f32[1,34,1,132]{3,2,1,0:T(1,128)S(1)} %get-tuple-element.66, f32[1,34,20,131]{3,2,1,0:T(8,128)S(1)} %get-tuple-element.64, f32[1,34,20,1]{3,2,1,0:T(8,128)} %copy.99, ...), kind=kLoop, calls=%fused_computation.54 | loop fusion | flops 1166880 | bytes 4308480 | tf_op jit(solution)/shard_map/sub | solution.py:50
  80.6 2.2 %slice_add_fusion = f32[3,34,20,132]{3,2,1,0:T(8,128)S(1)} fusion(f32[7,36,20,132]{3,2,1,0:T(8,128)} %copy-done.2, f32[1,34,20,132]{3,2,1,0:T(8,128)S(1)} %get-tuple-element.34, f32[1,34,20,132]{3,2,1,0:T(8,128)S(1)} %get-tuple-element.35, f32[1,34,20,132]{3,2,1,0:T(8,128)S(1)} %get-tuple-element.33, f32[34,20,132]{2,1,0:T(8,128)S(1)} %copy-done.20), kind=kLoop, calls=%fused_computation.12 | loop fusion | flops 1077120 | bytes 3590400 | tf_op jit(solution)/shard_map/add | solution.py:78
  85.6 1.2 slice_bitcast_fusion.10
  88.6 1.2 slice_bitcast_fusion.9
  89.8 1.2 copy.102
  91.0 1.0 copy.103
  92.0 1.2 copy.104
  93.3 1.0 copy.105
  94.3 2.9 %fusion.20 = (f32[1,33,20,132]{3,2,1,0:T(8,128)S(1)}, f32[1,33,20,132]{3,2,1,0:T(8,128)S(1)}, f32[1,33,20,132]{3,2,1,0:T(8,128)S(1)}) fusion(f32[1,33,1,132]{3,2,1,0:T(1,128)S(1)} %slice_bitcast_fusion.31, f32[1,33,19,132]{3,2,1,0:T(8,128)} %slice_bitcast_fusion.11, f32[1,33,20,1]{3,2,1,0:T(8,128)} %copy.103, f32[1,33,20,131]{3,2,1,0:T(8,128)} %slice_bitcast_fusion.10, ...), kind=kLoop, calls=%fused_computation.68 | loop fusion | flops 1132560 | bytes 4181760 | tf_op jit(solution)/shard_map/sub | solution.py:50
  105.1 1.2 copy.107
  107.3 1.2 copy.109
  109.5 4.0 %fusion.25 = (f32[1,32,20,132]{3,2,1,0:T(8,128)S(1)}, f32[1,32,20,132]{3,2,1,0:T(8,128)S(1)}, f32[1,32,20,132]{3,2,1,0:T(8,128)S(1)}) fusion(f32[1,32,19,132]{3,2,1,0:T(8,128)} %slice_bitcast_fusion.15, f32[1,32,1,132]{3,2,1,0:T(1,128)S(1)} %slice_bitcast_fusion.33, f32[1,32,20,131]{3,2,1,0:T(8,128)} %slice_bitcast_fusion.14, f32[1,32,20,1]{3,2,1,0:T(8,128)} %copy.108, ...), kind=kLoop, calls=%fused_computation.90 | loop fusion | flops 1098240 | bytes 4055040 | tf_op jit(solution)/shard_map/sub | solution.py:50
  115.7 1.4 fusion
  117.2 1.5 %multiply_reduce_fusion.2 = (f32[4,32,16,128]{3,2,1,0:T(8,128)S(1)}, f32[4,32,16,128]{3,2,1,0:T(8,128)S(1)}) fusion(f32[4,128]{1,0:T(4,128)S(1)} %copy-done.29, f32[4,4,32,16,128]{4,3,2,1,0:T(8,128)S(1)} %fusion, f32[4,128]{1,0:T(4,128)S(1)} %copy-done.28, f32[4,32,16,128]{3,2,1,0:T(8,128)S(1)} %pad_maximum_fusion.2), kind=kOutput, calls=%fused_computation.6 | output fusion | flops 4726911 | bytes 7344128 | tf_op jit(solution)/shard_map/mul | solution.py:99
  121.8 12.3 %all-to-all-start = ((f32[32,2,4]{2,1,0:T(2,128)}), f32[32,2,4]{2,1,0:T(2,128)S(1)}, u32[]{:S(2)}, u32[]{:S(2)}) async-start(f32[32,2,4]{2,1,0:T(2,128)} %copy.117), calls=%async_computation | async-start | bytes 65536 | tf_op jit(solution)/shard_map/all_to_all | solution.py:114
  134.2 2.1 %slice.509 = f32[3,32,16,128]{3,2,1,0:T(8,128)} slice(f32[3,33,20,132]{3,2,1,0:T(8,128)} %copy-done.7), slice={[0:3], [1:33], [0:16], [0:128]} | slice | bytes 1572864 | tf_op jit(solution)/shard_map/slice | solution.py:82
  136.3 2.1 %slice.508 = f32[3,32,16,128]{3,2,1,0:T(8,128)} slice(f32[3,32,20,132]{3,2,1,0:T(8,128)} %copy-done.12), slice={[0:3], [0:32], [0:16], [0:128]} | slice | bytes 1572864 | tf_op jit(solution)/shard_map/slice | solution.py:82
  138.4 3.2 %all-to-all-done = f32[32,2,4]{2,1,0:T(2,128)S(1)} async-done(((f32[32,2,4]{2,1,0:T(2,128)}), f32[32,2,4]{2,1,0:T(2,128)S(1)}, u32[]{:S(2)}, u32[]{:S(2)}) %all-to-all-start) | async-done | bytes 1056 | tf_op jit(solution)/shard_map/all_to_all | solution.py:114
  (149 shorter events, 30.8 us)
Async XLA Ops:
  0.6 16.5 %copy-start = (bf16[4,2,4,256,64]{3,4,2,1,0:T(8,128)(2,1)S(1)}, bf16[4,2,4,256,64]{3,4,2,1,0:T(8,128)(2,1)}, u32[]{:S(2)}) copy-start(bf16[4,2,4,256,64]{3,4,2,1,0:T(8,128)(2,1)} %param.13) | copy-start | bytes 3145732
  4.2 10.8 %copy-start.33 = (s32[4]{0:T(128)S(1)}, s32[4]{0:T(128)}, u32[]{:S(2)}) copy-start(s32[4]{0:T(128)} %param.12) | copy-start | bytes 52
  4.2 11.0 %copy-start.32 = (f32[16]{0:T(128)S(1)}, f32[16]{0:T(128)}, u32[]{:S(2)}) copy-start(f32[16]{0:T(128)} %param.11) | copy-start | bytes 196
  6.5 16.4 %collective-permute-start.1 = (f32[7,32,16,2]{1,2,3,0:T(8,128)S(1)}, f32[7,32,16,2]{1,2,3,0:T(8,128)S(1)}, u32[]{:S(2)}, u32[]{:S(2)}) collective-permute-start(f32[7,32,16,2]{1,2,3,0:T(8,128)S(1)} %copy.88), channel_id=1, source_target_pairs={{0,1},{1,2},{2,3},{3,4},{4,5},{5,6},{6,7},{8,9},{9,10},{10,11},{11... | collective-permute-start | bytes 86024 | tf_op jit(solution)/shard_map/ppermute | solution.py:21
  13.0 8.2 %collective-permute-start = (f32[7,32,16,2]{1,2,3,0:T(8,128)}, f32[7,32,16,2]{1,2,3,0:T(8,128)}, u32[]{:S(2)}, u32[]{:S(2)}) collective-permute-start(f32[7,32,16,2]{1,2,3,0:T(8,128)} %copy.87), channel_id=1, source_target_pairs={{1,0},{2,1},{3,2},{4,3},{5,4},{6,5},{7,6},{9,8},{10,9},{11,10},{12... | collective-permute-start | bytes 86024 | tf_op jit(solution)/shard_map/ppermute | solution.py:21
  16.1 8.9 %copy-start.11 = (f32[32,16,128]{2,1,0:T(8,128)S(1)}, f32[32,16,128]{2,1,0:T(8,128)}, u32[]{:S(2)}) copy-start(f32[32,16,128]{2,1,0:T(8,128)} %param.9) | copy-start | bytes 786436
  25.0 16.6 %copy-start.5 = (f32[7,32,16,2]{3,2,1,0:T(8,128)S(1)}, f32[7,32,16,2]{3,2,1,0:T(8,128)}, u32[]{:S(2)}) copy-start(f32[7,32,16,2]{3,2,1,0:T(8,128)} %copy.90) | copy-start | bytes 86020
  25.0 16.6 %copy-start.8 = (f32[3,32,16,128]{3,2,1,0:T(8,128)S(1)}, f32[3,32,16,128]{3,2,1,0:T(8,128)}, u32[]{:S(2)}) copy-start(f32[3,32,16,128]{3,2,1,0:T(8,128)} %param.8) | copy-start | bytes 2359300
  25.0 16.6 %copy-start.9 = (f32[3,32,16,128]{3,2,1,0:T(8,128)S(1)}, f32[3,32,16,128]{3,2,1,0:T(8,128)}, u32[]{:S(2)}) copy-start(f32[3,32,16,128]{3,2,1,0:T(8,128)} %param.7) | copy-start | bytes 2359300
  27.7 12.7 %collective-permute-start.2 = (f32[7,32,2,132]{3,2,1,0:T(2,128)S(1)}, f32[7,32,2,132]{3,2,1,0:T(2,128)S(1)}, u32[]{:S(2)}, u32[]{:S(2)}) collective-permute-start(f32[7,32,2,132]{3,2,1,0:T(2,128)S(1)} %get-tuple-element.31), channel_id=1, source_target_pairs={{8,0},{16,8},{24,16},{9,1},{17,9},{25,17},{10,2},{18,10},{26,18},{... | collective-permute-start | bytes 709640 | tf_op jit(solution)/shard_map/ppermute | solution.py:21
  29.0 12.6 %collective-permute-start.3 = (f32[7,32,2,132]{3,2,1,0:T(2,128)S(1)}, f32[7,32,2,132]{3,2,1,0:T(2,128)S(1)}, u32[]{:S(2)}, u32[]{:S(2)}) collective-permute-start(f32[7,32,2,132]{3,2,1,0:T(2,128)S(1)} %get-tuple-element.32), channel_id=1, source_target_pairs={{0,8},{8,16},{16,24},{1,9},{9,17},{17,25},{2,10},{10,18},{18,26},{... | collective-permute-start | bytes 709640 | tf_op jit(solution)/shard_map/ppermute | solution.py:21
  40.4 2.2 %copy-start.14 = (f32[7,32,2,132]{3,2,1,0:T(2,128)}, f32[7,32,2,132]{3,2,1,0:T(2,128)S(1)}, u32[]{:S(2)}) copy-start(f32[7,32,2,132]{3,2,1,0:T(2,128)S(1)} %collective-permute-done.2) | copy-start | bytes 709636
  41.6 1.1 copy-start.16
  42.7 7.7 %collective-permute-start.4 = (f32[7,2,20,132]{3,2,1,0:T(8,128)}, f32[7,2,20,132]{3,2,1,0:T(8,128)}, u32[]{:S(2)}, u32[]{:S(2)}) collective-permute-start(f32[7,2,20,132]{3,2,1,0:T(8,128)} %get-tuple-element.22), channel_id=1, source_target_pairs={{0,32},{32,64},{64,96},{96,128},{128,160},{160,192},{192,224},{1,3... | collective-permute-start | bytes 443528 | tf_op jit(solution)/shard_map/ppermute | solution.py:21
  44.8 5.7 %collective-permute-start.5 = (f32[7,2,20,132]{3,2,1,0:T(8,128)}, f32[7,2,20,132]{3,2,1,0:T(8,128)}, u32[]{:S(2)}, u32[]{:S(2)}) collective-permute-start(f32[7,2,20,132]{3,2,1,0:T(8,128)} %get-tuple-element.23), channel_id=1, source_target_pairs={{32,0},{64,32},{96,64},{128,96},{160,128},{192,160},{224,192},{33,... | collective-permute-start | bytes 443528 | tf_op jit(solution)/shard_map/ppermute | solution.py:21
  48.2 2.3 %copy-start.6 = (f32[7,32,16,2]{3,2,1,0:T(8,128)S(1)}, f32[7,32,16,2]{3,2,1,0:T(8,128)}, u32[]{:S(2)}) copy-start(f32[7,32,16,2]{3,2,1,0:T(8,128)} %copy.90) | copy-start | bytes 86020
  48.2 2.3 %copy-start.10 = (f32[3,32,16,128]{3,2,1,0:T(8,128)S(1)}, f32[3,32,16,128]{3,2,1,0:T(8,128)}, u32[]{:S(2)}) copy-start(f32[3,32,16,128]{3,2,1,0:T(8,128)} %param.7) | copy-start | bytes 2359300
  48.2 2.3 %copy-start.15 = (f32[7,32,2,132]{3,2,1,0:T(2,128)S(1)}, f32[7,32,2,132]{3,2,1,0:T(2,128)}, u32[]{:S(2)}) copy-start(f32[7,32,2,132]{3,2,1,0:T(2,128)} %copy-done.14) | copy-start | bytes 709636
  48.2 2.3 %copy-start.17 = (f32[7,32,2,132]{3,2,1,0:T(2,128)S(1)}, f32[7,32,2,132]{3,2,1,0:T(2,128)}, u32[]{:S(2)}) copy-start(f32[7,32,2,132]{3,2,1,0:T(2,128)} %copy-done.16) | copy-start | bytes 709636
  54.3 2.8 %copy-start.2 = (f32[7,36,20,132]{3,2,1,0:T(8,128)}, f32[7,36,20,132]{3,2,1,0:T(8,128)S(1)}, u32[]{:S(2)}) copy-start(f32[7,36,20,132]{3,2,1,0:T(8,128)S(1)} %pad_maximum_fusion) | copy-start | bytes 7983364
  62.4 2.9 %copy-start.18 = (f32[35,20,132]{2,1,0:T(8,128)S(1)}, f32[35,20,132]{2,1,0:T(8,128)}, u32[]{:S(2)}) copy-start(f32[35,20,132]{2,1,0:T(8,128)} %and_convert_fusion) | copy-start | bytes 1108804
  62.4 2.9 %copy-start.19 = (f32[1,35,20,132]{3,2,1,0:T(8,128)S(1)}, f32[1,35,20,132]{3,2,1,0:T(8,128)}, u32[]{:S(2)}) copy-start(f32[1,35,20,132]{3,2,1,0:T(8,128)} %get-tuple-element.24) | copy-start | bytes 1108804
  67.7 1.7 %copy-start.3 = (f32[3,35,20,132]{3,2,1,0:T(8,128)}, f32[3,35,20,132]{3,2,1,0:T(8,128)S(1)}, u32[]{:S(2)}) copy-start(f32[3,35,20,132]{3,2,1,0:T(8,128)S(1)} %fusion.4) | copy-start | bytes 3326404
  77.0 3.6 %copy-start.20 = (f32[34,20,132]{2,1,0:T(8,128)S(1)}, f32[34,20,132]{2,1,0:T(8,128)}, u32[]{:S(2)}) copy-start(f32[34,20,132]{2,1,0:T(8,128)} %fusion.16) | copy-start | bytes 1077124
  94.3 2.9 %copy-start.4 = (f32[3,35,20,132]{3,2,1,0:T(8,128)S(1)}, f32[3,35,20,132]{3,2,1,0:T(8,128)}, u32[]{:S(2)}) copy-start(f32[3,35,20,132]{3,2,1,0:T(8,128)} %copy-done.3) | copy-start | bytes 3326404
  94.3 3.1 %copy-start.21 = (f32[33,20,132]{2,1,0:T(8,128)S(1)}, f32[33,20,132]{2,1,0:T(8,128)}, u32[]{:S(2)}) copy-start(f32[33,20,132]{2,1,0:T(8,128)} %and_convert_fusion.1) | copy-start | bytes 1045444
  97.9 1.6 %copy-start.7 = (f32[3,33,20,132]{3,2,1,0:T(8,128)}, f32[3,33,20,132]{3,2,1,0:T(8,128)S(1)}, u32[]{:S(2)}) copy-start(f32[3,33,20,132]{3,2,1,0:T(8,128)S(1)} %fusion.5) | copy-start | bytes 3136324
  109.5 4.0 %copy-start.22 = (f32[32,20,132]{2,1,0:T(8,128)S(1)}, f32[32,20,132]{2,1,0:T(8,128)}, u32[]{:S(2)}) copy-start(f32[32,20,132]{2,1,0:T(8,128)} %fusion.24) | copy-start | bytes 1013764
  113.5 1.0 copy-start.23
  113.5 1.2 copy-start.24
  114.1 1.6 %copy-start.12 = (f32[3,32,20,132]{3,2,1,0:T(8,128)}, f32[3,32,20,132]{3,2,1,0:T(8,128)S(1)}, u32[]{:S(2)}) copy-start(f32[3,32,20,132]{3,2,1,0:T(8,128)S(1)} %slice_add_fusion.1) | copy-start | bytes 3041284
  114.1 1.5 %copy-start.25 = (f32[2,32,16,128]{3,2,1,0:T(8,128)S(1)}, f32[2,32,16,128]{3,2,1,0:T(8,128)}, u32[]{:S(2)}) copy-start(f32[2,32,16,128]{3,2,1,0:T(8,128)} %slice.513) | copy-start | bytes 1572868
  114.1 1.6 %copy-start.28 = (f32[4,128]{1,0:T(4,128)S(1)}, f32[4,128]{1,0:T(4,128)}, u32[]{:S(2)}) copy-start(f32[4,128]{1,0:T(4,128)} %get-tuple-element.67) | copy-start | bytes 6148
  115.7 1.4 copy-start.29
  117.1 1.6 %copy-start.26 = (f32[4,32,16,128]{3,2,1,0:T(8,128)S(1)}, f32[4,32,16,128]{3,2,1,0:T(8,128)}, u32[]{:S(2)}) copy-start(f32[4,32,16,128]{3,2,1,0:T(8,128)} %param.10) | copy-start | bytes 3145732
  117.1 1.6 %copy-start.30 = (f32[128]{0:T(128)S(1)}, f32[128]{0:T(128)}, u32[]{:S(2)}) copy-start(f32[128]{0:T(128)} %mul.185) | copy-start | bytes 1540
  117.2 1.6 %copy-start.31 = (f32[128]{0:T(128)S(1)}, f32[128]{0:T(128)}, u32[]{:S(2)}) copy-start(f32[128]{0:T(128)} %mul.177) | copy-start | bytes 1540
  118.7 0.9 copy-start.27
  118.7 23.6 %copy-start.1 = (bf16[4,2,4,256,64]{3,4,2,1,0:T(8,128)(2,1)S(1)}, bf16[4,2,4,256,64]{3,4,2,1,0:T(8,128)(2,1)}, u32[]{:S(2)}) copy-start(bf16[4,2,4,256,64]{3,4,2,1,0:T(8,128)(2,1)} %param.13) | copy-start | bytes 3145732
  118.9 23.4 %copy-start.13 = (f32[4,32,16,128]{3,2,1,0:T(8,128)}, f32[4,32,16,128]{3,2,1,0:T(8,128)S(1)}, u32[]{:S(2)}) copy-start(f32[4,32,16,128]{3,2,1,0:T(8,128)S(1)} %multiply_add_fusion) | copy-start | bytes 3145732
  121.8 19.7 %all-to-all-start = ((f32[32,2,4]{2,1,0:T(2,128)}), f32[32,2,4]{2,1,0:T(2,128)S(1)}, u32[]{:S(2)}, u32[]{:S(2)}) async-start(f32[32,2,4]{2,1,0:T(2,128)} %copy.117), calls=%async_computation | async-start | bytes 65536 | tf_op jit(solution)/shard_map/all_to_all | solution.py:114

commit v6 on v4

--- a/solution.py
+++ b/solution.py
@@ -28,6 +28,26 @@
     from_below = shifted(high, axis, 1)
     from_above = shifted(low, axis, -1)
     return jnp.concatenate([from_below, stack, from_above], axis=dim)
+
+
+def widen_lanes(stack, axis):
+    lanes = stack.shape[-1]
+    flat = stack.reshape(-1, lanes)
+    lane = jnp.arange(lanes)
+    edges = jnp.concatenate([jnp.arange(HALO), jnp.arange(lanes - HALO, lanes)])
+    pick = (lane[None, :] == edges[:, None]).astype(jnp.float32)
+    faces = jnp.einsum("kz,rz->kr", pick, flat, precision=lax.Precision.HIGHEST)
+    from_above = shifted(faces[:HALO], axis, -1)
+    from_below = shifted(faces[HALO:], axis, 1)
+    ghosts = jnp.concatenate([from_below, from_above], axis=0)
+    out = jnp.arange(lanes + 2 * HALO)
+    spots = jnp.concatenate([jnp.arange(HALO), jnp.arange(lanes + HALO, lanes + 2 * HALO)])
+    move = (out[None, :] == lane[:, None] + HALO).astype(jnp.float32)
+    place = (out[None, :] == spots[:, None]).astype(jnp.float32)
+    wide = jnp.dot(flat, move, precision=lax.Precision.HIGHEST) + jnp.einsum(
+        "kr,kl->rl", ghosts, place, precision=lax.Precision.HIGHEST
+    )
+    return wide.reshape(stack.shape[:-1] + (lanes + 2 * HALO,))
 
 
 def box(value, start, size):
@@ -72,8 +92,11 @@
     cells_x, cells_y, cells_z = cells
     ports_here = dft_sums.shape[0]
     stack = jnp.concatenate([e_field, h_field, inv_permittivity[None]], axis=0)
-    for dim, axis in enumerate(AXES):
-        stack = pin(widen(stack, dim + 1, axis))
+    stack = pin(widen(stack, 1, "gx"))
+    stack = widen(stack, 2, "gy")
+    spare = -stack.shape[2] % 8
+    stack = pin(jnp.pad(stack, ((0, 0), (0, 0), (0, spare), (0, 0))))
+    stack = pin(widen_lanes(stack, "gz"))
     e0, h0, inv = stack[0:3], stack[3:6], stack[6]
     n = lambda k: tuple(c + k for c in cells)
     h1 = box(h0, (0, 0, 0), n(3)) - 0.5 * curl(e0, (0, 0, 0), n(3), 1)

time: 94.6 us -> 80.7 us (0.85)
  local copies, waits for them, and re-layouts: 26.3 us -> 10.8 us
  other arithmetic: 24.7 us -> 16.3 us
  matrix products: 0.97 us -> 8.01 us
  waiting for transfers between devices: 15.7 us -> 18.9 us
    slice x3 -> x1, local copies, waits for them, and re-layouts: 10.1 us -> 0.05 us  [widen_lanes(): from_below = shifted(faces[HALO:], axis, 1)]
    concatenate x2 -> x1, other arithmetic: 10.1 us -> 2.46 us  [widen(): return jnp.concatenate([from_below, stack, from_above], axis=dim)]
    dot_general x0 -> x3, matrix products: none -> 7.04 us  [the longest x1 2.84 us: widen_lanes(): jnp.dot(flat, move, precision=lax.Precision.HIGHEST)]
    ppermute x2 -> x0, local copies, waits for them, and re-layouts: 6.25 us -> none  [shifted(): lax.ppermute(value, axis, [(source, source + steps) for source in range(f...]
    ppermute x6, waiting for transfers between devices: 9.49 us -> 12.7 us  [shifted(): lax.ppermute(value, axis, [(source, source + steps) for source in range(f...]
    unnamed x24 -> x28, local copies, waits for them, and re-layouts: 3.6 us -> 3.98 us
  transfers between devices with their start and end apart: 7 -> 7, of which waited for: 5 -> 4; matrix products, arithmetic and copies ran while one was open for 13% -> 7% of each run, Pallas kernels for 0% -> 0%
where the time goes in v6:
time: 80.7 us; the launch traced here: 79.9 us
  starting transfers between devices  24.8 us (31%)
  waiting for transfers between devices  18.9 us (23%)
  other arithmetic  16.3 us (20%)
  local copies, waits for them, and re-layouts  10.8 us (13%)
  matrix products  8.01 us (10%)
  between operations  1.14 us (1%)
    ppermute x6, starting transfers between devices, shifted(): lax.ppermute(value, axis, [(source, source + steps) for source in range(f...  15 us
    ppermute x6, waiting for transfers between devices, shifted(): lax.ppermute(value, axis, [(source, source + steps) for source in range(f...  12.7 us
    all_to_all x1, starting transfers between devices, per_device(): lax.all_to_all(pieces, ('gx', 'gy'), 0, 0, tiled=False)  9.84 us
    all_to_all x1, waiting for transfers between devices, per_device(): lax.all_to_all(pieces, ('gx', 'gy'), 0, 0, tiled=False)  6.23 us
    unnamed x28, local copies, waits for them, and re-layouts  3.98 us
    another operation x4, other arithmetic, curl(): jnp.stack([d(vz, 1) - d(vy, 2), d(vx, 2) - d(vz, 0), d(vy, 0) - d(vx, 1)])  3.58 us
    dot_general x1, matrix products, widen_lanes(): jnp.dot(flat, move, precision=lax.Precision.HIGHEST)  2.84 us
    dot_general x1, matrix products, widen_lanes(): jnp.einsum('kr,kl->rl', ghosts, place, precision=lax.Precision.HIGHEST)  2.69 us
  transfers between devices with their start and end apart: 7, of which 4 were waited for; matrix products, arithmetic and copies ran while one was open for 7% of the time, Pallas kernels for 0%

profile of v6, /device:TPU:96, one launch (start us, length us, event | category | flops | bytes accessed | tf_op | source)
XLA Modules:
  0.0 79.9 jit_solution(5039577841561006547)
XLA Ops:
  0.7 1.1 %pad_maximum_fusion.9 = (f32[7,2,16,128]{3,2,1,0:T(8,128)S(1)}, f32[7,2,16,128]{3,2,1,0:T(8,128)S(1)}) fusion(f32[1,32,16,128]{3,2,1,0:T(8,128)} %bitcast.80, f32[3,32,16,128]{3,2,1,0:T(8,128)} %param.8, f32[3,32,16,128]{3,2,1,0:T(8,128)} %param.7), kind=kLoop, calls=%fused_computation.113 | loop fusion | flops 114688 | bytes 2064384 | tf_op jit(solution)/shard_map/slice | solution.py:27
  1.8 1.7 %collective-permute-start = (f32[7,2,16,128]{3,2,1,0:T(8,128)S(1)}, f32[7,2,16,128]{3,2,1,0:T(8,128)S(1)}, u32[]{:S(2)}, u32[]{:S(2)}) collective-permute-start(f32[7,2,16,128]{3,2,1,0:T(8,128)S(1)} %get-tuple-element.37), channel_id=1, source_target_pairs={{0,32},{32,64},{64,96},{96,128},{128,160},{160,192},{192,224},{1,3... | collective-permute-start | bytes 344072 | tf_op jit(solution)/shard_map/ppermute | solution.py:21
  3.5 1.3 %collective-permute-start.1 = (f32[7,2,16,128]{3,2,1,0:T(8,128)S(1)}, f32[7,2,16,128]{3,2,1,0:T(8,128)S(1)}, u32[]{:S(2)}, u32[]{:S(2)}) collective-permute-start(f32[7,2,16,128]{3,2,1,0:T(8,128)S(1)} %get-tuple-element.38), channel_id=1, source_target_pairs={{32,0},{64,32},{96,64},{128,96},{160,128},{192,160},{224,192},{33,... | collective-permute-start | bytes 344072 | tf_op jit(solution)/shard_map/ppermute | solution.py:21
  4.9 0.7 broadcast_subtract_fusion
  5.6 0.7 cosine_bitcast_fusion.1
  6.4 1.1 %and_convert_fusion.1 = f32[33,17,129]{2,1,0:T(8,128)} fusion(pred[129]{0:T(512)(128)(4,1)S(1)} %compare_and_fusion, pred[33,17]{1,0:T(8,128)(4,1)S(1)} %broadcast_and_fusion), kind=kLoop, calls=%fused_computation.89 | loop fusion | flops 144738 | bytes 290166 | tf_op jit(solution)/shard_map/convert_element_type | solution.py:87
  7.7 0.8 constant_dynamic-slice_fusion
  8.7 3.5 %collective-permute-start.2 = (f32[7,36,2,128]{3,2,1,0:T(2,128)S(1)}, f32[7,36,2,128]{3,2,1,0:T(2,128)S(1)}, u32[]{:S(2)}, u32[]{:S(2)}) collective-permute-start(f32[7,36,2,128]{3,2,1,0:T(2,128)S(1)} %get-tuple-element.35), channel_id=1, source_target_pairs={{0,8},{8,16},{16,24},{1,9},{9,17},{17,25},{2,10},{10,18},{18,26},{... | collective-permute-start | bytes 774152 | tf_op jit(solution)/shard_map/ppermute | solution.py:21
  12.2 1.3 %collective-permute-start.3 = (f32[7,36,2,128]{3,2,1,0:T(2,128)S(1)}, f32[7,36,2,128]{3,2,1,0:T(2,128)S(1)}, u32[]{:S(2)}, u32[]{:S(2)}) collective-permute-start(f32[7,36,2,128]{3,2,1,0:T(2,128)S(1)} %get-tuple-element.36), channel_id=1, source_target_pairs={{8,0},{16,8},{24,16},{9,1},{17,9},{25,17},{10,2},{18,10},{26,18},{... | collective-permute-start | bytes 774152 | tf_op jit(solution)/shard_map/ppermute | solution.py:21
  13.7 3.1 %collective-permute-done.2 = f32[7,36,2,128]{3,2,1,0:T(2,128)S(1)} collective-permute-done((f32[7,36,2,128]{3,2,1,0:T(2,128)S(1)}, f32[7,36,2,128]{3,2,1,0:T(2,128)S(1)}, u32[]{:S(2)}, u32[]{:S(2)}) %collective-permute-start.2) | collective-permute-done | bytes 258080 | tf_op jit(solution)/shard_map/ppermute | solution.py:21
  16.8 4.7 %collective-permute-done.3 = f32[7,36,2,128]{3,2,1,0:T(2,128)S(1)} collective-permute-done((f32[7,36,2,128]{3,2,1,0:T(2,128)S(1)}, f32[7,36,2,128]{3,2,1,0:T(2,128)S(1)}, u32[]{:S(2)}, u32[]{:S(2)}) %collective-permute-start.3) | collective-permute-done | bytes 258080 | tf_op jit(solution)/shard_map/ppermute | solution.py:21
  21.5 2.5 %select_maximum_fusion = f32[7,36,24,128]{3,2,1,0:T(8,128)S(1)} fusion(f32[7,36,2,128]{3,2,1,0:T(2,128)S(1)} %collective-permute-done.3, f32[7,36,2,128]{3,2,1,0:T(2,128)S(1)} %collective-permute-done.2, f32[7,2,16,128]{3,2,1,0:T(8,128)} %copy-done.12, f32[7,2,16,128]{3,2,1,0:T(8,128)} %copy-done.11, f32[1,32,16,128]{3,2,1,0:T(8,128)} %bitcast.81, ...), kind=kLoop, calls=%fused_computation.9 | loop fusion | flops 10838016 | bytes 5677056 | tf_op jit(solution)/shard_map/concatenate | solution.py:30
  24.0 1.6 %copy-done.1 = f32[7,36,24,128]{3,2,1,0:T(8,128)} copy-done((f32[7,36,24,128]{3,2,1,0:T(8,128)}, f32[7,36,24,128]{3,2,1,0:T(8,128)S(1)}, u32[]{:S(2)}) %copy-start.1) | copy-done | bytes 3096600
  25.6 1.5 %fusion.51 = f32[4,6048]{1,0:T(4,128)S(1)} fusion(f32[6048,128]{1,0:T(8,128)S(1)} %bitcast.78, s32[4]{0:T(128)S(1)} %get-tuple-element.62), kind=kOutput, calls=%fused_computation.130 | convolution fusion | flops 37159424 | bytes 3193360 | tf_op jit(solution)/shard_map/kz,rz->kr/dot_general | solution.py:39
  27.2 5.0 %collective-permute-start.4 = (f32[2,6048]{1,0:T(2,128)S(1)}, f32[2,6048]{1,0:T(2,128)S(1)}, u32[]{:S(2)}, u32[]{:S(2)}) collective-permute-start(f32[2,6048]{1,0:T(2,128)S(1)} %get-tuple-element.55), channel_id=1, source_target_pairs={{0,1},{1,2},{2,3},{3,4},{4,5},{5,6},{6,7},{8,9},{9,10},{10,11},{11... | collective-permute-start | bytes 145160 | tf_op jit(solution)/shard_map/ppermute | solution.py:21
  32.2 2.1 %collective-permute-start.5 = (f32[2,6048]{1,0:T(2,128)S(1)}, f32[2,6048]{1,0:T(2,128)S(1)}, u32[]{:S(2)}, u32[]{:S(2)}) collective-permute-start(f32[2,6048]{1,0:T(2,128)S(1)} %get-tuple-element.56), channel_id=1, source_target_pairs={{1,0},{2,1},{3,2},{4,3},{5,4},{6,5},{7,6},{9,8},{10,9},{11,10},{12... | collective-permute-start | bytes 145160 | tf_op jit(solution)/shard_map/ppermute | solution.py:21
  34.7 4.9 %collective-permute-done.5 = f32[2,6048]{1,0:T(2,128)S(1)} collective-permute-done((f32[2,6048]{1,0:T(2,128)S(1)}, f32[2,6048]{1,0:T(2,128)S(1)}, u32[]{:S(2)}, u32[]{:S(2)}) %collective-permute-start.5) | collective-permute-done | bytes 48416 | tf_op jit(solution)/shard_map/ppermute | solution.py:21
  39.6 2.7 %fusion.44 = f32[6048,132]{1,0:T(8,128)S(1)} fusion(f32[2,6048]{1,0:T(2,128)S(1)} %collective-permute-done.5, f32[2,6048]{1,0:T(2,128)S(1)} %collective-permute-done.4, s32[4]{0:T(128)S(1)} %get-tuple-element.61), kind=kOutput, calls=%fused_computation.114 | convolution fusion | flops 38344848 | bytes 3290128 | tf_op jit(solution)/shard_map/kr,kl->rl/dot_general | solution.py:47
  42.3 2.8 %convolution_add_fusion = f32[6048,132]{1,0:T(8,128)S(1)} fusion(f32[6048,132]{1,0:T(8,128)S(1)} %fusion.44, f32[6048,128]{1,0:T(8,128)S(1)} %bitcast.79, s32[128]{0:T(128)S(1)} %iota_add_fusion.2), kind=kOutput, calls=%fused_computation.2 | convolution fusion | flops 1227059328 | bytes 9483776 | tf_op jit(solution)/shard_map/dot_general | solution.py:47
  45.2 0.3 slice_bitcast_fusion.3
  45.5 0.8 fusion.25
  46.3 0.4 fusion.13
  46.8 0.2 slice_bitcast_fusion.6
  47.0 0.2 slice.374
  47.2 0.3 slice_multiply_fusion
  47.5 1.6 %fusion.31 = (f32[1,34,18,130]{3,2,1,0:T(8,128)S(1)}, f32[1,34,18,130]{3,2,1,0:T(8,128)S(1)}, f32[1,34,18,130]{3,2,1,0:T(8,128)S(1)}) fusion(f32[35,19,131]{2,1,0:T(8,128)S(1)} %get-tuple-element.28, f32[35,19,131]{2,1,0:T(8,128)S(1)} %get-tuple-element.26, f32[35,19,131]{2,1,0:T(8,128)S(1)} %get-tuple-element.27), kind=kLoop, calls=%fused_computation.71 | loop fusion | flops 716040 | bytes 3818880 | tf_op jit(solution)/shard_map/stack | solution.py:75
  49.1 1.0 %slice_add_fusion = f32[3,34,18,130]{3,2,1,0:T(8,128)S(1)} fusion(f32[7,36,24,132]{3,2,1,0:T(8,128)S(1)} %bitcast.77, f32[1,34,18,130]{3,2,1,0:T(8,128)S(1)} %get-tuple-element.44, f32[1,34,18,130]{3,2,1,0:T(8,128)S(1)} %get-tuple-element.43, f32[1,34,18,130]{3,2,1,0:T(8,128)S(1)} %get-tuple-element.42, f32[34,18,130]{2,1,0:T(8,128)S(1)} %slice_multiply_fusion), kind=kLoop, calls=%fused_computation.24 | loop fusion | flops 954720 | bytes 3182400 | tf_op jit(solution)/shard_map/add | solution.py:104
  50.1 0.2 slice.373
  50.3 0.2 slice_bitcast_fusion.9
  50.7 0.5 fusion.37
  51.2 0.6 copy-done.6
  51.8 0.8 fusion.14
  52.6 0.2 slice_bitcast_fusion.12
  52.8 0.4 slice.376
  53.2 0.6 fusion.43
  53.8 0.3 slice_add_fusion.1
  54.4 1.2 %fusion = f32[4,4,32,16,128]{4,3,2,1,0:T(8,128)S(1)} fusion(f32[4,32,16,128]{3,2,1,0:T(8,128)S(1)} %pad_maximum_fusion.1, f32[4,128]{1,0:T(4,128)S(1)} %get-tuple-element.65), kind=kOutput, calls=%fused_computation | output fusion | flops 1056895 | bytes 5244928 | tf_op jit(solution)/shard_map/mul | solution.py:123
  55.6 1.5 %multiply_reduce_fusion.2 = (f32[4,32,16,128]{3,2,1,0:T(8,128)S(1)}, f32[4,32,16,128]{3,2,1,0:T(8,128)S(1)}) fusion(f32[4,128]{1,0:T(4,128)S(1)} %get-tuple-element.66, f32[4,4,32,16,128]{4,3,2,1,0:T(8,128)S(1)} %fusion, f32[4,128]{1,0:T(4,128)S(1)} %get-tuple-element.65, f32[4,32,16,128]{3,2,1,0:T(8,128)S(1)} %pad_maximum_fusion), kind=kOutput, calls=%fused_computation.6 | output fusion | flops 4726911 | bytes 7344128 | tf_op jit(solution)/shard_map/mul | solution.py:123
  57.1 0.2 multiply_add_fusion
  57.3 1.0 %copy-done.5 = f32[4,32,16,128]{3,2,1,0:T(8,128)} copy-done((f32[4,32,16,128]{3,2,1,0:T(8,128)}, f32[4,32,16,128]{3,2,1,0:T(8,128)S(1)}, u32[]{:S(2)}) %copy-start.5) | copy-done | bytes 1048600
  58.3 1.0 %convolution_bitcast_fusion = f32[4,8,128]{2,1,0:T(8,128)S(1)} fusion(bf16[4,8,32,16]{2,1,3,0:T(8,128)(2,1)S(1)} %bitcast.83, f32[4,32,16,128]{3,2,1,0:T(8,128)S(1)} %multiply_add_fusion), kind=kOutput, calls=%fused_computation.33 | convolution fusion | flops 25165824 | bytes 1097728 | tf_op jit(solution)/shard_map/pxyl,pnxy->pnl/dot_general | solution.py:133
  59.3 0.9 %reshape.208 = f32[4,2,4,4,2,16]{5,4,3,2,1,0:T(2,128)} reshape(f32[4,8,128]{2,1,0:T(8,128)S(1)} %convolution_bitcast_fusion) | data formatting | bytes 32768 | tf_op jit(solution)/shard_map/reshape | solution.py:134
  60.2 0.7 fusion.56
  61.0 0.9 %copy.37 = f32[32,2,4]{2,1,0:T(2,128)} copy(f32[32,2,4]{1,0,2:T(8,128)S(1)} %reshape_reshape.3) | data formatting | bytes 2048 | tf_op jit(solution)/shard_map/reshape;reshape | solution.py:137
  61.9 9.8 %all-to-all-start = ((f32[32,2,4]{2,1,0:T(2,128)}), f32[32,2,4]{2,1,0:T(2,128)S(1)}, u32[]{:S(2)}, u32[]{:S(2)}) async-start(f32[32,2,4]{2,1,0:T(2,128)} %copy.37), calls=%async_computation | async-start | bytes 65536 | tf_op jit(solution)/shard_map/all_to_all | solution.py:138
  71.8 1.2 %slice.372 = f32[3,32,16,128]{3,2,1,0:T(8,128)} slice(f32[3,33,17,129]{3,2,1,0:T(8,128)S(1)} %fusion.14), slice={[0:3], [1:33], [1:17], [1:129]} | slice | bytes 1572864 | tf_op jit(solution)/shard_map/slice | solution.py:55
  72.9 6.2 %all-to-all-done = f32[32,2,4]{2,1,0:T(2,128)S(1)} async-done(((f32[32,2,4]{2,1,0:T(2,128)}), f32[32,2,4]{2,1,0:T(2,128)S(1)}, u32[]{:S(2)}, u32[]{:S(2)}) %all-to-all-start) | async-done | bytes 1056 | tf_op jit(solution)/shard_map/all_to_all | solution.py:138
  79.3 0.7 copy.40
  (59 shorter events, 1.8 us)
Async XLA Ops:
  0.6 7.0 %copy-start = (bf16[4,2,4,256,64]{3,4,2,1,0:T(8,128)(2,1)S(1)}, bf16[4,2,4,256,64]{3,4,2,1,0:T(8,128)(2,1)}, u32[]{:S(2)}) copy-start(bf16[4,2,4,256,64]{3,4,2,1,0:T(8,128)(2,1)} %param.13) | copy-start | bytes 3145732
  0.6 7.8 %copy-start.7 = (f32[32,16,128]{2,1,0:T(8,128)S(1)}, f32[32,16,128]{2,1,0:T(8,128)}, u32[]{:S(2)}) copy-start(f32[32,16,128]{2,1,0:T(8,128)} %param.9) | copy-start | bytes 786436
  0.7 7.8 %copy-start.4 = (f32[3,32,16,128]{3,2,1,0:T(8,128)S(1)}, f32[3,32,16,128]{3,2,1,0:T(8,128)}, u32[]{:S(2)}) copy-start(f32[3,32,16,128]{3,2,1,0:T(8,128)} %param.7) | copy-start | bytes 2359300
  0.7 7.8 %copy-start.3 = (f32[3,32,16,128]{3,2,1,0:T(8,128)S(1)}, f32[3,32,16,128]{3,2,1,0:T(8,128)}, u32[]{:S(2)}) copy-start(f32[3,32,16,128]{3,2,1,0:T(8,128)} %param.8) | copy-start | bytes 2359300
  1.8 6.7 %collective-permute-start = (f32[7,2,16,128]{3,2,1,0:T(8,128)S(1)}, f32[7,2,16,128]{3,2,1,0:T(8,128)S(1)}, u32[]{:S(2)}, u32[]{:S(2)}) collective-permute-start(f32[7,2,16,128]{3,2,1,0:T(8,128)S(1)} %get-tuple-element.37), channel_id=1, source_target_pairs={{0,32},{32,64},{64,96},{96,128},{128,160},{160,192},{192,224},{1,3... | collective-permute-start | bytes 344072 | tf_op jit(solution)/shard_map/ppermute | solution.py:21
  3.5 5.0 %collective-permute-start.1 = (f32[7,2,16,128]{3,2,1,0:T(8,128)S(1)}, f32[7,2,16,128]{3,2,1,0:T(8,128)S(1)}, u32[]{:S(2)}, u32[]{:S(2)}) collective-permute-start(f32[7,2,16,128]{3,2,1,0:T(8,128)S(1)} %get-tuple-element.38), channel_id=1, source_target_pairs={{32,0},{64,32},{96,64},{128,96},{160,128},{192,160},{224,192},{33,... | collective-permute-start | bytes 344072 | tf_op jit(solution)/shard_map/ppermute | solution.py:21
  8.5 5.0 %copy-start.11 = (f32[7,2,16,128]{3,2,1,0:T(8,128)}, f32[7,2,16,128]{3,2,1,0:T(8,128)S(1)}, u32[]{:S(2)}) copy-start(f32[7,2,16,128]{3,2,1,0:T(8,128)S(1)} %collective-permute-done) | copy-start | bytes 344068
  8.5 5.0 %copy-start.12 = (f32[7,2,16,128]{3,2,1,0:T(8,128)}, f32[7,2,16,128]{3,2,1,0:T(8,128)S(1)}, u32[]{:S(2)}) copy-start(f32[7,2,16,128]{3,2,1,0:T(8,128)S(1)} %collective-permute-done.1) | copy-start | bytes 344068
  8.7 8.1 %collective-permute-start.2 = (f32[7,36,2,128]{3,2,1,0:T(2,128)S(1)}, f32[7,36,2,128]{3,2,1,0:T(2,128)S(1)}, u32[]{:S(2)}, u32[]{:S(2)}) collective-permute-start(f32[7,36,2,128]{3,2,1,0:T(2,128)S(1)} %get-tuple-element.35), channel_id=1, source_target_pairs={{0,8},{8,16},{16,24},{1,9},{9,17},{17,25},{2,10},{10,18},{18,26},{... | collective-permute-start | bytes 774152 | tf_op jit(solution)/shard_map/ppermute | solution.py:21
  12.2 9.3 %collective-permute-start.3 = (f32[7,36,2,128]{3,2,1,0:T(2,128)S(1)}, f32[7,36,2,128]{3,2,1,0:T(2,128)S(1)}, u32[]{:S(2)}, u32[]{:S(2)}) collective-permute-start(f32[7,36,2,128]{3,2,1,0:T(2,128)S(1)} %get-tuple-element.36), channel_id=1, source_target_pairs={{8,0},{16,8},{24,16},{9,1},{17,9},{25,17},{10,2},{18,10},{26,18},{... | collective-permute-start | bytes 774152 | tf_op jit(solution)/shard_map/ppermute | solution.py:21
  24.0 1.6 %copy-start.1 = (f32[7,36,24,128]{3,2,1,0:T(8,128)}, f32[7,36,24,128]{3,2,1,0:T(8,128)S(1)}, u32[]{:S(2)}) copy-start(f32[7,36,24,128]{3,2,1,0:T(8,128)S(1)} %select_maximum_fusion) | copy-start | bytes 9289732
  24.0 10.7 %copy-start.10 = (bf16[4,2,4,32,16]{3,4,2,1,0:T(8,128)(2,1)S(1)}, bf16[4,2,4,32,16]{3,4,2,1,0:T(8,128)(2,1)}, u32[]{:S(2)}) copy-start(bf16[4,2,4,32,16]{3,4,2,1,0:T(8,128)(2,1)} %constant_dynamic-slice_fusion) | copy-start | bytes 98308
  27.2 7.6 %collective-permute-start.4 = (f32[2,6048]{1,0:T(2,128)S(1)}, f32[2,6048]{1,0:T(2,128)S(1)}, u32[]{:S(2)}, u32[]{:S(2)}) collective-permute-start(f32[2,6048]{1,0:T(2,128)S(1)} %get-tuple-element.55), channel_id=1, source_target_pairs={{0,1},{1,2},{2,3},{3,4},{4,5},{5,6},{6,7},{8,9},{9,10},{10,11},{11... | collective-permute-start | bytes 145160 | tf_op jit(solution)/shard_map/ppermute | solution.py:21
  32.2 7.4 %collective-permute-start.5 = (f32[2,6048]{1,0:T(2,128)S(1)}, f32[2,6048]{1,0:T(2,128)S(1)}, u32[]{:S(2)}, u32[]{:S(2)}) collective-permute-start(f32[2,6048]{1,0:T(2,128)S(1)} %get-tuple-element.56), channel_id=1, source_target_pairs={{1,0},{2,1},{3,2},{4,3},{5,4},{6,5},{7,6},{9,8},{10,9},{11,10},{12... | collective-permute-start | bytes 145160 | tf_op jit(solution)/shard_map/ppermute | solution.py:21
  39.6 2.7 %copy-start.2 = (f32[7,36,24,128]{3,2,1,0:T(8,128)S(1)}, f32[7,36,24,128]{3,2,1,0:T(8,128)}, u32[]{:S(2)}) copy-start(f32[7,36,24,128]{3,2,1,0:T(8,128)} %copy-done.1) | copy-start | bytes 9289732
  50.7 1.1 %copy-start.6 = (f32[33,17,129]{2,1,0:T(8,128)S(1)}, f32[33,17,129]{2,1,0:T(8,128)}, u32[]{:S(2)}) copy-start(f32[33,17,129]{2,1,0:T(8,128)} %and_convert_fusion.1) | copy-start | bytes 868432
  54.2 1.4 %copy-start.8 = (f32[3,32,16,128]{3,2,1,0:T(8,128)}, f32[3,32,16,128]{3,2,1,0:T(8,128)S(1)}, u32[]{:S(2)}) copy-start(f32[3,32,16,128]{3,2,1,0:T(8,128)S(1)} %slice_add_fusion.1) | copy-start | bytes 2359300
  55.6 1.5 %copy-start.9 = (f32[4,32,16,128]{3,2,1,0:T(8,128)S(1)}, f32[4,32,16,128]{3,2,1,0:T(8,128)}, u32[]{:S(2)}) copy-start(f32[4,32,16,128]{3,2,1,0:T(8,128)} %param.10) | copy-start | bytes 3145732
  57.3 1.0 %copy-start.5 = (f32[4,32,16,128]{3,2,1,0:T(8,128)}, f32[4,32,16,128]{3,2,1,0:T(8,128)S(1)}, u32[]{:S(2)}) copy-start(f32[4,32,16,128]{3,2,1,0:T(8,128)S(1)} %multiply_add_fusion) | copy-start | bytes 3145732
  61.9 17.2 %all-to-all-start = ((f32[32,2,4]{2,1,0:T(2,128)}), f32[32,2,4]{2,1,0:T(2,128)S(1)}, u32[]{:S(2)}, u32[]{:S(2)}) async-start(f32[32,2,4]{2,1,0:T(2,128)} %copy.37), calls=%async_computation | async-start | bytes 65536 | tf_op jit(solution)/shard_map/all_to_all | solution.py:138

commit v7 on v6

--- a/solution.py
+++ b/solution.py
@@ -114,9 +114,23 @@
     lane_part = jnp.arange(lanes) // (lanes // 4)
     spread_of = (lane_part[None, :] == jnp.arange(4)[:, None]).astype(jnp.float32)
     dft = dft_sums
-    for step, (e_now, h_now) in enumerate(((e1_here, h1_here), (e2, h2_here))):
-        tangent = pin(jnp.stack([e_now[0], e_now[1], h_now[0], h_now[1]]))
-        planes = jnp.sum(tangent[None] * onehot[:, None, None, None, :], axis=-1)
+    at = lambda value: jnp.sum(value[None] * onehot[:, None, None, :], axis=-1)
+    near = lambda v, x, y, z: at(box(v, (x, y, z), cells))
+    h2x, h2y, h2z = h2[0], h2[1], h2[2]
+    half_inv = 0.5 * near(inv, 2, 2, 2)
+    e2x = near(e1[0], 1, 1, 1) + half_inv * (
+        (near(h2z, 1, 1, 1) - near(h2z, 1, 0, 1)) - (near(h2y, 1, 1, 1) - near(h2y, 1, 1, 0))
+    )
+    e2y = near(e1[1], 1, 1, 1) + half_inv * (
+        (near(h2x, 1, 1, 1) - near(h2x, 1, 1, 0)) - (near(h2z, 1, 1, 1) - near(h2z, 0, 1, 1))
+    )
+    ported = jnp.stack([e2x, e2y, near(h2x, 1, 1, 1), near(h2y, 1, 1, 1)], axis=1)
+    for step, (e_now, h_now) in enumerate(((e1_here, h1_here), (None, None))):
+        if e_now is None:
+            planes = ported
+        else:
+            tangent = pin(jnp.stack([e_now[0], e_now[1], h_now[0], h_now[1]]))
+            planes = jnp.sum(tangent[None] * onehot[:, None, None, None, :], axis=-1)
         phase = omega * jnp.float32(step + 1)
         trig = jnp.stack([jnp.cos(phase), jnp.sin(phase)])
         coef = jnp.tile(trig.reshape(-1), 4)

time: 80.7 us -> 102 us (1.26)
  other arithmetic: 16.3 us -> 36.2 us
  local copies, waits for them, and re-layouts: 10.8 us -> 17.2 us
  waiting for transfers between devices: 18.9 us -> 14.4 us
    mul x2 -> x1, other arithmetic: 2.66 us -> 14.3 us  [per_device(): planes[..., None] * spread_of[None, :, None, None, :]]
    all_to_all x1, waiting for transfers between devices: 6.23 us -> 2.2 us  [per_device(): lax.all_to_all(pieces, ('gx', 'gy'), 0, 0, tiled=False)]
    reduce_sum x0 -> x1, other arithmetic: none -> 2.77 us  [per_device(): at = lambda value: jnp.sum(value[None] * onehot[:, None, None, :], axis=-1)]
    slice x0 -> x2, other arithmetic: none -> 2.32 us  [box(): lax.slice(value, (0,) * lead + tuple(start), value.shape[:lead] + tuple((...]
    another operation x2, local copies, waits for them, and re-layouts: 1 us -> 3.14 us  [per_device(): pieces = partial_sums.reshape(groups, owned, MODES * 2)]
    add x1, other arithmetic: 0.34 us -> 2.34 us  [per_device(): box(e1, (1, 1, 1), n(0))]
    slice x1 -> x3, local copies, waits for them, and re-layouts: 1.15 us -> 3.08 us  [box(): lax.slice(value, (0,) * lead + tuple(start), value.shape[:lead] + tuple((...]
    mul x2, local copies, waits for them, and re-layouts: 0.17 us -> 1.19 us  [per_device(): dft = pin(dft + spread * coef)]
  transfers between devices with their start and end apart: 7 -> 7, of which waited for: 4 -> 4; matrix products, arithmetic and copies ran while one was open for 7% -> 11% of each run, Pallas kernels for 0% -> 0%
where the time goes in v7:
time: 102 us; the launch traced here: 101 us
  other arithmetic  36.2 us (35%)
  starting transfers between devices  23.9 us (23%)
  local copies, waits for them, and re-layouts  17.2 us (17%)
  waiting for transfers between devices  14.4 us (14%)
  matrix products  8.65 us (8%)
  between operations  1.16 us (1%)
    ppermute x6, starting transfers between devices, shifted(): lax.ppermute(value, axis, [(source, source + steps) for source in range(f...  15 us
    mul x1, other arithmetic, per_device(): planes[..., None] * spread_of[None, :, None, None, :]  14.3 us
    ppermute x6, waiting for transfers between devices, shifted(): lax.ppermute(value, axis, [(source, source + steps) for source in range(f...  12.2 us
    all_to_all x1, starting transfers between devices, per_device(): lax.all_to_all(pieces, ('gx', 'gy'), 0, 0, tiled=False)  8.9 us
    unnamed x36, local copies, waits for them, and re-layouts  4.92 us
    another operation x2, local copies, waits for them, and re-layouts, per_device(): pieces = partial_sums.reshape(groups, owned, MODES * 2)  3.14 us
    slice x3, local copies, waits for them, and re-layouts, box(): lax.slice(value, (0,) * lead + tuple(start), value.shape[:lead] + tuple((...  3.08 us
    another operation x3, other arithmetic, curl(): jnp.stack([d(vz, 1) - d(vy, 2), d(vx, 2) - d(vz, 0), d(vy, 0) - d(vx, 1)])  2.98 us
  transfers between devices with their start and end apart: 7, of which 4 were waited for; matrix products, arithmetic and copies ran while one was open for 11% of the time, Pallas kernels for 0%

profile of v7, /device:TPU:96, one launch (start us, length us, event | category | flops | bytes accessed | tf_op | source)
XLA Modules:
  0.0 101.5 jit_solution(17415895419786225526)
XLA Ops:
  0.7 1.1 %pad_maximum_fusion.9 = (f32[7,2,16,128]{3,2,1,0:T(8,128)S(1)}, f32[7,2,16,128]{3,2,1,0:T(8,128)S(1)}) fusion(f32[1,32,16,128]{3,2,1,0:T(8,128)} %bitcast.111, f32[3,32,16,128]{3,2,1,0:T(8,128)} %param.8, f32[3,32,16,128]{3,2,1,0:T(8,128)} %param.7), kind=kLoop, calls=%fused_computation.112 | loop fusion | flops 114688 | bytes 2064384 | tf_op jit(solution)/shard_map/slice | solution.py:27
  1.8 1.7 %collective-permute-start = (f32[7,2,16,128]{3,2,1,0:T(8,128)S(1)}, f32[7,2,16,128]{3,2,1,0:T(8,128)S(1)}, u32[]{:S(2)}, u32[]{:S(2)}) collective-permute-start(f32[7,2,16,128]{3,2,1,0:T(8,128)S(1)} %get-tuple-element.47), channel_id=1, source_target_pairs={{0,32},{32,64},{64,96},{96,128},{128,160},{160,192},{192,224},{1,3... | collective-permute-start | bytes 344072 | tf_op jit(solution)/shard_map/ppermute | solution.py:21
  3.5 1.3 %collective-permute-start.1 = (f32[7,2,16,128]{3,2,1,0:T(8,128)S(1)}, f32[7,2,16,128]{3,2,1,0:T(8,128)S(1)}, u32[]{:S(2)}, u32[]{:S(2)}) collective-permute-start(f32[7,2,16,128]{3,2,1,0:T(8,128)S(1)} %get-tuple-element.48), channel_id=1, source_target_pairs={{32,0},{64,32},{96,64},{128,96},{160,128},{192,160},{224,192},{33,... | collective-permute-start | bytes 344072 | tf_op jit(solution)/shard_map/ppermute | solution.py:21
  4.9 0.7 broadcast_subtract_fusion
  5.6 0.7 cosine_bitcast_fusion.1
  6.4 1.1 %and_convert_fusion.1 = f32[33,17,129]{2,1,0:T(8,128)} fusion(pred[129]{0:T(512)(128)(4,1)S(1)} %compare_and_fusion, pred[33,17]{1,0:T(8,128)(4,1)S(1)} %broadcast_and_fusion), kind=kLoop, calls=%fused_computation.93 | loop fusion | flops 144738 | bytes 290166 | tf_op jit(solution)/shard_map/convert_element_type | solution.py:87
  7.5 0.6 fusion.49
  8.2 0.8 constant_dynamic-slice_fusion
  9.3 3.5 %collective-permute-start.2 = (f32[7,36,2,128]{3,2,1,0:T(2,128)S(1)}, f32[7,36,2,128]{3,2,1,0:T(2,128)S(1)}, u32[]{:S(2)}, u32[]{:S(2)}) collective-permute-start(f32[7,36,2,128]{3,2,1,0:T(2,128)S(1)} %get-tuple-element.45), channel_id=1, source_target_pairs={{0,8},{8,16},{16,24},{1,9},{9,17},{17,25},{2,10},{10,18},{18,26},{... | collective-permute-start | bytes 774152 | tf_op jit(solution)/shard_map/ppermute | solution.py:21
  12.8 1.3 %collective-permute-start.3 = (f32[7,36,2,128]{3,2,1,0:T(2,128)S(1)}, f32[7,36,2,128]{3,2,1,0:T(2,128)S(1)}, u32[]{:S(2)}, u32[]{:S(2)}) collective-permute-start(f32[7,36,2,128]{3,2,1,0:T(2,128)S(1)} %get-tuple-element.46), channel_id=1, source_target_pairs={{8,0},{16,8},{24,16},{9,1},{17,9},{25,17},{10,2},{18,10},{26,18},{... | collective-permute-start | bytes 774152 | tf_op jit(solution)/shard_map/ppermute | solution.py:21
  14.3 3.6 %collective-permute-done.2 = f32[7,36,2,128]{3,2,1,0:T(2,128)S(1)} collective-permute-done((f32[7,36,2,128]{3,2,1,0:T(2,128)S(1)}, f32[7,36,2,128]{3,2,1,0:T(2,128)S(1)}, u32[]{:S(2)}, u32[]{:S(2)}) %collective-permute-start.2) | collective-permute-done | bytes 258080 | tf_op jit(solution)/shard_map/ppermute | solution.py:21
  17.9 4.7 %collective-permute-done.3 = f32[7,36,2,128]{3,2,1,0:T(2,128)S(1)} collective-permute-done((f32[7,36,2,128]{3,2,1,0:T(2,128)S(1)}, f32[7,36,2,128]{3,2,1,0:T(2,128)S(1)}, u32[]{:S(2)}, u32[]{:S(2)}) %collective-permute-start.3) | collective-permute-done | bytes 258080 | tf_op jit(solution)/shard_map/ppermute | solution.py:21
  22.6 2.5 %select_maximum_fusion = f32[7,36,24,128]{3,2,1,0:T(8,128)S(1)} fusion(f32[7,36,2,128]{3,2,1,0:T(2,128)S(1)} %collective-permute-done.3, f32[7,36,2,128]{3,2,1,0:T(2,128)S(1)} %collective-permute-done.2, f32[7,2,16,128]{3,2,1,0:T(8,128)} %copy-done.12, f32[7,2,16,128]{3,2,1,0:T(8,128)} %copy-done.11, f32[1,32,16,128]{3,2,1,0:T(8,128)} %bitcast.112, ...), kind=kLoop, calls=%fused_computation.6 | loop fusion | flops 10838016 | bytes 5677056 | tf_op jit(solution)/shard_map/concatenate | solution.py:30
  25.1 1.6 %copy-done.1 = f32[7,36,24,128]{3,2,1,0:T(8,128)} copy-done((f32[7,36,24,128]{3,2,1,0:T(8,128)}, f32[7,36,24,128]{3,2,1,0:T(8,128)S(1)}, u32[]{:S(2)}) %copy-start.1) | copy-done | bytes 3096600
  26.7 1.5 %fusion.48 = f32[4,6048]{1,0:T(4,128)S(1)} fusion(f32[6048,128]{1,0:T(8,128)S(1)} %bitcast.109, s32[4]{0:T(128)S(1)} %get-tuple-element.83), kind=kOutput, calls=%fused_computation.137 | convolution fusion | flops 37159424 | bytes 3193360 | tf_op jit(solution)/shard_map/kz,rz->kr/dot_general | solution.py:39
  28.3 5.0 %collective-permute-start.4 = (f32[2,6048]{1,0:T(2,128)S(1)}, f32[2,6048]{1,0:T(2,128)S(1)}, u32[]{:S(2)}, u32[]{:S(2)}) collective-permute-start(f32[2,6048]{1,0:T(2,128)S(1)} %get-tuple-element.76), channel_id=1, source_target_pairs={{0,1},{1,2},{2,3},{3,4},{4,5},{5,6},{6,7},{8,9},{9,10},{10,11},{11... | collective-permute-start | bytes 145160 | tf_op jit(solution)/shard_map/ppermute | solution.py:21
  33.3 2.1 %collective-permute-start.5 = (f32[2,6048]{1,0:T(2,128)S(1)}, f32[2,6048]{1,0:T(2,128)S(1)}, u32[]{:S(2)}, u32[]{:S(2)}) collective-permute-start(f32[2,6048]{1,0:T(2,128)S(1)} %get-tuple-element.77), channel_id=1, source_target_pairs={{1,0},{2,1},{3,2},{4,3},{5,4},{6,5},{7,6},{9,8},{10,9},{11,10},{12... | collective-permute-start | bytes 145160 | tf_op jit(solution)/shard_map/ppermute | solution.py:21
  35.5 0.6 mul.331
  36.2 0.6 mul.363
  36.9 3.9 %collective-permute-done.5 = f32[2,6048]{1,0:T(2,128)S(1)} collective-permute-done((f32[2,6048]{1,0:T(2,128)S(1)}, f32[2,6048]{1,0:T(2,128)S(1)}, u32[]{:S(2)}, u32[]{:S(2)}) %collective-permute-start.5) | collective-permute-done | bytes 48416 | tf_op jit(solution)/shard_map/ppermute | solution.py:21
  40.8 2.7 %fusion.36 = f32[6048,132]{1,0:T(8,128)S(1)} fusion(f32[2,6048]{1,0:T(2,128)S(1)} %collective-permute-done.5, f32[2,6048]{1,0:T(2,128)S(1)} %collective-permute-done.4, s32[4]{0:T(128)S(1)} %get-tuple-element.82), kind=kOutput, calls=%fused_computation.113 | convolution fusion | flops 38344848 | bytes 3290128 | tf_op jit(solution)/shard_map/kr,kl->rl/dot_general | solution.py:47
  43.5 2.9 %convolution_add_fusion = f32[6048,132]{1,0:T(8,128)S(1)} fusion(f32[6048,132]{1,0:T(8,128)S(1)} %fusion.36, f32[6048,128]{1,0:T(8,128)S(1)} %bitcast.110, s32[128]{0:T(128)S(1)} %iota_add_fusion.2), kind=kOutput, calls=%fused_computation.1 | convolution fusion | flops 1227059328 | bytes 9483776 | tf_op jit(solution)/shard_map/dot_general | solution.py:47
  47.0 0.8 fusion.53
  47.8 0.8 fusion.21
  48.6 0.5 fusion.11
  49.3 1.7 %fusion.27 = (f32[1,34,18,130]{3,2,1,0:T(8,128)S(1)}, f32[1,34,18,130]{3,2,1,0:T(8,128)S(1)}, f32[1,34,18,130]{3,2,1,0:T(8,128)S(1)}) fusion(f32[35,19,131]{2,1,0:T(8,128)S(1)} %get-tuple-element.38, f32[35,19,131]{2,1,0:T(8,128)S(1)} %get-tuple-element.36, f32[35,19,131]{2,1,0:T(8,128)S(1)} %get-tuple-element.37), kind=kLoop, calls=%fused_computation.75 | loop fusion | flops 716040 | bytes 3818880 | tf_op jit(solution)/shard_map/stack | solution.py:75
  51.0 0.9 slice_add_fusion
  52.8 0.5 fusion.33
  53.3 0.6 copy-done.7
  53.9 0.8 fusion.12
  54.7 0.4 slice_bitcast_fusion.12
  55.2 0.9 copy-done.3
  56.1 1.5 %fusion.54 = (f32[32,16,128]{2,1,0:T(8,128)S(1)}, f32[1,32,16,128]{3,2,1,0:T(8,128)}, f32[32,16,128]{2,1,0:T(8,128)S(1)}, f32[32,16,128]{2,1,0:T(8,128)S(1)}, f3...) fusion(f32[33,17,129]{2,1,0:T(8,128)S(1)} %get-tuple-element.42, ...), kind=kLoop, calls=%fused_computation.166 | loop fusion | flops 589824 | bytes 4980736 | tf_op jit(solution)/shard_map/slice | solution.py:55
  57.6 2.8 %multiply_reduce_fusion.9 = (f32[4,32,16]{2,1,0:T(8,128)S(1)}, f32[4,32,16]{2,1,0:T(8,128)S(1)}, f32[4,32,16]{2,1,0:T(8,128)S(1)}, f32[4,32,16]{2,1,0:T(8,128)S(...) fusion(f32[32,16,128]{2,1,0:T(8,128)S(1)} %get-tuple-element.68, ...), kind=kLoop, calls=%fused_computation.38 | loop fusion | flops 5222400 | bytes 2705408 | tf_op jit(solution)/shard_map/reduce_sum | solution.py:117
  60.5 14.3 %multiply_reduce_fusion.1 = (f32[4,32,16,128]{3,2,1,0:T(8,128)S(1)}, f32[4,32,16,128]{3,2,1,0:T(8,128)S(1)}) fusion(f32[4,128]{1,0:T(4,128)S(1)} %copy-done.16, f32[4,128]{1,0:T(4,128)S(1)} %copy-done.13, f32[4,32,16,128]{3,2,1,0:T(8,128)S(1)} %pad_maximum_fusion, f32[4,1,32,16]{3,2,0,1:T(8,128)S(1)} %bitcast.115, f32[4,1,32,16]{3,2,0,1:T(8,128)S(1)} %bitcast.116, ...), kind=kOutput, calls=%fused_computation.3 | output fusion | flops 4751487 | bytes 3182592 | tf_op jit(solution)/shard_map/mul | solution.py:137
  75.1 1.0 copy-done.6
  76.0 1.6 %convolution_bitcast_fusion = f32[4,8,128]{2,1,0:T(8,128)} fusion(bf16[4,8,32,16]{2,1,3,0:T(8,128)(2,1)S(1)} %bitcast.114, f32[4,32,16,128]{3,2,1,0:T(8,128)S(1)} %multiply_add_fusion), kind=kOutput, calls=%fused_computation.28 | convolution fusion | flops 25165824 | bytes 1097728 | tf_op jit(solution)/shard_map/pxyl,pnxy->pnl/dot_general | solution.py:147
  77.6 1.6 %reshape.318 = f32[4,2,4,4,2,16]{5,4,3,2,1,0:T(2,128)} reshape(f32[4,8,128]{2,1,0:T(8,128)} %convolution_bitcast_fusion) | data formatting | bytes 32768 | tf_op jit(solution)/shard_map/reshape | solution.py:148
  79.2 0.7 fusion.55
  79.9 0.6 fusion.46
  80.5 1.4 %reshape_reshape.3 = f32[32,2,4]{1,0,2:T(8,128)} reshape(f32[4,16,2,2]{1,0,3,2:T(4,128)} %fusion.46) | data formatting | bytes 2048 | tf_op jit(solution)/shard_map/reshape;reshape | solution.py:151
  81.9 1.7 %copy.41 = f32[32,2,4]{2,1,0:T(2,128)} copy(f32[32,2,4]{1,0,2:T(8,128)} %reshape_reshape.3) | data formatting | bytes 2048 | tf_op jit(solution)/shard_map/reshape;reshape | solution.py:151
  83.7 8.9 %all-to-all-start = ((f32[32,2,4]{2,1,0:T(2,128)}), f32[32,2,4]{2,1,0:T(2,128)}, u32[]{:S(2)}, u32[]{:S(2)}) async-start(f32[32,2,4]{2,1,0:T(2,128)} %copy.41), calls=%async_computation | async-start | bytes 65536 | tf_op jit(solution)/shard_map/all_to_all | solution.py:152
  92.6 2.3 %slice_add_fusion.1 = f32[3,32,16,128]{3,2,1,0:T(8,128)} fusion(f32[3,34,18,130]{3,2,1,0:T(8,128)S(1)} %slice_add_fusion, f32[1,32,16,128]{3,2,1,0:T(8,128)} %get-tuple-element.64, f32[1,32,16,128]{3,2,1,0:T(8,128)} %get-tuple-element.65, f32[1,32,16,128]{3,2,1,0:T(8,128)} %get-tuple-element.61, f32[32,16,128]{2,1,0:T(8,128)} %get-tuple-element.50), kind=kLoop, calls=%fused_computation.94 | loop fusion | flops 786432 | bytes 2621440 | tf_op jit(solution)/shard_map/add | solution.py:107
  94.9 2.8 %slice.382 = f32[3,32,16,128]{3,2,1,0:T(8,128)} slice(f32[3,33,17,129]{3,2,1,0:T(8,128)} %copy-done.3), slice={[0:3], [1:33], [1:17], [1:129]} | slice | bytes 1572864 | tf_op jit(solution)/shard_map/slice | solution.py:55
  97.7 2.2 %all-to-all-done = f32[32,2,4]{2,1,0:T(2,128)} async-done(((f32[32,2,4]{2,1,0:T(2,128)}), f32[32,2,4]{2,1,0:T(2,128)}, u32[]{:S(2)}, u32[]{:S(2)}) %all-to-all-start) | async-done | bytes 1056 | tf_op jit(solution)/shard_map/all_to_all | solution.py:152
  99.9 0.8 reduce_sum.169
  100.8 0.7 copy.44
  (67 shorter events, 3.1 us)
Async XLA Ops:
  0.6 7.6 %copy-start = (bf16[4,2,4,256,64]{3,4,2,1,0:T(8,128)(2,1)S(1)}, bf16[4,2,4,256,64]{3,4,2,1,0:T(8,128)(2,1)}, u32[]{:S(2)}) copy-start(bf16[4,2,4,256,64]{3,4,2,1,0:T(8,128)(2,1)} %param.13) | copy-start | bytes 3145732
  0.6 8.4 %copy-start.8 = (f32[32,16,128]{2,1,0:T(8,128)S(1)}, f32[32,16,128]{2,1,0:T(8,128)}, u32[]{:S(2)}) copy-start(f32[32,16,128]{2,1,0:T(8,128)} %param.9) | copy-start | bytes 786436
  0.7 8.4 %copy-start.5 = (f32[3,32,16,128]{3,2,1,0:T(8,128)S(1)}, f32[3,32,16,128]{3,2,1,0:T(8,128)}, u32[]{:S(2)}) copy-start(f32[3,32,16,128]{3,2,1,0:T(8,128)} %param.7) | copy-start | bytes 2359300
  0.7 8.4 %copy-start.4 = (f32[3,32,16,128]{3,2,1,0:T(8,128)S(1)}, f32[3,32,16,128]{3,2,1,0:T(8,128)}, u32[]{:S(2)}) copy-start(f32[3,32,16,128]{3,2,1,0:T(8,128)} %param.8) | copy-start | bytes 2359300
  1.8 7.3 %collective-permute-start = (f32[7,2,16,128]{3,2,1,0:T(8,128)S(1)}, f32[7,2,16,128]{3,2,1,0:T(8,128)S(1)}, u32[]{:S(2)}, u32[]{:S(2)}) collective-permute-start(f32[7,2,16,128]{3,2,1,0:T(8,128)S(1)} %get-tuple-element.47), channel_id=1, source_target_pairs={{0,32},{32,64},{64,96},{96,128},{128,160},{160,192},{192,224},{1,3... | collective-permute-start | bytes 344072 | tf_op jit(solution)/shard_map/ppermute | solution.py:21
  3.5 5.5 %collective-permute-start.1 = (f32[7,2,16,128]{3,2,1,0:T(8,128)S(1)}, f32[7,2,16,128]{3,2,1,0:T(8,128)S(1)}, u32[]{:S(2)}, u32[]{:S(2)}) collective-permute-start(f32[7,2,16,128]{3,2,1,0:T(8,128)S(1)} %get-tuple-element.48), channel_id=1, source_target_pairs={{32,0},{64,32},{96,64},{128,96},{160,128},{192,160},{224,192},{33,... | collective-permute-start | bytes 344072 | tf_op jit(solution)/shard_map/ppermute | solution.py:21
  9.0 5.0 %copy-start.11 = (f32[7,2,16,128]{3,2,1,0:T(8,128)}, f32[7,2,16,128]{3,2,1,0:T(8,128)S(1)}, u32[]{:S(2)}) copy-start(f32[7,2,16,128]{3,2,1,0:T(8,128)S(1)} %collective-permute-done) | copy-start | bytes 344068
  9.1 5.0 %copy-start.12 = (f32[7,2,16,128]{3,2,1,0:T(8,128)}, f32[7,2,16,128]{3,2,1,0:T(8,128)S(1)}, u32[]{:S(2)}) copy-start(f32[7,2,16,128]{3,2,1,0:T(8,128)S(1)} %collective-permute-done.1) | copy-start | bytes 344068
  9.3 8.6 %collective-permute-start.2 = (f32[7,36,2,128]{3,2,1,0:T(2,128)S(1)}, f32[7,36,2,128]{3,2,1,0:T(2,128)S(1)}, u32[]{:S(2)}, u32[]{:S(2)}) collective-permute-start(f32[7,36,2,128]{3,2,1,0:T(2,128)S(1)} %get-tuple-element.45), channel_id=1, source_target_pairs={{0,8},{8,16},{16,24},{1,9},{9,17},{17,25},{2,10},{10,18},{18,26},{... | collective-permute-start | bytes 774152 | tf_op jit(solution)/shard_map/ppermute | solution.py:21
  12.8 9.8 %collective-permute-start.3 = (f32[7,36,2,128]{3,2,1,0:T(2,128)S(1)}, f32[7,36,2,128]{3,2,1,0:T(2,128)S(1)}, u32[]{:S(2)}, u32[]{:S(2)}) collective-permute-start(f32[7,36,2,128]{3,2,1,0:T(2,128)S(1)} %get-tuple-element.46), channel_id=1, source_target_pairs={{8,0},{16,8},{24,16},{9,1},{17,9},{25,17},{10,2},{18,10},{26,18},{... | collective-permute-start | bytes 774152 | tf_op jit(solution)/shard_map/ppermute | solution.py:21
  25.1 1.6 %copy-start.1 = (f32[7,36,24,128]{3,2,1,0:T(8,128)}, f32[7,36,24,128]{3,2,1,0:T(8,128)S(1)}, u32[]{:S(2)}) copy-start(f32[7,36,24,128]{3,2,1,0:T(8,128)S(1)} %select_maximum_fusion) | copy-start | bytes 9289732
  25.1 11.7 %copy-start.10 = (bf16[4,2,4,32,16]{3,4,2,1,0:T(8,128)(2,1)S(1)}, bf16[4,2,4,32,16]{3,4,2,1,0:T(8,128)(2,1)}, u32[]{:S(2)}) copy-start(bf16[4,2,4,32,16]{3,4,2,1,0:T(8,128)(2,1)} %constant_dynamic-slice_fusion) | copy-start | bytes 98308
  28.3 8.6 %collective-permute-start.4 = (f32[2,6048]{1,0:T(2,128)S(1)}, f32[2,6048]{1,0:T(2,128)S(1)}, u32[]{:S(2)}, u32[]{:S(2)}) collective-permute-start(f32[2,6048]{1,0:T(2,128)S(1)} %get-tuple-element.76), channel_id=1, source_target_pairs={{0,1},{1,2},{2,3},{3,4},{4,5},{5,6},{6,7},{8,9},{9,10},{10,11},{11... | collective-permute-start | bytes 145160 | tf_op jit(solution)/shard_map/ppermute | solution.py:21
  33.3 7.5 %collective-permute-start.5 = (f32[2,6048]{1,0:T(2,128)S(1)}, f32[2,6048]{1,0:T(2,128)S(1)}, u32[]{:S(2)}, u32[]{:S(2)}) collective-permute-start(f32[2,6048]{1,0:T(2,128)S(1)} %get-tuple-element.77), channel_id=1, source_target_pairs={{1,0},{2,1},{3,2},{4,3},{5,4},{6,5},{7,6},{9,8},{10,9},{11,10},{12... | collective-permute-start | bytes 145160 | tf_op jit(solution)/shard_map/ppermute | solution.py:21
  40.8 2.7 %copy-start.2 = (f32[7,36,24,128]{3,2,1,0:T(8,128)S(1)}, f32[7,36,24,128]{3,2,1,0:T(8,128)}, u32[]{:S(2)}) copy-start(f32[7,36,24,128]{3,2,1,0:T(8,128)} %copy-done.1) | copy-start | bytes 9289732
  52.8 1.1 %copy-start.7 = (f32[33,17,129]{2,1,0:T(8,128)S(1)}, f32[33,17,129]{2,1,0:T(8,128)}, u32[]{:S(2)}) copy-start(f32[33,17,129]{2,1,0:T(8,128)} %and_convert_fusion.1) | copy-start | bytes 868432
  54.7 1.4 %copy-start.3 = (f32[3,33,17,129]{3,2,1,0:T(8,128)}, f32[3,33,17,129]{3,2,1,0:T(8,128)S(1)}, u32[]{:S(2)}) copy-start(f32[3,33,17,129]{3,2,1,0:T(8,128)S(1)} %fusion.12) | copy-start | bytes 2605288
  55.1 2.5 %copy-start.13 = (f32[4,128]{1,0:T(4,128)S(1)}, f32[4,128]{1,0:T(4,128)}, u32[]{:S(2)}) copy-start(f32[4,128]{1,0:T(4,128)} %get-tuple-element.86) | copy-start | bytes 6148
  57.6 2.9 %copy-start.16 = (f32[4,128]{1,0:T(4,128)S(1)}, f32[4,128]{1,0:T(4,128)}, u32[]{:S(2)}) copy-start(f32[4,128]{1,0:T(4,128)} %get-tuple-element.87) | copy-start | bytes 6148
  60.5 14.3 %copy-start.9 = (f32[4,32,16,128]{3,2,1,0:T(8,128)S(1)}, f32[4,32,16,128]{3,2,1,0:T(8,128)}, u32[]{:S(2)}) copy-start(f32[4,32,16,128]{3,2,1,0:T(8,128)} %param.10) | copy-start | bytes 3145732
  60.5 14.3 %copy-start.14 = (f32[128]{0:T(128)S(1)}, f32[128]{0:T(128)}, u32[]{:S(2)}) copy-start(f32[128]{0:T(128)} %mul.331) | copy-start | bytes 1540
  60.5 14.3 %copy-start.15 = (f32[128]{0:T(128)S(1)}, f32[128]{0:T(128)}, u32[]{:S(2)}) copy-start(f32[128]{0:T(128)} %mul.363) | copy-start | bytes 1540
  75.1 1.0 copy-start.6
  83.7 16.3 %all-to-all-start = ((f32[32,2,4]{2,1,0:T(2,128)}), f32[32,2,4]{2,1,0:T(2,128)}, u32[]{:S(2)}, u32[]{:S(2)}) async-start(f32[32,2,4]{2,1,0:T(2,128)} %copy.41), calls=%async_computation | async-start | bytes 65536 | tf_op jit(solution)/shard_map/all_to_all | solution.py:152

commit v8 on v6

--- a/solution.py
+++ b/solution.py
@@ -3,6 +3,8 @@
 from jax import lax
 from jax.sharding import PartitionSpec as P
 from jax.experimental.layout import Layout, with_layout_constraint
+from jax.experimental import pallas as pl
+from jax.experimental.pallas import tpu as pltpu
 
 STEPS = 2
 NF = 16
@@ -87,6 +89,31 @@
     ).astype(jnp.float32)
 
 
+def port_kernel(onehot_ref, spread_ref, coef_ref, tangent_ref, dft_ref, weight_ref, out_ref, part_ref):
+    ports = dft_ref.shape[0]
+    comps = spread_ref.shape[0]
+    for p in range(ports):
+        pick = onehot_ref[p:p + 1, :]
+        acc = dft_ref[p]
+        for step in range(coef_ref.shape[0]):
+            inc = None
+            for c in range(comps):
+                plane = jnp.sum(tangent_ref[step * comps + c] * pick, axis=-1, keepdims=True)
+                term = plane * spread_ref[c:c + 1, :]
+                inc = term if inc is None else inc + term
+            acc = acc + inc * coef_ref[step:step + 1, :]
+        out_ref[p] = acc
+        flat = acc.reshape(-1, acc.shape[-1])
+        high = flat.astype(jnp.bfloat16)
+        rest = flat - high.astype(jnp.float32)
+        middle = rest.astype(jnp.bfloat16)
+        low = (rest - middle.astype(jnp.float32)).astype(jnp.bfloat16)
+        weight = weight_ref[p]
+        total = jnp.dot(weight, high, preferred_element_type=jnp.float32)
+        total = total + jnp.dot(weight, middle, preferred_element_type=jnp.float32)
+        part_ref[p] = total + jnp.dot(weight, low, preferred_element_type=jnp.float32)
+
+
 def per_device(e_field, h_field, inv_permittivity, dft_sums, omega, port_z, mode_profiles):
     cells = e_field.shape[1:]
     cells_x, cells_y, cells_z = cells
@@ -113,15 +140,15 @@
     lanes = dft_sums.shape[-1]
     lane_part = jnp.arange(lanes) // (lanes // 4)
     spread_of = (lane_part[None, :] == jnp.arange(4)[:, None]).astype(jnp.float32)
-    dft = dft_sums
-    for step, (e_now, h_now) in enumerate(((e1_here, h1_here), (e2, h2_here))):
-        tangent = pin(jnp.stack([e_now[0], e_now[1], h_now[0], h_now[1]]))
-        planes = jnp.sum(tangent[None] * onehot[:, None, None, None, :], axis=-1)
+    coefs = []
+    for step in range(STEPS):
         phase = omega * jnp.float32(step + 1)
-        trig = jnp.stack([jnp.cos(phase), jnp.sin(phase)])
-        coef = jnp.tile(trig.reshape(-1), 4)
-        spread = jnp.sum(planes[..., None] * spread_of[None, :, None, None, :], axis=1)
-        dft = pin(dft + spread * coef)
+        coefs.append(jnp.tile(jnp.stack([jnp.cos(phase), jnp.sin(phase)]).reshape(-1), 4))
+    coefs = jnp.stack(coefs)
+    tangent = pin(jnp.concatenate([
+        jnp.stack([e1_here[0], e1_here[1], h1_here[0], h1_here[1]]),
+        jnp.stack([e2[0], e2[1], h2_here[0], h2_here[1]]),
+    ]))
     groups = lax.axis_size(("gx", "gy"))
     owned = ports_here * NF // groups
     start_x = lax.axis_index("gx") * cells_x
@@ -129,8 +156,17 @@
     tile = lax.dynamic_slice(
         mode_profiles, (0, 0, 0, start_x, start_y), (ports_here, MODES, 4, cells_x, cells_y)
     )
-    weights = tile.reshape(ports_here, MODES * 4, cells_x, cells_y).astype(jnp.float32)
-    crossed = jnp.einsum("pxyl,pnxy->pnl", dft, weights, precision=lax.Precision.HIGHEST)
+    weights = tile.reshape(ports_here, MODES * 4, cells_x * cells_y)
+    vmem = pl.BlockSpec(memory_space=pltpu.VMEM)
+    dft, crossed = pl.pallas_call(
+        port_kernel,
+        out_shape=(
+            jax.ShapeDtypeStruct(dft_sums.shape, jnp.float32),
+            jax.ShapeDtypeStruct((ports_here, MODES * 4, lanes), jnp.float32),
+        ),
+        in_specs=[vmem] * 6,
+        out_specs=(vmem, vmem),
+    )(onehot, spread_of, coefs, tangent, dft_sums, weights)
     crossed = crossed.reshape(ports_here, MODES, 4, 4, 2, NF)
     diagonal = sum(crossed[:, :, c, c] for c in range(4))
     partial_sums = jnp.transpose(diagonal, (0, 3, 1, 2)).reshape(ports_here * NF, MODES * 2)

time: 80.7 us -> 83.8 us (1.038)
  Pallas kernels: 0 us -> 5.14 us
  starting transfers between devices: 24.8 us -> 23.7 us
  matrix products: 8.01 us -> 7.09 us
    pallas_call x0 -> x1, Pallas kernels: none -> 5.14 us  [per_device(): pl.pallas_call(port_kernel, out_shape=(jax.ShapeDtypeStruct(dft_sums.shap...]
    mul x2 -> x0, other arithmetic: 2.66 us -> none  [per_device(): planes[..., None] * spread_of[None, :, None, None, :]]
    concatenate x0 -> x1, other arithmetic: none -> 1.56 us  [per_device(): jnp.concatenate([jnp.stack([e1_here[0], e1_here[1], h1_here[0], h1_here[1...]
    all_to_all x1, starting transfers between devices: 9.84 us -> 8.77 us  [per_device(): lax.all_to_all(pieces, ('gx', 'gy'), 0, 0, tiled=False)]
    unnamed x28 -> x24, local copies, waits for them, and re-layouts: 3.98 us -> 2.99 us
    dot_general x1 -> x0, matrix products: 0.97 us -> none  [per_device(): jnp.einsum('pxyl,pnxy->pnl', dft, weights, precision=lax.Precision.HIGHEST)]
    reshape x0 -> x1, local copies, waits for them, and re-layouts: none -> 0.93 us  [per_device(): weights = tile.reshape(ports_here, MODES * 4, cells_x * cells_y)]
  transfers between devices with their start and end apart: 7 -> 7, of which waited for: 4 -> 4; matrix products, arithmetic and copies ran while one was open for 7% -> 9% of each run, Pallas kernels for 0% -> 0%
where the time goes in v8:
time: 83.8 us; the launch traced here: 83 us
  starting transfers between devices  23.7 us (28%)
  waiting for transfers between devices  18.7 us (22%)
  other arithmetic  15.8 us (19%)
  local copies, waits for them, and re-layouts  11.5 us (14%)
  matrix products  7.09 us (8%)
  Pallas kernels  5.14 us (6%)
  between operations  1.07 us (1%)
    ppermute x6, starting transfers between devices, shifted(): lax.ppermute(value, axis, [(source, source + steps) for source in range(f...  15 us
    ppermute x6, waiting for transfers between devices, shifted(): lax.ppermute(value, axis, [(source, source + steps) for source in range(f...  12.5 us
    all_to_all x1, starting transfers between devices, per_device(): lax.all_to_all(pieces, ('gx', 'gy'), 0, 0, tiled=False)  8.77 us
    all_to_all x1, waiting for transfers between devices, per_device(): lax.all_to_all(pieces, ('gx', 'gy'), 0, 0, tiled=False)  6.23 us
    pallas_call x1, Pallas kernels, per_device(): pl.pallas_call(port_kernel, out_shape=(jax.ShapeDtypeStruct(dft_sums.shap...  5.14 us
    another operation x4, other arithmetic, curl(): jnp.stack([d(vz, 1) - d(vy, 2), d(vx, 2) - d(vz, 0), d(vy, 0) - d(vx, 1)])  3.35 us
    unnamed x24, local copies, waits for them, and re-layouts  2.99 us
    dot_general x1, matrix products, widen_lanes(): jnp.dot(flat, move, precision=lax.Precision.HIGHEST)  2.9 us
  transfers between devices with their start and end apart: 7, of which 4 were waited for; matrix products, arithmetic and copies ran while one was open for 9% of the time, Pallas kernels for 0%

profile of v8, /device:TPU:96, one launch (start us, length us, event | category | flops | bytes accessed | tf_op | source)
XLA Modules:
  0.0 83.0 jit_solution(13835552382190563536)
XLA Ops:
  0.7 1.1 %pad_maximum_fusion.8 = (f32[7,2,16,128]{3,2,1,0:T(8,128)S(1)}, f32[7,2,16,128]{3,2,1,0:T(8,128)S(1)}) fusion(f32[1,32,16,128]{3,2,1,0:T(8,128)} %bitcast.77, f32[3,32,16,128]{3,2,1,0:T(8,128)} %param.8, f32[3,32,16,128]{3,2,1,0:T(8,128)} %param.7), kind=kLoop, calls=%fused_computation.97 | loop fusion | flops 114688 | bytes 2064384 | tf_op jit(solution)/shard_map/slice | solution.py:29
  1.8 1.7 %collective-permute-start = (f32[7,2,16,128]{3,2,1,0:T(8,128)S(1)}, f32[7,2,16,128]{3,2,1,0:T(8,128)S(1)}, u32[]{:S(2)}, u32[]{:S(2)}) collective-permute-start(f32[7,2,16,128]{3,2,1,0:T(8,128)S(1)} %get-tuple-element.35), channel_id=1, source_target_pairs={{0,32},{32,64},{64,96},{96,128},{128,160},{160,192},{192,224},{1,3... | collective-permute-start | bytes 344072 | tf_op jit(solution)/shard_map/ppermute | solution.py:23
  3.5 1.3 %collective-permute-start.1 = (f32[7,2,16,128]{3,2,1,0:T(8,128)S(1)}, f32[7,2,16,128]{3,2,1,0:T(8,128)S(1)}, u32[]{:S(2)}, u32[]{:S(2)}) collective-permute-start(f32[7,2,16,128]{3,2,1,0:T(8,128)S(1)} %get-tuple-element.36), channel_id=1, source_target_pairs={{32,0},{64,32},{96,64},{128,96},{160,128},{192,160},{224,192},{33,... | collective-permute-start | bytes 344072 | tf_op jit(solution)/shard_map/ppermute | solution.py:23
  4.9 0.7 cosine_bitcast_fusion.1
  6.0 0.7 broadcast_subtract_fusion
  6.8 1.1 %and_convert_fusion.1 = f32[33,17,129]{2,1,0:T(8,128)} fusion(pred[129]{0:T(512)(128)(4,1)S(1)} %compare_and_fusion, pred[33,17]{1,0:T(8,128)(4,1)S(1)} %broadcast_and_fusion), kind=kLoop, calls=%fused_computation.73 | loop fusion | flops 144738 | bytes 290166 | tf_op jit(solution)/shard_map/convert_element_type | solution.py:89
  7.9 0.6 pad_maximum_fusion.11.coef_ref
  8.4 0.7 fusion.43
  9.2 0.8 constant_dynamic-slice_fusion
  10.2 3.5 %collective-permute-start.2 = (f32[7,36,2,128]{3,2,1,0:T(2,128)S(1)}, f32[7,36,2,128]{3,2,1,0:T(2,128)S(1)}, u32[]{:S(2)}, u32[]{:S(2)}) collective-permute-start(f32[7,36,2,128]{3,2,1,0:T(2,128)S(1)} %get-tuple-element.33), channel_id=1, source_target_pairs={{0,8},{8,16},{16,24},{1,9},{9,17},{17,25},{2,10},{10,18},{18,26},{... | collective-permute-start | bytes 774152 | tf_op jit(solution)/shard_map/ppermute | solution.py:23
  13.7 1.3 %collective-permute-start.3 = (f32[7,36,2,128]{3,2,1,0:T(2,128)S(1)}, f32[7,36,2,128]{3,2,1,0:T(2,128)S(1)}, u32[]{:S(2)}, u32[]{:S(2)}) collective-permute-start(f32[7,36,2,128]{3,2,1,0:T(2,128)S(1)} %get-tuple-element.34), channel_id=1, source_target_pairs={{8,0},{16,8},{24,16},{9,1},{17,9},{25,17},{10,2},{18,10},{26,18},{... | collective-permute-start | bytes 774152 | tf_op jit(solution)/shard_map/ppermute | solution.py:23
  15.2 3.6 %collective-permute-done.2 = f32[7,36,2,128]{3,2,1,0:T(2,128)S(1)} collective-permute-done((f32[7,36,2,128]{3,2,1,0:T(2,128)S(1)}, f32[7,36,2,128]{3,2,1,0:T(2,128)S(1)}, u32[]{:S(2)}, u32[]{:S(2)}) %collective-permute-start.2) | collective-permute-done | bytes 258080 | tf_op jit(solution)/shard_map/ppermute | solution.py:23
  18.8 4.7 %collective-permute-done.3 = f32[7,36,2,128]{3,2,1,0:T(2,128)S(1)} collective-permute-done((f32[7,36,2,128]{3,2,1,0:T(2,128)S(1)}, f32[7,36,2,128]{3,2,1,0:T(2,128)S(1)}, u32[]{:S(2)}, u32[]{:S(2)}) %collective-permute-start.3) | collective-permute-done | bytes 258080 | tf_op jit(solution)/shard_map/ppermute | solution.py:23
  23.5 2.5 %select_maximum_fusion = f32[7,36,24,128]{3,2,1,0:T(8,128)S(1)} fusion(f32[7,36,2,128]{3,2,1,0:T(2,128)S(1)} %collective-permute-done.3, f32[7,36,2,128]{3,2,1,0:T(2,128)S(1)} %collective-permute-done.2, f32[7,2,16,128]{3,2,1,0:T(8,128)} %copy-done.10, f32[7,2,16,128]{3,2,1,0:T(8,128)} %copy-done.9, f32[1,32,16,128]{3,2,1,0:T(8,128)} %bitcast.78, ...), kind=kLoop, calls=%fused_computation.1 | loop fusion | flops 10838016 | bytes 5677056 | tf_op jit(solution)/shard_map/concatenate | solution.py:32
  26.0 1.6 %copy-done.1 = f32[7,36,24,128]{3,2,1,0:T(8,128)} copy-done((f32[7,36,24,128]{3,2,1,0:T(8,128)}, f32[7,36,24,128]{3,2,1,0:T(8,128)S(1)}, u32[]{:S(2)}) %copy-start.1) | copy-done | bytes 3096600
  27.6 1.5 %fusion.42 = f32[4,6048]{1,0:T(4,128)S(1)} fusion(f32[6048,128]{1,0:T(8,128)S(1)} %bitcast.75, s32[4]{0:T(128)S(1)} %get-tuple-element.60), kind=kOutput, calls=%fused_computation.114 | convolution fusion | flops 37159424 | bytes 3193360 | tf_op jit(solution)/shard_map/kz,rz->kr/dot_general | solution.py:41
  29.2 5.0 %collective-permute-start.4 = (f32[2,6048]{1,0:T(2,128)S(1)}, f32[2,6048]{1,0:T(2,128)S(1)}, u32[]{:S(2)}, u32[]{:S(2)}) collective-permute-start(f32[2,6048]{1,0:T(2,128)S(1)} %get-tuple-element.53), channel_id=1, source_target_pairs={{0,1},{1,2},{2,3},{3,4},{4,5},{5,6},{6,7},{8,9},{9,10},{10,11},{11... | collective-permute-start | bytes 145160 | tf_op jit(solution)/shard_map/ppermute | solution.py:23
  34.2 2.1 %collective-permute-start.5 = (f32[2,6048]{1,0:T(2,128)S(1)}, f32[2,6048]{1,0:T(2,128)S(1)}, u32[]{:S(2)}, u32[]{:S(2)}) collective-permute-start(f32[2,6048]{1,0:T(2,128)S(1)} %get-tuple-element.54), channel_id=1, source_target_pairs={{1,0},{2,1},{3,2},{4,3},{5,4},{6,5},{7,6},{9,8},{10,9},{11,10},{12... | collective-permute-start | bytes 145160 | tf_op jit(solution)/shard_map/ppermute | solution.py:23
  36.5 0.9 %reshape.163.weight_ref = bf16[4,8,512]{2,1,0:T(8,128)(2,1)} reshape(bf16[4,2,4,32,16]{4,3,2,1,0:T(8,128)(2,1)S(1)} %copy.19) | data formatting | bytes 65536 | tf_op jit(solution)/shard_map/reshape | solution.py:159
  37.5 4.2 %collective-permute-done.5 = f32[2,6048]{1,0:T(2,128)S(1)} collective-permute-done((f32[2,6048]{1,0:T(2,128)S(1)}, f32[2,6048]{1,0:T(2,128)S(1)}, u32[]{:S(2)}, u32[]{:S(2)}) %collective-permute-start.5) | collective-permute-done | bytes 48416 | tf_op jit(solution)/shard_map/ppermute | solution.py:23
  41.7 2.7 %fusion.35 = f32[6048,132]{1,0:T(8,128)S(1)} fusion(f32[2,6048]{1,0:T(2,128)S(1)} %collective-permute-done.5, f32[2,6048]{1,0:T(2,128)S(1)} %collective-permute-done.4, s32[4]{0:T(128)S(1)} %get-tuple-element.59), kind=kOutput, calls=%fused_computation.98 | convolution fusion | flops 38344848 | bytes 3290128 | tf_op jit(solution)/shard_map/kr,kl->rl/dot_general | solution.py:49
  44.4 2.9 %convolution_add_fusion = f32[6048,132]{1,0:T(8,128)S(1)} fusion(f32[6048,132]{1,0:T(8,128)S(1)} %fusion.35, f32[6048,128]{1,0:T(8,128)S(1)} %bitcast.76, s32[128]{0:T(128)S(1)} %iota_add_fusion.2), kind=kOutput, calls=%fused_computation | convolution fusion | flops 1227059328 | bytes 9483776 | tf_op jit(solution)/shard_map/dot_general | solution.py:49
  47.3 0.2 slice_bitcast_fusion.3
  47.6 0.3 slice_multiply_fusion
  48.0 0.6 fusion.16
  48.6 0.5 fusion.9
  49.1 0.2 slice_bitcast_fusion.6
  49.3 1.7 %fusion.22 = (f32[1,34,18,130]{3,2,1,0:T(8,128)S(1)}, f32[1,34,18,130]{3,2,1,0:T(8,128)S(1)}, f32[1,34,18,130]{3,2,1,0:T(8,128)S(1)}) fusion(f32[35,19,131]{2,1,0:T(8,128)S(1)} %get-tuple-element.26, f32[35,19,131]{2,1,0:T(8,128)S(1)} %get-tuple-element.24, f32[35,19,131]{2,1,0:T(8,128)S(1)} %get-tuple-element.25), kind=kLoop, calls=%fused_computation.55 | loop fusion | flops 716040 | bytes 3818880 | tf_op jit(solution)/shard_map/stack | solution.py:77
  50.9 0.9 %slice_add_fusion = f32[3,34,18,130]{3,2,1,0:T(8,128)S(1)} fusion(f32[7,36,24,132]{3,2,1,0:T(8,128)S(1)} %bitcast.74, f32[1,34,18,130]{3,2,1,0:T(8,128)S(1)} %get-tuple-element.42, f32[1,34,18,130]{3,2,1,0:T(8,128)S(1)} %get-tuple-element.41, f32[1,34,18,130]{3,2,1,0:T(8,128)S(1)} %get-tuple-element.40, f32[34,18,130]{2,1,0:T(8,128)S(1)} %slice_multiply_fusion), kind=kLoop, calls=%fused_computation.16 | loop fusion | flops 954720 | bytes 3182400 | tf_op jit(solution)/shard_map/add | solution.py:131
  51.9 0.2 slice_bitcast_fusion.9
  52.1 0.5 fusion.28
  52.7 0.6 copy-done.5
  53.2 0.8 fusion.10
  54.0 0.2 slice_bitcast_fusion.12
  54.2 0.2 slice.376
  54.4 0.4 slice.373
  54.8 0.2 slice.374
  55.1 0.6 fusion.34
  55.7 0.3 slice_add_fusion.1
  56.0 1.6 %pad_maximum_fusion.tangent_ref = f32[8,32,16,128]{3,2,1,0:T(8,128)} fusion(f32[2,32,16,128]{3,2,1,0:T(8,128)S(1)} %slice.376, f32[2,32,16,128]{3,2,1,0:T(8,128)S(1)} %slice.375, f32[2,32,16,128]{3,2,1,0:T(8,128)S(1)} %slice.374, f32[2,32,16,128]{3,2,1,0:T(8,128)S(1)} %slice.373), kind=kLoop, calls=%fused_computation.21 | loop fusion | flops 1572864 | bytes 4194304 | tf_op jit(solution)/shard_map/concatenate | solution.py:148
  57.6 5.1 %shard_map.102 = (f32[4,32,16,128]{3,2,1,0:T(8,128)}, f32[4,8,128]{2,1,0:T(8,128)}) custom-call(f32[4,128]{1,0:T(4,128)} %get-tuple-element.65.onehot_ref, f32[4,128]{1,0:T(4,128)} %get-tuple-element.66.spread_ref, f32[2,128]{1,0:T(2,128)} %pad_maximum_fusion.11.coef_ref, f32[8,32,16,128]{3,2,1,0:T(8,128)} %pad_maximum_fusion.tangent_ref, ...), custom_call_target="tpu_custom_call" | custom-call | tf_op jit(solution)/shard_map/pallas_call | solution.py:161
  62.7 1.6 %reshape.164 = f32[4,2,4,4,2,16]{5,4,3,2,1,0:T(2,128)} reshape(f32[4,8,128]{2,1,0:T(8,128)} %get-tuple-element.7) | data formatting | bytes 32768 | tf_op jit(solution)/shard_map/reshape | solution.py:170
  64.3 0.7 fusion.47
  65.2 0.9 %copy.24 = f32[32,2,4]{2,1,0:T(2,128)} copy(f32[32,2,4]{1,0,2:T(8,128)S(1)} %reshape_reshape.3) | data formatting | bytes 2048 | tf_op jit(solution)/shard_map/reshape;reshape | solution.py:173
  66.1 8.8 %all-to-all-start = ((f32[32,2,4]{2,1,0:T(2,128)}), f32[32,2,4]{2,1,0:T(2,128)S(1)}, u32[]{:S(2)}, u32[]{:S(2)}) async-start(f32[32,2,4]{2,1,0:T(2,128)} %copy.24), calls=%async_computation | async-start | bytes 65536 | tf_op jit(solution)/shard_map/all_to_all | solution.py:174
  74.9 1.2 %slice.372 = f32[3,32,16,128]{3,2,1,0:T(8,128)} slice(f32[3,33,17,129]{3,2,1,0:T(8,128)S(1)} %fusion.10), slice={[0:3], [1:33], [1:17], [1:129]} | slice | bytes 1572864 | tf_op jit(solution)/shard_map/slice | solution.py:57
  76.0 6.2 %all-to-all-done = f32[32,2,4]{2,1,0:T(2,128)S(1)} async-done(((f32[32,2,4]{2,1,0:T(2,128)}), f32[32,2,4]{2,1,0:T(2,128)S(1)}, u32[]{:S(2)}, u32[]{:S(2)}) %all-to-all-start) | async-done | bytes 1056 | tf_op jit(solution)/shard_map/all_to_all | solution.py:174
  82.4 0.7 copy.27
  (53 shorter events, 1.7 us)
Async XLA Ops:
  0.6 8.6 %copy-start = (bf16[4,2,4,256,64]{3,4,2,1,0:T(8,128)(2,1)S(1)}, bf16[4,2,4,256,64]{3,4,2,1,0:T(8,128)(2,1)}, u32[]{:S(2)}) copy-start(bf16[4,2,4,256,64]{3,4,2,1,0:T(8,128)(2,1)} %param.13) | copy-start | bytes 3145732
  0.6 9.3 %copy-start.6 = (f32[32,16,128]{2,1,0:T(8,128)S(1)}, f32[32,16,128]{2,1,0:T(8,128)}, u32[]{:S(2)}) copy-start(f32[32,16,128]{2,1,0:T(8,128)} %param.9) | copy-start | bytes 786436
  0.7 9.3 %copy-start.4 = (f32[3,32,16,128]{3,2,1,0:T(8,128)S(1)}, f32[3,32,16,128]{3,2,1,0:T(8,128)}, u32[]{:S(2)}) copy-start(f32[3,32,16,128]{3,2,1,0:T(8,128)} %param.7) | copy-start | bytes 2359300
  0.7 9.3 %copy-start.3 = (f32[3,32,16,128]{3,2,1,0:T(8,128)S(1)}, f32[3,32,16,128]{3,2,1,0:T(8,128)}, u32[]{:S(2)}) copy-start(f32[3,32,16,128]{3,2,1,0:T(8,128)} %param.8) | copy-start | bytes 2359300
  1.8 8.2 %collective-permute-start = (f32[7,2,16,128]{3,2,1,0:T(8,128)S(1)}, f32[7,2,16,128]{3,2,1,0:T(8,128)S(1)}, u32[]{:S(2)}, u32[]{:S(2)}) collective-permute-start(f32[7,2,16,128]{3,2,1,0:T(8,128)S(1)} %get-tuple-element.35), channel_id=1, source_target_pairs={{0,32},{32,64},{64,96},{96,128},{128,160},{160,192},{192,224},{1,3... | collective-permute-start | bytes 344072 | tf_op jit(solution)/shard_map/ppermute | solution.py:23
  3.5 6.5 %collective-permute-start.1 = (f32[7,2,16,128]{3,2,1,0:T(8,128)S(1)}, f32[7,2,16,128]{3,2,1,0:T(8,128)S(1)}, u32[]{:S(2)}, u32[]{:S(2)}) collective-permute-start(f32[7,2,16,128]{3,2,1,0:T(8,128)S(1)} %get-tuple-element.36), channel_id=1, source_target_pairs={{32,0},{64,32},{96,64},{128,96},{160,128},{192,160},{224,192},{33,... | collective-permute-start | bytes 344072 | tf_op jit(solution)/shard_map/ppermute | solution.py:23
  10.0 5.0 %copy-start.9 = (f32[7,2,16,128]{3,2,1,0:T(8,128)}, f32[7,2,16,128]{3,2,1,0:T(8,128)S(1)}, u32[]{:S(2)}) copy-start(f32[7,2,16,128]{3,2,1,0:T(8,128)S(1)} %collective-permute-done) | copy-start | bytes 344068
  10.0 5.0 %copy-start.10 = (f32[7,2,16,128]{3,2,1,0:T(8,128)}, f32[7,2,16,128]{3,2,1,0:T(8,128)S(1)}, u32[]{:S(2)}) copy-start(f32[7,2,16,128]{3,2,1,0:T(8,128)S(1)} %collective-permute-done.1) | copy-start | bytes 344068
  10.2 8.6 %collective-permute-start.2 = (f32[7,36,2,128]{3,2,1,0:T(2,128)S(1)}, f32[7,36,2,128]{3,2,1,0:T(2,128)S(1)}, u32[]{:S(2)}, u32[]{:S(2)}) collective-permute-start(f32[7,36,2,128]{3,2,1,0:T(2,128)S(1)} %get-tuple-element.33), channel_id=1, source_target_pairs={{0,8},{8,16},{16,24},{1,9},{9,17},{17,25},{2,10},{10,18},{18,26},{... | collective-permute-start | bytes 774152 | tf_op jit(solution)/shard_map/ppermute | solution.py:23
  13.7 9.8 %collective-permute-start.3 = (f32[7,36,2,128]{3,2,1,0:T(2,128)S(1)}, f32[7,36,2,128]{3,2,1,0:T(2,128)S(1)}, u32[]{:S(2)}, u32[]{:S(2)}) collective-permute-start(f32[7,36,2,128]{3,2,1,0:T(2,128)S(1)} %get-tuple-element.34), channel_id=1, source_target_pairs={{8,0},{16,8},{24,16},{9,1},{17,9},{25,17},{10,2},{18,10},{26,18},{... | collective-permute-start | bytes 774152 | tf_op jit(solution)/shard_map/ppermute | solution.py:23
  26.0 1.6 %copy-start.1 = (f32[7,36,24,128]{3,2,1,0:T(8,128)}, f32[7,36,24,128]{3,2,1,0:T(8,128)S(1)}, u32[]{:S(2)}) copy-start(f32[7,36,24,128]{3,2,1,0:T(8,128)S(1)} %select_maximum_fusion) | copy-start | bytes 9289732
  26.0 10.4 %copy-start.8 = (bf16[4,2,4,32,16]{3,4,2,1,0:T(8,128)(2,1)S(1)}, bf16[4,2,4,32,16]{3,4,2,1,0:T(8,128)(2,1)}, u32[]{:S(2)}) copy-start(bf16[4,2,4,32,16]{3,4,2,1,0:T(8,128)(2,1)} %constant_dynamic-slice_fusion) | copy-start | bytes 98308
  29.2 8.3 %collective-permute-start.4 = (f32[2,6048]{1,0:T(2,128)S(1)}, f32[2,6048]{1,0:T(2,128)S(1)}, u32[]{:S(2)}, u32[]{:S(2)}) collective-permute-start(f32[2,6048]{1,0:T(2,128)S(1)} %get-tuple-element.53), channel_id=1, source_target_pairs={{0,1},{1,2},{2,3},{3,4},{4,5},{5,6},{6,7},{8,9},{9,10},{10,11},{11... | collective-permute-start | bytes 145160 | tf_op jit(solution)/shard_map/ppermute | solution.py:23
  34.2 7.5 %collective-permute-start.5 = (f32[2,6048]{1,0:T(2,128)S(1)}, f32[2,6048]{1,0:T(2,128)S(1)}, u32[]{:S(2)}, u32[]{:S(2)}) collective-permute-start(f32[2,6048]{1,0:T(2,128)S(1)} %get-tuple-element.54), channel_id=1, source_target_pairs={{1,0},{2,1},{3,2},{4,3},{5,4},{6,5},{7,6},{9,8},{10,9},{11,10},{12... | collective-permute-start | bytes 145160 | tf_op jit(solution)/shard_map/ppermute | solution.py:23
  41.7 2.7 %copy-start.2 = (f32[7,36,24,128]{3,2,1,0:T(8,128)S(1)}, f32[7,36,24,128]{3,2,1,0:T(8,128)}, u32[]{:S(2)}) copy-start(f32[7,36,24,128]{3,2,1,0:T(8,128)} %copy-done.1) | copy-start | bytes 9289732
  52.1 1.1 %copy-start.5 = (f32[33,17,129]{2,1,0:T(8,128)S(1)}, f32[33,17,129]{2,1,0:T(8,128)}, u32[]{:S(2)}) copy-start(f32[33,17,129]{2,1,0:T(8,128)} %and_convert_fusion.1) | copy-start | bytes 868432
  56.0 1.6 %copy-start.7 = (f32[3,32,16,128]{3,2,1,0:T(8,128)}, f32[3,32,16,128]{3,2,1,0:T(8,128)S(1)}, u32[]{:S(2)}) copy-start(f32[3,32,16,128]{3,2,1,0:T(8,128)S(1)} %slice_add_fusion.1) | copy-start | bytes 2359300
  66.1 16.2 %all-to-all-start = ((f32[32,2,4]{2,1,0:T(2,128)}), f32[32,2,4]{2,1,0:T(2,128)S(1)}, u32[]{:S(2)}, u32[]{:S(2)}) async-start(f32[32,2,4]{2,1,0:T(2,128)} %copy.24), calls=%async_computation | async-start | bytes 65536 | tf_op jit(solution)/shard_map/all_to_all | solution.py:174

commit v9 on v6

--- a/solution.py
+++ b/solution.py
@@ -76,15 +76,13 @@
 
 
 def inside(origin, size, cells):
-    masks = []
+    keep = None
     for dim, axis in enumerate(AXES):
-        count = lax.axis_size(axis)
         first = lax.axis_index(axis) * cells[dim] + origin
-        where = first + jnp.arange(size[dim])
-        masks.append((where >= 0) & (where < count * cells[dim]))
-    return (
-        masks[0][:, None, None] & masks[1][None, :, None] & masks[2][None, None, :]
-    ).astype(jnp.float32)
+        where = lax.broadcasted_iota(jnp.int32, size, dim) + first
+        test = (where >= 0) & (where < lax.axis_size(axis) * cells[dim])
+        keep = test if keep is None else keep & test
+    return keep
 
 
 def per_device(e_field, h_field, inv_permittivity, dft_sums, omega, port_z, mode_profiles):
@@ -100,10 +98,10 @@
     e0, h0, inv = stack[0:3], stack[3:6], stack[6]
     n = lambda k: tuple(c + k for c in cells)
     h1 = box(h0, (0, 0, 0), n(3)) - 0.5 * curl(e0, (0, 0, 0), n(3), 1)
-    h1 = pin(h1 * inside(-2, n(3), cells))
+    h1 = pin(jnp.where(inside(-2, n(3), cells), h1, 0.0))
     e1 = pin(box(e0, (1, 1, 1), n(2)) + 0.5 * box(inv, (1, 1, 1), n(2)) * curl(h1, (1, 1, 1), n(2), -1))
     h2 = box(h1, (1, 1, 1), n(1)) - 0.5 * curl(e1, (0, 0, 0), n(1), 1)
-    h2 = pin(h2 * inside(-1, n(1), cells))
+    h2 = pin(jnp.where(inside(-1, n(1), cells), h2, 0.0))
     e2 = pin(box(e1, (1, 1, 1), n(0)) + 0.5 * box(inv, (2, 2, 2), n(0)) * curl(h2, (1, 1, 1), n(0), -1))
     e1_here = box(e1, (1, 1, 1), n(0))
     h1_here = box(h1, (2, 2, 2), n(0))

time: 80.7 us -> 81.1 us (level)
  starting transfers between devices: 24.8 us -> 26 us
  local copies, waits for them, and re-layouts: 10.8 us -> 9.91 us
    slice x2, other arithmetic: 1.25 us -> 2.86 us  [widen(): high = lax.slice_in_dim(stack, count - HALO, count, axis=dim)]
    select_n x0 -> x2, other arithmetic: none -> 1.29 us  [the longest x1 0.78 us: per_device(): h2 = pin(jnp.where(inside(-1, n(1), cells), h2, 0.0))]
    convert_element_type x2 -> x0, other arithmetic: 1.25 us -> none  [inside(): return (masks[0][:, None, None] & masks[1][None, :, None] & masks[2][None...]
    all_to_all x1, starting transfers between devices: 9.84 us -> 11.1 us  [per_device(): lax.all_to_all(pieces, ('gx', 'gy'), 0, 0, tiled=False)]
    mul x2 -> x0, other arithmetic: 1.2 us -> none  [the longest x1 0.78 us: per_device(): h2 = pin(h2 * inside(-1, n(1), cells))]
    concatenate x1, other arithmetic: 2.46 us -> 1.5 us  [widen(): return jnp.concatenate([from_below, stack, from_above], axis=dim)]
    and x8, other arithmetic: 0.21 us -> 1.11 us  [the longest x2 1.05 us: inside(): keep = test if keep is None else keep & test]
    unnamed x28 -> x22, local copies, waits for them, and re-layouts: 3.98 us -> 3.76 us
  transfers between devices with their start and end apart: 7 -> 7, of which waited for: 4 -> 5; matrix products, arithmetic and copies ran while one was open for 7% -> 5% of each run, Pallas kernels for 0% -> 0%
where the time goes in v9:
time: 81.1 us; the launch traced here: 80.4 us
  starting transfers between devices  26 us (32%)
  waiting for transfers between devices  18.7 us (23%)
  other arithmetic  16.7 us (21%)
  local copies, waits for them, and re-layouts  9.91 us (12%)
  matrix products  8.01 us (10%)
  between operations  1.08 us (1%)
    ppermute x6, starting transfers between devices, shifted(): lax.ppermute(value, axis, [(source, source + steps) for source in range(f...  15 us
    ppermute x6, waiting for transfers between devices, shifted(): lax.ppermute(value, axis, [(source, source + steps) for source in range(f...  12.5 us
    all_to_all x1, starting transfers between devices, per_device(): lax.all_to_all(pieces, ('gx', 'gy'), 0, 0, tiled=False)  11.1 us
    all_to_all x1, waiting for transfers between devices, per_device(): lax.all_to_all(pieces, ('gx', 'gy'), 0, 0, tiled=False)  6.23 us
    unnamed x22, local copies, waits for them, and re-layouts  3.76 us
    another operation x4, other arithmetic, curl(): jnp.stack([d(vz, 1) - d(vy, 2), d(vx, 2) - d(vz, 0), d(vy, 0) - d(vx, 1)])  3.58 us
    slice x2, other arithmetic, widen(): high = lax.slice_in_dim(stack, count - HALO, count, axis=dim)  2.86 us
    dot_general x1, matrix products, widen_lanes(): jnp.dot(flat, move, precision=lax.Precision.HIGHEST)  2.85 us
  transfers between devices with their start and end apart: 7, of which 5 were waited for; matrix products, arithmetic and copies ran while one was open for 5% of the time, Pallas kernels for 0%

profile of v9, /device:TPU:96, one launch (start us, length us, event | category | flops | bytes accessed | tf_op | source)
XLA Modules:
  0.0 80.4 jit_solution(7377136872156267366)
XLA Ops:
  0.7 1.7 %pad_maximum_fusion.9 = (f32[7,2,16,128]{3,2,1,0:T(8,128)}, f32[7,2,16,128]{3,2,1,0:T(8,128)S(1)}) fusion(f32[1,32,16,128]{3,2,1,0:T(8,128)} %bitcast.80, f32[3,32,16,128]{3,2,1,0:T(8,128)} %param.8, f32[3,32,16,128]{3,2,1,0:T(8,128)} %param.7), kind=kLoop, calls=%fused_computation.113 | loop fusion | flops 114688 | bytes 2064384 | tf_op jit(solution)/shard_map/slice | solution.py:27
  2.4 1.7 %collective-permute-start = (f32[7,2,16,128]{3,2,1,0:T(8,128)}, f32[7,2,16,128]{3,2,1,0:T(8,128)S(1)}, u32[]{:S(2)}, u32[]{:S(2)}) collective-permute-start(f32[7,2,16,128]{3,2,1,0:T(8,128)} %get-tuple-element.37), channel_id=1, source_target_pairs={{0,32},{32,64},{64,96},{96,128},{128,160},{160,192},{192,224},{1,3... | collective-permute-start | bytes 344072 | tf_op jit(solution)/shard_map/ppermute | solution.py:21
  4.1 1.3 %collective-permute-start.1 = (f32[7,2,16,128]{3,2,1,0:T(8,128)S(1)}, f32[7,2,16,128]{3,2,1,0:T(8,128)S(1)}, u32[]{:S(2)}, u32[]{:S(2)}) collective-permute-start(f32[7,2,16,128]{3,2,1,0:T(8,128)S(1)} %get-tuple-element.38), channel_id=1, source_target_pairs={{32,0},{64,32},{96,64},{128,96},{160,128},{192,160},{224,192},{33,... | collective-permute-start | bytes 344072 | tf_op jit(solution)/shard_map/ppermute | solution.py:21
  5.5 0.7 broadcast_subtract_fusion
  6.2 0.7 cosine_bitcast_fusion.1
  7.1 0.9 %and_and_fusion.1 = pred[33,17,129]{2,1,0:T(8,128)(4,1)} fusion(pred[129]{0:T(512)(128)(4,1)S(1)} %compare_and_fusion, pred[17]{0:T(512)(128)(4,1)S(1)} %compare_and_fusion.1, pred[33]{0:T(512)(128)(4,1)S(1)} %compare_and_fusion.2), kind=kLoop, calls=%fused_computation.89 | loop fusion | flops 144738 | bytes 72548 | tf_op jit(solution)/shard_map/and | solution.py:84
  8.1 0.5 collective-permute-done.1
  8.6 1.1 %pad_maximum_fusion.6 = (f32[7,36,2,128]{3,2,1,0:T(2,128)S(1)}, f32[7,36,2,128]{3,2,1,0:T(2,128)S(1)}) fusion(f32[7,2,16,128]{3,2,1,0:T(8,128)S(1)} %collective-permute-done.1, f32[7,2,16,128]{3,2,1,0:T(8,128)S(1)} %collective-permute-done, f32[1,32,16,128]{3,2,1,0:T(8,128)} %bitcast.81, f32[3,32,16,128]{3,2,1,0:T(8,128)S(1)} %copy-done.3, ...), kind=kLoop, calls=%fused_computation.109 | loop fusion | flops 516096 | bytes 2580480 | tf_op jit(solution)/shard_map/slice | solution.py:27
  9.8 3.5 %collective-permute-start.2 = (f32[7,36,2,128]{3,2,1,0:T(2,128)S(1)}, f32[7,36,2,128]{3,2,1,0:T(2,128)S(1)}, u32[]{:S(2)}, u32[]{:S(2)}) collective-permute-start(f32[7,36,2,128]{3,2,1,0:T(2,128)S(1)} %get-tuple-element.35), channel_id=1, source_target_pairs={{0,8},{8,16},{16,24},{1,9},{9,17},{17,25},{2,10},{10,18},{18,26},{... | collective-permute-start | bytes 774152 | tf_op jit(solution)/shard_map/ppermute | solution.py:21
  13.3 1.3 %collective-permute-start.3 = (f32[7,36,2,128]{3,2,1,0:T(2,128)S(1)}, f32[7,36,2,128]{3,2,1,0:T(2,128)S(1)}, u32[]{:S(2)}, u32[]{:S(2)}) collective-permute-start(f32[7,36,2,128]{3,2,1,0:T(2,128)S(1)} %get-tuple-element.36), channel_id=1, source_target_pairs={{8,0},{16,8},{24,16},{9,1},{17,9},{25,17},{10,2},{18,10},{26,18},{... | collective-permute-start | bytes 774152 | tf_op jit(solution)/shard_map/ppermute | solution.py:21
  14.8 2.6 %collective-permute-done.2 = f32[7,36,2,128]{3,2,1,0:T(2,128)S(1)} collective-permute-done((f32[7,36,2,128]{3,2,1,0:T(2,128)S(1)}, f32[7,36,2,128]{3,2,1,0:T(2,128)S(1)}, u32[]{:S(2)}, u32[]{:S(2)}) %collective-permute-start.2) | collective-permute-done | bytes 258080 | tf_op jit(solution)/shard_map/ppermute | solution.py:21
  17.4 4.7 %collective-permute-done.3 = f32[7,36,2,128]{3,2,1,0:T(2,128)S(1)} collective-permute-done((f32[7,36,2,128]{3,2,1,0:T(2,128)S(1)}, f32[7,36,2,128]{3,2,1,0:T(2,128)S(1)}, u32[]{:S(2)}, u32[]{:S(2)}) %collective-permute-start.3) | collective-permute-done | bytes 258080 | tf_op jit(solution)/shard_map/ppermute | solution.py:21
  22.1 1.5 %select_maximum_fusion = f32[7,36,24,128]{3,2,1,0:T(8,128)S(1)} fusion(f32[7,36,2,128]{3,2,1,0:T(2,128)S(1)} %collective-permute-done.3, f32[7,36,2,128]{3,2,1,0:T(2,128)S(1)} %collective-permute-done.2, f32[7,2,16,128]{3,2,1,0:T(8,128)S(1)} %collective-permute-done.1, f32[7,2,16,128]{3,2,1,0:T(8,128)S(1)} %collective-permute-done, ...), kind=kLoop, calls=%fused_computation.9 | loop fusion | flops 10838016 | bytes 5677056 | tf_op jit(solution)/shard_map/concatenate | solution.py:30
  23.6 1.6 %copy-done.1 = f32[7,36,24,128]{3,2,1,0:T(8,128)} copy-done((f32[7,36,24,128]{3,2,1,0:T(8,128)}, f32[7,36,24,128]{3,2,1,0:T(8,128)S(1)}, u32[]{:S(2)}) %copy-start.1) | copy-done | bytes 3096600
  25.2 1.5 %fusion.51 = f32[4,6048]{1,0:T(4,128)S(1)} fusion(f32[6048,128]{1,0:T(8,128)S(1)} %bitcast.78, s32[4]{0:T(128)S(1)} %get-tuple-element.62), kind=kOutput, calls=%fused_computation.128 | convolution fusion | flops 37159424 | bytes 3193360 | tf_op jit(solution)/shard_map/kz,rz->kr/dot_general | solution.py:39
  26.8 5.0 %collective-permute-start.4 = (f32[2,6048]{1,0:T(2,128)S(1)}, f32[2,6048]{1,0:T(2,128)S(1)}, u32[]{:S(2)}, u32[]{:S(2)}) collective-permute-start(f32[2,6048]{1,0:T(2,128)S(1)} %get-tuple-element.55), channel_id=1, source_target_pairs={{0,1},{1,2},{2,3},{3,4},{4,5},{5,6},{6,7},{8,9},{9,10},{10,11},{11... | collective-permute-start | bytes 145160 | tf_op jit(solution)/shard_map/ppermute | solution.py:21
  31.8 2.1 %collective-permute-start.5 = (f32[2,6048]{1,0:T(2,128)S(1)}, f32[2,6048]{1,0:T(2,128)S(1)}, u32[]{:S(2)}, u32[]{:S(2)}) collective-permute-start(f32[2,6048]{1,0:T(2,128)S(1)} %get-tuple-element.56), channel_id=1, source_target_pairs={{1,0},{2,1},{3,2},{4,3},{5,4},{6,5},{7,6},{9,8},{10,9},{11,10},{12... | collective-permute-start | bytes 145160 | tf_op jit(solution)/shard_map/ppermute | solution.py:21
  34.4 4.7 %collective-permute-done.5 = f32[2,6048]{1,0:T(2,128)S(1)} collective-permute-done((f32[2,6048]{1,0:T(2,128)S(1)}, f32[2,6048]{1,0:T(2,128)S(1)}, u32[]{:S(2)}, u32[]{:S(2)}) %collective-permute-start.5) | collective-permute-done | bytes 48416 | tf_op jit(solution)/shard_map/ppermute | solution.py:21
  39.0 2.7 %fusion.44 = f32[6048,132]{1,0:T(8,128)S(1)} fusion(f32[2,6048]{1,0:T(2,128)S(1)} %collective-permute-done.5, f32[2,6048]{1,0:T(2,128)S(1)} %collective-permute-done.4, s32[4]{0:T(128)S(1)} %get-tuple-element.61), kind=kOutput, calls=%fused_computation.114 | convolution fusion | flops 38344848 | bytes 3290128 | tf_op jit(solution)/shard_map/kr,kl->rl/dot_general | solution.py:47
  41.7 2.8 %convolution_add_fusion = f32[6048,132]{1,0:T(8,128)S(1)} fusion(f32[6048,132]{1,0:T(8,128)S(1)} %fusion.44, f32[6048,128]{1,0:T(8,128)S(1)} %bitcast.79, s32[128]{0:T(128)S(1)} %iota_add_fusion.2), kind=kOutput, calls=%fused_computation.2 | convolution fusion | flops 1227059328 | bytes 9483776 | tf_op jit(solution)/shard_map/dot_general | solution.py:47
  44.6 0.3 slice_bitcast_fusion.3
  44.9 0.8 fusion.25
  45.7 0.5 fusion.13
  46.2 0.2 slice_bitcast_fusion.6
  46.4 0.2 slice.374
  46.6 0.3 slice_multiply_fusion
  46.9 1.6 %fusion.31 = (f32[1,34,18,130]{3,2,1,0:T(8,128)S(1)}, f32[1,34,18,130]{3,2,1,0:T(8,128)S(1)}, f32[1,34,18,130]{3,2,1,0:T(8,128)S(1)}) fusion(f32[35,19,131]{2,1,0:T(8,128)S(1)} %get-tuple-element.28, f32[35,19,131]{2,1,0:T(8,128)S(1)} %get-tuple-element.26, f32[35,19,131]{2,1,0:T(8,128)S(1)} %get-tuple-element.27), kind=kLoop, calls=%fused_computation.71 | loop fusion | flops 716040 | bytes 3818880 | tf_op jit(solution)/shard_map/stack | solution.py:75
  48.6 1.0 %slice_add_fusion = f32[3,34,18,130]{3,2,1,0:T(8,128)S(1)} fusion(f32[7,36,24,132]{3,2,1,0:T(8,128)S(1)} %bitcast.77, f32[1,34,18,130]{3,2,1,0:T(8,128)S(1)} %get-tuple-element.44, f32[1,34,18,130]{3,2,1,0:T(8,128)S(1)} %get-tuple-element.43, f32[1,34,18,130]{3,2,1,0:T(8,128)S(1)} %get-tuple-element.42, f32[34,18,130]{2,1,0:T(8,128)S(1)} %slice_multiply_fusion), kind=kLoop, calls=%fused_computation.24 | loop fusion | flops 954720 | bytes 3182400 | tf_op jit(solution)/shard_map/add | solution.py:102
  49.5 0.2 slice.373
  49.8 0.2 slice_bitcast_fusion.9
  50.1 0.5 fusion.37
  50.7 0.4 copy-done.9
  51.1 0.8 fusion.14
  52.0 0.4 slice.376
  52.5 0.6 fusion.43
  53.1 0.3 slice_add_fusion.1
  53.7 1.2 %fusion = f32[4,4,32,16,128]{4,3,2,1,0:T(8,128)S(1)} fusion(f32[4,32,16,128]{3,2,1,0:T(8,128)S(1)} %pad_maximum_fusion.1, f32[4,128]{1,0:T(4,128)S(1)} %get-tuple-element.65), kind=kOutput, calls=%fused_computation | output fusion | flops 1056895 | bytes 5244928 | tf_op jit(solution)/shard_map/mul | solution.py:121
  54.8 1.5 %multiply_reduce_fusion.2 = (f32[4,32,16,128]{3,2,1,0:T(8,128)S(1)}, f32[4,32,16,128]{3,2,1,0:T(8,128)S(1)}) fusion(f32[4,128]{1,0:T(4,128)S(1)} %get-tuple-element.66, f32[4,4,32,16,128]{4,3,2,1,0:T(8,128)S(1)} %fusion, f32[4,128]{1,0:T(4,128)S(1)} %get-tuple-element.65, f32[4,32,16,128]{3,2,1,0:T(8,128)S(1)} %pad_maximum_fusion), kind=kOutput, calls=%fused_computation.6 | output fusion | flops 4726911 | bytes 7344128 | tf_op jit(solution)/shard_map/mul | solution.py:121
  56.4 0.2 multiply_add_fusion
  56.6 1.0 %copy-done.5 = f32[4,32,16,128]{3,2,1,0:T(8,128)} copy-done((f32[4,32,16,128]{3,2,1,0:T(8,128)}, f32[4,32,16,128]{3,2,1,0:T(8,128)S(1)}, u32[]{:S(2)}) %copy-start.5) | copy-done | bytes 1048600
  57.6 1.0 %convolution_bitcast_fusion = f32[4,8,128]{2,1,0:T(8,128)S(1)} fusion(bf16[4,8,32,16]{2,1,3,0:T(8,128)(2,1)S(1)} %bitcast.83, f32[4,32,16,128]{3,2,1,0:T(8,128)S(1)} %multiply_add_fusion), kind=kOutput, calls=%fused_computation.33 | convolution fusion | flops 25165824 | bytes 1097728 | tf_op jit(solution)/shard_map/pxyl,pnxy->pnl/dot_general | solution.py:131
  58.5 0.9 %reshape.98 = f32[4,2,4,4,2,16]{5,4,3,2,1,0:T(2,128)} reshape(f32[4,8,128]{2,1,0:T(8,128)S(1)} %convolution_bitcast_fusion) | data formatting | bytes 32768 | tf_op jit(solution)/shard_map/reshape | solution.py:132
  59.4 0.7 fusion.56
  60.3 0.9 %copy.37 = f32[32,2,4]{2,1,0:T(2,128)} copy(f32[32,2,4]{1,0,2:T(8,128)S(1)} %reshape_reshape.3) | data formatting | bytes 2048 | tf_op jit(solution)/shard_map/reshape;reshape | solution.py:135
  61.2 11.1 %all-to-all-start = ((f32[32,2,4]{2,1,0:T(2,128)}), f32[32,2,4]{2,1,0:T(2,128)S(1)}, u32[]{:S(2)}, u32[]{:S(2)}) async-start(f32[32,2,4]{2,1,0:T(2,128)} %copy.37), calls=%async_computation | async-start | bytes 65536 | tf_op jit(solution)/shard_map/all_to_all | solution.py:136
  72.2 1.2 %slice.372 = f32[3,32,16,128]{3,2,1,0:T(8,128)} slice(f32[3,33,17,129]{3,2,1,0:T(8,128)S(1)} %fusion.14), slice={[0:3], [1:33], [1:17], [1:129]} | slice | bytes 1572864 | tf_op jit(solution)/shard_map/slice | solution.py:55
  73.4 6.2 %all-to-all-done = f32[32,2,4]{2,1,0:T(2,128)S(1)} async-done(((f32[32,2,4]{2,1,0:T(2,128)}), f32[32,2,4]{2,1,0:T(2,128)S(1)}, u32[]{:S(2)}, u32[]{:S(2)}) %all-to-all-start) | async-done | bytes 1056 | tf_op jit(solution)/shard_map/all_to_all | solution.py:136
  79.8 0.7 copy.40
  (51 shorter events, 1.8 us)
Async XLA Ops:
  0.6 7.3 %copy-start = (bf16[4,2,4,256,64]{3,4,2,1,0:T(8,128)(2,1)S(1)}, bf16[4,2,4,256,64]{3,4,2,1,0:T(8,128)(2,1)}, u32[]{:S(2)}) copy-start(bf16[4,2,4,256,64]{3,4,2,1,0:T(8,128)(2,1)} %param.13) | copy-start | bytes 3145732
  0.6 21.4 %copy-start.6 = (f32[32,16,128]{2,1,0:T(8,128)S(1)}, f32[32,16,128]{2,1,0:T(8,128)}, u32[]{:S(2)}) copy-start(f32[32,16,128]{2,1,0:T(8,128)} %param.9) | copy-start | bytes 786436
  0.7 8.0 %copy-start.4 = (f32[3,32,16,128]{3,2,1,0:T(8,128)S(1)}, f32[3,32,16,128]{3,2,1,0:T(8,128)}, u32[]{:S(2)}) copy-start(f32[3,32,16,128]{3,2,1,0:T(8,128)} %param.7) | copy-start | bytes 2359300
  0.7 8.0 %copy-start.3 = (f32[3,32,16,128]{3,2,1,0:T(8,128)S(1)}, f32[3,32,16,128]{3,2,1,0:T(8,128)}, u32[]{:S(2)}) copy-start(f32[3,32,16,128]{3,2,1,0:T(8,128)} %param.8) | copy-start | bytes 2359300
  2.4 5.7 %collective-permute-start = (f32[7,2,16,128]{3,2,1,0:T(8,128)}, f32[7,2,16,128]{3,2,1,0:T(8,128)S(1)}, u32[]{:S(2)}, u32[]{:S(2)}) collective-permute-start(f32[7,2,16,128]{3,2,1,0:T(8,128)} %get-tuple-element.37), channel_id=1, source_target_pairs={{0,32},{32,64},{64,96},{96,128},{128,160},{160,192},{192,224},{1,3... | collective-permute-start | bytes 344072 | tf_op jit(solution)/shard_map/ppermute | solution.py:21
  4.1 4.5 %collective-permute-start.1 = (f32[7,2,16,128]{3,2,1,0:T(8,128)S(1)}, f32[7,2,16,128]{3,2,1,0:T(8,128)S(1)}, u32[]{:S(2)}, u32[]{:S(2)}) collective-permute-start(f32[7,2,16,128]{3,2,1,0:T(8,128)S(1)} %get-tuple-element.38), channel_id=1, source_target_pairs={{32,0},{64,32},{96,64},{128,96},{160,128},{192,160},{224,192},{33,... | collective-permute-start | bytes 344072 | tf_op jit(solution)/shard_map/ppermute | solution.py:21
  9.8 7.6 %collective-permute-start.2 = (f32[7,36,2,128]{3,2,1,0:T(2,128)S(1)}, f32[7,36,2,128]{3,2,1,0:T(2,128)S(1)}, u32[]{:S(2)}, u32[]{:S(2)}) collective-permute-start(f32[7,36,2,128]{3,2,1,0:T(2,128)S(1)} %get-tuple-element.35), channel_id=1, source_target_pairs={{0,8},{8,16},{16,24},{1,9},{9,17},{17,25},{2,10},{10,18},{18,26},{... | collective-permute-start | bytes 774152 | tf_op jit(solution)/shard_map/ppermute | solution.py:21
  13.3 8.8 %collective-permute-start.3 = (f32[7,36,2,128]{3,2,1,0:T(2,128)S(1)}, f32[7,36,2,128]{3,2,1,0:T(2,128)S(1)}, u32[]{:S(2)}, u32[]{:S(2)}) collective-permute-start(f32[7,36,2,128]{3,2,1,0:T(2,128)S(1)} %get-tuple-element.36), channel_id=1, source_target_pairs={{8,0},{16,8},{24,16},{9,1},{17,9},{25,17},{10,2},{18,10},{26,18},{... | collective-permute-start | bytes 774152 | tf_op jit(solution)/shard_map/ppermute | solution.py:21
  23.6 1.6 %copy-start.1 = (f32[7,36,24,128]{3,2,1,0:T(8,128)}, f32[7,36,24,128]{3,2,1,0:T(8,128)S(1)}, u32[]{:S(2)}) copy-start(f32[7,36,24,128]{3,2,1,0:T(8,128)S(1)} %select_maximum_fusion) | copy-start | bytes 9289732
  26.8 7.6 %collective-permute-start.4 = (f32[2,6048]{1,0:T(2,128)S(1)}, f32[2,6048]{1,0:T(2,128)S(1)}, u32[]{:S(2)}, u32[]{:S(2)}) collective-permute-start(f32[2,6048]{1,0:T(2,128)S(1)} %get-tuple-element.55), channel_id=1, source_target_pairs={{0,1},{1,2},{2,3},{3,4},{4,5},{5,6},{6,7},{8,9},{9,10},{10,11},{11... | collective-permute-start | bytes 145160 | tf_op jit(solution)/shard_map/ppermute | solution.py:21
  31.8 7.2 %collective-permute-start.5 = (f32[2,6048]{1,0:T(2,128)S(1)}, f32[2,6048]{1,0:T(2,128)S(1)}, u32[]{:S(2)}, u32[]{:S(2)}) collective-permute-start(f32[2,6048]{1,0:T(2,128)S(1)} %get-tuple-element.56), channel_id=1, source_target_pairs={{1,0},{2,1},{3,2},{4,3},{5,4},{6,5},{7,6},{9,8},{10,9},{11,10},{12... | collective-permute-start | bytes 145160 | tf_op jit(solution)/shard_map/ppermute | solution.py:21
  39.0 2.7 %copy-start.2 = (f32[7,36,24,128]{3,2,1,0:T(8,128)S(1)}, f32[7,36,24,128]{3,2,1,0:T(8,128)}, u32[]{:S(2)}) copy-start(f32[7,36,24,128]{3,2,1,0:T(8,128)} %copy-done.1) | copy-start | bytes 9289732
  50.1 0.9 %copy-start.9 = (pred[33,17,129]{2,1,0:T(8,128)(4,1)S(1)}, pred[33,17,129]{2,1,0:T(8,128)(4,1)}, u32[]{:S(2)}) copy-start(pred[33,17,129]{2,1,0:T(8,128)(4,1)} %and_and_fusion.1) | copy-start | bytes 217111
  53.4 1.4 %copy-start.7 = (f32[3,32,16,128]{3,2,1,0:T(8,128)}, f32[3,32,16,128]{3,2,1,0:T(8,128)S(1)}, u32[]{:S(2)}) copy-start(f32[3,32,16,128]{3,2,1,0:T(8,128)S(1)} %slice_add_fusion.1) | copy-start | bytes 2359300
  54.8 1.5 %copy-start.8 = (f32[4,32,16,128]{3,2,1,0:T(8,128)S(1)}, f32[4,32,16,128]{3,2,1,0:T(8,128)}, u32[]{:S(2)}) copy-start(f32[4,32,16,128]{3,2,1,0:T(8,128)} %param.10) | copy-start | bytes 3145732
  56.6 1.0 %copy-start.5 = (f32[4,32,16,128]{3,2,1,0:T(8,128)}, f32[4,32,16,128]{3,2,1,0:T(8,128)S(1)}, u32[]{:S(2)}) copy-start(f32[4,32,16,128]{3,2,1,0:T(8,128)S(1)} %multiply_add_fusion) | copy-start | bytes 3145732
  61.2 18.5 %all-to-all-start = ((f32[32,2,4]{2,1,0:T(2,128)}), f32[32,2,4]{2,1,0:T(2,128)S(1)}, u32[]{:S(2)}, u32[]{:S(2)}) async-start(f32[32,2,4]{2,1,0:T(2,128)} %copy.37), calls=%async_computation | async-start | bytes 65536 | tf_op jit(solution)/shard_map/all_to_all | solution.py:136

commit v10 on v6

--- a/solution.py
+++ b/solution.py
@@ -70,9 +70,9 @@
 
 
 def curl(field, start, size, step):
-    vx, vy, vz = field[0], field[1], field[2]
+    vx, vy, vz = field
     d = lambda v, dim: differ(v, start, size, dim, step)
-    return jnp.stack([d(vz, 1) - d(vy, 2), d(vx, 2) - d(vz, 0), d(vy, 0) - d(vx, 1)])
+    return [d(vz, 1) - d(vy, 2), d(vx, 2) - d(vz, 0), d(vy, 0) - d(vx, 1)]
 
 
 def inside(origin, size, cells):
@@ -97,17 +97,22 @@
     spare = -stack.shape[2] % 8
     stack = pin(jnp.pad(stack, ((0, 0), (0, 0), (0, spare), (0, 0))))
     stack = pin(widen_lanes(stack, "gz"))
-    e0, h0, inv = stack[0:3], stack[3:6], stack[6]
+    e0 = [stack[i] for i in range(3)]
+    h0 = [stack[3 + i] for i in range(3)]
+    inv = stack[6]
     n = lambda k: tuple(c + k for c in cells)
-    h1 = box(h0, (0, 0, 0), n(3)) - 0.5 * curl(e0, (0, 0, 0), n(3), 1)
-    h1 = pin(h1 * inside(-2, n(3), cells))
-    e1 = pin(box(e0, (1, 1, 1), n(2)) + 0.5 * box(inv, (1, 1, 1), n(2)) * curl(h1, (1, 1, 1), n(2), -1))
-    h2 = box(h1, (1, 1, 1), n(1)) - 0.5 * curl(e1, (0, 0, 0), n(1), 1)
-    h2 = pin(h2 * inside(-1, n(1), cells))
-    e2 = pin(box(e1, (1, 1, 1), n(0)) + 0.5 * box(inv, (2, 2, 2), n(0)) * curl(h2, (1, 1, 1), n(0), -1))
-    e1_here = box(e1, (1, 1, 1), n(0))
-    h1_here = box(h1, (2, 2, 2), n(0))
-    h2_here = box(h2, (1, 1, 1), n(0))
+    at = lambda v, k, size: box(v, (k, k, k), size)
+    keep = inside(-2, n(3), cells)
+    h1 = [pin((at(v, 0, n(3)) - 0.5 * c) * keep) for v, c in zip(h0, curl(e0, (0, 0, 0), n(3), 1))]
+    scale = 0.5 * at(inv, 1, n(2))
+    e1 = [pin(at(v, 1, n(2)) + scale * c) for v, c in zip(e0, curl(h1, (1, 1, 1), n(2), -1))]
+    keep = inside(-1, n(1), cells)
+    h2 = [pin((at(v, 1, n(1)) - 0.5 * c) * keep) for v, c in zip(h1, curl(e1, (0, 0, 0), n(1), 1))]
+    scale = 0.5 * at(inv, 2, n(0))
+    e2 = [at(v, 1, n(0)) + scale * c for v, c in zip(e1, curl(h2, (1, 1, 1), n(0), -1))]
+    e1_here = [at(v, 1, n(0)) for v in e1]
+    h1_here = [at(v, 2, n(0)) for v in h1]
+    h2_here = [at(v, 1, n(0)) for v in h2]
     local_z = port_z - lax.axis_index("gz") * cells_z
     onehot = (local_z[:, None] == jnp.arange(cells_z)[None, :]).astype(jnp.float32)
     lanes = dft_sums.shape[-1]
@@ -136,7 +141,7 @@
     partial_sums = jnp.transpose(diagonal, (0, 3, 1, 2)).reshape(ports_here * NF, MODES * 2)
     pieces = partial_sums.reshape(groups, owned, MODES * 2)
     result = jnp.sum(lax.all_to_all(pieces, ("gx", "gy"), 0, 0, tiled=False), axis=0)
-    return (e2, h2_here, dft, result.reshape(owned, 1, MODES * 2))
+    return (jnp.stack(e2), jnp.stack(h2_here), dft, result.reshape(owned, 1, MODES * 2))
 
 
 def solution(mesh):

time: 80.7 us -> 79.8 us (0.989)
  other arithmetic: 16.3 us -> 20.7 us
  local copies, waits for them, and re-layouts: 10.8 us -> 6.51 us
  waiting for transfers between devices: 18.9 us -> 17.1 us
  starting transfers between devices: 24.8 us -> 25.7 us
    slice x2, other arithmetic: 1.25 us -> 3.55 us  [widen(): high = lax.slice_in_dim(stack, count - HALO, count, axis=dim)]
    slice x5 -> x0, local copies, waits for them, and re-layouts: 2.03 us -> none  [the longest x1 1.15 us: box(): lax.slice(value, (0,) * lead + tuple(start), value.shape[:lead] + tuple((...]
    another operation x0 -> x6, local copies, waits for them, and re-layouts: none -> 1.73 us  [the longest x3 1.33 us: per_device(): jnp.stack(h2_here)]
    all_to_all x1, waiting for transfers between devices: 6.23 us -> 4.57 us  [per_device(): lax.all_to_all(pieces, ('gx', 'gy'), 0, 0, tiled=False)]
    unnamed x28 -> x18, local copies, waits for them, and re-layouts: 3.98 us -> 2.4 us
    add x2 -> x1, other arithmetic: 1.29 us -> 2.58 us  [per_device(): at(v, 1, n(2)) + scale * c]
    convert_element_type x2 -> x0, other arithmetic: 1.25 us -> none  [inside(): return (masks[0][:, None, None] & masks[1][None, :, None] & masks[2][None...]
    all_to_all x1, starting transfers between devices: 9.84 us -> 10.7 us  [per_device(): lax.all_to_all(pieces, ('gx', 'gy'), 0, 0, tiled=False)]
  transfers between devices with their start and end apart: 7 -> 7, of which waited for: 4 -> 5; matrix products, arithmetic and copies ran while one was open for 7% -> 8% of each run, Pallas kernels for 0% -> 0%
where the time goes in v10:
time: 79.8 us; the launch traced here: 79.1 us
  starting transfers between devices  25.7 us (32%)
  other arithmetic  20.7 us (26%)
  waiting for transfers between devices  17.1 us (21%)
  matrix products  8.02 us (10%)
  local copies, waits for them, and re-layouts  6.51 us (8%)
  between operations  1.06 us (1%)
    ppermute x6, starting transfers between devices, shifted(): lax.ppermute(value, axis, [(source, source + steps) for source in range(f...  15 us
    ppermute x6, waiting for transfers between devices, shifted(): lax.ppermute(value, axis, [(source, source + steps) for source in range(f...  12.5 us
    all_to_all x1, starting transfers between devices, per_device(): lax.all_to_all(pieces, ('gx', 'gy'), 0, 0, tiled=False)  10.7 us
    all_to_all x1, waiting for transfers between devices, per_device(): lax.all_to_all(pieces, ('gx', 'gy'), 0, 0, tiled=False)  4.57 us
    slice x2, other arithmetic, widen(): high = lax.slice_in_dim(stack, count - HALO, count, axis=dim)  3.55 us
    dot_general x1, matrix products, widen_lanes(): jnp.dot(flat, move, precision=lax.Precision.HIGHEST)  2.85 us
    dot_general x1, matrix products, widen_lanes(): jnp.einsum('kr,kl->rl', ghosts, place, precision=lax.Precision.HIGHEST)  2.69 us
    mul x2, other arithmetic, per_device(): planes[..., None] * spread_of[None, :, None, None, :]  2.66 us
  transfers between devices with their start and end apart: 7, of which 5 were waited for; matrix products, arithmetic and copies ran while one was open for 8% of the time, Pallas kernels for 0%

profile of v10, /device:TPU:96, one launch (start us, length us, event | category | flops | bytes accessed | tf_op | source)
XLA Modules:
  0.0 79.1 jit_solution(9055697296985568221)
XLA Ops:
  0.7 1.1 %pad_maximum_fusion.11 = (f32[7,2,16,128]{3,2,1,0:T(8,128)S(1)}, f32[7,2,16,128]{3,2,1,0:T(8,128)S(1)}) fusion(f32[1,32,16,128]{3,2,1,0:T(8,128)} %bitcast.62, f32[3,32,16,128]{3,2,1,0:T(8,128)} %param.8, f32[3,32,16,128]{3,2,1,0:T(8,128)} %param.7), kind=kLoop, calls=%fused_computation.125 | loop fusion | flops 114688 | bytes 2064384 | tf_op jit(solution)/shard_map/slice | solution.py:27
  1.8 1.7 %collective-permute-start = (f32[7,2,16,128]{3,2,1,0:T(8,128)S(1)}, f32[7,2,16,128]{3,2,1,0:T(8,128)S(1)}, u32[]{:S(2)}, u32[]{:S(2)}) collective-permute-start(f32[7,2,16,128]{3,2,1,0:T(8,128)S(1)} %get-tuple-element.31), channel_id=1, source_target_pairs={{0,32},{32,64},{64,96},{96,128},{128,160},{160,192},{192,224},{1,3... | collective-permute-start | bytes 344072 | tf_op jit(solution)/shard_map/ppermute | solution.py:21
  3.5 1.3 %collective-permute-start.1 = (f32[7,2,16,128]{3,2,1,0:T(8,128)S(1)}, f32[7,2,16,128]{3,2,1,0:T(8,128)S(1)}, u32[]{:S(2)}, u32[]{:S(2)}) collective-permute-start(f32[7,2,16,128]{3,2,1,0:T(8,128)S(1)} %get-tuple-element.32), channel_id=1, source_target_pairs={{32,0},{64,32},{96,64},{128,96},{160,128},{192,160},{224,192},{33,... | collective-permute-start | bytes 344072 | tf_op jit(solution)/shard_map/ppermute | solution.py:21
  4.9 0.7 broadcast_subtract_fusion
  5.6 0.7 cosine_bitcast_fusion.1
  6.5 0.1 constant_dynamic-slice_fusion
  6.7 1.3 %collective-permute-done.1 = f32[7,2,16,128]{3,2,1,0:T(8,128)S(1)} collective-permute-done((f32[7,2,16,128]{3,2,1,0:T(8,128)S(1)}, f32[7,2,16,128]{3,2,1,0:T(8,128)S(1)}, u32[]{:S(2)}, u32[]{:S(2)}) %collective-permute-start.1) | collective-permute-done | bytes 114720 | tf_op jit(solution)/shard_map/ppermute | solution.py:21
  8.0 2.5 %pad_maximum_fusion.8 = (f32[7,36,2,128]{3,2,1,0:T(2,128)}, f32[7,36,2,128]{3,2,1,0:T(2,128)}) fusion(f32[7,2,16,128]{3,2,1,0:T(8,128)S(1)} %collective-permute-done.1, f32[7,2,16,128]{3,2,1,0:T(8,128)S(1)} %collective-permute-done, f32[1,32,16,128]{3,2,1,0:T(8,128)} %bitcast.63, f32[3,32,16,128]{3,2,1,0:T(8,128)} %param.8, f32[3,32,16,128]{3,2,1,0:T(8,128)} %param.7), kind=kLoop, calls=%fused_computation.116 | loop fusion | flops 516096 | bytes 2580480 | tf_op jit(solution)/shard_map/slice | solution.py:27
  10.5 3.5 %collective-permute-start.2 = (f32[7,36,2,128]{3,2,1,0:T(2,128)}, f32[7,36,2,128]{3,2,1,0:T(2,128)S(1)}, u32[]{:S(2)}, u32[]{:S(2)}) collective-permute-start(f32[7,36,2,128]{3,2,1,0:T(2,128)} %get-tuple-element.29), channel_id=1, source_target_pairs={{0,8},{8,16},{16,24},{1,9},{9,17},{17,25},{2,10},{10,18},{18,26},{... | collective-permute-start | bytes 774152 | tf_op jit(solution)/shard_map/ppermute | solution.py:21
  14.0 1.3 %collective-permute-start.3 = (f32[7,36,2,128]{3,2,1,0:T(2,128)}, f32[7,36,2,128]{3,2,1,0:T(2,128)}, u32[]{:S(2)}, u32[]{:S(2)}) collective-permute-start(f32[7,36,2,128]{3,2,1,0:T(2,128)} %get-tuple-element.30), channel_id=1, source_target_pairs={{8,0},{16,8},{24,16},{9,1},{17,9},{25,17},{10,2},{18,10},{26,18},{... | collective-permute-start | bytes 774152 | tf_op jit(solution)/shard_map/ppermute | solution.py:21
  15.3 0.5 compare_and_fusion.2
  15.8 0.7 broadcast_and_fusion
  16.5 1.9 %collective-permute-done.2 = f32[7,36,2,128]{3,2,1,0:T(2,128)S(1)} collective-permute-done((f32[7,36,2,128]{3,2,1,0:T(2,128)}, f32[7,36,2,128]{3,2,1,0:T(2,128)S(1)}, u32[]{:S(2)}, u32[]{:S(2)}) %collective-permute-start.2) | collective-permute-done | bytes 258080 | tf_op jit(solution)/shard_map/ppermute | solution.py:21
  18.4 4.7 %collective-permute-done.3 = f32[7,36,2,128]{3,2,1,0:T(2,128)} collective-permute-done((f32[7,36,2,128]{3,2,1,0:T(2,128)}, f32[7,36,2,128]{3,2,1,0:T(2,128)}, u32[]{:S(2)}, u32[]{:S(2)}) %collective-permute-start.3) | collective-permute-done | bytes 258080 | tf_op jit(solution)/shard_map/ppermute | solution.py:21
  23.1 2.4 %select_maximum_fusion = f32[7,36,24,128]{3,2,1,0:T(8,128)S(1)} fusion(f32[7,36,2,128]{3,2,1,0:T(2,128)} %collective-permute-done.3, f32[7,36,2,128]{3,2,1,0:T(2,128)S(1)} %collective-permute-done.2, f32[7,2,16,128]{3,2,1,0:T(8,128)S(1)} %collective-permute-done.1, f32[7,2,16,128]{3,2,1,0:T(8,128)S(1)} %collective-permute-done, ...), kind=kLoop, calls=%fused_computation.9 | loop fusion | flops 10838016 | bytes 5677056 | tf_op jit(solution)/shard_map/concatenate | solution.py:30
  25.5 1.6 %copy-done.1 = f32[7,36,24,128]{3,2,1,0:T(8,128)} copy-done((f32[7,36,24,128]{3,2,1,0:T(8,128)}, f32[7,36,24,128]{3,2,1,0:T(8,128)S(1)}, u32[]{:S(2)}) %copy-start.1) | copy-done | bytes 3096600
  27.1 1.5 %fusion.64 = f32[4,6048]{1,0:T(4,128)S(1)} fusion(f32[6048,128]{1,0:T(8,128)S(1)} %bitcast.59, s32[4]{0:T(128)S(1)} %get-tuple-element.57), kind=kOutput, calls=%fused_computation.142 | convolution fusion | flops 37159424 | bytes 3193360 | tf_op jit(solution)/shard_map/kz,rz->kr/dot_general | solution.py:39
  28.7 5.0 %collective-permute-start.4 = (f32[2,6048]{1,0:T(2,128)S(1)}, f32[2,6048]{1,0:T(2,128)S(1)}, u32[]{:S(2)}, u32[]{:S(2)}) collective-permute-start(f32[2,6048]{1,0:T(2,128)S(1)} %get-tuple-element.50), channel_id=1, source_target_pairs={{0,1},{1,2},{2,3},{3,4},{4,5},{5,6},{6,7},{8,9},{9,10},{10,11},{11... | collective-permute-start | bytes 145160 | tf_op jit(solution)/shard_map/ppermute | solution.py:21
  33.7 2.1 %collective-permute-start.5 = (f32[2,6048]{1,0:T(2,128)S(1)}, f32[2,6048]{1,0:T(2,128)S(1)}, u32[]{:S(2)}, u32[]{:S(2)}) collective-permute-start(f32[2,6048]{1,0:T(2,128)S(1)} %get-tuple-element.51), channel_id=1, source_target_pairs={{1,0},{2,1},{3,2},{4,3},{5,4},{6,5},{7,6},{9,8},{10,9},{11,10},{12... | collective-permute-start | bytes 145160 | tf_op jit(solution)/shard_map/ppermute | solution.py:21
  35.9 0.1 tile.14
  35.9 0.1 mul.185
  36.1 0.1 mul.193
  36.3 4.7 %collective-permute-done.5 = f32[2,6048]{1,0:T(2,128)S(1)} collective-permute-done((f32[2,6048]{1,0:T(2,128)S(1)}, f32[2,6048]{1,0:T(2,128)S(1)}, u32[]{:S(2)}, u32[]{:S(2)}) %collective-permute-start.5) | collective-permute-done | bytes 48416 | tf_op jit(solution)/shard_map/ppermute | solution.py:21
  40.9 2.7 %fusion.57 = f32[6048,132]{1,0:T(8,128)S(1)} fusion(f32[2,6048]{1,0:T(2,128)S(1)} %collective-permute-done.5, f32[2,6048]{1,0:T(2,128)S(1)} %collective-permute-done.4, s32[4]{0:T(128)S(1)} %get-tuple-element.56), kind=kOutput, calls=%fused_computation.126 | convolution fusion | flops 38344848 | bytes 3290128 | tf_op jit(solution)/shard_map/kr,kl->rl/dot_general | solution.py:47
  43.6 2.8 %convolution_add_fusion = f32[6048,132]{1,0:T(8,128)S(1)} fusion(f32[6048,132]{1,0:T(8,128)S(1)} %fusion.57, f32[6048,128]{1,0:T(8,128)S(1)} %bitcast.60, s32[128]{0:T(128)S(1)} %iota_add_fusion.2), kind=kOutput, calls=%fused_computation.2 | convolution fusion | flops 1227059328 | bytes 9483776 | tf_op jit(solution)/shard_map/dot_general | solution.py:47
  46.5 0.6 slice_bitcast_fusion.2
  47.1 1.1 %and_select_fusion.1 = (f32[35,19,131]{2,1,0:T(8,128)S(1)}, f32[35,19,131]{2,1,0:T(8,128)S(1)}, f32[35,19,131]{2,1,0:T(8,128)S(1)}) fusion(f32[36,24,132]{2,1,0:T(8,128)S(1)} %get-tuple-element.23, f32[36,24,132]{2,1,0:T(8,128)S(1)} %get-tuple-element.27, f32[36,24,132]{2,1,0:T(8,128)S(1)} %get-tuple-element.22, pred[131]{0:T(512)(128)(4,1)S(1)} %compare_and_fusion.3, ...), kind=kLoop, calls=%fused_computation.26 | loop fusion | flops 1655185 | bytes 5227696 | tf_op jit(solution)/shard_map/mul | solution.py:106
  48.2 0.1 slice_bitcast_fusion.7
  48.3 0.1 slice_bitcast_fusion.8
  48.4 2.6 %fusion.35 = (f32[34,18,130]{2,1,0:T(8,128)S(1)}, f32[34,18,130]{2,1,0:T(8,128)S(1)}, f32[34,18,130]{2,1,0:T(8,128)S(1)}) fusion(f32[35,19,131]{2,1,0:T(8,128)S(1)} %get-tuple-element.39, f32[35,19,131]{2,1,0:T(8,128)S(1)} %get-tuple-element.40, f32[36,24,132]{2,1,0:T(8,128)S(1)} %get-tuple-element.27, f32[36,24,132]{2,1,0:T(8,128)S(1)} %get-tuple-element.26, ...), kind=kLoop, calls=%fused_computation.71 | loop fusion | flops 1272960 | bytes 5091840 | tf_op jit(solution)/shard_map/add | solution.py:108
  51.0 0.1 slice_bitcast_fusion.10
  51.2 1.4 %and_select_fusion.5 = (f32[33,17,129]{2,1,0:T(8,128)S(1)}, f32[33,17,129]{2,1,0:T(8,128)S(1)}, f32[33,17,129]{2,1,0:T(8,128)S(1)}) fusion(f32[34,18,130]{2,1,0:T(8,128)S(1)} %get-tuple-element.33, f32[34,18,130]{2,1,0:T(8,128)S(1)} %get-tuple-element.34, f32[35,19,131]{2,1,0:T(8,128)S(1)} %get-tuple-element.40, pred[129]{0:T(512)(128)(4,1)S(1)} %compare_and_fusion, ...), kind=kLoop, calls=%fused_computation.30 | loop fusion | flops 1375011 | bytes 4342830 | tf_op jit(solution)/shard_map/mul | solution.py:110
  52.6 0.1 slice_bitcast_fusion.11
  52.7 0.1 slice_bitcast_fusion.12
  52.8 0.9 %fusion.56 = (f32[1,32,16,128]{3,2,1,0:T(8,128)S(1)}, f32[1,32,16,128]{3,2,1,0:T(8,128)S(1)}, f32[1,32,16,128]{3,2,1,0:T(8,128)S(1)}, f32[1,32,16,128]{3,2,1,0:T(8,128)S(1)}) fusion(f32[33,17,129]{2,1,0:T(8,128)S(1)} %get-tuple-element.44, f32[33,17,129]{2,1,0:T(8,128)S(1)} %get-tuple-element.42, f32[34,18,130]{2,1,0:T(8,128)S(1)} %get-tuple-element.33, ...), kind=kLoop, calls=%fused_computation.109 | loop fusion | flops 1048576 | bytes 4456448 | tf_op jit(solution)/shard_map/stack | solution.py:144
  53.8 1.1 %slice_bitcast_fusion.13 = f32[1,32,16,128]{3,2,1,0:T(8,128)} fusion(f32[33,17,129]{2,1,0:T(8,128)S(1)} %get-tuple-element.42), kind=kLoop, calls=%fused_computation.121 | loop fusion | bytes 524288 | tf_op jit(solution)/shard_map/stack | solution.py:144
  54.9 1.2 %fusion = f32[4,4,32,16,128]{4,3,2,1,0:T(8,128)S(1)} fusion(f32[4,32,16,128]{3,2,1,0:T(8,128)S(1)} %pad_maximum_fusion.1, f32[4,128]{1,0:T(4,128)S(1)} %get-tuple-element.60), kind=kOutput, calls=%fused_computation | output fusion | flops 1056895 | bytes 5244928 | tf_op jit(solution)/shard_map/mul | solution.py:128
  56.2 1.5 %multiply_reduce_fusion.2 = (f32[4,32,16,128]{3,2,1,0:T(8,128)S(1)}, f32[4,32,16,128]{3,2,1,0:T(8,128)S(1)}) fusion(f32[4,128]{1,0:T(4,128)S(1)} %get-tuple-element.61, f32[4,4,32,16,128]{4,3,2,1,0:T(8,128)S(1)} %fusion, f32[4,128]{1,0:T(4,128)S(1)} %get-tuple-element.60, f32[4,32,16,128]{3,2,1,0:T(8,128)S(1)} %pad_maximum_fusion), kind=kOutput, calls=%fused_computation.6 | output fusion | flops 4726911 | bytes 7344128 | tf_op jit(solution)/shard_map/mul | solution.py:128
  57.7 0.2 multiply_add_fusion
  57.9 1.0 %convolution_bitcast_fusion = f32[4,8,128]{2,1,0:T(8,128)S(1)} fusion(bf16[4,8,32,16]{2,1,3,0:T(8,128)(2,1)S(1)} %bitcast.65, f32[4,32,16,128]{3,2,1,0:T(8,128)S(1)} %multiply_add_fusion), kind=kOutput, calls=%fused_computation.31 | convolution fusion | flops 25165824 | bytes 1097728 | tf_op jit(solution)/shard_map/pxyl,pnxy->pnl/dot_general | solution.py:138
  58.9 0.2 reshape.202
  59.3 0.9 %copy.37 = f32[32,2,4]{2,1,0:T(2,128)} copy(f32[32,2,4]{1,0,2:T(8,128)S(1)} %reshape_reshape.3) | data formatting | bytes 2048 | tf_op jit(solution)/shard_map/reshape;reshape | solution.py:142
  60.2 10.7 %all-to-all-start = ((f32[32,2,4]{2,1,0:T(2,128)}), f32[32,2,4]{2,1,0:T(2,128)S(1)}, u32[]{:S(2)}, u32[]{:S(2)}) async-start(f32[32,2,4]{2,1,0:T(2,128)} %copy.37), calls=%async_computation | async-start | bytes 65536 | tf_op jit(solution)/shard_map/all_to_all | solution.py:143
  70.9 1.9 %pad_maximum_fusion.3 = f32[3,32,16,128]{3,2,1,0:T(8,128)} fusion(f32[1,32,16,128]{3,2,1,0:T(8,128)} %slice_bitcast_fusion.13, f32[1,32,16,128]{3,2,1,0:T(8,128)S(1)} %slice_bitcast_fusion.12, f32[1,32,16,128]{3,2,1,0:T(8,128)S(1)} %slice_bitcast_fusion.11), kind=kLoop, calls=%fused_computation.90 | loop fusion | flops 393216 | bytes 1572864 | tf_op jit(solution)/shard_map/stack | solution.py:144
  72.8 0.9 %pad_maximum_fusion.2 = f32[3,32,16,128]{3,2,1,0:T(8,128)} fusion(f32[1,32,16,128]{3,2,1,0:T(8,128)S(1)} %get-tuple-element.38, f32[1,32,16,128]{3,2,1,0:T(8,128)S(1)} %get-tuple-element.37, f32[1,32,16,128]{3,2,1,0:T(8,128)S(1)} %get-tuple-element.36), kind=kLoop, calls=%fused_computation.89 | loop fusion | flops 393216 | bytes 1572864 | tf_op jit(solution)/shard_map/stack | solution.py:144
  73.7 4.6 %all-to-all-done = f32[32,2,4]{2,1,0:T(2,128)S(1)} async-done(((f32[32,2,4]{2,1,0:T(2,128)}), f32[32,2,4]{2,1,0:T(2,128)S(1)}, u32[]{:S(2)}, u32[]{:S(2)}) %all-to-all-start) | async-done | bytes 1056 | tf_op jit(solution)/shard_map/all_to_all | solution.py:143
  78.3 0.1 copy.44
  78.4 0.7 copy.40
  (41 shorter events, 0.8 us)
Async XLA Ops:
  0.6 5.9 %copy-start = (bf16[4,2,4,256,64]{3,4,2,1,0:T(8,128)(2,1)S(1)}, bf16[4,2,4,256,64]{3,4,2,1,0:T(8,128)(2,1)}, u32[]{:S(2)}) copy-start(bf16[4,2,4,256,64]{3,4,2,1,0:T(8,128)(2,1)} %param.13) | copy-start | bytes 3145732
  0.6 22.4 %copy-start.6 = (f32[32,16,128]{2,1,0:T(8,128)S(1)}, f32[32,16,128]{2,1,0:T(8,128)}, u32[]{:S(2)}) copy-start(f32[32,16,128]{2,1,0:T(8,128)} %param.9) | copy-start | bytes 786436
  0.7 22.4 %copy-start.4 = (f32[3,32,16,128]{3,2,1,0:T(8,128)S(1)}, f32[3,32,16,128]{3,2,1,0:T(8,128)}, u32[]{:S(2)}) copy-start(f32[3,32,16,128]{3,2,1,0:T(8,128)} %param.7) | copy-start | bytes 2359300
  0.7 22.4 %copy-start.3 = (f32[3,32,16,128]{3,2,1,0:T(8,128)S(1)}, f32[3,32,16,128]{3,2,1,0:T(8,128)}, u32[]{:S(2)}) copy-start(f32[3,32,16,128]{3,2,1,0:T(8,128)} %param.8) | copy-start | bytes 2359300
  1.8 4.9 %collective-permute-start = (f32[7,2,16,128]{3,2,1,0:T(8,128)S(1)}, f32[7,2,16,128]{3,2,1,0:T(8,128)S(1)}, u32[]{:S(2)}, u32[]{:S(2)}) collective-permute-start(f32[7,2,16,128]{3,2,1,0:T(8,128)S(1)} %get-tuple-element.31), channel_id=1, source_target_pairs={{0,32},{32,64},{64,96},{96,128},{128,160},{160,192},{192,224},{1,3... | collective-permute-start | bytes 344072 | tf_op jit(solution)/shard_map/ppermute | solution.py:21
  3.5 4.5 %collective-permute-start.1 = (f32[7,2,16,128]{3,2,1,0:T(8,128)S(1)}, f32[7,2,16,128]{3,2,1,0:T(8,128)S(1)}, u32[]{:S(2)}, u32[]{:S(2)}) collective-permute-start(f32[7,2,16,128]{3,2,1,0:T(8,128)S(1)} %get-tuple-element.32), channel_id=1, source_target_pairs={{32,0},{64,32},{96,64},{128,96},{160,128},{192,160},{224,192},{33,... | collective-permute-start | bytes 344072 | tf_op jit(solution)/shard_map/ppermute | solution.py:21
  10.5 7.9 %collective-permute-start.2 = (f32[7,36,2,128]{3,2,1,0:T(2,128)}, f32[7,36,2,128]{3,2,1,0:T(2,128)S(1)}, u32[]{:S(2)}, u32[]{:S(2)}) collective-permute-start(f32[7,36,2,128]{3,2,1,0:T(2,128)} %get-tuple-element.29), channel_id=1, source_target_pairs={{0,8},{8,16},{16,24},{1,9},{9,17},{17,25},{2,10},{10,18},{18,26},{... | collective-permute-start | bytes 774152 | tf_op jit(solution)/shard_map/ppermute | solution.py:21
  14.0 9.1 %collective-permute-start.3 = (f32[7,36,2,128]{3,2,1,0:T(2,128)}, f32[7,36,2,128]{3,2,1,0:T(2,128)}, u32[]{:S(2)}, u32[]{:S(2)}) collective-permute-start(f32[7,36,2,128]{3,2,1,0:T(2,128)} %get-tuple-element.30), channel_id=1, source_target_pairs={{8,0},{16,8},{24,16},{9,1},{17,9},{25,17},{10,2},{18,10},{26,18},{... | collective-permute-start | bytes 774152 | tf_op jit(solution)/shard_map/ppermute | solution.py:21
  25.5 1.6 %copy-start.1 = (f32[7,36,24,128]{3,2,1,0:T(8,128)}, f32[7,36,24,128]{3,2,1,0:T(8,128)S(1)}, u32[]{:S(2)}) copy-start(f32[7,36,24,128]{3,2,1,0:T(8,128)S(1)} %select_maximum_fusion) | copy-start | bytes 9289732
  28.7 7.6 %collective-permute-start.4 = (f32[2,6048]{1,0:T(2,128)S(1)}, f32[2,6048]{1,0:T(2,128)S(1)}, u32[]{:S(2)}, u32[]{:S(2)}) collective-permute-start(f32[2,6048]{1,0:T(2,128)S(1)} %get-tuple-element.50), channel_id=1, source_target_pairs={{0,1},{1,2},{2,3},{3,4},{4,5},{5,6},{6,7},{8,9},{9,10},{10,11},{11... | collective-permute-start | bytes 145160 | tf_op jit(solution)/shard_map/ppermute | solution.py:21
  33.7 7.2 %collective-permute-start.5 = (f32[2,6048]{1,0:T(2,128)S(1)}, f32[2,6048]{1,0:T(2,128)S(1)}, u32[]{:S(2)}, u32[]{:S(2)}) collective-permute-start(f32[2,6048]{1,0:T(2,128)S(1)} %get-tuple-element.51), channel_id=1, source_target_pairs={{1,0},{2,1},{3,2},{4,3},{5,4},{6,5},{7,6},{9,8},{10,9},{11,10},{12... | collective-permute-start | bytes 145160 | tf_op jit(solution)/shard_map/ppermute | solution.py:21
  40.9 2.7 %copy-start.2 = (f32[7,36,24,128]{3,2,1,0:T(8,128)S(1)}, f32[7,36,24,128]{3,2,1,0:T(8,128)}, u32[]{:S(2)}) copy-start(f32[7,36,24,128]{3,2,1,0:T(8,128)} %copy-done.1) | copy-start | bytes 9289732
  56.2 1.5 %copy-start.7 = (f32[4,32,16,128]{3,2,1,0:T(8,128)S(1)}, f32[4,32,16,128]{3,2,1,0:T(8,128)}, u32[]{:S(2)}) copy-start(f32[4,32,16,128]{3,2,1,0:T(8,128)} %param.10) | copy-start | bytes 3145732
  57.9 21.2 %copy-start.5 = (f32[4,32,16,128]{3,2,1,0:T(8,128)}, f32[4,32,16,128]{3,2,1,0:T(8,128)S(1)}, u32[]{:S(2)}) copy-start(f32[4,32,16,128]{3,2,1,0:T(8,128)S(1)} %multiply_add_fusion) | copy-start | bytes 3145732
  60.2 18.1 %all-to-all-start = ((f32[32,2,4]{2,1,0:T(2,128)}), f32[32,2,4]{2,1,0:T(2,128)S(1)}, u32[]{:S(2)}, u32[]{:S(2)}) async-start(f32[32,2,4]{2,1,0:T(2,128)} %copy.37), calls=%async_computation | async-start | bytes 65536 | tf_op jit(solution)/shard_map/all_to_all | solution.py:143

commit v11 on v10

--- a/solution.py
+++ b/solution.py
@@ -119,9 +119,11 @@
     lane_part = jnp.arange(lanes) // (lanes // 4)
     spread_of = (lane_part[None, :] == jnp.arange(4)[:, None]).astype(jnp.float32)
     dft = dft_sums
-    for step, (e_now, h_now) in enumerate(((e1_here, h1_here), (e2, h2_here))):
-        tangent = pin(jnp.stack([e_now[0], e_now[1], h_now[0], h_now[1]]))
-        planes = jnp.sum(tangent[None] * onehot[:, None, None, None, :], axis=-1)
+    both = ((e1_here, h1_here), (e2, h2_here))
+    tangent = pin(jnp.stack([v for e_now, h_now in both for v in (e_now[0], e_now[1], h_now[0], h_now[1])]))
+    every_plane = jnp.sum(tangent[None] * onehot[:, None, None, None, :], axis=-1)
+    for step in range(STEPS):
+        planes = every_plane[:, 4 * step:4 * step + 4]
         phase = omega * jnp.float32(step + 1)
         trig = jnp.stack([jnp.cos(phase), jnp.sin(phase)])
         coef = jnp.tile(trig.reshape(-1), 4)

time: 79.8 us -> 82.8 us (1.038)
  other arithmetic: 20.7 us -> 24.3 us
    reduce_sum x0 -> x2, other arithmetic: none -> 4.82 us  [the longest x1 2.59 us: per_device(): jnp.sum(planes[..., None] * spread_of[None, :, None, None, :], axis=1)]
    mul x2 -> x0, other arithmetic: 2.66 us -> none  [per_device(): planes[..., None] * spread_of[None, :, None, None, :]]
    unnamed x0 -> x2, other arithmetic: none -> 1.61 us
    another operation x3 -> x1, local copies, waits for them, and re-layouts: 1.33 us -> 0.13 us  [per_device(): jnp.stack(h2_here)]
    unnamed x18 -> x23, local copies, waits for them, and re-layouts: 2.4 us -> 3.09 us
    another operation x1 -> x2, other arithmetic: 1.88 us -> 1.67 us  [per_device(): jnp.stack(h2_here)]
    another operation x2 -> x1, other arithmetic: 1.87 us -> 1.89 us  [per_device(): jnp.stack(e2)]
where the time goes in v11:
time: 82.8 us; the launch traced here: 82.1 us
  starting transfers between devices  25.7 us (31%)
  other arithmetic  24.3 us (29%)
  waiting for transfers between devices  17.1 us (21%)
  matrix products  8.02 us (10%)
  local copies, waits for them, and re-layouts  5.89 us (7%)
  between operations  1.07 us (1%)
    ppermute x6, starting transfers between devices, shifted(): lax.ppermute(value, axis, [(source, source + steps) for source in range(f...  15 us
    ppermute x6, waiting for transfers between devices, shifted(): lax.ppermute(value, axis, [(source, source + steps) for source in range(f...  12.5 us
    all_to_all x1, starting transfers between devices, per_device(): lax.all_to_all(pieces, ('gx', 'gy'), 0, 0, tiled=False)  10.7 us
    all_to_all x1, waiting for transfers between devices, per_device(): lax.all_to_all(pieces, ('gx', 'gy'), 0, 0, tiled=False)  4.56 us
    slice x2, other arithmetic, widen(): high = lax.slice_in_dim(stack, count - HALO, count, axis=dim)  3.55 us
    unnamed x23, local copies, waits for them, and re-layouts  3.09 us
    dot_general x1, matrix products, widen_lanes(): jnp.dot(flat, move, precision=lax.Precision.HIGHEST)  2.85 us
    dot_general x1, matrix products, widen_lanes(): jnp.einsum('kr,kl->rl', ghosts, place, precision=lax.Precision.HIGHEST)  2.68 us
  transfers between devices with their start and end apart: 7, of which 5 were waited for; matrix products, arithmetic and copies ran while one was open for 8% of the time, Pallas kernels for 0%

profile of v11, /device:TPU:96, one launch (start us, length us, event | category | flops | bytes accessed | tf_op | source)
XLA Modules:
  0.0 82.1 jit_solution(7253173829192025012)
XLA Ops:
  0.7 1.1 %pad_maximum_fusion.9 = (f32[7,2,16,128]{3,2,1,0:T(8,128)S(1)}, f32[7,2,16,128]{3,2,1,0:T(8,128)S(1)}) fusion(f32[1,32,16,128]{3,2,1,0:T(8,128)} %bitcast.72, f32[3,32,16,128]{3,2,1,0:T(8,128)} %param.8, f32[3,32,16,128]{3,2,1,0:T(8,128)} %param.7), kind=kLoop, calls=%fused_computation.116 | loop fusion | flops 114688 | bytes 2064384 | tf_op jit(solution)/shard_map/slice | solution.py:27
  1.8 1.7 %collective-permute-start = (f32[7,2,16,128]{3,2,1,0:T(8,128)S(1)}, f32[7,2,16,128]{3,2,1,0:T(8,128)S(1)}, u32[]{:S(2)}, u32[]{:S(2)}) collective-permute-start(f32[7,2,16,128]{3,2,1,0:T(8,128)S(1)} %get-tuple-element.35), channel_id=1, source_target_pairs={{0,32},{32,64},{64,96},{96,128},{128,160},{160,192},{192,224},{1,3... | collective-permute-start | bytes 344072 | tf_op jit(solution)/shard_map/ppermute | solution.py:21
  3.5 1.3 %collective-permute-start.1 = (f32[7,2,16,128]{3,2,1,0:T(8,128)S(1)}, f32[7,2,16,128]{3,2,1,0:T(8,128)S(1)}, u32[]{:S(2)}, u32[]{:S(2)}) collective-permute-start(f32[7,2,16,128]{3,2,1,0:T(8,128)S(1)} %get-tuple-element.36), channel_id=1, source_target_pairs={{32,0},{64,32},{96,64},{128,96},{160,128},{192,160},{224,192},{33,... | collective-permute-start | bytes 344072 | tf_op jit(solution)/shard_map/ppermute | solution.py:21
  4.9 0.7 broadcast_subtract_fusion
  5.7 0.7 cosine_bitcast_fusion.1
  6.5 0.1 constant_dynamic-slice_fusion
  6.7 1.3 %collective-permute-done.1 = f32[7,2,16,128]{3,2,1,0:T(8,128)S(1)} collective-permute-done((f32[7,2,16,128]{3,2,1,0:T(8,128)S(1)}, f32[7,2,16,128]{3,2,1,0:T(8,128)S(1)}, u32[]{:S(2)}, u32[]{:S(2)}) %collective-permute-start.1) | collective-permute-done | bytes 114720 | tf_op jit(solution)/shard_map/ppermute | solution.py:21
  8.0 2.5 %pad_maximum_fusion.6 = (f32[7,36,2,128]{3,2,1,0:T(2,128)}, f32[7,36,2,128]{3,2,1,0:T(2,128)}) fusion(f32[7,2,16,128]{3,2,1,0:T(8,128)S(1)} %collective-permute-done.1, f32[7,2,16,128]{3,2,1,0:T(8,128)S(1)} %collective-permute-done, f32[1,32,16,128]{3,2,1,0:T(8,128)} %bitcast.73, f32[3,32,16,128]{3,2,1,0:T(8,128)} %param.8, f32[3,32,16,128]{3,2,1,0:T(8,128)} %param.7), kind=kLoop, calls=%fused_computation.109 | loop fusion | flops 516096 | bytes 2580480 | tf_op jit(solution)/shard_map/slice | solution.py:27
  10.5 3.5 %collective-permute-start.2 = (f32[7,36,2,128]{3,2,1,0:T(2,128)}, f32[7,36,2,128]{3,2,1,0:T(2,128)S(1)}, u32[]{:S(2)}, u32[]{:S(2)}) collective-permute-start(f32[7,36,2,128]{3,2,1,0:T(2,128)} %get-tuple-element.33), channel_id=1, source_target_pairs={{0,8},{8,16},{16,24},{1,9},{9,17},{17,25},{2,10},{10,18},{18,26},{... | collective-permute-start | bytes 774152 | tf_op jit(solution)/shard_map/ppermute | solution.py:21
  14.0 1.3 %collective-permute-start.3 = (f32[7,36,2,128]{3,2,1,0:T(2,128)}, f32[7,36,2,128]{3,2,1,0:T(2,128)}, u32[]{:S(2)}, u32[]{:S(2)}) collective-permute-start(f32[7,36,2,128]{3,2,1,0:T(2,128)} %get-tuple-element.34), channel_id=1, source_target_pairs={{8,0},{16,8},{24,16},{9,1},{17,9},{25,17},{10,2},{18,10},{26,18},{... | collective-permute-start | bytes 774152 | tf_op jit(solution)/shard_map/ppermute | solution.py:21
  15.3 0.5 compare_and_fusion.2
  15.8 0.7 broadcast_and_fusion
  16.5 1.9 %collective-permute-done.2 = f32[7,36,2,128]{3,2,1,0:T(2,128)S(1)} collective-permute-done((f32[7,36,2,128]{3,2,1,0:T(2,128)}, f32[7,36,2,128]{3,2,1,0:T(2,128)S(1)}, u32[]{:S(2)}, u32[]{:S(2)}) %collective-permute-start.2) | collective-permute-done | bytes 258080 | tf_op jit(solution)/shard_map/ppermute | solution.py:21
  18.4 4.7 %collective-permute-done.3 = f32[7,36,2,128]{3,2,1,0:T(2,128)} collective-permute-done((f32[7,36,2,128]{3,2,1,0:T(2,128)}, f32[7,36,2,128]{3,2,1,0:T(2,128)}, u32[]{:S(2)}, u32[]{:S(2)}) %collective-permute-start.3) | collective-permute-done | bytes 258080 | tf_op jit(solution)/shard_map/ppermute | solution.py:21
  23.1 2.4 %select_maximum_fusion = f32[7,36,24,128]{3,2,1,0:T(8,128)S(1)} fusion(f32[7,36,2,128]{3,2,1,0:T(2,128)} %collective-permute-done.3, f32[7,36,2,128]{3,2,1,0:T(2,128)S(1)} %collective-permute-done.2, f32[7,2,16,128]{3,2,1,0:T(8,128)S(1)} %collective-permute-done.1, f32[7,2,16,128]{3,2,1,0:T(8,128)S(1)} %collective-permute-done, ...), kind=kLoop, calls=%fused_computation.4 | loop fusion | flops 10838016 | bytes 5677056 | tf_op jit(solution)/shard_map/concatenate | solution.py:30
  25.5 1.6 %copy-done.1 = f32[7,36,24,128]{3,2,1,0:T(8,128)} copy-done((f32[7,36,24,128]{3,2,1,0:T(8,128)}, f32[7,36,24,128]{3,2,1,0:T(8,128)S(1)}, u32[]{:S(2)}) %copy-start.1) | copy-done | bytes 3096600
  27.1 1.5 %fusion.58 = f32[4,6048]{1,0:T(4,128)S(1)} fusion(f32[6048,128]{1,0:T(8,128)S(1)} %bitcast.69, s32[4]{0:T(128)S(1)} %get-tuple-element.62), kind=kOutput, calls=%fused_computation.137 | convolution fusion | flops 37159424 | bytes 3193360 | tf_op jit(solution)/shard_map/kz,rz->kr/dot_general | solution.py:39
  28.7 5.0 %collective-permute-start.4 = (f32[2,6048]{1,0:T(2,128)S(1)}, f32[2,6048]{1,0:T(2,128)S(1)}, u32[]{:S(2)}, u32[]{:S(2)}) collective-permute-start(f32[2,6048]{1,0:T(2,128)S(1)} %get-tuple-element.55), channel_id=1, source_target_pairs={{0,1},{1,2},{2,3},{3,4},{4,5},{5,6},{6,7},{8,9},{9,10},{10,11},{11... | collective-permute-start | bytes 145160 | tf_op jit(solution)/shard_map/ppermute | solution.py:21
  33.7 2.1 %collective-permute-start.5 = (f32[2,6048]{1,0:T(2,128)S(1)}, f32[2,6048]{1,0:T(2,128)S(1)}, u32[]{:S(2)}, u32[]{:S(2)}) collective-permute-start(f32[2,6048]{1,0:T(2,128)S(1)} %get-tuple-element.56), channel_id=1, source_target_pairs={{1,0},{2,1},{3,2},{4,3},{5,4},{6,5},{7,6},{9,8},{10,9},{11,10},{12... | collective-permute-start | bytes 145160 | tf_op jit(solution)/shard_map/ppermute | solution.py:21
  36.3 4.7 %collective-permute-done.5 = f32[2,6048]{1,0:T(2,128)S(1)} collective-permute-done((f32[2,6048]{1,0:T(2,128)S(1)}, f32[2,6048]{1,0:T(2,128)S(1)}, u32[]{:S(2)}, u32[]{:S(2)}) %collective-permute-start.5) | collective-permute-done | bytes 48416 | tf_op jit(solution)/shard_map/ppermute | solution.py:21
  40.9 2.7 %fusion.51 = f32[6048,132]{1,0:T(8,128)S(1)} fusion(f32[2,6048]{1,0:T(2,128)S(1)} %collective-permute-done.5, f32[2,6048]{1,0:T(2,128)S(1)} %collective-permute-done.4, s32[4]{0:T(128)S(1)} %get-tuple-element.61), kind=kOutput, calls=%fused_computation.117 | convolution fusion | flops 38344848 | bytes 3290128 | tf_op jit(solution)/shard_map/kr,kl->rl/dot_general | solution.py:47
  43.6 2.8 %convolution_add_fusion = f32[6048,132]{1,0:T(8,128)S(1)} fusion(f32[6048,132]{1,0:T(8,128)S(1)} %fusion.51, f32[6048,128]{1,0:T(8,128)S(1)} %bitcast.70, s32[128]{0:T(128)S(1)} %iota_add_fusion.2), kind=kOutput, calls=%fused_computation.1 | convolution fusion | flops 1227059328 | bytes 9483776 | tf_op jit(solution)/shard_map/dot_general | solution.py:47
  46.5 0.7 slice_bitcast_fusion.2
  47.2 1.1 %and_select_fusion.1 = (f32[35,19,131]{2,1,0:T(8,128)S(1)}, f32[35,19,131]{2,1,0:T(8,128)S(1)}, f32[35,19,131]{2,1,0:T(8,128)S(1)}) fusion(f32[36,24,132]{2,1,0:T(8,128)S(1)} %get-tuple-element.27, f32[36,24,132]{2,1,0:T(8,128)S(1)} %get-tuple-element.31, f32[36,24,132]{2,1,0:T(8,128)S(1)} %get-tuple-element.26, pred[131]{0:T(512)(128)(4,1)S(1)} %compare_and_fusion.3, ...), kind=kLoop, calls=%fused_computation.17 | loop fusion | flops 1655185 | bytes 5227696 | tf_op jit(solution)/shard_map/mul | solution.py:106
  48.3 2.6 %fusion.27 = (f32[34,18,130]{2,1,0:T(8,128)S(1)}, f32[34,18,130]{2,1,0:T(8,128)S(1)}, f32[34,18,130]{2,1,0:T(8,128)S(1)}) fusion(f32[35,19,131]{2,1,0:T(8,128)S(1)} %get-tuple-element.40, f32[35,19,131]{2,1,0:T(8,128)S(1)} %get-tuple-element.41, f32[36,24,132]{2,1,0:T(8,128)S(1)} %get-tuple-element.31, f32[36,24,132]{2,1,0:T(8,128)S(1)} %get-tuple-element.30, ...), kind=kLoop, calls=%fused_computation.60 | loop fusion | flops 1272960 | bytes 5091840 | tf_op jit(solution)/shard_map/add | solution.py:108
  50.9 0.1 bitcast_dynamic-update-slice_fusion.1
  51.1 0.1 bitcast_dynamic-update-slice_fusion
  51.2 0.1 fusion.38
  51.4 0.1 fusion.37
  51.5 1.5 %and_select_fusion.5 = (f32[33,17,129]{2,1,0:T(8,128)S(1)}, f32[33,17,129]{2,1,0:T(8,128)S(1)}, f32[33,17,129]{2,1,0:T(8,128)S(1)}) fusion(f32[34,18,130]{2,1,0:T(8,128)S(1)} %get-tuple-element.37, f32[34,18,130]{2,1,0:T(8,128)S(1)} %get-tuple-element.38, f32[35,19,131]{2,1,0:T(8,128)S(1)} %get-tuple-element.41, pred[129]{0:T(512)(128)(4,1)S(1)} %compare_and_fusion, ...), kind=kLoop, calls=%fused_computation.21 | loop fusion | flops 1375011 | bytes 4342830 | tf_op jit(solution)/shard_map/mul | solution.py:110
  53.0 0.1 slice_bitcast_fusion.11
  53.1 0.4 constant_dynamic-update-slice_fusion.3
  53.6 0.7 slice_bitcast_fusion.9
  54.3 1.2 %constant_dynamic-update-slice_fusion.2 = (f32[8,32,16,128]{3,2,1,0:T(8,128)S(1)}, f32[1,32,16,128]{3,2,1,0:T(8,128)}) fusion(f32[8,32,16,128]{3,2,1,0:T(8,128)S(1)} %get-tuple-element.24, f32[33,17,129]{2,1,0:T(8,128)S(1)} %get-tuple-element.43, f32[33,17,129]{2,1,0:T(8,128)S(1)} %get-tuple-element.44, f32[36,24,132]{2,1,0:T(8,128)S(1)} %get-tuple-element.30, ...), kind=kLoop, calls=%fused_computation.124 | loop fusion | flops 393216 | bytes 2097152
  55.5 0.1 constant_dynamic-update-slice_fusion.1
  55.6 0.1 constant_dynamic-update-slice_fusion
  55.8 2.2 %multiply_reduce_fusion = f32[4,8,32,16]{3,2,1,0:T(8,128)S(1)} fusion(f32[4,128]{1,0:T(4,128)S(1)} %fusion.59, f32[8,32,16,128]{3,2,1,0:T(8,128)S(1)} %constant_dynamic-update-slice_fusion), kind=kLoop, calls=%fused_computation | loop fusion | flops 4177920 | bytes 2164736 | tf_op jit(solution)/shard_map/reduce_sum | solution.py:124
  58.1 2.6 %multiply_reduce_fusion.2 = (f32[4,32,16,128]{3,2,1,0:T(8,128)S(1)}, f32[4,32,16,128]{3,2,1,0:T(8,128)S(1)}) fusion(f32[4,128]{1,0:T(4,128)S(1)} %fusion.60, f32[4,4,32,16]{3,2,1,0:T(8,128)S(1)} %get-tuple-element.50, f32[4,4,32,16]{3,2,1,0:T(8,128)S(1)} %get-tuple-element.49), kind=kLoop, calls=%fused_computation.3 | loop fusion | flops 3670016 | bytes 2164736 | tf_op jit(solution)/shard_map/reduce_sum | solution.py:130
  60.7 0.2 multiply_add_fusion
  60.9 1.0 %convolution_bitcast_fusion = f32[4,8,128]{2,1,0:T(8,128)S(1)} fusion(bf16[4,8,32,16]{2,1,3,0:T(8,128)(2,1)S(1)} %bitcast.75, f32[4,32,16,128]{3,2,1,0:T(8,128)S(1)} %multiply_add_fusion), kind=kOutput, calls=%fused_computation.22 | convolution fusion | flops 25165824 | bytes 1097728 | tf_op jit(solution)/shard_map/pxyl,pnxy->pnl/dot_general | solution.py:140
  61.9 0.2 reshape.201
  62.2 0.9 %copy.37 = f32[32,2,4]{2,1,0:T(2,128)} copy(f32[32,2,4]{1,0,2:T(8,128)S(1)} %reshape_reshape.3) | data formatting | bytes 2048 | tf_op jit(solution)/shard_map/reshape;reshape | solution.py:144
  63.2 10.7 %all-to-all-start = ((f32[32,2,4]{2,1,0:T(2,128)}), f32[32,2,4]{2,1,0:T(2,128)S(1)}, u32[]{:S(2)}, u32[]{:S(2)}) async-start(f32[32,2,4]{2,1,0:T(2,128)} %copy.37), calls=%async_computation | async-start | bytes 65536 | tf_op jit(solution)/shard_map/all_to_all | solution.py:145
  73.9 0.9 %pad_maximum_fusion.1 = f32[3,32,16,128]{3,2,1,0:T(8,128)} fusion(f32[1,32,16,128]{3,2,1,0:T(8,128)S(1)} %slice_bitcast_fusion.11, f32[1,32,16,128]{3,2,1,0:T(8,128)S(1)} %get-tuple-element.48, f32[1,32,16,128]{3,2,1,0:T(8,128)S(1)} %get-tuple-element.46), kind=kLoop, calls=%fused_computation.79 | loop fusion | flops 393216 | bytes 1572864 | tf_op jit(solution)/shard_map/stack | solution.py:146
  74.8 1.9 %pad_maximum_fusion = f32[3,32,16,128]{3,2,1,0:T(8,128)} fusion(f32[1,32,16,128]{3,2,1,0:T(8,128)S(1)} %get-tuple-element.47, f32[1,32,16,128]{3,2,1,0:T(8,128)} %get-tuple-element.23, f32[1,32,16,128]{3,2,1,0:T(8,128)S(1)} %get-tuple-element.25), kind=kLoop, calls=%fused_computation.78 | loop fusion | flops 393216 | bytes 1572864 | tf_op jit(solution)/shard_map/stack | solution.py:146
  76.7 4.6 %all-to-all-done = f32[32,2,4]{2,1,0:T(2,128)S(1)} async-done(((f32[32,2,4]{2,1,0:T(2,128)}), f32[32,2,4]{2,1,0:T(2,128)S(1)}, u32[]{:S(2)}, u32[]{:S(2)}) %all-to-all-start) | async-done | bytes 1056 | tf_op jit(solution)/shard_map/all_to_all | solution.py:145
  81.3 0.1 copy.44
  81.4 0.7 copy.40
  (44 shorter events, 1.0 us)
Async XLA Ops:
  0.6 5.9 %copy-start = (bf16[4,2,4,256,64]{3,4,2,1,0:T(8,128)(2,1)S(1)}, bf16[4,2,4,256,64]{3,4,2,1,0:T(8,128)(2,1)}, u32[]{:S(2)}) copy-start(bf16[4,2,4,256,64]{3,4,2,1,0:T(8,128)(2,1)} %param.13) | copy-start | bytes 3145732
  0.6 22.4 %copy-start.6 = (f32[32,16,128]{2,1,0:T(8,128)S(1)}, f32[32,16,128]{2,1,0:T(8,128)}, u32[]{:S(2)}) copy-start(f32[32,16,128]{2,1,0:T(8,128)} %param.9) | copy-start | bytes 786436
  0.7 22.4 %copy-start.4 = (f32[3,32,16,128]{3,2,1,0:T(8,128)S(1)}, f32[3,32,16,128]{3,2,1,0:T(8,128)}, u32[]{:S(2)}) copy-start(f32[3,32,16,128]{3,2,1,0:T(8,128)} %param.7) | copy-start | bytes 2359300
  0.7 22.4 %copy-start.3 = (f32[3,32,16,128]{3,2,1,0:T(8,128)S(1)}, f32[3,32,16,128]{3,2,1,0:T(8,128)}, u32[]{:S(2)}) copy-start(f32[3,32,16,128]{3,2,1,0:T(8,128)} %param.8) | copy-start | bytes 2359300
  1.8 4.9 %collective-permute-start = (f32[7,2,16,128]{3,2,1,0:T(8,128)S(1)}, f32[7,2,16,128]{3,2,1,0:T(8,128)S(1)}, u32[]{:S(2)}, u32[]{:S(2)}) collective-permute-start(f32[7,2,16,128]{3,2,1,0:T(8,128)S(1)} %get-tuple-element.35), channel_id=1, source_target_pairs={{0,32},{32,64},{64,96},{96,128},{128,160},{160,192},{192,224},{1,3... | collective-permute-start | bytes 344072 | tf_op jit(solution)/shard_map/ppermute | solution.py:21
  3.5 4.5 %collective-permute-start.1 = (f32[7,2,16,128]{3,2,1,0:T(8,128)S(1)}, f32[7,2,16,128]{3,2,1,0:T(8,128)S(1)}, u32[]{:S(2)}, u32[]{:S(2)}) collective-permute-start(f32[7,2,16,128]{3,2,1,0:T(8,128)S(1)} %get-tuple-element.36), channel_id=1, source_target_pairs={{32,0},{64,32},{96,64},{128,96},{160,128},{192,160},{224,192},{33,... | collective-permute-start | bytes 344072 | tf_op jit(solution)/shard_map/ppermute | solution.py:21
  10.5 7.9 %collective-permute-start.2 = (f32[7,36,2,128]{3,2,1,0:T(2,128)}, f32[7,36,2,128]{3,2,1,0:T(2,128)S(1)}, u32[]{:S(2)}, u32[]{:S(2)}) collective-permute-start(f32[7,36,2,128]{3,2,1,0:T(2,128)} %get-tuple-element.33), channel_id=1, source_target_pairs={{0,8},{8,16},{16,24},{1,9},{9,17},{17,25},{2,10},{10,18},{18,26},{... | collective-permute-start | bytes 774152 | tf_op jit(solution)/shard_map/ppermute | solution.py:21
  14.0 9.1 %collective-permute-start.3 = (f32[7,36,2,128]{3,2,1,0:T(2,128)}, f32[7,36,2,128]{3,2,1,0:T(2,128)}, u32[]{:S(2)}, u32[]{:S(2)}) collective-permute-start(f32[7,36,2,128]{3,2,1,0:T(2,128)} %get-tuple-element.34), channel_id=1, source_target_pairs={{8,0},{16,8},{24,16},{9,1},{17,9},{25,17},{10,2},{18,10},{26,18},{... | collective-permute-start | bytes 774152 | tf_op jit(solution)/shard_map/ppermute | solution.py:21
  25.5 1.6 %copy-start.1 = (f32[7,36,24,128]{3,2,1,0:T(8,128)}, f32[7,36,24,128]{3,2,1,0:T(8,128)S(1)}, u32[]{:S(2)}) copy-start(f32[7,36,24,128]{3,2,1,0:T(8,128)S(1)} %select_maximum_fusion) | copy-start | bytes 9289732
  28.7 7.6 %collective-permute-start.4 = (f32[2,6048]{1,0:T(2,128)S(1)}, f32[2,6048]{1,0:T(2,128)S(1)}, u32[]{:S(2)}, u32[]{:S(2)}) collective-permute-start(f32[2,6048]{1,0:T(2,128)S(1)} %get-tuple-element.55), channel_id=1, source_target_pairs={{0,1},{1,2},{2,3},{3,4},{4,5},{5,6},{6,7},{8,9},{9,10},{10,11},{11... | collective-permute-start | bytes 145160 | tf_op jit(solution)/shard_map/ppermute | solution.py:21
  33.7 7.2 %collective-permute-start.5 = (f32[2,6048]{1,0:T(2,128)S(1)}, f32[2,6048]{1,0:T(2,128)S(1)}, u32[]{:S(2)}, u32[]{:S(2)}) collective-permute-start(f32[2,6048]{1,0:T(2,128)S(1)} %get-tuple-element.56), channel_id=1, source_target_pairs={{1,0},{2,1},{3,2},{4,3},{5,4},{6,5},{7,6},{9,8},{10,9},{11,10},{12... | collective-permute-start | bytes 145160 | tf_op jit(solution)/shard_map/ppermute | solution.py:21
  40.9 2.7 %copy-start.2 = (f32[7,36,24,128]{3,2,1,0:T(8,128)S(1)}, f32[7,36,24,128]{3,2,1,0:T(8,128)}, u32[]{:S(2)}) copy-start(f32[7,36,24,128]{3,2,1,0:T(8,128)} %copy-done.1) | copy-start | bytes 9289732
  55.8 4.9 %copy-start.7 = (f32[4,32,16,128]{3,2,1,0:T(8,128)S(1)}, f32[4,32,16,128]{3,2,1,0:T(8,128)}, u32[]{:S(2)}) copy-start(f32[4,32,16,128]{3,2,1,0:T(8,128)} %param.10) | copy-start | bytes 3145732
  60.9 21.2 %copy-start.5 = (f32[4,32,16,128]{3,2,1,0:T(8,128)}, f32[4,32,16,128]{3,2,1,0:T(8,128)S(1)}, u32[]{:S(2)}) copy-start(f32[4,32,16,128]{3,2,1,0:T(8,128)S(1)} %multiply_add_fusion) | copy-start | bytes 3145732
  63.2 18.1 %all-to-all-start = ((f32[32,2,4]{2,1,0:T(2,128)}), f32[32,2,4]{2,1,0:T(2,128)S(1)}, u32[]{:S(2)}, u32[]{:S(2)}) async-start(f32[32,2,4]{2,1,0:T(2,128)} %copy.37), calls=%async_computation | async-start | bytes 65536 | tf_op jit(solution)/shard_map/all_to_all | solution.py:145

commit v12 on v10

--- a/solution.py
+++ b/solution.py
@@ -92,8 +92,8 @@
     cells_x, cells_y, cells_z = cells
     ports_here = dft_sums.shape[0]
     stack = jnp.concatenate([e_field, h_field, inv_permittivity[None]], axis=0)
-    stack = pin(widen(stack, 1, "gx"))
-    stack = widen(stack, 2, "gy")
+    stack = pin(widen(stack, 2, "gy"))
+    stack = widen(stack, 1, "gx")
     spare = -stack.shape[2] % 8
     stack = pin(jnp.pad(stack, ((0, 0), (0, 0), (0, spare), (0, 0))))
     stack = pin(widen_lanes(stack, "gz"))

time: 79.8 us -> 79.7 us (level)
  waiting for transfers between devices: 17.1 us -> 18.5 us
  starting transfers between devices: 25.7 us -> 24.6 us
    ppermute x6, waiting for transfers between devices: 12.5 us -> 14 us  [shifted(): lax.ppermute(value, axis, [(source, source + steps) for source in range(f...]
    all_to_all x1, starting transfers between devices: 10.7 us -> 9.42 us  [per_device(): lax.all_to_all(pieces, ('gx', 'gy'), 0, 0, tiled=False)]
  transfers between devices with their start and end apart: 7 -> 7, of which waited for: 5 -> 5; matrix products, arithmetic and copies ran while one was open for 8% -> 6% of each run, Pallas kernels for 0% -> 0%
where the time goes in v12:
time: 79.7 us; the launch traced here: 79 us
  starting transfers between devices  24.6 us (31%)
  other arithmetic  20.3 us (25%)
  waiting for transfers between devices  18.5 us (23%)
  matrix products  8.02 us (10%)
  local copies, waits for them, and re-layouts  6.51 us (8%)
  between operations  1.04 us (1%)
    ppermute x6, starting transfers between devices, shifted(): lax.ppermute(value, axis, [(source, source + steps) for source in range(f...  15.1 us
    ppermute x6, waiting for transfers between devices, shifted(): lax.ppermute(value, axis, [(source, source + steps) for source in range(f...  14 us
    all_to_all x1, starting transfers between devices, per_device(): lax.all_to_all(pieces, ('gx', 'gy'), 0, 0, tiled=False)  9.42 us
    all_to_all x1, waiting for transfers between devices, per_device(): lax.all_to_all(pieces, ('gx', 'gy'), 0, 0, tiled=False)  4.57 us
    slice x2, other arithmetic, widen(): high = lax.slice_in_dim(stack, count - HALO, count, axis=dim)  4.26 us
    dot_general x1, matrix products, widen_lanes(): jnp.dot(flat, move, precision=lax.Precision.HIGHEST)  2.85 us
    dot_general x1, matrix products, widen_lanes(): jnp.einsum('kr,kl->rl', ghosts, place, precision=lax.Precision.HIGHEST)  2.69 us
    mul x2, other arithmetic, per_device(): planes[..., None] * spread_of[None, :, None, None, :]  2.66 us
  transfers between devices with their start and end apart: 7, of which 5 were waited for; matrix products, arithmetic and copies ran while one was open for 6% of the time, Pallas kernels for 0%

profile of v12, /device:TPU:96, one launch (start us, length us, event | category | flops | bytes accessed | tf_op | source)
XLA Modules:
  0.0 79.0 jit_solution(13407470016860354778)
XLA Ops:
  0.7 2.6 %pad_maximum_fusion.6 = (f32[7,32,2,128]{3,2,1,0:T(2,128)}, f32[7,32,2,128]{3,2,1,0:T(2,128)}) fusion(f32[1,32,16,128]{3,2,1,0:T(8,128)} %bitcast.62, f32[3,32,16,128]{3,2,1,0:T(8,128)} %param.8, f32[3,32,16,128]{3,2,1,0:T(8,128)} %param.7), kind=kLoop, calls=%fused_computation.119 | loop fusion | flops 229376 | bytes 2293760 | tf_op jit(solution)/shard_map/slice | solution.py:27
  3.3 3.5 %collective-permute-start = (f32[7,32,2,128]{3,2,1,0:T(2,128)}, f32[7,32,2,128]{3,2,1,0:T(2,128)S(1)}, u32[]{:S(2)}, u32[]{:S(2)}) collective-permute-start(f32[7,32,2,128]{3,2,1,0:T(2,128)} %get-tuple-element.31), channel_id=1, source_target_pairs={{0,8},{8,16},{16,24},{1,9},{9,17},{17,25},{2,10},{10,18},{18,26},{... | collective-permute-start | bytes 688136 | tf_op jit(solution)/shard_map/ppermute | solution.py:21
  6.7 1.3 %collective-permute-start.1 = (f32[7,32,2,128]{3,2,1,0:T(2,128)}, f32[7,32,2,128]{3,2,1,0:T(2,128)S(1)}, u32[]{:S(2)}, u32[]{:S(2)}) collective-permute-start(f32[7,32,2,128]{3,2,1,0:T(2,128)} %get-tuple-element.32), channel_id=1, source_target_pairs={{8,0},{16,8},{24,16},{9,1},{17,9},{25,17},{10,2},{18,10},{26,18},{... | collective-permute-start | bytes 688136 | tf_op jit(solution)/shard_map/ppermute | solution.py:21
  8.1 0.7 cosine_bitcast_fusion.1
  8.9 0.7 broadcast_subtract_fusion
  9.8 2.0 %collective-permute-done = f32[7,32,2,128]{3,2,1,0:T(2,128)S(1)} collective-permute-done((f32[7,32,2,128]{3,2,1,0:T(2,128)}, f32[7,32,2,128]{3,2,1,0:T(2,128)S(1)}, u32[]{:S(2)}, u32[]{:S(2)}) %collective-permute-start) | collective-permute-done | bytes 229408 | tf_op jit(solution)/shard_map/ppermute | solution.py:21
  11.9 4.0 %collective-permute-done.1 = f32[7,32,2,128]{3,2,1,0:T(2,128)S(1)} collective-permute-done((f32[7,32,2,128]{3,2,1,0:T(2,128)}, f32[7,32,2,128]{3,2,1,0:T(2,128)S(1)}, u32[]{:S(2)}, u32[]{:S(2)}) %collective-permute-start.1) | collective-permute-done | bytes 229408 | tf_op jit(solution)/shard_map/ppermute | solution.py:21
  15.9 1.7 %pad_maximum_fusion.11 = (f32[7,2,20,128]{3,2,1,0:T(8,128)}, f32[7,2,20,128]{3,2,1,0:T(8,128)}) fusion(f32[7,32,2,128]{3,2,1,0:T(2,128)S(1)} %collective-permute-done.1, f32[7,32,2,128]{3,2,1,0:T(2,128)S(1)} %collective-permute-done, f32[1,32,16,128]{3,2,1,0:T(8,128)} %bitcast.63, f32[3,32,16,128]{3,2,1,0:T(8,128)} %param.8, f32[3,32,16,128]{3,2,1,0:T(8,128)} %param.7), kind=kLoop, calls=%fused_computation.124 | loop fusion | flops 286720 | bytes 2580480 | tf_op jit(solution)/shard_map/slice | solution.py:27
  17.6 2.0 %collective-permute-start.2 = (f32[7,2,20,128]{3,2,1,0:T(8,128)}, f32[7,2,20,128]{3,2,1,0:T(8,128)}, u32[]{:S(2)}, u32[]{:S(2)}) collective-permute-start(f32[7,2,20,128]{3,2,1,0:T(8,128)} %get-tuple-element.29), channel_id=1, source_target_pairs={{0,32},{32,64},{64,96},{96,128},{128,160},{160,192},{192,224},{1,3... | collective-permute-start | bytes 430088 | tf_op jit(solution)/shard_map/ppermute | solution.py:21
  19.5 1.3 %collective-permute-start.3 = (f32[7,2,20,128]{3,2,1,0:T(8,128)}, f32[7,2,20,128]{3,2,1,0:T(8,128)}, u32[]{:S(2)}, u32[]{:S(2)}) collective-permute-start(f32[7,2,20,128]{3,2,1,0:T(8,128)} %get-tuple-element.30), channel_id=1, source_target_pairs={{32,0},{64,32},{96,64},{128,96},{160,128},{192,160},{224,192},{33,... | collective-permute-start | bytes 430088 | tf_op jit(solution)/shard_map/ppermute | solution.py:21
  20.9 0.1 constant_dynamic-slice_fusion
  21.0 3.3 %collective-permute-done.3 = f32[7,2,20,128]{3,2,1,0:T(8,128)} collective-permute-done((f32[7,2,20,128]{3,2,1,0:T(8,128)}, f32[7,2,20,128]{3,2,1,0:T(8,128)}, u32[]{:S(2)}, u32[]{:S(2)}) %collective-permute-start.3) | collective-permute-done | bytes 143392 | tf_op jit(solution)/shard_map/ppermute | solution.py:21
  24.3 2.4 %select_maximum_fusion = f32[7,36,24,128]{3,2,1,0:T(8,128)S(1)} fusion(f32[7,2,20,128]{3,2,1,0:T(8,128)} %collective-permute-done.3, f32[7,2,20,128]{3,2,1,0:T(8,128)} %collective-permute-done.2, f32[7,32,2,128]{3,2,1,0:T(2,128)S(1)} %collective-permute-done.1, f32[7,32,2,128]{3,2,1,0:T(2,128)S(1)} %collective-permute-done, ...), kind=kLoop, calls=%fused_computation.9 | loop fusion | flops 10838016 | bytes 5677056 | tf_op jit(solution)/shard_map/concatenate | solution.py:30
  26.7 1.6 %copy-done.1 = f32[7,36,24,128]{3,2,1,0:T(8,128)} copy-done((f32[7,36,24,128]{3,2,1,0:T(8,128)}, f32[7,36,24,128]{3,2,1,0:T(8,128)S(1)}, u32[]{:S(2)}) %copy-start.1) | copy-done | bytes 3096600
  28.3 1.5 %fusion.64 = f32[4,6048]{1,0:T(4,128)S(1)} fusion(f32[6048,128]{1,0:T(8,128)S(1)} %bitcast.59, s32[4]{0:T(128)S(1)} %get-tuple-element.57), kind=kOutput, calls=%fused_computation.142 | convolution fusion | flops 37159424 | bytes 3193360 | tf_op jit(solution)/shard_map/kz,rz->kr/dot_general | solution.py:39
  29.9 5.0 %collective-permute-start.4 = (f32[2,6048]{1,0:T(2,128)S(1)}, f32[2,6048]{1,0:T(2,128)S(1)}, u32[]{:S(2)}, u32[]{:S(2)}) collective-permute-start(f32[2,6048]{1,0:T(2,128)S(1)} %get-tuple-element.50), channel_id=1, source_target_pairs={{0,1},{1,2},{2,3},{3,4},{4,5},{5,6},{6,7},{8,9},{9,10},{10,11},{11... | collective-permute-start | bytes 145160 | tf_op jit(solution)/shard_map/ppermute | solution.py:21
  34.9 2.1 %collective-permute-start.5 = (f32[2,6048]{1,0:T(2,128)S(1)}, f32[2,6048]{1,0:T(2,128)S(1)}, u32[]{:S(2)}, u32[]{:S(2)}) collective-permute-start(f32[2,6048]{1,0:T(2,128)S(1)} %get-tuple-element.51), channel_id=1, source_target_pairs={{1,0},{2,1},{3,2},{4,3},{5,4},{6,5},{7,6},{9,8},{10,9},{11,10},{12... | collective-permute-start | bytes 145160 | tf_op jit(solution)/shard_map/ppermute | solution.py:21
  37.1 0.1 tile.14
  37.1 0.1 mul.185
  37.2 0.1 tile.16
  37.3 0.1 mul.193
  37.5 4.7 %collective-permute-done.5 = f32[2,6048]{1,0:T(2,128)S(1)} collective-permute-done((f32[2,6048]{1,0:T(2,128)S(1)}, f32[2,6048]{1,0:T(2,128)S(1)}, u32[]{:S(2)}, u32[]{:S(2)}) %collective-permute-start.5) | collective-permute-done | bytes 48416 | tf_op jit(solution)/shard_map/ppermute | solution.py:21
  42.1 2.7 %fusion.57 = f32[6048,132]{1,0:T(8,128)S(1)} fusion(f32[2,6048]{1,0:T(2,128)S(1)} %collective-permute-done.5, f32[2,6048]{1,0:T(2,128)S(1)} %collective-permute-done.4, s32[4]{0:T(128)S(1)} %get-tuple-element.56), kind=kOutput, calls=%fused_computation.126 | convolution fusion | flops 38344848 | bytes 3290128 | tf_op jit(solution)/shard_map/kr,kl->rl/dot_general | solution.py:47
  44.8 2.8 %convolution_add_fusion = f32[6048,132]{1,0:T(8,128)S(1)} fusion(f32[6048,132]{1,0:T(8,128)S(1)} %fusion.57, f32[6048,128]{1,0:T(8,128)S(1)} %bitcast.60, s32[128]{0:T(128)S(1)} %iota_add_fusion.2), kind=kOutput, calls=%fused_computation.2 | convolution fusion | flops 1227059328 | bytes 9483776 | tf_op jit(solution)/shard_map/dot_general | solution.py:47
  47.7 0.6 slice_bitcast_fusion.2
  48.3 1.1 %and_select_fusion.1 = (f32[35,19,131]{2,1,0:T(8,128)S(1)}, f32[35,19,131]{2,1,0:T(8,128)S(1)}, f32[35,19,131]{2,1,0:T(8,128)S(1)}) fusion(f32[36,24,132]{2,1,0:T(8,128)S(1)} %get-tuple-element.23, f32[36,24,132]{2,1,0:T(8,128)S(1)} %get-tuple-element.27, f32[36,24,132]{2,1,0:T(8,128)S(1)} %get-tuple-element.22, pred[131]{0:T(512)(128)(4,1)S(1)} %compare_and_fusion.3, ...), kind=kLoop, calls=%fused_computation.26 | loop fusion | flops 1655185 | bytes 5227696 | tf_op jit(solution)/shard_map/mul | solution.py:106
  49.3 0.1 slice_bitcast_fusion.7
  49.5 0.1 slice_bitcast_fusion.8
  49.6 2.6 %fusion.35 = (f32[34,18,130]{2,1,0:T(8,128)S(1)}, f32[34,18,130]{2,1,0:T(8,128)S(1)}, f32[34,18,130]{2,1,0:T(8,128)S(1)}) fusion(f32[35,19,131]{2,1,0:T(8,128)S(1)} %get-tuple-element.39, f32[35,19,131]{2,1,0:T(8,128)S(1)} %get-tuple-element.40, f32[36,24,132]{2,1,0:T(8,128)S(1)} %get-tuple-element.27, f32[36,24,132]{2,1,0:T(8,128)S(1)} %get-tuple-element.26, ...), kind=kLoop, calls=%fused_computation.71 | loop fusion | flops 1272960 | bytes 5091840 | tf_op jit(solution)/shard_map/add | solution.py:108
  52.2 0.1 slice_bitcast_fusion.10
  52.4 1.4 %and_select_fusion.5 = (f32[33,17,129]{2,1,0:T(8,128)S(1)}, f32[33,17,129]{2,1,0:T(8,128)S(1)}, f32[33,17,129]{2,1,0:T(8,128)S(1)}) fusion(f32[34,18,130]{2,1,0:T(8,128)S(1)} %get-tuple-element.33, f32[34,18,130]{2,1,0:T(8,128)S(1)} %get-tuple-element.34, f32[35,19,131]{2,1,0:T(8,128)S(1)} %get-tuple-element.40, pred[129]{0:T(512)(128)(4,1)S(1)} %compare_and_fusion, ...), kind=kLoop, calls=%fused_computation.30 | loop fusion | flops 1375011 | bytes 4342830 | tf_op jit(solution)/shard_map/mul | solution.py:110
  53.7 0.1 slice_bitcast_fusion.11
  53.9 0.1 slice_bitcast_fusion.12
  54.0 0.9 %fusion.56 = (f32[1,32,16,128]{3,2,1,0:T(8,128)S(1)}, f32[1,32,16,128]{3,2,1,0:T(8,128)S(1)}, f32[1,32,16,128]{3,2,1,0:T(8,128)S(1)}, f32[1,32,16,128]{3,2,1,0:T(8,128)S(1)}) fusion(f32[33,17,129]{2,1,0:T(8,128)S(1)} %get-tuple-element.44, f32[33,17,129]{2,1,0:T(8,128)S(1)} %get-tuple-element.42, f32[34,18,130]{2,1,0:T(8,128)S(1)} %get-tuple-element.33, ...), kind=kLoop, calls=%fused_computation.109 | loop fusion | flops 1048576 | bytes 4456448 | tf_op jit(solution)/shard_map/stack | solution.py:144
  55.0 1.1 %slice_bitcast_fusion.13 = f32[1,32,16,128]{3,2,1,0:T(8,128)} fusion(f32[33,17,129]{2,1,0:T(8,128)S(1)} %get-tuple-element.42), kind=kLoop, calls=%fused_computation.116 | loop fusion | bytes 524288 | tf_op jit(solution)/shard_map/stack | solution.py:144
  56.1 1.2 %fusion = f32[4,4,32,16,128]{4,3,2,1,0:T(8,128)S(1)} fusion(f32[4,32,16,128]{3,2,1,0:T(8,128)S(1)} %pad_maximum_fusion.1, f32[4,128]{1,0:T(4,128)S(1)} %get-tuple-element.60), kind=kOutput, calls=%fused_computation | output fusion | flops 1056895 | bytes 5244928 | tf_op jit(solution)/shard_map/mul | solution.py:128
  57.4 1.5 %multiply_reduce_fusion.2 = (f32[4,32,16,128]{3,2,1,0:T(8,128)S(1)}, f32[4,32,16,128]{3,2,1,0:T(8,128)S(1)}) fusion(f32[4,128]{1,0:T(4,128)S(1)} %get-tuple-element.61, f32[4,4,32,16,128]{4,3,2,1,0:T(8,128)S(1)} %fusion, f32[4,128]{1,0:T(4,128)S(1)} %get-tuple-element.60, f32[4,32,16,128]{3,2,1,0:T(8,128)S(1)} %pad_maximum_fusion), kind=kOutput, calls=%fused_computation.6 | output fusion | flops 4726911 | bytes 7344128 | tf_op jit(solution)/shard_map/mul | solution.py:128
  58.9 0.2 multiply_add_fusion
  59.1 1.0 %convolution_bitcast_fusion = f32[4,8,128]{2,1,0:T(8,128)S(1)} fusion(bf16[4,8,32,16]{2,1,3,0:T(8,128)(2,1)S(1)} %bitcast.65, f32[4,32,16,128]{3,2,1,0:T(8,128)S(1)} %multiply_add_fusion), kind=kOutput, calls=%fused_computation.31 | convolution fusion | flops 25165824 | bytes 1097728 | tf_op jit(solution)/shard_map/pxyl,pnxy->pnl/dot_general | solution.py:138
  60.1 0.2 reshape.202
  60.4 0.1 reshape_reshape.3
  60.5 0.9 %copy.37 = f32[32,2,4]{2,1,0:T(2,128)} copy(f32[32,2,4]{1,0,2:T(8,128)S(1)} %reshape_reshape.3) | data formatting | bytes 2048 | tf_op jit(solution)/shard_map/reshape;reshape | solution.py:142
  61.4 9.4 %all-to-all-start = ((f32[32,2,4]{2,1,0:T(2,128)}), f32[32,2,4]{2,1,0:T(2,128)S(1)}, u32[]{:S(2)}, u32[]{:S(2)}) async-start(f32[32,2,4]{2,1,0:T(2,128)} %copy.37), calls=%async_computation | async-start | bytes 65536 | tf_op jit(solution)/shard_map/all_to_all | solution.py:143
  70.8 1.9 %pad_maximum_fusion.3 = f32[3,32,16,128]{3,2,1,0:T(8,128)} fusion(f32[1,32,16,128]{3,2,1,0:T(8,128)} %slice_bitcast_fusion.13, f32[1,32,16,128]{3,2,1,0:T(8,128)S(1)} %slice_bitcast_fusion.12, f32[1,32,16,128]{3,2,1,0:T(8,128)S(1)} %slice_bitcast_fusion.11), kind=kLoop, calls=%fused_computation.90 | loop fusion | flops 393216 | bytes 1572864 | tf_op jit(solution)/shard_map/stack | solution.py:144
  72.7 0.9 %pad_maximum_fusion.2 = f32[3,32,16,128]{3,2,1,0:T(8,128)} fusion(f32[1,32,16,128]{3,2,1,0:T(8,128)S(1)} %get-tuple-element.38, f32[1,32,16,128]{3,2,1,0:T(8,128)S(1)} %get-tuple-element.37, f32[1,32,16,128]{3,2,1,0:T(8,128)S(1)} %get-tuple-element.36), kind=kLoop, calls=%fused_computation.89 | loop fusion | flops 393216 | bytes 1572864 | tf_op jit(solution)/shard_map/stack | solution.py:144
  73.6 4.6 %all-to-all-done = f32[32,2,4]{2,1,0:T(2,128)S(1)} async-done(((f32[32,2,4]{2,1,0:T(2,128)}), f32[32,2,4]{2,1,0:T(2,128)S(1)}, u32[]{:S(2)}, u32[]{:S(2)}) %all-to-all-start) | async-done | bytes 1056 | tf_op jit(solution)/shard_map/all_to_all | solution.py:143
  78.2 0.1 copy.44
  78.3 0.7 copy.40
  (41 shorter events, 0.8 us)
Async XLA Ops:
  0.6 20.2 %copy-start = (bf16[4,2,4,256,64]{3,4,2,1,0:T(8,128)(2,1)S(1)}, bf16[4,2,4,256,64]{3,4,2,1,0:T(8,128)(2,1)}, u32[]{:S(2)}) copy-start(bf16[4,2,4,256,64]{3,4,2,1,0:T(8,128)(2,1)} %param.13) | copy-start | bytes 3145732
  0.6 23.6 %copy-start.6 = (f32[32,16,128]{2,1,0:T(8,128)S(1)}, f32[32,16,128]{2,1,0:T(8,128)}, u32[]{:S(2)}) copy-start(f32[32,16,128]{2,1,0:T(8,128)} %param.9) | copy-start | bytes 786436
  0.7 23.6 %copy-start.4 = (f32[3,32,16,128]{3,2,1,0:T(8,128)S(1)}, f32[3,32,16,128]{3,2,1,0:T(8,128)}, u32[]{:S(2)}) copy-start(f32[3,32,16,128]{3,2,1,0:T(8,128)} %param.7) | copy-start | bytes 2359300
  0.7 23.6 %copy-start.3 = (f32[3,32,16,128]{3,2,1,0:T(8,128)S(1)}, f32[3,32,16,128]{3,2,1,0:T(8,128)}, u32[]{:S(2)}) copy-start(f32[3,32,16,128]{3,2,1,0:T(8,128)} %param.8) | copy-start | bytes 2359300
  3.3 8.6 %collective-permute-start = (f32[7,32,2,128]{3,2,1,0:T(2,128)}, f32[7,32,2,128]{3,2,1,0:T(2,128)S(1)}, u32[]{:S(2)}, u32[]{:S(2)}) collective-permute-start(f32[7,32,2,128]{3,2,1,0:T(2,128)} %get-tuple-element.31), channel_id=1, source_target_pairs={{0,8},{8,16},{16,24},{1,9},{9,17},{17,25},{2,10},{10,18},{18,26},{... | collective-permute-start | bytes 688136 | tf_op jit(solution)/shard_map/ppermute | solution.py:21
  6.7 9.2 %collective-permute-start.1 = (f32[7,32,2,128]{3,2,1,0:T(2,128)}, f32[7,32,2,128]{3,2,1,0:T(2,128)S(1)}, u32[]{:S(2)}, u32[]{:S(2)}) collective-permute-start(f32[7,32,2,128]{3,2,1,0:T(2,128)} %get-tuple-element.32), channel_id=1, source_target_pairs={{8,0},{16,8},{24,16},{9,1},{17,9},{25,17},{10,2},{18,10},{26,18},{... | collective-permute-start | bytes 688136 | tf_op jit(solution)/shard_map/ppermute | solution.py:21
  17.6 3.4 %collective-permute-start.2 = (f32[7,2,20,128]{3,2,1,0:T(8,128)}, f32[7,2,20,128]{3,2,1,0:T(8,128)}, u32[]{:S(2)}, u32[]{:S(2)}) collective-permute-start(f32[7,2,20,128]{3,2,1,0:T(8,128)} %get-tuple-element.29), channel_id=1, source_target_pairs={{0,32},{32,64},{64,96},{96,128},{128,160},{160,192},{192,224},{1,3... | collective-permute-start | bytes 430088 | tf_op jit(solution)/shard_map/ppermute | solution.py:21
  19.5 4.7 %collective-permute-start.3 = (f32[7,2,20,128]{3,2,1,0:T(8,128)}, f32[7,2,20,128]{3,2,1,0:T(8,128)}, u32[]{:S(2)}, u32[]{:S(2)}) collective-permute-start(f32[7,2,20,128]{3,2,1,0:T(8,128)} %get-tuple-element.30), channel_id=1, source_target_pairs={{32,0},{64,32},{96,64},{128,96},{160,128},{192,160},{224,192},{33,... | collective-permute-start | bytes 430088 | tf_op jit(solution)/shard_map/ppermute | solution.py:21
  26.7 1.6 %copy-start.1 = (f32[7,36,24,128]{3,2,1,0:T(8,128)}, f32[7,36,24,128]{3,2,1,0:T(8,128)S(1)}, u32[]{:S(2)}) copy-start(f32[7,36,24,128]{3,2,1,0:T(8,128)S(1)} %select_maximum_fusion) | copy-start | bytes 9289732
  29.9 7.6 %collective-permute-start.4 = (f32[2,6048]{1,0:T(2,128)S(1)}, f32[2,6048]{1,0:T(2,128)S(1)}, u32[]{:S(2)}, u32[]{:S(2)}) collective-permute-start(f32[2,6048]{1,0:T(2,128)S(1)} %get-tuple-element.50), channel_id=1, source_target_pairs={{0,1},{1,2},{2,3},{3,4},{4,5},{5,6},{6,7},{8,9},{9,10},{10,11},{11... | collective-permute-start | bytes 145160 | tf_op jit(solution)/shard_map/ppermute | solution.py:21
  34.9 7.2 %collective-permute-start.5 = (f32[2,6048]{1,0:T(2,128)S(1)}, f32[2,6048]{1,0:T(2,128)S(1)}, u32[]{:S(2)}, u32[]{:S(2)}) collective-permute-start(f32[2,6048]{1,0:T(2,128)S(1)} %get-tuple-element.51), channel_id=1, source_target_pairs={{1,0},{2,1},{3,2},{4,3},{5,4},{6,5},{7,6},{9,8},{10,9},{11,10},{12... | collective-permute-start | bytes 145160 | tf_op jit(solution)/shard_map/ppermute | solution.py:21
  42.1 2.7 %copy-start.2 = (f32[7,36,24,128]{3,2,1,0:T(8,128)S(1)}, f32[7,36,24,128]{3,2,1,0:T(8,128)}, u32[]{:S(2)}) copy-start(f32[7,36,24,128]{3,2,1,0:T(8,128)} %copy-done.1) | copy-start | bytes 9289732
  57.4 1.5 %copy-start.7 = (f32[4,32,16,128]{3,2,1,0:T(8,128)S(1)}, f32[4,32,16,128]{3,2,1,0:T(8,128)}, u32[]{:S(2)}) copy-start(f32[4,32,16,128]{3,2,1,0:T(8,128)} %param.10) | copy-start | bytes 3145732
  59.1 19.8 %copy-start.5 = (f32[4,32,16,128]{3,2,1,0:T(8,128)}, f32[4,32,16,128]{3,2,1,0:T(8,128)S(1)}, u32[]{:S(2)}) copy-start(f32[4,32,16,128]{3,2,1,0:T(8,128)S(1)} %multiply_add_fusion) | copy-start | bytes 3145732
  61.4 16.8 %all-to-all-start = ((f32[32,2,4]{2,1,0:T(2,128)}), f32[32,2,4]{2,1,0:T(2,128)S(1)}, u32[]{:S(2)}, u32[]{:S(2)}) async-start(f32[32,2,4]{2,1,0:T(2,128)} %copy.37), calls=%async_computation | async-start | bytes 65536 | tf_op jit(solution)/shard_map/all_to_all | solution.py:143

commit v13 on v12

--- a/solution.py
+++ b/solution.py
@@ -135,7 +135,7 @@
         mode_profiles, (0, 0, 0, start_x, start_y), (ports_here, MODES, 4, cells_x, cells_y)
     )
     weights = tile.reshape(ports_here, MODES * 4, cells_x, cells_y).astype(jnp.float32)
-    crossed = jnp.einsum("pxyl,pnxy->pnl", dft, weights, precision=lax.Precision.HIGHEST)
+    crossed = jnp.einsum("pxyl,pnxy->pnl", dft, weights, precision=lax.Precision.HIGH)
     crossed = crossed.reshape(ports_here, MODES, 4, 4, 2, NF)
     diagonal = sum(crossed[:, :, c, c] for c in range(4))
     partial_sums = jnp.transpose(diagonal, (0, 3, 1, 2)).reshape(ports_here * NF, MODES * 2)

time: 79.7 us -> 79.4 us (level)
  no operation moved by 1% of the time
where the time goes in v13:
time: 79.4 us; the launch traced here: 78.7 us
  starting transfers between devices  24.6 us (31%)
  other arithmetic  20.3 us (26%)
  waiting for transfers between devices  18.5 us (23%)
  matrix products  7.79 us (10%)
  local copies, waits for them, and re-layouts  6.51 us (8%)
  between operations  1.04 us (1%)
    ppermute x6, starting transfers between devices, shifted(): lax.ppermute(value, axis, [(source, source + steps) for source in range(f...  15.1 us
    ppermute x6, waiting for transfers between devices, shifted(): lax.ppermute(value, axis, [(source, source + steps) for source in range(f...  14 us
    all_to_all x1, starting transfers between devices, per_device(): lax.all_to_all(pieces, ('gx', 'gy'), 0, 0, tiled=False)  9.42 us
    all_to_all x1, waiting for transfers between devices, per_device(): lax.all_to_all(pieces, ('gx', 'gy'), 0, 0, tiled=False)  4.57 us
    slice x2, other arithmetic, widen(): high = lax.slice_in_dim(stack, count - HALO, count, axis=dim)  4.26 us
    dot_general x1, matrix products, widen_lanes(): jnp.dot(flat, move, precision=lax.Precision.HIGHEST)  2.85 us
    dot_general x1, matrix products, widen_lanes(): jnp.einsum('kr,kl->rl', ghosts, place, precision=lax.Precision.HIGHEST)  2.69 us
    mul x2, other arithmetic, per_device(): planes[..., None] * spread_of[None, :, None, None, :]  2.66 us
  transfers between devices with their start and end apart: 7, of which 5 were waited for; matrix products, arithmetic and copies ran while one was open for 6% of the time, Pallas kernels for 0%

profile of v13, /device:TPU:96, one launch (start us, length us, event | category | flops | bytes accessed | tf_op | source)
XLA Modules:
  0.0 78.7 jit_solution(1347553530859222563)
XLA Ops:
  0.7 2.6 %pad_maximum_fusion.6 = (f32[7,32,2,128]{3,2,1,0:T(2,128)}, f32[7,32,2,128]{3,2,1,0:T(2,128)}) fusion(f32[1,32,16,128]{3,2,1,0:T(8,128)} %bitcast.62, f32[3,32,16,128]{3,2,1,0:T(8,128)} %param.8, f32[3,32,16,128]{3,2,1,0:T(8,128)} %param.7), kind=kLoop, calls=%fused_computation.119 | loop fusion | flops 229376 | bytes 2293760 | tf_op jit(solution)/shard_map/slice | solution.py:27
  3.3 3.5 %collective-permute-start = (f32[7,32,2,128]{3,2,1,0:T(2,128)}, f32[7,32,2,128]{3,2,1,0:T(2,128)S(1)}, u32[]{:S(2)}, u32[]{:S(2)}) collective-permute-start(f32[7,32,2,128]{3,2,1,0:T(2,128)} %get-tuple-element.31), channel_id=1, source_target_pairs={{0,8},{8,16},{16,24},{1,9},{9,17},{17,25},{2,10},{10,18},{18,26},{... | collective-permute-start | bytes 688136 | tf_op jit(solution)/shard_map/ppermute | solution.py:21
  6.7 1.3 %collective-permute-start.1 = (f32[7,32,2,128]{3,2,1,0:T(2,128)}, f32[7,32,2,128]{3,2,1,0:T(2,128)S(1)}, u32[]{:S(2)}, u32[]{:S(2)}) collective-permute-start(f32[7,32,2,128]{3,2,1,0:T(2,128)} %get-tuple-element.32), channel_id=1, source_target_pairs={{8,0},{16,8},{24,16},{9,1},{17,9},{25,17},{10,2},{18,10},{26,18},{... | collective-permute-start | bytes 688136 | tf_op jit(solution)/shard_map/ppermute | solution.py:21
  8.1 0.7 cosine_bitcast_fusion.1
  8.9 0.7 broadcast_subtract_fusion
  9.8 2.0 %collective-permute-done = f32[7,32,2,128]{3,2,1,0:T(2,128)S(1)} collective-permute-done((f32[7,32,2,128]{3,2,1,0:T(2,128)}, f32[7,32,2,128]{3,2,1,0:T(2,128)S(1)}, u32[]{:S(2)}, u32[]{:S(2)}) %collective-permute-start) | collective-permute-done | bytes 229408 | tf_op jit(solution)/shard_map/ppermute | solution.py:21
  11.9 4.0 %collective-permute-done.1 = f32[7,32,2,128]{3,2,1,0:T(2,128)S(1)} collective-permute-done((f32[7,32,2,128]{3,2,1,0:T(2,128)}, f32[7,32,2,128]{3,2,1,0:T(2,128)S(1)}, u32[]{:S(2)}, u32[]{:S(2)}) %collective-permute-start.1) | collective-permute-done | bytes 229408 | tf_op jit(solution)/shard_map/ppermute | solution.py:21
  15.9 1.7 %pad_maximum_fusion.11 = (f32[7,2,20,128]{3,2,1,0:T(8,128)}, f32[7,2,20,128]{3,2,1,0:T(8,128)}) fusion(f32[7,32,2,128]{3,2,1,0:T(2,128)S(1)} %collective-permute-done.1, f32[7,32,2,128]{3,2,1,0:T(2,128)S(1)} %collective-permute-done, f32[1,32,16,128]{3,2,1,0:T(8,128)} %bitcast.63, f32[3,32,16,128]{3,2,1,0:T(8,128)} %param.8, f32[3,32,16,128]{3,2,1,0:T(8,128)} %param.7), kind=kLoop, calls=%fused_computation.124 | loop fusion | flops 286720 | bytes 2580480 | tf_op jit(solution)/shard_map/slice | solution.py:27
  17.6 2.0 %collective-permute-start.2 = (f32[7,2,20,128]{3,2,1,0:T(8,128)}, f32[7,2,20,128]{3,2,1,0:T(8,128)}, u32[]{:S(2)}, u32[]{:S(2)}) collective-permute-start(f32[7,2,20,128]{3,2,1,0:T(8,128)} %get-tuple-element.29), channel_id=1, source_target_pairs={{0,32},{32,64},{64,96},{96,128},{128,160},{160,192},{192,224},{1,3... | collective-permute-start | bytes 430088 | tf_op jit(solution)/shard_map/ppermute | solution.py:21
  19.5 1.3 %collective-permute-start.3 = (f32[7,2,20,128]{3,2,1,0:T(8,128)}, f32[7,2,20,128]{3,2,1,0:T(8,128)}, u32[]{:S(2)}, u32[]{:S(2)}) collective-permute-start(f32[7,2,20,128]{3,2,1,0:T(8,128)} %get-tuple-element.30), channel_id=1, source_target_pairs={{32,0},{64,32},{96,64},{128,96},{160,128},{192,160},{224,192},{33,... | collective-permute-start | bytes 430088 | tf_op jit(solution)/shard_map/ppermute | solution.py:21
  20.9 0.1 constant_dynamic-slice_fusion
  21.0 3.3 %collective-permute-done.3 = f32[7,2,20,128]{3,2,1,0:T(8,128)} collective-permute-done((f32[7,2,20,128]{3,2,1,0:T(8,128)}, f32[7,2,20,128]{3,2,1,0:T(8,128)}, u32[]{:S(2)}, u32[]{:S(2)}) %collective-permute-start.3) | collective-permute-done | bytes 143392 | tf_op jit(solution)/shard_map/ppermute | solution.py:21
  24.3 2.4 %select_maximum_fusion = f32[7,36,24,128]{3,2,1,0:T(8,128)S(1)} fusion(f32[7,2,20,128]{3,2,1,0:T(8,128)} %collective-permute-done.3, f32[7,2,20,128]{3,2,1,0:T(8,128)} %collective-permute-done.2, f32[7,32,2,128]{3,2,1,0:T(2,128)S(1)} %collective-permute-done.1, f32[7,32,2,128]{3,2,1,0:T(2,128)S(1)} %collective-permute-done, ...), kind=kLoop, calls=%fused_computation.9 | loop fusion | flops 10838016 | bytes 5677056 | tf_op jit(solution)/shard_map/concatenate | solution.py:30
  26.7 1.6 %copy-done.1 = f32[7,36,24,128]{3,2,1,0:T(8,128)} copy-done((f32[7,36,24,128]{3,2,1,0:T(8,128)}, f32[7,36,24,128]{3,2,1,0:T(8,128)S(1)}, u32[]{:S(2)}) %copy-start.1) | copy-done | bytes 3096600
  28.3 1.5 %fusion.64 = f32[4,6048]{1,0:T(4,128)S(1)} fusion(f32[6048,128]{1,0:T(8,128)S(1)} %bitcast.59, s32[4]{0:T(128)S(1)} %get-tuple-element.57), kind=kOutput, calls=%fused_computation.142 | convolution fusion | flops 37159424 | bytes 3193360 | tf_op jit(solution)/shard_map/kz,rz->kr/dot_general | solution.py:39
  29.9 5.0 %collective-permute-start.4 = (f32[2,6048]{1,0:T(2,128)S(1)}, f32[2,6048]{1,0:T(2,128)S(1)}, u32[]{:S(2)}, u32[]{:S(2)}) collective-permute-start(f32[2,6048]{1,0:T(2,128)S(1)} %get-tuple-element.50), channel_id=1, source_target_pairs={{0,1},{1,2},{2,3},{3,4},{4,5},{5,6},{6,7},{8,9},{9,10},{10,11},{11... | collective-permute-start | bytes 145160 | tf_op jit(solution)/shard_map/ppermute | solution.py:21
  34.9 2.1 %collective-permute-start.5 = (f32[2,6048]{1,0:T(2,128)S(1)}, f32[2,6048]{1,0:T(2,128)S(1)}, u32[]{:S(2)}, u32[]{:S(2)}) collective-permute-start(f32[2,6048]{1,0:T(2,128)S(1)} %get-tuple-element.51), channel_id=1, source_target_pairs={{1,0},{2,1},{3,2},{4,3},{5,4},{6,5},{7,6},{9,8},{10,9},{11,10},{12... | collective-permute-start | bytes 145160 | tf_op jit(solution)/shard_map/ppermute | solution.py:21
  37.1 0.1 tile.14
  37.1 0.1 mul.185
  37.2 0.1 tile.16
  37.3 0.1 mul.193
  37.5 4.7 %collective-permute-done.5 = f32[2,6048]{1,0:T(2,128)S(1)} collective-permute-done((f32[2,6048]{1,0:T(2,128)S(1)}, f32[2,6048]{1,0:T(2,128)S(1)}, u32[]{:S(2)}, u32[]{:S(2)}) %collective-permute-start.5) | collective-permute-done | bytes 48416 | tf_op jit(solution)/shard_map/ppermute | solution.py:21
  42.1 2.7 %fusion.57 = f32[6048,132]{1,0:T(8,128)S(1)} fusion(f32[2,6048]{1,0:T(2,128)S(1)} %collective-permute-done.5, f32[2,6048]{1,0:T(2,128)S(1)} %collective-permute-done.4, s32[4]{0:T(128)S(1)} %get-tuple-element.56), kind=kOutput, calls=%fused_computation.126 | convolution fusion | flops 38344848 | bytes 3290128 | tf_op jit(solution)/shard_map/kr,kl->rl/dot_general | solution.py:47
  44.8 2.8 %convolution_add_fusion = f32[6048,132]{1,0:T(8,128)S(1)} fusion(f32[6048,132]{1,0:T(8,128)S(1)} %fusion.57, f32[6048,128]{1,0:T(8,128)S(1)} %bitcast.60, s32[128]{0:T(128)S(1)} %iota_add_fusion.2), kind=kOutput, calls=%fused_computation.2 | convolution fusion | flops 1227059328 | bytes 9483776 | tf_op jit(solution)/shard_map/dot_general | solution.py:47
  47.7 0.6 slice_bitcast_fusion.2
  48.3 1.1 %and_select_fusion.1 = (f32[35,19,131]{2,1,0:T(8,128)S(1)}, f32[35,19,131]{2,1,0:T(8,128)S(1)}, f32[35,19,131]{2,1,0:T(8,128)S(1)}) fusion(f32[36,24,132]{2,1,0:T(8,128)S(1)} %get-tuple-element.23, f32[36,24,132]{2,1,0:T(8,128)S(1)} %get-tuple-element.27, f32[36,24,132]{2,1,0:T(8,128)S(1)} %get-tuple-element.22, pred[131]{0:T(512)(128)(4,1)S(1)} %compare_and_fusion.3, ...), kind=kLoop, calls=%fused_computation.26 | loop fusion | flops 1655185 | bytes 5227696 | tf_op jit(solution)/shard_map/mul | solution.py:106
  49.3 0.1 slice_bitcast_fusion.7
  49.5 0.1 slice_bitcast_fusion.8
  49.6 2.6 %fusion.35 = (f32[34,18,130]{2,1,0:T(8,128)S(1)}, f32[34,18,130]{2,1,0:T(8,128)S(1)}, f32[34,18,130]{2,1,0:T(8,128)S(1)}) fusion(f32[35,19,131]{2,1,0:T(8,128)S(1)} %get-tuple-element.39, f32[35,19,131]{2,1,0:T(8,128)S(1)} %get-tuple-element.40, f32[36,24,132]{2,1,0:T(8,128)S(1)} %get-tuple-element.27, f32[36,24,132]{2,1,0:T(8,128)S(1)} %get-tuple-element.26, ...), kind=kLoop, calls=%fused_computation.71 | loop fusion | flops 1272960 | bytes 5091840 | tf_op jit(solution)/shard_map/add | solution.py:108
  52.2 0.1 slice_bitcast_fusion.10
  52.4 1.4 %and_select_fusion.5 = (f32[33,17,129]{2,1,0:T(8,128)S(1)}, f32[33,17,129]{2,1,0:T(8,128)S(1)}, f32[33,17,129]{2,1,0:T(8,128)S(1)}) fusion(f32[34,18,130]{2,1,0:T(8,128)S(1)} %get-tuple-element.33, f32[34,18,130]{2,1,0:T(8,128)S(1)} %get-tuple-element.34, f32[35,19,131]{2,1,0:T(8,128)S(1)} %get-tuple-element.40, pred[129]{0:T(512)(128)(4,1)S(1)} %compare_and_fusion, ...), kind=kLoop, calls=%fused_computation.30 | loop fusion | flops 1375011 | bytes 4342830 | tf_op jit(solution)/shard_map/mul | solution.py:110
  53.7 0.1 slice_bitcast_fusion.11
  53.9 0.1 slice_bitcast_fusion.12
  54.0 0.9 %fusion.56 = (f32[1,32,16,128]{3,2,1,0:T(8,128)S(1)}, f32[1,32,16,128]{3,2,1,0:T(8,128)S(1)}, f32[1,32,16,128]{3,2,1,0:T(8,128)S(1)}, f32[1,32,16,128]{3,2,1,0:T(8,128)S(1)}) fusion(f32[33,17,129]{2,1,0:T(8,128)S(1)} %get-tuple-element.44, f32[33,17,129]{2,1,0:T(8,128)S(1)} %get-tuple-element.42, f32[34,18,130]{2,1,0:T(8,128)S(1)} %get-tuple-element.33, ...), kind=kLoop, calls=%fused_computation.109 | loop fusion | flops 1048576 | bytes 4456448 | tf_op jit(solution)/shard_map/stack | solution.py:144
  55.0 1.1 %slice_bitcast_fusion.13 = f32[1,32,16,128]{3,2,1,0:T(8,128)} fusion(f32[33,17,129]{2,1,0:T(8,128)S(1)} %get-tuple-element.42), kind=kLoop, calls=%fused_computation.116 | loop fusion | bytes 524288 | tf_op jit(solution)/shard_map/stack | solution.py:144
  56.1 1.2 %fusion = f32[4,4,32,16,128]{4,3,2,1,0:T(8,128)S(1)} fusion(f32[4,32,16,128]{3,2,1,0:T(8,128)S(1)} %pad_maximum_fusion.1, f32[4,128]{1,0:T(4,128)S(1)} %get-tuple-element.60), kind=kOutput, calls=%fused_computation | output fusion | flops 1056895 | bytes 5244928 | tf_op jit(solution)/shard_map/mul | solution.py:128
  57.4 1.5 %multiply_reduce_fusion.2 = (f32[4,32,16,128]{3,2,1,0:T(8,128)S(1)}, f32[4,32,16,128]{3,2,1,0:T(8,128)S(1)}) fusion(f32[4,128]{1,0:T(4,128)S(1)} %get-tuple-element.61, f32[4,4,32,16,128]{4,3,2,1,0:T(8,128)S(1)} %fusion, f32[4,128]{1,0:T(4,128)S(1)} %get-tuple-element.60, f32[4,32,16,128]{3,2,1,0:T(8,128)S(1)} %pad_maximum_fusion), kind=kOutput, calls=%fused_computation.6 | output fusion | flops 4726911 | bytes 7344128 | tf_op jit(solution)/shard_map/mul | solution.py:128
  58.9 0.2 multiply_add_fusion
  59.1 0.8 convolution_bitcast_fusion
  59.9 0.2 reshape.202
  60.1 0.1 reshape_reshape.3
  60.2 0.9 %copy.37 = f32[32,2,4]{2,1,0:T(2,128)} copy(f32[32,2,4]{1,0,2:T(8,128)S(1)} %reshape_reshape.3) | data formatting | bytes 2048 | tf_op jit(solution)/shard_map/reshape;reshape | solution.py:142
  61.1 9.4 %all-to-all-start = ((f32[32,2,4]{2,1,0:T(2,128)}), f32[32,2,4]{2,1,0:T(2,128)S(1)}, u32[]{:S(2)}, u32[]{:S(2)}) async-start(f32[32,2,4]{2,1,0:T(2,128)} %copy.37), calls=%async_computation | async-start | bytes 65536 | tf_op jit(solution)/shard_map/all_to_all | solution.py:143
  70.6 1.9 %pad_maximum_fusion.3 = f32[3,32,16,128]{3,2,1,0:T(8,128)} fusion(f32[1,32,16,128]{3,2,1,0:T(8,128)} %slice_bitcast_fusion.13, f32[1,32,16,128]{3,2,1,0:T(8,128)S(1)} %slice_bitcast_fusion.12, f32[1,32,16,128]{3,2,1,0:T(8,128)S(1)} %slice_bitcast_fusion.11), kind=kLoop, calls=%fused_computation.90 | loop fusion | flops 393216 | bytes 1572864 | tf_op jit(solution)/shard_map/stack | solution.py:144
  72.4 0.9 %pad_maximum_fusion.2 = f32[3,32,16,128]{3,2,1,0:T(8,128)} fusion(f32[1,32,16,128]{3,2,1,0:T(8,128)S(1)} %get-tuple-element.38, f32[1,32,16,128]{3,2,1,0:T(8,128)S(1)} %get-tuple-element.37, f32[1,32,16,128]{3,2,1,0:T(8,128)S(1)} %get-tuple-element.36), kind=kLoop, calls=%fused_computation.89 | loop fusion | flops 393216 | bytes 1572864 | tf_op jit(solution)/shard_map/stack | solution.py:144
  73.4 4.6 %all-to-all-done = f32[32,2,4]{2,1,0:T(2,128)S(1)} async-done(((f32[32,2,4]{2,1,0:T(2,128)}), f32[32,2,4]{2,1,0:T(2,128)S(1)}, u32[]{:S(2)}, u32[]{:S(2)}) %all-to-all-start) | async-done | bytes 1056 | tf_op jit(solution)/shard_map/all_to_all | solution.py:143
  78.0 0.1 copy.44
  78.1 0.7 copy.40
  (41 shorter events, 0.8 us)
Async XLA Ops:
  0.6 20.2 %copy-start = (bf16[4,2,4,256,64]{3,4,2,1,0:T(8,128)(2,1)S(1)}, bf16[4,2,4,256,64]{3,4,2,1,0:T(8,128)(2,1)}, u32[]{:S(2)}) copy-start(bf16[4,2,4,256,64]{3,4,2,1,0:T(8,128)(2,1)} %param.13) | copy-start | bytes 3145732
  0.6 23.6 %copy-start.6 = (f32[32,16,128]{2,1,0:T(8,128)S(1)}, f32[32,16,128]{2,1,0:T(8,128)}, u32[]{:S(2)}) copy-start(f32[32,16,128]{2,1,0:T(8,128)} %param.9) | copy-start | bytes 786436
  0.7 23.6 %copy-start.4 = (f32[3,32,16,128]{3,2,1,0:T(8,128)S(1)}, f32[3,32,16,128]{3,2,1,0:T(8,128)}, u32[]{:S(2)}) copy-start(f32[3,32,16,128]{3,2,1,0:T(8,128)} %param.7) | copy-start | bytes 2359300
  0.7 23.6 %copy-start.3 = (f32[3,32,16,128]{3,2,1,0:T(8,128)S(1)}, f32[3,32,16,128]{3,2,1,0:T(8,128)}, u32[]{:S(2)}) copy-start(f32[3,32,16,128]{3,2,1,0:T(8,128)} %param.8) | copy-start | bytes 2359300
  3.3 8.6 %collective-permute-start = (f32[7,32,2,128]{3,2,1,0:T(2,128)}, f32[7,32,2,128]{3,2,1,0:T(2,128)S(1)}, u32[]{:S(2)}, u32[]{:S(2)}) collective-permute-start(f32[7,32,2,128]{3,2,1,0:T(2,128)} %get-tuple-element.31), channel_id=1, source_target_pairs={{0,8},{8,16},{16,24},{1,9},{9,17},{17,25},{2,10},{10,18},{18,26},{... | collective-permute-start | bytes 688136 | tf_op jit(solution)/shard_map/ppermute | solution.py:21
  6.7 9.2 %collective-permute-start.1 = (f32[7,32,2,128]{3,2,1,0:T(2,128)}, f32[7,32,2,128]{3,2,1,0:T(2,128)S(1)}, u32[]{:S(2)}, u32[]{:S(2)}) collective-permute-start(f32[7,32,2,128]{3,2,1,0:T(2,128)} %get-tuple-element.32), channel_id=1, source_target_pairs={{8,0},{16,8},{24,16},{9,1},{17,9},{25,17},{10,2},{18,10},{26,18},{... | collective-permute-start | bytes 688136 | tf_op jit(solution)/shard_map/ppermute | solution.py:21
  17.6 3.4 %collective-permute-start.2 = (f32[7,2,20,128]{3,2,1,0:T(8,128)}, f32[7,2,20,128]{3,2,1,0:T(8,128)}, u32[]{:S(2)}, u32[]{:S(2)}) collective-permute-start(f32[7,2,20,128]{3,2,1,0:T(8,128)} %get-tuple-element.29), channel_id=1, source_target_pairs={{0,32},{32,64},{64,96},{96,128},{128,160},{160,192},{192,224},{1,3... | collective-permute-start | bytes 430088 | tf_op jit(solution)/shard_map/ppermute | solution.py:21
  19.5 4.7 %collective-permute-start.3 = (f32[7,2,20,128]{3,2,1,0:T(8,128)}, f32[7,2,20,128]{3,2,1,0:T(8,128)}, u32[]{:S(2)}, u32[]{:S(2)}) collective-permute-start(f32[7,2,20,128]{3,2,1,0:T(8,128)} %get-tuple-element.30), channel_id=1, source_target_pairs={{32,0},{64,32},{96,64},{128,96},{160,128},{192,160},{224,192},{33,... | collective-permute-start | bytes 430088 | tf_op jit(solution)/shard_map/ppermute | solution.py:21
  26.7 1.6 %copy-start.1 = (f32[7,36,24,128]{3,2,1,0:T(8,128)}, f32[7,36,24,128]{3,2,1,0:T(8,128)S(1)}, u32[]{:S(2)}) copy-start(f32[7,36,24,128]{3,2,1,0:T(8,128)S(1)} %select_maximum_fusion) | copy-start | bytes 9289732
  29.9 7.6 %collective-permute-start.4 = (f32[2,6048]{1,0:T(2,128)S(1)}, f32[2,6048]{1,0:T(2,128)S(1)}, u32[]{:S(2)}, u32[]{:S(2)}) collective-permute-start(f32[2,6048]{1,0:T(2,128)S(1)} %get-tuple-element.50), channel_id=1, source_target_pairs={{0,1},{1,2},{2,3},{3,4},{4,5},{5,6},{6,7},{8,9},{9,10},{10,11},{11... | collective-permute-start | bytes 145160 | tf_op jit(solution)/shard_map/ppermute | solution.py:21
  34.9 7.2 %collective-permute-start.5 = (f32[2,6048]{1,0:T(2,128)S(1)}, f32[2,6048]{1,0:T(2,128)S(1)}, u32[]{:S(2)}, u32[]{:S(2)}) collective-permute-start(f32[2,6048]{1,0:T(2,128)S(1)} %get-tuple-element.51), channel_id=1, source_target_pairs={{1,0},{2,1},{3,2},{4,3},{5,4},{6,5},{7,6},{9,8},{10,9},{11,10},{12... | collective-permute-start | bytes 145160 | tf_op jit(solution)/shard_map/ppermute | solution.py:21
  42.1 2.7 %copy-start.2 = (f32[7,36,24,128]{3,2,1,0:T(8,128)S(1)}, f32[7,36,24,128]{3,2,1,0:T(8,128)}, u32[]{:S(2)}) copy-start(f32[7,36,24,128]{3,2,1,0:T(8,128)} %copy-done.1) | copy-start | bytes 9289732
  57.4 1.5 %copy-start.7 = (f32[4,32,16,128]{3,2,1,0:T(8,128)S(1)}, f32[4,32,16,128]{3,2,1,0:T(8,128)}, u32[]{:S(2)}) copy-start(f32[4,32,16,128]{3,2,1,0:T(8,128)} %param.10) | copy-start | bytes 3145732
  59.1 19.6 %copy-start.5 = (f32[4,32,16,128]{3,2,1,0:T(8,128)}, f32[4,32,16,128]{3,2,1,0:T(8,128)S(1)}, u32[]{:S(2)}) copy-start(f32[4,32,16,128]{3,2,1,0:T(8,128)S(1)} %multiply_add_fusion) | copy-start | bytes 3145732
  61.1 16.8 %all-to-all-start = ((f32[32,2,4]{2,1,0:T(2,128)}), f32[32,2,4]{2,1,0:T(2,128)S(1)}, u32[]{:S(2)}, u32[]{:S(2)}) async-start(f32[32,2,4]{2,1,0:T(2,128)} %copy.37), calls=%async_computation | async-start | bytes 65536 | tf_op jit(solution)/shard_map/all_to_all | solution.py:143

commit v14 on v12

--- a/solution.py
+++ b/solution.py
@@ -36,7 +36,7 @@
     lane = jnp.arange(lanes)
     edges = jnp.concatenate([jnp.arange(HALO), jnp.arange(lanes - HALO, lanes)])
     pick = (lane[None, :] == edges[:, None]).astype(jnp.float32)
-    faces = jnp.einsum("kz,rz->kr", pick, flat, precision=lax.Precision.HIGHEST)
+    faces = jnp.einsum("kz,rz->kr", pick, flat, precision=lax.Precision.HIGH)
     from_above = shifted(faces[:HALO], axis, -1)
     from_below = shifted(faces[HALO:], axis, 1)
     ghosts = jnp.concatenate([from_below, from_above], axis=0)
@@ -44,8 +44,8 @@
     spots = jnp.concatenate([jnp.arange(HALO), jnp.arange(lanes + HALO, lanes + 2 * HALO)])
     move = (out[None, :] == lane[:, None] + HALO).astype(jnp.float32)
     place = (out[None, :] == spots[:, None]).astype(jnp.float32)
-    wide = jnp.dot(flat, move, precision=lax.Precision.HIGHEST) + jnp.einsum(
-        "kr,kl->rl", ghosts, place, precision=lax.Precision.HIGHEST
+    wide = jnp.dot(flat, move, precision=lax.Precision.HIGH) + jnp.einsum(
+        "kr,kl->rl", ghosts, place, precision=lax.Precision.HIGH
     )
     return wide.reshape(stack.shape[:-1] + (lanes + 2 * HALO,))
 

time: 79.7 us -> 77.3 us (0.970)
  matrix products: 8.02 us -> 5.58 us
    dot_general x3, matrix products: 7.04 us -> 4.6 us  [the longest x1 1.83 us: widen_lanes(): jnp.dot(flat, move, precision=lax.Precision.HIGH)]
  transfers between devices with their start and end apart: 7 -> 7, of which waited for: 5 -> 5; matrix products, arithmetic and copies ran while one was open for 6% -> 7% of each run, Pallas kernels for 0% -> 0%
where the time goes in v14:
time: 77.3 us; the launch traced here: 76.6 us
  starting transfers between devices  24.6 us (32%)
  other arithmetic  20.5 us (27%)
  waiting for transfers between devices  18.5 us (24%)
  local copies, waits for them, and re-layouts  6.35 us (8%)
  matrix products  5.58 us (7%)
  between operations  1.04 us (1%)
    ppermute x6, starting transfers between devices, shifted(): lax.ppermute(value, axis, [(source, source + steps) for source in range(f...  15.1 us
    ppermute x6, waiting for transfers between devices, shifted(): lax.ppermute(value, axis, [(source, source + steps) for source in range(f...  14 us
    all_to_all x1, starting transfers between devices, per_device(): lax.all_to_all(pieces, ('gx', 'gy'), 0, 0, tiled=False)  9.42 us
    all_to_all x1, waiting for transfers between devices, per_device(): lax.all_to_all(pieces, ('gx', 'gy'), 0, 0, tiled=False)  4.57 us
    slice x2, other arithmetic, widen(): high = lax.slice_in_dim(stack, count - HALO, count, axis=dim)  4.26 us
    mul x2, other arithmetic, per_device(): planes[..., None] * spread_of[None, :, None, None, :]  2.88 us
    add x1, other arithmetic, per_device(): at(v, 1, n(2)) + scale * c  2.58 us
    unnamed x18, local copies, waits for them, and re-layouts  2.46 us
  transfers between devices with their start and end apart: 7, of which 5 were waited for; matrix products, arithmetic and copies ran while one was open for 7% of the time, Pallas kernels for 0%

profile of v14, /device:TPU:96, one launch (start us, length us, event | category | flops | bytes accessed | tf_op | source)
XLA Modules:
  0.0 76.6 jit_solution(7422747236009528120)
XLA Ops:
  0.7 2.6 %pad_maximum_fusion.6 = (f32[7,32,2,128]{3,2,1,0:T(2,128)}, f32[7,32,2,128]{3,2,1,0:T(2,128)}) fusion(f32[1,32,16,128]{3,2,1,0:T(8,128)} %bitcast.62, f32[3,32,16,128]{3,2,1,0:T(8,128)} %param.8, f32[3,32,16,128]{3,2,1,0:T(8,128)} %param.7), kind=kLoop, calls=%fused_computation.119 | loop fusion | flops 229376 | bytes 2293760 | tf_op jit(solution)/shard_map/slice | solution.py:27
  3.3 3.5 %collective-permute-start = (f32[7,32,2,128]{3,2,1,0:T(2,128)}, f32[7,32,2,128]{3,2,1,0:T(2,128)S(1)}, u32[]{:S(2)}, u32[]{:S(2)}) collective-permute-start(f32[7,32,2,128]{3,2,1,0:T(2,128)} %get-tuple-element.31), channel_id=1, source_target_pairs={{0,8},{8,16},{16,24},{1,9},{9,17},{17,25},{2,10},{10,18},{18,26},{... | collective-permute-start | bytes 688136 | tf_op jit(solution)/shard_map/ppermute | solution.py:21
  6.7 1.3 %collective-permute-start.1 = (f32[7,32,2,128]{3,2,1,0:T(2,128)}, f32[7,32,2,128]{3,2,1,0:T(2,128)S(1)}, u32[]{:S(2)}, u32[]{:S(2)}) collective-permute-start(f32[7,32,2,128]{3,2,1,0:T(2,128)} %get-tuple-element.32), channel_id=1, source_target_pairs={{8,0},{16,8},{24,16},{9,1},{17,9},{25,17},{10,2},{18,10},{26,18},{... | collective-permute-start | bytes 688136 | tf_op jit(solution)/shard_map/ppermute | solution.py:21
  8.1 0.7 cosine_bitcast_fusion.1
  8.9 0.7 broadcast_subtract_fusion
  9.8 2.0 %collective-permute-done = f32[7,32,2,128]{3,2,1,0:T(2,128)S(1)} collective-permute-done((f32[7,32,2,128]{3,2,1,0:T(2,128)}, f32[7,32,2,128]{3,2,1,0:T(2,128)S(1)}, u32[]{:S(2)}, u32[]{:S(2)}) %collective-permute-start) | collective-permute-done | bytes 229408 | tf_op jit(solution)/shard_map/ppermute | solution.py:21
  11.9 4.0 %collective-permute-done.1 = f32[7,32,2,128]{3,2,1,0:T(2,128)S(1)} collective-permute-done((f32[7,32,2,128]{3,2,1,0:T(2,128)}, f32[7,32,2,128]{3,2,1,0:T(2,128)S(1)}, u32[]{:S(2)}, u32[]{:S(2)}) %collective-permute-start.1) | collective-permute-done | bytes 229408 | tf_op jit(solution)/shard_map/ppermute | solution.py:21
  15.9 1.7 %pad_maximum_fusion.11 = (f32[7,2,20,128]{3,2,1,0:T(8,128)}, f32[7,2,20,128]{3,2,1,0:T(8,128)}) fusion(f32[7,32,2,128]{3,2,1,0:T(2,128)S(1)} %collective-permute-done.1, f32[7,32,2,128]{3,2,1,0:T(2,128)S(1)} %collective-permute-done, f32[1,32,16,128]{3,2,1,0:T(8,128)} %bitcast.63, f32[3,32,16,128]{3,2,1,0:T(8,128)} %param.8, f32[3,32,16,128]{3,2,1,0:T(8,128)} %param.7), kind=kLoop, calls=%fused_computation.124 | loop fusion | flops 286720 | bytes 2580480 | tf_op jit(solution)/shard_map/slice | solution.py:27
  17.6 2.0 %collective-permute-start.2 = (f32[7,2,20,128]{3,2,1,0:T(8,128)}, f32[7,2,20,128]{3,2,1,0:T(8,128)}, u32[]{:S(2)}, u32[]{:S(2)}) collective-permute-start(f32[7,2,20,128]{3,2,1,0:T(8,128)} %get-tuple-element.29), channel_id=1, source_target_pairs={{0,32},{32,64},{64,96},{96,128},{128,160},{160,192},{192,224},{1,3... | collective-permute-start | bytes 430088 | tf_op jit(solution)/shard_map/ppermute | solution.py:21
  19.5 1.3 %collective-permute-start.3 = (f32[7,2,20,128]{3,2,1,0:T(8,128)}, f32[7,2,20,128]{3,2,1,0:T(8,128)}, u32[]{:S(2)}, u32[]{:S(2)}) collective-permute-start(f32[7,2,20,128]{3,2,1,0:T(8,128)} %get-tuple-element.30), channel_id=1, source_target_pairs={{32,0},{64,32},{96,64},{128,96},{160,128},{192,160},{224,192},{33,... | collective-permute-start | bytes 430088 | tf_op jit(solution)/shard_map/ppermute | solution.py:21
  20.9 0.1 constant_dynamic-slice_fusion
  21.0 3.3 %collective-permute-done.3 = f32[7,2,20,128]{3,2,1,0:T(8,128)} collective-permute-done((f32[7,2,20,128]{3,2,1,0:T(8,128)}, f32[7,2,20,128]{3,2,1,0:T(8,128)}, u32[]{:S(2)}, u32[]{:S(2)}) %collective-permute-start.3) | collective-permute-done | bytes 143392 | tf_op jit(solution)/shard_map/ppermute | solution.py:21
  24.3 2.4 %select_maximum_fusion = f32[7,36,24,128]{3,2,1,0:T(8,128)S(1)} fusion(f32[7,2,20,128]{3,2,1,0:T(8,128)} %collective-permute-done.3, f32[7,2,20,128]{3,2,1,0:T(8,128)} %collective-permute-done.2, f32[7,32,2,128]{3,2,1,0:T(2,128)S(1)} %collective-permute-done.1, f32[7,32,2,128]{3,2,1,0:T(2,128)S(1)} %collective-permute-done, ...), kind=kLoop, calls=%fused_computation.9 | loop fusion | flops 10838016 | bytes 5677056 | tf_op jit(solution)/shard_map/concatenate | solution.py:30
  26.7 1.6 %copy-done.1 = f32[7,36,24,128]{3,2,1,0:T(8,128)} copy-done((f32[7,36,24,128]{3,2,1,0:T(8,128)}, f32[7,36,24,128]{3,2,1,0:T(8,128)S(1)}, u32[]{:S(2)}) %copy-start.1) | copy-done | bytes 3096600
  28.3 1.0 %fusion.64 = f32[4,6048]{1,0:T(4,128)S(1)} fusion(f32[6048,128]{1,0:T(8,128)S(1)} %bitcast.59, s32[4]{0:T(128)S(1)} %get-tuple-element.57), kind=kOutput, calls=%fused_computation.142 | convolution fusion | flops 18579968 | bytes 3193360 | tf_op jit(solution)/shard_map/kz,rz->kr/dot_general | solution.py:39
  29.3 5.0 %collective-permute-start.4 = (f32[2,6048]{1,0:T(2,128)S(1)}, f32[2,6048]{1,0:T(2,128)S(1)}, u32[]{:S(2)}, u32[]{:S(2)}) collective-permute-start(f32[2,6048]{1,0:T(2,128)S(1)} %get-tuple-element.50), channel_id=1, source_target_pairs={{0,1},{1,2},{2,3},{3,4},{4,5},{5,6},{6,7},{8,9},{9,10},{10,11},{11... | collective-permute-start | bytes 145160 | tf_op jit(solution)/shard_map/ppermute | solution.py:21
  34.4 2.1 %collective-permute-start.5 = (f32[2,6048]{1,0:T(2,128)S(1)}, f32[2,6048]{1,0:T(2,128)S(1)}, u32[]{:S(2)}, u32[]{:S(2)}) collective-permute-start(f32[2,6048]{1,0:T(2,128)S(1)} %get-tuple-element.51), channel_id=1, source_target_pairs={{1,0},{2,1},{3,2},{4,3},{5,4},{6,5},{7,6},{9,8},{10,9},{11,10},{12... | collective-permute-start | bytes 145160 | tf_op jit(solution)/shard_map/ppermute | solution.py:21
  36.5 0.1 tile.14
  36.6 0.1 mul.185
  36.7 0.1 tile.16
  36.8 0.1 mul.193
  36.9 4.7 %collective-permute-done.5 = f32[2,6048]{1,0:T(2,128)S(1)} collective-permute-done((f32[2,6048]{1,0:T(2,128)S(1)}, f32[2,6048]{1,0:T(2,128)S(1)}, u32[]{:S(2)}, u32[]{:S(2)}) %collective-permute-start.5) | collective-permute-done | bytes 48416 | tf_op jit(solution)/shard_map/ppermute | solution.py:21
  41.6 1.8 %fusion.57 = f32[6048,132]{1,0:T(8,128)S(1)} fusion(f32[2,6048]{1,0:T(2,128)S(1)} %collective-permute-done.5, f32[2,6048]{1,0:T(2,128)S(1)} %collective-permute-done.4, s32[4]{0:T(128)S(1)} %get-tuple-element.56), kind=kOutput, calls=%fused_computation.126 | convolution fusion | flops 19184784 | bytes 3290128 | tf_op jit(solution)/shard_map/kr,kl->rl/dot_general | solution.py:47
  43.5 1.8 %convolution_add_fusion = f32[6048,132]{1,0:T(8,128)S(1)} fusion(f32[6048,132]{1,0:T(8,128)S(1)} %fusion.57, f32[6048,128]{1,0:T(8,128)S(1)} %bitcast.60, s32[128]{0:T(128)S(1)} %iota_add_fusion.2), kind=kOutput, calls=%fused_computation.2 | convolution fusion | flops 613937280 | bytes 9483776 | tf_op jit(solution)/shard_map/dot_general | solution.py:47
  45.3 0.6 slice_bitcast_fusion.2
  45.9 1.1 %and_select_fusion.1 = (f32[35,19,131]{2,1,0:T(8,128)S(1)}, f32[35,19,131]{2,1,0:T(8,128)S(1)}, f32[35,19,131]{2,1,0:T(8,128)S(1)}) fusion(f32[36,24,132]{2,1,0:T(8,128)S(1)} %get-tuple-element.23, f32[36,24,132]{2,1,0:T(8,128)S(1)} %get-tuple-element.27, f32[36,24,132]{2,1,0:T(8,128)S(1)} %get-tuple-element.22, pred[131]{0:T(512)(128)(4,1)S(1)} %compare_and_fusion.3, ...), kind=kLoop, calls=%fused_computation.26 | loop fusion | flops 1655185 | bytes 5227696 | tf_op jit(solution)/shard_map/mul | solution.py:106
  47.0 0.1 slice_bitcast_fusion.7
  47.1 0.1 slice_bitcast_fusion.8
  47.2 2.6 %fusion.35 = (f32[34,18,130]{2,1,0:T(8,128)S(1)}, f32[34,18,130]{2,1,0:T(8,128)S(1)}, f32[34,18,130]{2,1,0:T(8,128)S(1)}) fusion(f32[35,19,131]{2,1,0:T(8,128)S(1)} %get-tuple-element.39, f32[35,19,131]{2,1,0:T(8,128)S(1)} %get-tuple-element.40, f32[36,24,132]{2,1,0:T(8,128)S(1)} %get-tuple-element.27, f32[36,24,132]{2,1,0:T(8,128)S(1)} %get-tuple-element.26, ...), kind=kLoop, calls=%fused_computation.71 | loop fusion | flops 1272960 | bytes 5091840 | tf_op jit(solution)/shard_map/add | solution.py:108
  49.8 0.1 slice_bitcast_fusion.10
  50.0 1.4 %and_select_fusion.5 = (f32[33,17,129]{2,1,0:T(8,128)S(1)}, f32[33,17,129]{2,1,0:T(8,128)S(1)}, f32[33,17,129]{2,1,0:T(8,128)S(1)}) fusion(f32[34,18,130]{2,1,0:T(8,128)S(1)} %get-tuple-element.33, f32[34,18,130]{2,1,0:T(8,128)S(1)} %get-tuple-element.34, f32[35,19,131]{2,1,0:T(8,128)S(1)} %get-tuple-element.40, pred[129]{0:T(512)(128)(4,1)S(1)} %compare_and_fusion, ...), kind=kLoop, calls=%fused_computation.30 | loop fusion | flops 1375011 | bytes 4342830 | tf_op jit(solution)/shard_map/mul | solution.py:110
  51.3 0.1 slice_bitcast_fusion.11
  51.5 0.1 slice_bitcast_fusion.12
  51.6 0.9 %fusion.56 = (f32[1,32,16,128]{3,2,1,0:T(8,128)S(1)}, f32[1,32,16,128]{3,2,1,0:T(8,128)S(1)}, f32[1,32,16,128]{3,2,1,0:T(8,128)S(1)}, f32[1,32,16,128]{3,2,1,0:T(8,128)S(1)}) fusion(f32[33,17,129]{2,1,0:T(8,128)S(1)} %get-tuple-element.44, f32[33,17,129]{2,1,0:T(8,128)S(1)} %get-tuple-element.42, f32[34,18,130]{2,1,0:T(8,128)S(1)} %get-tuple-element.33, ...), kind=kLoop, calls=%fused_computation.109 | loop fusion | flops 1048576 | bytes 4456448 | tf_op jit(solution)/shard_map/stack | solution.py:144
  52.6 0.8 %slice_bitcast_fusion.13 = f32[1,32,16,128]{3,2,1,0:T(8,128)} fusion(f32[33,17,129]{2,1,0:T(8,128)S(1)} %get-tuple-element.42), kind=kLoop, calls=%fused_computation.116 | loop fusion | bytes 524288 | tf_op jit(solution)/shard_map/stack | solution.py:144
  53.5 1.2 %fusion = f32[4,4,32,16,128]{4,3,2,1,0:T(8,128)S(1)} fusion(f32[4,32,16,128]{3,2,1,0:T(8,128)S(1)} %pad_maximum_fusion.1, f32[4,128]{1,0:T(4,128)S(1)} %get-tuple-element.60), kind=kOutput, calls=%fused_computation | output fusion | flops 1056895 | bytes 5244928 | tf_op jit(solution)/shard_map/mul | solution.py:128
  54.8 1.7 %multiply_reduce_fusion.2 = (f32[4,32,16,128]{3,2,1,0:T(8,128)S(1)}, f32[4,32,16,128]{3,2,1,0:T(8,128)S(1)}) fusion(f32[4,128]{1,0:T(4,128)S(1)} %get-tuple-element.61, f32[4,4,32,16,128]{4,3,2,1,0:T(8,128)S(1)} %fusion, f32[4,128]{1,0:T(4,128)S(1)} %get-tuple-element.60, f32[4,32,16,128]{3,2,1,0:T(8,128)S(1)} %pad_maximum_fusion), kind=kOutput, calls=%fused_computation.6 | output fusion | flops 4726911 | bytes 7344128 | tf_op jit(solution)/shard_map/mul | solution.py:128
  56.5 0.2 multiply_add_fusion
  56.7 1.0 %convolution_bitcast_fusion = f32[4,8,128]{2,1,0:T(8,128)S(1)} fusion(bf16[4,8,32,16]{2,1,3,0:T(8,128)(2,1)S(1)} %bitcast.65, f32[4,32,16,128]{3,2,1,0:T(8,128)S(1)} %multiply_add_fusion), kind=kOutput, calls=%fused_computation.31 | convolution fusion | flops 25165824 | bytes 1097728 | tf_op jit(solution)/shard_map/pxyl,pnxy->pnl/dot_general | solution.py:138
  57.7 0.2 reshape.202
  58.0 0.1 reshape_reshape.3
  58.1 0.9 %copy.37 = f32[32,2,4]{2,1,0:T(2,128)} copy(f32[32,2,4]{1,0,2:T(8,128)S(1)} %reshape_reshape.3) | data formatting | bytes 2048 | tf_op jit(solution)/shard_map/reshape;reshape | solution.py:142
  59.0 9.4 %all-to-all-start = ((f32[32,2,4]{2,1,0:T(2,128)}), f32[32,2,4]{2,1,0:T(2,128)S(1)}, u32[]{:S(2)}, u32[]{:S(2)}) async-start(f32[32,2,4]{2,1,0:T(2,128)} %copy.37), calls=%async_computation | async-start | bytes 65536 | tf_op jit(solution)/shard_map/all_to_all | solution.py:143
  68.4 1.9 %pad_maximum_fusion.3 = f32[3,32,16,128]{3,2,1,0:T(8,128)} fusion(f32[1,32,16,128]{3,2,1,0:T(8,128)} %slice_bitcast_fusion.13, f32[1,32,16,128]{3,2,1,0:T(8,128)S(1)} %slice_bitcast_fusion.12, f32[1,32,16,128]{3,2,1,0:T(8,128)S(1)} %slice_bitcast_fusion.11), kind=kLoop, calls=%fused_computation.90 | loop fusion | flops 393216 | bytes 1572864 | tf_op jit(solution)/shard_map/stack | solution.py:144
  70.3 0.9 %pad_maximum_fusion.2 = f32[3,32,16,128]{3,2,1,0:T(8,128)} fusion(f32[1,32,16,128]{3,2,1,0:T(8,128)S(1)} %get-tuple-element.38, f32[1,32,16,128]{3,2,1,0:T(8,128)S(1)} %get-tuple-element.37, f32[1,32,16,128]{3,2,1,0:T(8,128)S(1)} %get-tuple-element.36), kind=kLoop, calls=%fused_computation.89 | loop fusion | flops 393216 | bytes 1572864 | tf_op jit(solution)/shard_map/stack | solution.py:144
  71.2 4.6 %all-to-all-done = f32[32,2,4]{2,1,0:T(2,128)S(1)} async-done(((f32[32,2,4]{2,1,0:T(2,128)}), f32[32,2,4]{2,1,0:T(2,128)S(1)}, u32[]{:S(2)}, u32[]{:S(2)}) %all-to-all-start) | async-done | bytes 1056 | tf_op jit(solution)/shard_map/all_to_all | solution.py:143
  75.8 0.1 copy.44
  75.9 0.7 copy.40
  (41 shorter events, 0.8 us)
Async XLA Ops:
  0.6 20.2 %copy-start = (bf16[4,2,4,256,64]{3,4,2,1,0:T(8,128)(2,1)S(1)}, bf16[4,2,4,256,64]{3,4,2,1,0:T(8,128)(2,1)}, u32[]{:S(2)}) copy-start(bf16[4,2,4,256,64]{3,4,2,1,0:T(8,128)(2,1)} %param.13) | copy-start | bytes 3145732
  0.6 23.6 %copy-start.6 = (f32[32,16,128]{2,1,0:T(8,128)S(1)}, f32[32,16,128]{2,1,0:T(8,128)}, u32[]{:S(2)}) copy-start(f32[32,16,128]{2,1,0:T(8,128)} %param.9) | copy-start | bytes 786436
  0.7 23.6 %copy-start.4 = (f32[3,32,16,128]{3,2,1,0:T(8,128)S(1)}, f32[3,32,16,128]{3,2,1,0:T(8,128)}, u32[]{:S(2)}) copy-start(f32[3,32,16,128]{3,2,1,0:T(8,128)} %param.7) | copy-start | bytes 2359300
  0.7 23.6 %copy-start.3 = (f32[3,32,16,128]{3,2,1,0:T(8,128)S(1)}, f32[3,32,16,128]{3,2,1,0:T(8,128)}, u32[]{:S(2)}) copy-start(f32[3,32,16,128]{3,2,1,0:T(8,128)} %param.8) | copy-start | bytes 2359300
  3.3 8.6 %collective-permute-start = (f32[7,32,2,128]{3,2,1,0:T(2,128)}, f32[7,32,2,128]{3,2,1,0:T(2,128)S(1)}, u32[]{:S(2)}, u32[]{:S(2)}) collective-permute-start(f32[7,32,2,128]{3,2,1,0:T(2,128)} %get-tuple-element.31), channel_id=1, source_target_pairs={{0,8},{8,16},{16,24},{1,9},{9,17},{17,25},{2,10},{10,18},{18,26},{... | collective-permute-start | bytes 688136 | tf_op jit(solution)/shard_map/ppermute | solution.py:21
  6.7 9.2 %collective-permute-start.1 = (f32[7,32,2,128]{3,2,1,0:T(2,128)}, f32[7,32,2,128]{3,2,1,0:T(2,128)S(1)}, u32[]{:S(2)}, u32[]{:S(2)}) collective-permute-start(f32[7,32,2,128]{3,2,1,0:T(2,128)} %get-tuple-element.32), channel_id=1, source_target_pairs={{8,0},{16,8},{24,16},{9,1},{17,9},{25,17},{10,2},{18,10},{26,18},{... | collective-permute-start | bytes 688136 | tf_op jit(solution)/shard_map/ppermute | solution.py:21
  17.6 3.4 %collective-permute-start.2 = (f32[7,2,20,128]{3,2,1,0:T(8,128)}, f32[7,2,20,128]{3,2,1,0:T(8,128)}, u32[]{:S(2)}, u32[]{:S(2)}) collective-permute-start(f32[7,2,20,128]{3,2,1,0:T(8,128)} %get-tuple-element.29), channel_id=1, source_target_pairs={{0,32},{32,64},{64,96},{96,128},{128,160},{160,192},{192,224},{1,3... | collective-permute-start | bytes 430088 | tf_op jit(solution)/shard_map/ppermute | solution.py:21
  19.5 4.7 %collective-permute-start.3 = (f32[7,2,20,128]{3,2,1,0:T(8,128)}, f32[7,2,20,128]{3,2,1,0:T(8,128)}, u32[]{:S(2)}, u32[]{:S(2)}) collective-permute-start(f32[7,2,20,128]{3,2,1,0:T(8,128)} %get-tuple-element.30), channel_id=1, source_target_pairs={{32,0},{64,32},{96,64},{128,96},{160,128},{192,160},{224,192},{33,... | collective-permute-start | bytes 430088 | tf_op jit(solution)/shard_map/ppermute | solution.py:21
  26.7 1.6 %copy-start.1 = (f32[7,36,24,128]{3,2,1,0:T(8,128)}, f32[7,36,24,128]{3,2,1,0:T(8,128)S(1)}, u32[]{:S(2)}) copy-start(f32[7,36,24,128]{3,2,1,0:T(8,128)S(1)} %select_maximum_fusion) | copy-start | bytes 9289732
  29.3 7.6 %collective-permute-start.4 = (f32[2,6048]{1,0:T(2,128)S(1)}, f32[2,6048]{1,0:T(2,128)S(1)}, u32[]{:S(2)}, u32[]{:S(2)}) collective-permute-start(f32[2,6048]{1,0:T(2,128)S(1)} %get-tuple-element.50), channel_id=1, source_target_pairs={{0,1},{1,2},{2,3},{3,4},{4,5},{5,6},{6,7},{8,9},{9,10},{10,11},{11... | collective-permute-start | bytes 145160 | tf_op jit(solution)/shard_map/ppermute | solution.py:21
  34.4 7.2 %collective-permute-start.5 = (f32[2,6048]{1,0:T(2,128)S(1)}, f32[2,6048]{1,0:T(2,128)S(1)}, u32[]{:S(2)}, u32[]{:S(2)}) collective-permute-start(f32[2,6048]{1,0:T(2,128)S(1)} %get-tuple-element.51), channel_id=1, source_target_pairs={{1,0},{2,1},{3,2},{4,3},{5,4},{6,5},{7,6},{9,8},{10,9},{11,10},{12... | collective-permute-start | bytes 145160 | tf_op jit(solution)/shard_map/ppermute | solution.py:21
  41.6 1.9 %copy-start.2 = (f32[7,36,24,128]{3,2,1,0:T(8,128)S(1)}, f32[7,36,24,128]{3,2,1,0:T(8,128)}, u32[]{:S(2)}) copy-start(f32[7,36,24,128]{3,2,1,0:T(8,128)} %copy-done.1) | copy-start | bytes 9289732
  54.7 1.7 %copy-start.7 = (f32[4,32,16,128]{3,2,1,0:T(8,128)S(1)}, f32[4,32,16,128]{3,2,1,0:T(8,128)}, u32[]{:S(2)}) copy-start(f32[4,32,16,128]{3,2,1,0:T(8,128)} %param.10) | copy-start | bytes 3145732
  56.7 19.8 %copy-start.5 = (f32[4,32,16,128]{3,2,1,0:T(8,128)}, f32[4,32,16,128]{3,2,1,0:T(8,128)S(1)}, u32[]{:S(2)}) copy-start(f32[4,32,16,128]{3,2,1,0:T(8,128)S(1)} %multiply_add_fusion) | copy-start | bytes 3145732
  59.0 16.8 %all-to-all-start = ((f32[32,2,4]{2,1,0:T(2,128)}), f32[32,2,4]{2,1,0:T(2,128)S(1)}, u32[]{:S(2)}, u32[]{:S(2)}) async-start(f32[32,2,4]{2,1,0:T(2,128)} %copy.37), calls=%async_computation | async-start | bytes 65536 | tf_op jit(solution)/shard_map/all_to_all | solution.py:143
